TPU v7x, 512 devices: a whole 4x8x8 slice. The times are simulated.
512 devices in a mesh: fsdp: 64 (over y, x, core), tp: 8 (over z).
Axes of the slice: x: 4, y: 8, z: 8, core: 2. Of those that a mesh axis runs over, the one named last changes fastest.
Arguments:
- grads: bfloat16 [2, 12288, 2560], P(None, 'fsdp', 'tp'), may hold values from -16 to 16
- weights: float32 [2, 12288, 2560], P(None, 'fsdp', 'tp'), may hold values from -0.3 to 0.3
- basis: bfloat16 [2560, 2, 256], P('tp'), may hold values from -0.375 to 0.375
- first_moment: float32 [2, 12288, 256], P(None, 'fsdp', 'tp'), may hold values from -12 to 12
- second_moment: float32 [2, 12288, 256], P(None, 'fsdp', 'tp'), may hold values from 0.05 to 5
Outputs:
- weight_next: float32 [2, 12288, 2560], P(None, 'fsdp', 'tp')
- first_next: float32 [2, 12288, 256], P(None, 'fsdp', 'tp')
- second_next: float32 [2, 12288, 256], P(None, 'fsdp', 'tp')
- basis_next: bfloat16 [2560, 2, 256], P('tp')
All inputs are finite; a program needn't handle non-finite values.
Results may differ from a plain program's by a relative error of at most 0.0034.
Values may be sent and summed in bfloat16 or wider, within the bound.
No kernel may reach another device: no remote copies, remote signals or barrier semaphores. Data moves between devices by JAX's collectives and lax.ppermute only.
A program may use at most 64 MiB of HBM per device.

v0:
```python
import jax
import jax.numpy as jnp
from jax import lax
from jax.sharding import PartitionSpec as P

D = 2560


BETA_FIRST = 0.9
BETA_SECOND = 0.999
BIAS_FIRST = 0.9999734386011124
BIAS_SECOND = 0.0952078528862904
EPSILON = 1e-08
EPSILON_NORM = 1e-06
LEARNING_RATE = 0.1
GALORE_SCALE = 0.25


def adam_share(grad_share, first_moment, second_moment):
    first_next = BETA_FIRST * first_moment + (1.0 - BETA_FIRST) * grad_share
    second_next = BETA_SECOND * second_moment + (1.0 - BETA_SECOND) * grad_share * grad_share
    normal = first_next / BIAS_FIRST / (jnp.sqrt(second_next / BIAS_SECOND) + EPSILON)
    return (first_next, second_next, normal.astype(jnp.bfloat16))


def rebuild(image, sum_total, sum_cross):
    highest = lax.Precision.HIGHEST
    rank_width = image.shape[2]
    total = sum_total(jnp.sum(image * image, axis=(0, 2))) + EPSILON_NORM
    scaled = image * jnp.sqrt(rank_width / total)[None, :, None]
    cross = sum_cross(jnp.einsum("dmr,dms->mrs", scaled, scaled, precision=highest))
    shaped = 1.5 * scaled - 0.5 * jnp.einsum("dmr,mrs->dms", scaled, cross, precision=highest)
    return (jnp.sqrt(D / rank_width) * shaped).astype(jnp.bfloat16)


def shards(grads, weights, basis, first_moment, second_moment):
    projected_part = jnp.einsum("mfd,dmr->mfr", grads, basis, preferred_element_type=jnp.float32)
    summed_share = lax.psum_scatter(projected_part, "tp", scatter_dimension=2, tiled=True)
    first_next, second_next, normal_half = adam_share(summed_share, first_moment, second_moment)
    projected_half, normal_full = (
        lax.all_gather(summed_share.astype(jnp.bfloat16), "tp", axis=2, tiled=True),
        lax.all_gather(normal_half, "tp", axis=2, tiled=True),
    )
    update = jnp.einsum("mfr,dmr->mfd", normal_full, basis, preferred_element_type=jnp.float32)
    weight_next = weights - LEARNING_RATE * GALORE_SCALE * update

    def block_total(value):
        return lax.psum(value, "tp")

    def block_gram(value):
        return lax.psum(value, "tp")

    image = lax.psum(
        jnp.einsum("mfd,mfr->dmr", grads, projected_half, preferred_element_type=jnp.float32),
        "fsdp",
    )
    basis_next = rebuild(image, block_total, block_gram)
    return (weight_next, first_next, second_next, basis_next)


def solution(mesh):
    in_specs = (
        P(None, "fsdp", "tp"),
        P(None, "fsdp", "tp"),
        P("tp", None, None),
        P(None, "fsdp", "tp"),
        P(None, "fsdp", "tp"),
    )
    out_specs = (
        P(None, "fsdp", "tp"),
        P(None, "fsdp", "tp"),
        P(None, "fsdp", "tp"),
        P("tp", None, None),
    )
    return jax.shard_map(shards, mesh=mesh, in_specs=in_specs, out_specs=out_specs, check_vma=False)
```

profile of v0, /device:TPU:1, one launch (start us, length us, event | category | flops | bytes accessed | tf_op | source)
XLA Modules:
  0.0 380.3 jit_solution(17990277985158223660)
XLA Ops:
  7.2 0.0 copy-start
  7.2 0.0 reduce-scatter.2.cloned.1.call-start
  7.2 0.9 copy-done
  8.1 2.1 fusion.11
  10.2 0.0 copy-start.4
  10.3 0.0 copy-start.5
  10.3 0.0 reduce-scatter.2.cloned.1.call-update
  10.3 0.0 copy-start.2
  10.3 0.0 all-reduce.3.cloned.1.call-start
  10.3 42.8 %reduce-scatter.2.cloned.1.call-done = f32[2,192,32]{1,2,0:T(8,128)} async-done(((f32[2,192,256]{1,2,0:T(8,128)}), f32[2,192,32]{1,2,0:T(8,128)}) %reduce-scatter.2.cloned.1.call-update) | async-done | bytes 49168 | tf_op jit(solution)/shard_map/reduce_scatter | solution.py:38
  53.2 0.0 copy-done.4
  53.2 0.0 copy-done.5
  53.2 1.6 divide_convert_fusion
  54.8 18.4 %all_gather.7 = bf16[2,192,256]{1,2,0:T(8,128)(2,1)S(1)} all-gather(bf16[2,192,32]{1,2,0:T(8,128)(2,1)S(1)} %get-tuple-element.11), channel_id=1, replica_groups=mesh['fsdp'=64,'tp'=8] {'tp'}, dimensions={2}, use_global_device_ids=true | all-gather | bytes 221184 | tf_op jit(solution)/shard_map/all_gather | solution.py:41
  73.2 0.0 copy-done.2
  73.2 1.2 convolution_bitcast_fusion
  74.4 0.0 all-reduce.3.cloned.1.call-update
  74.4 0.0 all-reduce.5.cloned.1.call-start
  74.4 202.8 %all-reduce.3.cloned.1.call-done = f32[320,2,256]{2,0,1:T(8,128)} async-done(((f32[320,2,256]{2,0,1:T(8,128)}), f32[320,2,256]{2,0,1:T(8,128)}) %all-reduce.3.cloned.1.call-update) | async-done | bytes 655376 | tf_op jit(solution)/shard_map/psum | solution.py:53
  277.2 0.0 copy-start.1
  277.2 1.3 multiply_reduce_fusion
  278.6 14.6 %psum.22 = f32[2]{0:T(128)S(1)} all-reduce(f32[2]{0:T(128)S(1)} %multiply_reduce_fusion), channel_id=1, replica_groups=mesh['fsdp'=64,'tp'=8] {'tp'}, use_global_device_ids=true, to_apply=%region_3.0 | all-reduce | flops 2 | bytes 16 | tf_op jit(solution)/shard_map/psum | solution.py:48
  293.1 0.0 copy-done.1
  293.1 2.4 fusion.5
  295.5 0.0 copy-start.3
  295.5 0.0 all-reduce.5.cloned.1.call-update
  295.6 18.8 %all_gather.6 = bf16[2,192,256]{1,2,0:T(8,128)(2,1)S(1)} all-gather(bf16[2,192,32]{1,2,0:T(8,128)(2,1)S(1)} %get-tuple-element.8), channel_id=1, replica_groups=mesh['fsdp'=64,'tp'=8] {'tp'}, dimensions={2}, use_global_device_ids=true | all-gather | bytes 221184 | tf_op jit(solution)/shard_map/all_gather | solution.py:42
  314.4 0.0 copy-done.3
  314.4 1.2 fusion.3
  315.6 55.3 %all-reduce.5.cloned.1.call-done = f32[2,256,256]{2,1,0:T(8,128)} async-done(((f32[2,256,256]{2,1,0:T(8,128)}), f32[2,256,256]{2,1,0:T(8,128)}) %all-reduce.5.cloned.1.call-update) | async-done | bytes 524304 | tf_op jit(solution)/shard_map/psum | solution.py:51
  370.8 1.9 fusion.4
  372.7 1.1 copy.11
  (1 shorter events, 0.0 us)
Async XLA Ops:
  7.2 1.0 copy-start
  7.2 46.0 %reduce-scatter.2.cloned.1.call-start = ((), (), s32[]{:S(2)}) async-start(), calls=%async_computation.1 | async-start | bytes 589824 | tf_op jit(solution)/shard_map/reduce_scatter | solution.py:38
  10.2 42.9 %copy-start.4 = (f32[2,192,32]{1,2,0:T(8,128)S(1)}, f32[2,192,32]{1,2,0:T(8,128)}, u32[]{:S(2)}) copy-start(f32[2,192,32]{1,2,0:T(8,128)} %param.8) | copy-start | bytes 147460
  10.3 42.9 %copy-start.5 = (f32[2,192,32]{1,2,0:T(8,128)S(1)}, f32[2,192,32]{1,2,0:T(8,128)}, u32[]{:S(2)}) copy-start(f32[2,192,32]{1,2,0:T(8,128)} %param.9) | copy-start | bytes 147460
  10.3 62.9 %copy-start.2 = (bf16[2,192,320]{2,1,0:T(8,128)(2,1)S(1)}, bf16[2,192,320]{2,1,0:T(8,128)(2,1)}, u32[]{:S(2)}) copy-start(bf16[2,192,320]{2,1,0:T(8,128)(2,1)} %param.5) | copy-start | bytes 737284
  10.3 266.9 %all-reduce.3.cloned.1.call-start = ((), (), s32[]{:S(2)}) async-start(), calls=%async_computation.2 | async-start | bytes 1310720 | tf_op jit(solution)/shard_map/psum | solution.py:53
  74.4 296.5 %all-reduce.5.cloned.1.call-start = ((), (), s32[]{:S(2)}) async-start(), calls=%async_computation.3 | async-start | bytes 1048576 | tf_op jit(solution)/shard_map/psum | solution.py:51
  277.2 15.9 %copy-start.1 = (f32[320,2,256]{2,0,1:T(8,128)S(1)}, f32[320,2,256]{2,0,1:T(8,128)}, u32[]{:S(2)}) copy-start(f32[320,2,256]{2,0,1:T(8,128)} %all-reduce.3.cloned.1.call-done) | copy-start | bytes 1966084
  295.5 18.9 %copy-start.3 = (f32[2,192,320]{2,1,0:T(8,128)S(1)}, f32[2,192,320]{2,1,0:T(8,128)}, u32[]{:S(2)}) copy-start(f32[2,192,320]{2,1,0:T(8,128)} %param.6) | copy-start | bytes 1474564
Sparse Core Ops, SparseCore 0:
  11.4 41.7 reduce-scatter.1
  74.5 202.6 all-reduce.2
  295.7 75.1 all-reduce.4
where the time goes:
time: 384 us; the launch traced here: 380 us
  waiting for transfers between devices  301 us (78%)
  blocking collectives  51.8 us (13%)
  between operations  13.8 us (4%)
  matrix products  8.7 us (2%)
    psum x1, waiting for transfers between devices, shards(): lax.psum(jnp.einsum('mfd,mfr->dmr', grads, projected_half, preferred_elem...  203 us
    psum x1, waiting for transfers between devices, block_gram(): return lax.psum(value, 'tp')  55.3 us
    reduce_scatter x1, waiting for transfers between devices, shards(): lax.psum_scatter(projected_part, 'tp', scatter_dimension=2, tiled=True)  42.8 us
    all_gather x1, blocking collectives, shards(): lax.all_gather(normal_half, 'tp', axis=2, tiled=True)  18.8 us
    all_gather x1, blocking collectives, shards(): lax.all_gather(summed_share.astype(jnp.bfloat16), 'tp', axis=2, tiled=True)  18.4 us
    psum x1, blocking collectives, block_total(): return lax.psum(value, 'tp')  14.6 us
  transfers between devices with their start and end apart: 3, of which 3 were waited for; matrix products, arithmetic and copies ran while one was open for 0% of the time, Pallas kernels for 0%

commit v1 on v0

v1 whole, which is shorter than its diff:
```python
import jax
import jax.numpy as jnp
from jax import lax
from jax.sharding import PartitionSpec as P

D = 2560


BETA_FIRST = 0.9
BETA_SECOND = 0.999
BIAS_FIRST = 0.9999734386011124
BIAS_SECOND = 0.0952078528862904
EPSILON = 1e-08
EPSILON_NORM = 1e-06
LEARNING_RATE = 0.1
GALORE_SCALE = 0.25


def adam_share(grad_share, first_moment, second_moment):
    first_next = BETA_FIRST * first_moment + (1.0 - BETA_FIRST) * grad_share
    second_next = BETA_SECOND * second_moment + (1.0 - BETA_SECOND) * grad_share * grad_share
    normal = first_next / BIAS_FIRST / (jnp.sqrt(second_next / BIAS_SECOND) + EPSILON)
    return (first_next, second_next, normal.astype(jnp.bfloat16))


def partner_perm(size, bit):
    return [(i, i ^ (1 << bit)) for i in range(size)]


def butterfly_sum(value, axis, size):
    bit = 0
    while (1 << bit) < size:
        value = value + lax.ppermute(value, axis, partner_perm(size, bit))
        bit += 1
    return value


def halving_scatter(value, axis, size, stages):
    index = lax.axis_index(axis)
    for bit, dim in stages:
        half = value.shape[dim] // 2
        mine = (index >> bit) & 1
        keep = lax.dynamic_slice_in_dim(value, mine * half, half, dim)
        send = lax.dynamic_slice_in_dim(value, (1 - mine) * half, half, dim)
        value = keep + lax.ppermute(send, axis, partner_perm(size, bit))
    return value


def doubling_gather(value, axis, size, stages):
    index = lax.axis_index(axis)
    for bit, dim in reversed(stages):
        mine = (index >> bit) & 1
        other = lax.ppermute(value, axis, partner_perm(size, bit))
        low = jnp.where(mine == 0, value, other)
        high = jnp.where(mine == 0, other, value)
        value = jnp.concatenate([low, high], axis=dim)
    return value


def shards(grads, weights, basis, first_moment, second_moment):
    highest = lax.Precision.HIGHEST
    fsdp = lax.axis_size("fsdp")
    tp = lax.axis_size("tp")
    width = first_moment.shape[2]
    rank_width = basis.shape[2]

    projected_part = jnp.einsum("mfd,dmr->mfr", grads, basis, preferred_element_type=jnp.float32)
    projected = butterfly_sum(projected_part, "tp", tp)
    own = lax.dynamic_slice_in_dim(projected, lax.axis_index("tp") * width, width, 2)
    first_next, second_next, normal_half = adam_share(own, first_moment, second_moment)
    projected_half = projected.astype(jnp.bfloat16)

    image_part = jnp.einsum("mfd,mfr->mdr", grads, projected_half, preferred_element_type=jnp.float32)
    stages = [(0, 0), (1, 2), (3, 1), (2, 1), (4, 1), (5, 1)]
    image = doubling_gather(halving_scatter(image_part, "fsdp", fsdp, stages), "fsdp", fsdp, stages)

    tp_bits = [(b, 2) for b in range(tp.bit_length() - 1)]
    normal_full = doubling_gather(normal_half, "tp", tp, list(reversed(tp_bits)))
    update = jnp.einsum("mfr,dmr->mfd", normal_full, basis, preferred_element_type=jnp.float32)
    weight_next = weights - LEARNING_RATE * GALORE_SCALE * update

    gram = butterfly_sum(jnp.einsum("mdr,mds->mrs", image, image, precision=highest), "tp", tp)
    total = jnp.sum(jnp.diagonal(gram, axis1=1, axis2=2), axis=1) + EPSILON_NORM
    factor = jnp.sqrt(rank_width / total)
    scaled = image * factor[:, None, None]
    cross = gram * (factor * factor)[:, None, None]
    shaped = 1.5 * scaled - 0.5 * jnp.einsum("mdr,mrs->mds", scaled, cross, precision=highest)
    basis_next = jnp.transpose((jnp.sqrt(D / rank_width) * shaped).astype(jnp.bfloat16), (1, 0, 2))
    return (weight_next, first_next, second_next, basis_next)


def solution(mesh):
    in_specs = (
        P(None, "fsdp", "tp"),
        P(None, "fsdp", "tp"),
        P("tp", None, None),
        P(None, "fsdp", "tp"),
        P(None, "fsdp", "tp"),
    )
    out_specs = (
        P(None, "fsdp", "tp"),
        P(None, "fsdp", "tp"),
        P(None, "fsdp", "tp"),
        P("tp", None, None),
    )
    return jax.shard_map(shards, mesh=mesh, in_specs=in_specs, out_specs=out_specs, check_vma=False)
```

time: 384 us -> 257 us (0.67)
  waiting for transfers between devices: 301 us -> 111 us
  starting transfers between devices: 0.12 us -> 108 us
  blocking collectives: 51.8 us -> 0 us
  local copies, waits for them, and re-layouts: 2.01 us -> 24.6 us
  between operations: 13.8 us -> 1.15 us
    psum x2 -> x0, waiting for transfers between devices: 258 us -> none  [the longest x1 203 us: shards(): lax.psum(jnp.einsum('mfd,mfr->dmr', grads, projected_half, preferred_elem...]
    ppermute x0 -> x21, waiting for transfers between devices: none -> 111 us  [the longest x6 64.4 us: butterfly_sum(): value = value + lax.ppermute(value, axis, partner_perm(size, bit))]
    ppermute x0 -> x21, starting transfers between devices: none -> 108 us  [the longest x9 45.3 us: doubling_gather(): other = lax.ppermute(value, axis, partner_perm(size, bit))]
    reduce_scatter x1 -> x0, waiting for transfers between devices: 42.8 us -> none  [shards(): lax.psum_scatter(projected_part, 'tp', scatter_dimension=2, tiled=True)]
    all_gather x2 -> x0, blocking collectives: 37.2 us -> none  [the longest x1 18.8 us: shards(): lax.all_gather(normal_half, 'tp', axis=2, tiled=True)]
    add x0 -> x1, local copies, waits for them, and re-layouts: none -> 16.8 us  [butterfly_sum(): value = value + lax.ppermute(value, axis, partner_perm(size, bit))]
    psum x1 -> x0, blocking collectives: 14.6 us -> none  [block_total(): return lax.psum(value, 'tp')]
  transfers between devices with their start and end apart: 3 -> 21, of which waited for: 3 -> 19; matrix products, arithmetic and copies ran while one was open for 0% -> 3% of each run, Pallas kernels for 0% -> 0%
where the time goes in v1:
time: 257 us; the launch traced here: 254 us
  waiting for transfers between devices  111 us (43%)
  starting transfers between devices  108 us (42%)
  local copies, waits for them, and re-layouts  24.6 us (10%)
  matrix products  7.13 us (3%)
    ppermute x6, waiting for transfers between devices, butterfly_sum(): value = value + lax.ppermute(value, axis, partner_perm(size, bit))  64.4 us
    ppermute x9, starting transfers between devices, doubling_gather(): other = lax.ppermute(value, axis, partner_perm(size, bit))  45.3 us
    ppermute x9, waiting for transfers between devices, doubling_gather(): other = lax.ppermute(value, axis, partner_perm(size, bit))  35.7 us
    ppermute x6, starting transfers between devices, butterfly_sum(): value = value + lax.ppermute(value, axis, partner_perm(size, bit))  34 us
    ppermute x6, starting transfers between devices, halving_scatter(): value = keep + lax.ppermute(send, axis, partner_perm(size, bit))  28.9 us
    add x1, local copies, waits for them, and re-layouts, butterfly_sum(): value = value + lax.ppermute(value, axis, partner_perm(size, bit))  16.8 us
    ppermute x6, waiting for transfers between devices, halving_scatter(): value = keep + lax.ppermute(send, axis, partner_perm(size, bit))  11.3 us
    unnamed x7, local copies, waits for them, and re-layouts  5.41 us
  transfers between devices with their start and end apart: 21, of which 19 were waited for; matrix products, arithmetic and copies ran while one was open for 3% of the time, Pallas kernels for 0%

profile of v1, /device:TPU:1, one launch (start us, length us, event | category | flops | bytes accessed | tf_op | source)
XLA Modules:
  0.0 253.8 jit_solution(10693490875183330735)
XLA Ops:
  0.6 1.0 copy-done
  1.6 1.2 fusion.11
  2.8 4.8 %collective-permute-start = (f32[2,192,256]{2,1,0:T(8,128)S(1)}, f32[2,192,256]{2,1,0:T(8,128)S(1)}, u32[]{:S(2)}, u32[]{:S(2)}) collective-permute-start(f32[2,192,256]{2,1,0:T(8,128)S(1)} %fusion.11), channel_id=1, source_target_pairs={{0,1},{1,0},{2,3},{3,2},{4,5},{5,4},{6,7},{7,6},{8,9},{9,8},{10,11... | collective-permute-start | bytes 1179656 | tf_op jit(solution)/shard_map/ppermute | solution.py:33
  7.7 5.2 %collective-permute-done = f32[2,192,256]{2,1,0:T(8,128)S(1)} collective-permute-done((f32[2,192,256]{2,1,0:T(8,128)S(1)}, f32[2,192,256]{2,1,0:T(8,128)S(1)}, u32[]{:S(2)}, u32[]{:S(2)}) %collective-permute-start) | collective-permute-done | bytes 393248 | tf_op jit(solution)/shard_map/ppermute | solution.py:33
  12.8 0.1 add.102
  12.9 9.5 %collective-permute-start.1 = (f32[2,192,256]{2,1,0:T(8,128)S(1)}, f32[2,192,256]{2,1,0:T(8,128)S(1)}, u32[]{:S(2)}, u32[]{:S(2)}) collective-permute-start(f32[2,192,256]{2,1,0:T(8,128)S(1)} %add.102), channel_id=1, source_target_pairs={{0,2},{1,3},{2,0},{3,1},{4,6},{5,7},{6,4},{7,5},{8,10},{9,11},{10,... | collective-permute-start | bytes 1179656 | tf_op jit(solution)/shard_map/ppermute | solution.py:33
  22.3 17.1 %collective-permute-done.1 = f32[2,192,256]{2,1,0:T(8,128)S(1)} collective-permute-done((f32[2,192,256]{2,1,0:T(8,128)S(1)}, f32[2,192,256]{2,1,0:T(8,128)S(1)}, u32[]{:S(2)}, u32[]{:S(2)}) %collective-permute-start.1) | collective-permute-done | bytes 393248 | tf_op jit(solution)/shard_map/ppermute | solution.py:33
  39.5 8.2 %collective-permute-start.2 = (f32[2,192,256]{2,1,0:T(8,128)S(1)}, f32[2,192,256]{2,1,0:T(8,128)S(1)}, u32[]{:S(2)}, u32[]{:S(2)}) collective-permute-start(f32[2,192,256]{2,1,0:T(8,128)S(1)} %add.103), channel_id=1, source_target_pairs={{0,4},{1,5},{2,6},{3,7},{4,0},{5,1},{6,2},{7,3},{8,12},{9,13},{10,... | collective-permute-start | bytes 1179656 | tf_op jit(solution)/shard_map/ppermute | solution.py:33
  47.7 14.0 %collective-permute-done.2 = f32[2,192,256]{2,1,0:T(8,128)S(1)} collective-permute-done((f32[2,192,256]{2,1,0:T(8,128)S(1)}, f32[2,192,256]{2,1,0:T(8,128)S(1)}, u32[]{:S(2)}, u32[]{:S(2)}) %collective-permute-start.2) | collective-permute-done | bytes 393248 | tf_op jit(solution)/shard_map/ppermute | solution.py:33
  61.7 0.1 add.104
  61.8 1.3 fusion.18
  63.1 6.4 %collective-permute-start.6 = (f32[1,320,256]{2,1,0:T(8,128)S(1)}, f32[1,320,256]{2,1,0:T(8,128)S(1)}, u32[]{:S(2)}, u32[]{:S(2)}) collective-permute-start(f32[1,320,256]{2,1,0:T(8,128)S(1)} %dynamic-slice_bitcast_fusion), channel_id=1, source_target_pairs={{0,8},{8,0},{16,24},{24,16},{32,40},{40,32},{48,56},{56,48},{64,72... | collective-permute-start | bytes 983048 | tf_op jit(solution)/shard_map/ppermute | solution.py:45
  69.5 1.2 collective-permute-done.6
  70.8 3.1 %collective-permute-start.7 = (f32[1,320,128]{2,1,0:T(8,128)S(1)}, f32[1,320,128]{2,1,0:T(8,128)S(1)}, u32[]{:S(2)}, u32[]{:S(2)}) collective-permute-start(f32[1,320,128]{2,1,0:T(8,128)S(1)} %constant_dynamic-slice_fusion.4), channel_id=1, source_target_pairs={{0,16},{8,24},{16,0},{24,8},{32,48},{40,56},{48,32},{56,40},{64,80... | collective-permute-start | bytes 491528 | tf_op jit(solution)/shard_map/ppermute | solution.py:45
  73.9 4.2 %collective-permute-done.7 = f32[1,320,128]{2,1,0:T(8,128)S(1)} collective-permute-done((f32[1,320,128]{2,1,0:T(8,128)S(1)}, f32[1,320,128]{2,1,0:T(8,128)S(1)}, u32[]{:S(2)}, u32[]{:S(2)}) %collective-permute-start.7) | collective-permute-done | bytes 163872 | tf_op jit(solution)/shard_map/ppermute | solution.py:45
  78.2 3.2 %collective-permute-start.8 = (f32[1,160,128]{2,1,0:T(8,128)S(1)}, f32[1,160,128]{2,1,0:T(8,128)S(1)}, u32[]{:S(2)}, u32[]{:S(2)}) collective-permute-start(f32[1,160,128]{2,1,0:T(8,128)S(1)} %constant_dynamic-slice_fusion.3), channel_id=1, source_target_pairs={{0,64},{8,72},{16,80},{24,88},{32,96},{40,104},{48,112},{56,120},{... | collective-permute-start | bytes 245768 | tf_op jit(solution)/shard_map/ppermute | solution.py:45
  81.4 2.0 collective-permute-done.8
  83.4 4.6 %collective-permute-start.9 = (f32[1,80,128]{2,1,0:T(8,128)S(1)}, f32[1,80,128]{2,1,0:T(8,128)S(1)}, u32[]{:S(2)}, u32[]{:S(2)}) collective-permute-start(f32[1,80,128]{2,1,0:T(8,128)S(1)} %constant_dynamic-slice_fusion.2), channel_id=1, source_target_pairs={{0,32},{8,40},{16,48},{24,56},{32,0},{40,8},{48,16},{56,24},{64,96... | collective-permute-start | bytes 122888 | tf_op jit(solution)/shard_map/ppermute | solution.py:45
  88.0 1.6 collective-permute-done.9
  89.6 4.2 %collective-permute-start.10 = (f32[1,40,128]{2,1,0:T(8,128)S(1)}, f32[1,40,128]{2,1,0:T(8,128)S(1)}, u32[]{:S(2)}, u32[]{:S(2)}) collective-permute-start(f32[1,40,128]{2,1,0:T(8,128)S(1)} %constant_dynamic-slice_fusion.1), channel_id=1, source_target_pairs={{0,128},{8,136},{16,144},{24,152},{32,160},{40,168},{48,176},{56,1... | collective-permute-start | bytes 61448 | tf_op jit(solution)/shard_map/ppermute | solution.py:45
  93.9 1.2 collective-permute-done.10
  95.1 7.4 %collective-permute-start.11 = (f32[1,20,128]{2,1,0:T(8,128)S(1)}, f32[1,20,128]{2,1,0:T(8,128)S(1)}, u32[]{:S(2)}, u32[]{:S(2)}) collective-permute-start(f32[1,20,128]{2,1,0:T(8,128)S(1)} %constant_dynamic-slice_fusion), channel_id=1, source_target_pairs={{0,256},{8,264},{16,272},{24,280},{32,288},{40,296},{48,304},{56,3... | collective-permute-start | bytes 30728 | tf_op jit(solution)/shard_map/ppermute | solution.py:45
  102.5 1.1 collective-permute-done.11
  103.6 7.3 %collective-permute-start.12 = (f32[1,20,128]{2,1,0:T(8,128)S(1)}, f32[1,20,128]{2,1,0:T(8,128)S(1)}, u32[]{:S(2)}, u32[]{:S(2)}) collective-permute-start(f32[1,20,128]{2,1,0:T(8,128)S(1)} %dynamic-slice_add_fusion.4), channel_id=1, source_target_pairs={{0,256},{8,264},{16,272},{24,280},{32,288},{40,296},{48,304},{56,3... | collective-permute-start | bytes 30728 | tf_op jit(solution)/shard_map/ppermute | solution.py:53
  110.8 1.1 collective-permute-done.12
  111.9 4.1 %collective-permute-start.13 = (f32[1,40,128]{2,1,0:T(8,128)S(1)}, f32[1,40,128]{2,1,0:T(8,128)S(1)}, u32[]{:S(2)}, u32[]{:S(2)}) collective-permute-start(f32[1,40,128]{2,1,0:T(8,128)S(1)} %pad_maximum_fusion.9), channel_id=1, source_target_pairs={{0,128},{8,136},{16,144},{24,152},{32,160},{40,168},{48,176},{56,1... | collective-permute-start | bytes 61448 | tf_op jit(solution)/shard_map/ppermute | solution.py:53
  116.1 1.6 collective-permute-done.13
  117.7 4.7 %collective-permute-start.14 = (f32[1,80,128]{2,1,0:T(8,128)S(1)}, f32[1,80,128]{2,1,0:T(8,128)S(1)}, u32[]{:S(2)}, u32[]{:S(2)}) collective-permute-start(f32[1,80,128]{2,1,0:T(8,128)S(1)} %pad_maximum_fusion.8), channel_id=1, source_target_pairs={{0,32},{8,40},{16,48},{24,56},{32,0},{40,8},{48,16},{56,24},{64,96... | collective-permute-start | bytes 122888 | tf_op jit(solution)/shard_map/ppermute | solution.py:53
  122.4 1.5 collective-permute-done.14
  124.0 3.1 %collective-permute-start.15 = (f32[1,160,128]{2,1,0:T(8,128)S(1)}, f32[1,160,128]{2,1,0:T(8,128)S(1)}, u32[]{:S(2)}, u32[]{:S(2)}) collective-permute-start(f32[1,160,128]{2,1,0:T(8,128)S(1)} %pad_maximum_fusion.7), channel_id=1, source_target_pairs={{0,64},{8,72},{16,80},{24,88},{32,96},{40,104},{48,112},{56,120},{... | collective-permute-start | bytes 245768 | tf_op jit(solution)/shard_map/ppermute | solution.py:53
  127.1 2.1 collective-permute-done.15
  129.2 3.1 %collective-permute-start.16 = (f32[1,320,128]{2,1,0:T(8,128)S(1)}, f32[1,320,128]{2,1,0:T(8,128)S(1)}, u32[]{:S(2)}, u32[]{:S(2)}) collective-permute-start(f32[1,320,128]{2,1,0:T(8,128)S(1)} %pad_maximum_fusion.4), channel_id=1, source_target_pairs={{0,16},{8,24},{16,0},{24,8},{32,48},{40,56},{48,32},{56,40},{64,80... | collective-permute-start | bytes 491528 | tf_op jit(solution)/shard_map/ppermute | solution.py:53
  132.3 2.9 %collective-permute-done.16 = f32[1,320,128]{2,1,0:T(8,128)S(1)} collective-permute-done((f32[1,320,128]{2,1,0:T(8,128)S(1)}, f32[1,320,128]{2,1,0:T(8,128)S(1)}, u32[]{:S(2)}, u32[]{:S(2)}) %collective-permute-start.16) | collective-permute-done | bytes 163872 | tf_op jit(solution)/shard_map/ppermute | solution.py:53
  135.3 13.1 %collective-permute-start.17 = (f32[1,320,256]{2,1,0:T(8,128)S(1)}, f32[1,320,256]{2,1,0:T(8,128)S(1)}, u32[]{:S(2)}, u32[]{:S(2)}) collective-permute-start(f32[1,320,256]{2,1,0:T(8,128)S(1)} %pad_maximum_fusion.3), channel_id=1, source_target_pairs={{0,8},{8,0},{16,24},{24,16},{32,40},{40,32},{48,56},{56,48},{64,72... | collective-permute-start | bytes 983048 | tf_op jit(solution)/shard_map/ppermute | solution.py:53
  148.4 1.2 collective-permute-done.17
  149.7 1.6 fusion.7
  151.2 1.9 collective-permute-start.18
  153.2 1.0 copy.17
  154.1 1.0 copy.19
  155.1 0.2 divide_convert_fusion
  155.3 3.4 %collective-permute-start.3 = (bf16[2,192,32]{2,1,0:T(8,128)(2,1)S(1)}, bf16[2,192,32]{2,1,0:T(8,128)(2,1)S(1)}, u32[]{:S(2)}, u32[]{:S(2)}) collective-permute-start(bf16[2,192,32]{2,1,0:T(8,128)(2,1)S(1)} %get-tuple-element.14), channel_id=1, source_target_pairs={{0,1},{1,0},{2,3},{3,2},{4,5},{5,4},{6,7},{7,6},{8,9},{9,8},{10,11... | collective-permute-start | bytes 73736 | tf_op jit(solution)/shard_map/ppermute | solution.py:53
  158.7 7.5 %collective-permute-done.18 = f32[2,256,256]{2,1,0:T(8,128)S(1)} collective-permute-done((f32[2,256,256]{2,1,0:T(8,128)S(1)}, f32[2,256,256]{2,1,0:T(8,128)S(1)}, u32[]{:S(2)}, u32[]{:S(2)}) %collective-permute-start.18) | collective-permute-done | bytes 524320 | tf_op jit(solution)/shard_map/ppermute | solution.py:33
  166.2 0.1 add.128
  166.3 4.9 %collective-permute-start.19 = (f32[2,256,256]{2,1,0:T(8,128)S(1)}, f32[2,256,256]{2,1,0:T(8,128)S(1)}, u32[]{:S(2)}, u32[]{:S(2)}) collective-permute-start(f32[2,256,256]{2,1,0:T(8,128)S(1)} %add.128), channel_id=1, source_target_pairs={{0,2},{1,3},{2,0},{3,1},{4,6},{5,7},{6,4},{7,5},{8,10},{9,11},{10,... | collective-permute-start | bytes 1572872 | tf_op jit(solution)/shard_map/ppermute | solution.py:33
  171.2 0.1 pad_maximum_fusion.5
  171.4 2.0 collective-permute-start.4
  173.4 24.8 %collective-permute-done.4 = bf16[2,192,64]{2,1,0:T(8,128)(2,1)S(1)} collective-permute-done((bf16[2,192,64]{2,1,0:T(8,128)(2,1)S(1)}, bf16[2,192,64]{2,1,0:T(8,128)(2,1)S(1)}, u32[]{:S(2)}, u32[]{:S(2)}) %collective-permute-start.4) | collective-permute-done | bytes 49184 | tf_op jit(solution)/shard_map/ppermute | solution.py:53
  198.1 0.1 broadcast_select_fusion.5
  198.3 0.1 pad_maximum_fusion.6
  198.4 4.5 %collective-permute-start.5 = (bf16[2,192,128]{2,1,0:T(8,128)(2,1)S(1)}, bf16[2,192,128]{2,1,0:T(8,128)(2,1)S(1)}, u32[]{:S(2)}, u32[]{:S(2)}) collective-permute-start(bf16[2,192,128]{2,1,0:T(8,128)(2,1)S(1)} %pad_maximum_fusion.6), channel_id=1, source_target_pairs={{0,4},{1,5},{2,6},{3,7},{4,0},{5,1},{6,2},{7,3},{8,12},{9,13},{10,... | collective-permute-start | bytes 294920 | tf_op jit(solution)/shard_map/ppermute | solution.py:53
  202.9 0.1 add.129
  202.9 4.7 %collective-permute-start.20 = (f32[2,256,256]{2,1,0:T(8,128)S(1)}, f32[2,256,256]{2,1,0:T(8,128)S(1)}, u32[]{:S(2)}, u32[]{:S(2)}) collective-permute-start(f32[2,256,256]{2,1,0:T(8,128)S(1)} %add.129), channel_id=1, source_target_pairs={{0,4},{1,5},{2,6},{3,7},{4,0},{5,1},{6,2},{7,3},{8,12},{9,13},{10,... | collective-permute-start | bytes 1572872 | tf_op jit(solution)/shard_map/ppermute | solution.py:33
  207.7 0.7 copy.22
  208.4 0.7 copy.23
  209.2 0.5 collective-permute-done.5
  209.7 0.1 broadcast_select_fusion.7
  209.8 2.2 fusion
  212.0 20.6 %collective-permute-done.20 = f32[2,256,256]{2,1,0:T(8,128)S(1)} collective-permute-done((f32[2,256,256]{2,1,0:T(8,128)S(1)}, f32[2,256,256]{2,1,0:T(8,128)S(1)}, u32[]{:S(2)}, u32[]{:S(2)}) %collective-permute-start.20) | collective-permute-done | bytes 524320 | tf_op jit(solution)/shard_map/ppermute | solution.py:33
  232.5 0.1 add.130
  232.6 16.8 %copy.21 = f32[2,256,256]{0,2,1:T(8,128)} copy(f32[2,256,256]{2,1,0:T(8,128)S(1)} %add.130) | data formatting | bytes 1048576 | tf_op jit(solution)/shard_map/add | solution.py:33
  249.4 2.3 gather_fusion
  251.7 0.1 reduce_sum.9
  251.8 0.9 fusion.4
  252.8 1.1 copy.24
  (30 shorter events, 0.5 us)
Async XLA Ops:
  0.6 1.0 copy-start
  2.8 10.0 %collective-permute-start = (f32[2,192,256]{2,1,0:T(8,128)S(1)}, f32[2,192,256]{2,1,0:T(8,128)S(1)}, u32[]{:S(2)}, u32[]{:S(2)}) collective-permute-start(f32[2,192,256]{2,1,0:T(8,128)S(1)} %fusion.11), channel_id=1, source_target_pairs={{0,1},{1,0},{2,3},{3,2},{4,5},{5,4},{6,7},{7,6},{8,9},{9,8},{10,11... | collective-permute-start | bytes 1179656 | tf_op jit(solution)/shard_map/ppermute | solution.py:33
  12.9 26.6 %collective-permute-start.1 = (f32[2,192,256]{2,1,0:T(8,128)S(1)}, f32[2,192,256]{2,1,0:T(8,128)S(1)}, u32[]{:S(2)}, u32[]{:S(2)}) collective-permute-start(f32[2,192,256]{2,1,0:T(8,128)S(1)} %add.102), channel_id=1, source_target_pairs={{0,2},{1,3},{2,0},{3,1},{4,6},{5,7},{6,4},{7,5},{8,10},{9,11},{10,... | collective-permute-start | bytes 1179656 | tf_op jit(solution)/shard_map/ppermute | solution.py:33
  39.5 22.3 %collective-permute-start.2 = (f32[2,192,256]{2,1,0:T(8,128)S(1)}, f32[2,192,256]{2,1,0:T(8,128)S(1)}, u32[]{:S(2)}, u32[]{:S(2)}) collective-permute-start(f32[2,192,256]{2,1,0:T(8,128)S(1)} %add.103), channel_id=1, source_target_pairs={{0,4},{1,5},{2,6},{3,7},{4,0},{5,1},{6,2},{7,3},{8,12},{9,13},{10,... | collective-permute-start | bytes 1179656 | tf_op jit(solution)/shard_map/ppermute | solution.py:33
  63.1 7.7 %collective-permute-start.6 = (f32[1,320,256]{2,1,0:T(8,128)S(1)}, f32[1,320,256]{2,1,0:T(8,128)S(1)}, u32[]{:S(2)}, u32[]{:S(2)}) collective-permute-start(f32[1,320,256]{2,1,0:T(8,128)S(1)} %dynamic-slice_bitcast_fusion), channel_id=1, source_target_pairs={{0,8},{8,0},{16,24},{24,16},{32,40},{40,32},{48,56},{56,48},{64,72... | collective-permute-start | bytes 983048 | tf_op jit(solution)/shard_map/ppermute | solution.py:45
  70.8 7.3 %collective-permute-start.7 = (f32[1,320,128]{2,1,0:T(8,128)S(1)}, f32[1,320,128]{2,1,0:T(8,128)S(1)}, u32[]{:S(2)}, u32[]{:S(2)}) collective-permute-start(f32[1,320,128]{2,1,0:T(8,128)S(1)} %constant_dynamic-slice_fusion.4), channel_id=1, source_target_pairs={{0,16},{8,24},{16,0},{24,8},{32,48},{40,56},{48,32},{56,40},{64,80... | collective-permute-start | bytes 491528 | tf_op jit(solution)/shard_map/ppermute | solution.py:45
  78.2 5.2 %collective-permute-start.8 = (f32[1,160,128]{2,1,0:T(8,128)S(1)}, f32[1,160,128]{2,1,0:T(8,128)S(1)}, u32[]{:S(2)}, u32[]{:S(2)}) collective-permute-start(f32[1,160,128]{2,1,0:T(8,128)S(1)} %constant_dynamic-slice_fusion.3), channel_id=1, source_target_pairs={{0,64},{8,72},{16,80},{24,88},{32,96},{40,104},{48,112},{56,120},{... | collective-permute-start | bytes 245768 | tf_op jit(solution)/shard_map/ppermute | solution.py:45
  83.4 6.3 %collective-permute-start.9 = (f32[1,80,128]{2,1,0:T(8,128)S(1)}, f32[1,80,128]{2,1,0:T(8,128)S(1)}, u32[]{:S(2)}, u32[]{:S(2)}) collective-permute-start(f32[1,80,128]{2,1,0:T(8,128)S(1)} %constant_dynamic-slice_fusion.2), channel_id=1, source_target_pairs={{0,32},{8,40},{16,48},{24,56},{32,0},{40,8},{48,16},{56,24},{64,96... | collective-permute-start | bytes 122888 | tf_op jit(solution)/shard_map/ppermute | solution.py:45
  89.6 5.4 %collective-permute-start.10 = (f32[1,40,128]{2,1,0:T(8,128)S(1)}, f32[1,40,128]{2,1,0:T(8,128)S(1)}, u32[]{:S(2)}, u32[]{:S(2)}) collective-permute-start(f32[1,40,128]{2,1,0:T(8,128)S(1)} %constant_dynamic-slice_fusion.1), channel_id=1, source_target_pairs={{0,128},{8,136},{16,144},{24,152},{32,160},{40,168},{48,176},{56,1... | collective-permute-start | bytes 61448 | tf_op jit(solution)/shard_map/ppermute | solution.py:45
  95.1 8.5 %collective-permute-start.11 = (f32[1,20,128]{2,1,0:T(8,128)S(1)}, f32[1,20,128]{2,1,0:T(8,128)S(1)}, u32[]{:S(2)}, u32[]{:S(2)}) collective-permute-start(f32[1,20,128]{2,1,0:T(8,128)S(1)} %constant_dynamic-slice_fusion), channel_id=1, source_target_pairs={{0,256},{8,264},{16,272},{24,280},{32,288},{40,296},{48,304},{56,3... | collective-permute-start | bytes 30728 | tf_op jit(solution)/shard_map/ppermute | solution.py:45
  103.6 8.3 %collective-permute-start.12 = (f32[1,20,128]{2,1,0:T(8,128)S(1)}, f32[1,20,128]{2,1,0:T(8,128)S(1)}, u32[]{:S(2)}, u32[]{:S(2)}) collective-permute-start(f32[1,20,128]{2,1,0:T(8,128)S(1)} %dynamic-slice_add_fusion.4), channel_id=1, source_target_pairs={{0,256},{8,264},{16,272},{24,280},{32,288},{40,296},{48,304},{56,3... | collective-permute-start | bytes 30728 | tf_op jit(solution)/shard_map/ppermute | solution.py:53
  111.9 5.7 %collective-permute-start.13 = (f32[1,40,128]{2,1,0:T(8,128)S(1)}, f32[1,40,128]{2,1,0:T(8,128)S(1)}, u32[]{:S(2)}, u32[]{:S(2)}) collective-permute-start(f32[1,40,128]{2,1,0:T(8,128)S(1)} %pad_maximum_fusion.9), channel_id=1, source_target_pairs={{0,128},{8,136},{16,144},{24,152},{32,160},{40,168},{48,176},{56,1... | collective-permute-start | bytes 61448 | tf_op jit(solution)/shard_map/ppermute | solution.py:53
  117.7 6.3 %collective-permute-start.14 = (f32[1,80,128]{2,1,0:T(8,128)S(1)}, f32[1,80,128]{2,1,0:T(8,128)S(1)}, u32[]{:S(2)}, u32[]{:S(2)}) collective-permute-start(f32[1,80,128]{2,1,0:T(8,128)S(1)} %pad_maximum_fusion.8), channel_id=1, source_target_pairs={{0,32},{8,40},{16,48},{24,56},{32,0},{40,8},{48,16},{56,24},{64,96... | collective-permute-start | bytes 122888 | tf_op jit(solution)/shard_map/ppermute | solution.py:53
  124.0 5.2 %collective-permute-start.15 = (f32[1,160,128]{2,1,0:T(8,128)S(1)}, f32[1,160,128]{2,1,0:T(8,128)S(1)}, u32[]{:S(2)}, u32[]{:S(2)}) collective-permute-start(f32[1,160,128]{2,1,0:T(8,128)S(1)} %pad_maximum_fusion.7), channel_id=1, source_target_pairs={{0,64},{8,72},{16,80},{24,88},{32,96},{40,104},{48,112},{56,120},{... | collective-permute-start | bytes 245768 | tf_op jit(solution)/shard_map/ppermute | solution.py:53
  129.2 6.1 %collective-permute-start.16 = (f32[1,320,128]{2,1,0:T(8,128)S(1)}, f32[1,320,128]{2,1,0:T(8,128)S(1)}, u32[]{:S(2)}, u32[]{:S(2)}) collective-permute-start(f32[1,320,128]{2,1,0:T(8,128)S(1)} %pad_maximum_fusion.4), channel_id=1, source_target_pairs={{0,16},{8,24},{16,0},{24,8},{32,48},{40,56},{48,32},{56,40},{64,80... | collective-permute-start | bytes 491528 | tf_op jit(solution)/shard_map/ppermute | solution.py:53
  135.3 14.3 %collective-permute-start.17 = (f32[1,320,256]{2,1,0:T(8,128)S(1)}, f32[1,320,256]{2,1,0:T(8,128)S(1)}, u32[]{:S(2)}, u32[]{:S(2)}) collective-permute-start(f32[1,320,256]{2,1,0:T(8,128)S(1)} %pad_maximum_fusion.3), channel_id=1, source_target_pairs={{0,8},{8,0},{16,24},{24,16},{32,40},{40,32},{48,56},{56,48},{64,72... | collective-permute-start | bytes 983048 | tf_op jit(solution)/shard_map/ppermute | solution.py:53
  151.2 15.0 %collective-permute-start.18 = (f32[2,256,256]{2,1,0:T(8,128)S(1)}, f32[2,256,256]{2,1,0:T(8,128)S(1)}, u32[]{:S(2)}, u32[]{:S(2)}) collective-permute-start(f32[2,256,256]{2,1,0:T(8,128)S(1)} %fusion.7), channel_id=1, source_target_pairs={{0,1},{1,0},{2,3},{3,2},{4,5},{5,4},{6,7},{7,6},{8,9},{9,8},{10,11... | collective-permute-start | bytes 1572872 | tf_op jit(solution)/shard_map/ppermute | solution.py:33
  155.3 15.9 %collective-permute-start.3 = (bf16[2,192,32]{2,1,0:T(8,128)(2,1)S(1)}, bf16[2,192,32]{2,1,0:T(8,128)(2,1)S(1)}, u32[]{:S(2)}, u32[]{:S(2)}) collective-permute-start(bf16[2,192,32]{2,1,0:T(8,128)(2,1)S(1)} %get-tuple-element.14), channel_id=1, source_target_pairs={{0,1},{1,0},{2,3},{3,2},{4,5},{5,4},{6,7},{7,6},{8,9},{9,8},{10,11... | collective-permute-start | bytes 73736 | tf_op jit(solution)/shard_map/ppermute | solution.py:53
  166.3 36.6 %collective-permute-start.19 = (f32[2,256,256]{2,1,0:T(8,128)S(1)}, f32[2,256,256]{2,1,0:T(8,128)S(1)}, u32[]{:S(2)}, u32[]{:S(2)}) collective-permute-start(f32[2,256,256]{2,1,0:T(8,128)S(1)} %add.128), channel_id=1, source_target_pairs={{0,2},{1,3},{2,0},{3,1},{4,6},{5,7},{6,4},{7,5},{8,10},{9,11},{10,... | collective-permute-start | bytes 1572872 | tf_op jit(solution)/shard_map/ppermute | solution.py:33
  171.4 26.8 %collective-permute-start.4 = (bf16[2,192,64]{2,1,0:T(8,128)(2,1)S(1)}, bf16[2,192,64]{2,1,0:T(8,128)(2,1)S(1)}, u32[]{:S(2)}, u32[]{:S(2)}) collective-permute-start(bf16[2,192,64]{2,1,0:T(8,128)(2,1)S(1)} %pad_maximum_fusion.5), channel_id=1, source_target_pairs={{0,2},{1,3},{2,0},{3,1},{4,6},{5,7},{6,4},{7,5},{8,10},{9,11},{10,... | collective-permute-start | bytes 147464 | tf_op jit(solution)/shard_map/ppermute | solution.py:53
  198.4 11.3 %collective-permute-start.5 = (bf16[2,192,128]{2,1,0:T(8,128)(2,1)S(1)}, bf16[2,192,128]{2,1,0:T(8,128)(2,1)S(1)}, u32[]{:S(2)}, u32[]{:S(2)}) collective-permute-start(bf16[2,192,128]{2,1,0:T(8,128)(2,1)S(1)} %pad_maximum_fusion.6), channel_id=1, source_target_pairs={{0,4},{1,5},{2,6},{3,7},{4,0},{5,1},{6,2},{7,3},{8,12},{9,13},{10,... | collective-permute-start | bytes 294920 | tf_op jit(solution)/shard_map/ppermute | solution.py:53
  202.9 29.6 %collective-permute-start.20 = (f32[2,256,256]{2,1,0:T(8,128)S(1)}, f32[2,256,256]{2,1,0:T(8,128)S(1)}, u32[]{:S(2)}, u32[]{:S(2)}) collective-permute-start(f32[2,256,256]{2,1,0:T(8,128)S(1)} %add.129), channel_id=1, source_target_pairs={{0,4},{1,5},{2,6},{3,7},{4,0},{5,1},{6,2},{7,3},{8,12},{9,13},{10,... | collective-permute-start | bytes 1572872 | tf_op jit(solution)/shard_map/ppermute | solution.py:33

commit v2 on v1

--- a/solution.py
+++ b/solution.py
@@ -57,36 +57,45 @@
     return value
 
 
+def reverse_blocks(value, bits, width):
+    lead = value.shape[:-1]
+    split = value.reshape(lead + (2,) * bits + (width,))
+    axes = tuple(range(len(lead))) + tuple(len(lead) + bits - 1 - i for i in range(bits)) + (len(lead) + bits,)
+    return jnp.transpose(split, axes).reshape(value.shape)
+
+
 def shards(grads, weights, basis, first_moment, second_moment):
     highest = lax.Precision.HIGHEST
     fsdp = lax.axis_size("fsdp")
     tp = lax.axis_size("tp")
     width = first_moment.shape[2]
     rank_width = basis.shape[2]
+    tp_bits = [(b, 2) for b in range(tp.bit_length() - 1)]
+    basis_order = reverse_blocks(basis, len(tp_bits), width)
 
-    projected_part = jnp.einsum("mfd,dmr->mfr", grads, basis, preferred_element_type=jnp.float32)
-    projected = butterfly_sum(projected_part, "tp", tp)
-    own = lax.dynamic_slice_in_dim(projected, lax.axis_index("tp") * width, width, 2)
+    projected_part = jnp.einsum("mfd,dmr->mfr", grads, basis_order, preferred_element_type=jnp.float32)
+    own = halving_scatter(projected_part, "tp", tp, tp_bits)
     first_next, second_next, normal_half = adam_share(own, first_moment, second_moment)
-    projected_half = projected.astype(jnp.bfloat16)
+    halves = jnp.stack([own.astype(jnp.bfloat16), normal_half], axis=0)
+    gathered = doubling_gather(halves, "tp", tp, [(b, 3) for b, _ in tp_bits])
+    projected_half, normal_full = gathered[0], gathered[1]
 
     image_part = jnp.einsum("mfd,mfr->mdr", grads, projected_half, preferred_element_type=jnp.float32)
     stages = [(0, 0), (1, 2), (3, 1), (2, 1), (4, 1), (5, 1)]
     image = doubling_gather(halving_scatter(image_part, "fsdp", fsdp, stages), "fsdp", fsdp, stages)
 
-    tp_bits = [(b, 2) for b in range(tp.bit_length() - 1)]
-    normal_full = doubling_gather(normal_half, "tp", tp, list(reversed(tp_bits)))
-    update = jnp.einsum("mfr,dmr->mfd", normal_full, basis, preferred_element_type=jnp.float32)
+    update = jnp.einsum("mfr,dmr->mfd", normal_full, basis_order, preferred_element_type=jnp.float32)
     weight_next = weights - LEARNING_RATE * GALORE_SCALE * update
 
     gram = butterfly_sum(jnp.einsum("mdr,mds->mrs", image, image, precision=highest), "tp", tp)
-    total = jnp.sum(jnp.diagonal(gram, axis1=1, axis2=2), axis=1) + EPSILON_NORM
+    diagonal = lax.broadcasted_iota(jnp.int32, gram.shape, 1) == lax.broadcasted_iota(jnp.int32, gram.shape, 2)
+    total = jnp.sum(jnp.where(diagonal, gram, 0.0), axis=(1, 2)) + EPSILON_NORM
     factor = jnp.sqrt(rank_width / total)
     scaled = image * factor[:, None, None]
     cross = gram * (factor * factor)[:, None, None]
     shaped = 1.5 * scaled - 0.5 * jnp.einsum("mdr,mrs->mds", scaled, cross, precision=highest)
-    basis_next = jnp.transpose((jnp.sqrt(D / rank_width) * shaped).astype(jnp.bfloat16), (1, 0, 2))
-    return (weight_next, first_next, second_next, basis_next)
+    basis_next = reverse_blocks((jnp.sqrt(D / rank_width) * shaped).astype(jnp.bfloat16), len(tp_bits), width)
+    return (weight_next, first_next, second_next, jnp.transpose(basis_next, (1, 0, 2)))
 
 
 def solution(mesh):

time: 257 us -> 241 us (0.938)
  local copies, waits for them, and re-layouts: 24.6 us -> 5.5 us
  waiting for transfers between devices: 111 us -> 117 us
  matrix products: 7.13 us -> 4.17 us
    ppermute x6 -> x3, starting transfers between devices: 34 us -> 10.3 us  [butterfly_sum(): value = value + lax.ppermute(value, axis, partner_perm(size, bit))]
    ppermute x6 -> x9, starting transfers between devices: 28.9 us -> 51.4 us  [halving_scatter(): value = keep + lax.ppermute(send, axis, partner_perm(size, bit))]
    ppermute x6 -> x9, waiting for transfers between devices: 11.3 us -> 28.9 us  [halving_scatter(): value = keep + lax.ppermute(send, axis, partner_perm(size, bit))]
    add x1 -> x0, local copies, waits for them, and re-layouts: 16.8 us -> none  [butterfly_sum(): value = value + lax.ppermute(value, axis, partner_perm(size, bit))]
    ppermute x9, waiting for transfers between devices: 35.7 us -> 27.3 us  [doubling_gather(): other = lax.ppermute(value, axis, partner_perm(size, bit))]
    ppermute x6 -> x3, waiting for transfers between devices: 64.4 us -> 60.6 us  [butterfly_sum(): value = value + lax.ppermute(value, axis, partner_perm(size, bit))]
    ppermute x9, starting transfers between devices: 45.3 us -> 48.3 us  [doubling_gather(): other = lax.ppermute(value, axis, partner_perm(size, bit))]
    unnamed x7 -> x14, local copies, waits for them, and re-layouts: 5.41 us -> 4.85 us
  transfers between devices with their start and end apart: 21 -> 21, of which waited for: 19 -> 21; matrix products, arithmetic and copies ran while one was open for 3% -> 1% of each run, Pallas kernels for 0% -> 0%
where the time goes in v2:
time: 241 us; the launch traced here: 240 us
  waiting for transfers between devices  117 us (49%)
  starting transfers between devices  110 us (46%)
  local copies, waits for them, and re-layouts  5.5 us (2%)
  matrix products  4.17 us (2%)
  other arithmetic  2.72 us (1%)
    ppermute x3, waiting for transfers between devices, butterfly_sum(): value = value + lax.ppermute(value, axis, partner_perm(size, bit))  60.6 us
    ppermute x9, starting transfers between devices, halving_scatter(): value = keep + lax.ppermute(send, axis, partner_perm(size, bit))  51.4 us
    ppermute x9, starting transfers between devices, doubling_gather(): other = lax.ppermute(value, axis, partner_perm(size, bit))  48.3 us
    ppermute x9, waiting for transfers between devices, halving_scatter(): value = keep + lax.ppermute(send, axis, partner_perm(size, bit))  28.9 us
    ppermute x9, waiting for transfers between devices, doubling_gather(): other = lax.ppermute(value, axis, partner_perm(size, bit))  27.3 us
    ppermute x3, starting transfers between devices, butterfly_sum(): value = value + lax.ppermute(value, axis, partner_perm(size, bit))  10.3 us
    unnamed x14, local copies, waits for them, and re-layouts  4.85 us
  transfers between devices with their start and end apart: 21, of which 21 were waited for; matrix products, arithmetic and copies ran while one was open for 1% of the time, Pallas kernels for 0%

profile of v2, /device:TPU:1, one launch (start us, length us, event | category | flops | bytes accessed | tf_op | source)
XLA Modules:
  0.0 240.3 jit_solution(3280592917202608704)
XLA Ops:
  0.7 1.3 copy.42
  2.1 0.3 fusion.23
  2.4 4.8 %collective-permute-start = (f32[2,192,128]{2,1,0:T(8,128)S(1)}, f32[2,192,128]{2,1,0:T(8,128)S(1)}, u32[]{:S(2)}, u32[]{:S(2)}) collective-permute-start(f32[2,192,128]{2,1,0:T(8,128)S(1)} %constant_dynamic-slice_fusion.7), channel_id=1, source_target_pairs={{0,1},{1,0},{2,3},{3,2},{4,5},{5,4},{6,7},{7,6},{8,9},{9,8},{10,11... | collective-permute-start | bytes 589832 | tf_op jit(solution)/shard_map/ppermute | solution.py:45
  7.3 3.0 %collective-permute-done = f32[2,192,128]{2,1,0:T(8,128)S(1)} collective-permute-done((f32[2,192,128]{2,1,0:T(8,128)S(1)}, f32[2,192,128]{2,1,0:T(8,128)S(1)}, u32[]{:S(2)}, u32[]{:S(2)}) %collective-permute-start) | collective-permute-done | bytes 196640 | tf_op jit(solution)/shard_map/ppermute | solution.py:45
  10.3 0.1 constant_dynamic-slice_fusion.6
  10.4 7.4 %collective-permute-start.1 = (f32[2,192,64]{2,1,0:T(8,128)S(1)}, f32[2,192,64]{2,1,0:T(8,128)S(1)}, u32[]{:S(2)}, u32[]{:S(2)}) collective-permute-start(f32[2,192,64]{2,1,0:T(8,128)S(1)} %constant_dynamic-slice_fusion.6), channel_id=1, source_target_pairs={{0,2},{1,3},{2,0},{3,1},{4,6},{5,7},{6,4},{7,5},{8,10},{9,11},{10,... | collective-permute-start | bytes 294920 | tf_op jit(solution)/shard_map/ppermute | solution.py:45
  17.8 8.4 %collective-permute-done.1 = f32[2,192,64]{2,1,0:T(8,128)S(1)} collective-permute-done((f32[2,192,64]{2,1,0:T(8,128)S(1)}, f32[2,192,64]{2,1,0:T(8,128)S(1)}, u32[]{:S(2)}, u32[]{:S(2)}) %collective-permute-start.1) | collective-permute-done | bytes 98336 | tf_op jit(solution)/shard_map/ppermute | solution.py:45
  26.2 0.1 dynamic-slice_add_fusion.1
  26.4 0.1 constant_dynamic-slice_fusion.5
  26.5 8.4 %collective-permute-start.2 = (f32[2,192,32]{2,1,0:T(8,128)S(1)}, f32[2,192,32]{2,1,0:T(8,128)S(1)}, u32[]{:S(2)}, u32[]{:S(2)}) collective-permute-start(f32[2,192,32]{2,1,0:T(8,128)S(1)} %constant_dynamic-slice_fusion.5), channel_id=1, source_target_pairs={{0,4},{1,5},{2,6},{3,7},{4,0},{5,1},{6,2},{7,3},{8,12},{9,13},{10,... | collective-permute-start | bytes 147464 | tf_op jit(solution)/shard_map/ppermute | solution.py:45
  34.9 0.1 copy.45
  35.0 0.7 copy-done.3
  35.9 5.8 %collective-permute-done.2 = f32[2,192,32]{2,1,0:T(8,128)S(1)} collective-permute-done((f32[2,192,32]{2,1,0:T(8,128)S(1)}, f32[2,192,32]{2,1,0:T(8,128)S(1)}, u32[]{:S(2)}, u32[]{:S(2)}) %collective-permute-start.2) | collective-permute-done | bytes 49184 | tf_op jit(solution)/shard_map/ppermute | solution.py:45
  41.7 0.1 convert_bitcast_fusion
  41.8 0.1 fusion.16
  42.0 5.5 %collective-permute-start.3 = (bf16[2,2,192,32]{3,2,1,0:T(8,128)(2,1)S(1)}, bf16[2,2,192,32]{3,2,1,0:T(8,128)(2,1)S(1)}, u32[]{:S(2)}, u32[]{:S(2)}) collective-permute-start(bf16[2,2,192,32]{3,2,1,0:T(8,128)(2,1)S(1)} %pad_maximum_fusion.5), channel_id=1, source_target_pairs={{0,4},{1,5},{2,6},{3,7},{4,0},{5,1},{6,2},{7,3},{8,12},{9,13},{10,... | collective-permute-start | bytes 147464 | tf_op jit(solution)/shard_map/ppermute | solution.py:53
  47.5 7.1 %collective-permute-done.3 = bf16[2,2,192,32]{3,2,1,0:T(8,128)(2,1)S(1)} collective-permute-done((bf16[2,2,192,32]{3,2,1,0:T(8,128)(2,1)S(1)}, bf16[2,2,192,32]{3,2,1,0:T(8,128)(2,1)S(1)}, u32[]{:S(2)}, u32[]{:S(2)}) %collective-permute-start.3) | collective-permute-done | bytes 49184 | tf_op jit(solution)/shard_map/ppermute | solution.py:53
  54.7 0.1 pad_maximum_fusion.6
  54.8 1.9 collective-permute-start.4
  56.7 5.4 %collective-permute-done.4 = bf16[2,2,192,64]{3,2,1,0:T(8,128)(2,1)S(1)} collective-permute-done((bf16[2,2,192,64]{3,2,1,0:T(8,128)(2,1)S(1)}, bf16[2,2,192,64]{3,2,1,0:T(8,128)(2,1)S(1)}, u32[]{:S(2)}, u32[]{:S(2)}) %collective-permute-start.4) | collective-permute-done | bytes 98336 | tf_op jit(solution)/shard_map/ppermute | solution.py:53
  62.1 0.2 broadcast_select_fusion.3
  62.3 0.1 pad_maximum_fusion.7
  62.4 7.0 %collective-permute-start.5 = (bf16[2,2,192,128]{3,2,1,0:T(8,128)(2,1)S(1)}, bf16[2,2,192,128]{3,2,1,0:T(8,128)(2,1)S(1)}, u32[]{:S(2)}, u32[]{:S(2)}) collective-permute-start(bf16[2,2,192,128]{3,2,1,0:T(8,128)(2,1)S(1)} %pad_maximum_fusion.7), channel_id=1, source_target_pairs={{0,1},{1,0},{2,3},{3,2},{4,5},{5,4},{6,7},{7,6},{8,9},{9,8},{10,11... | collective-permute-start | bytes 589832 | tf_op jit(solution)/shard_map/ppermute | solution.py:53
  69.5 3.1 %collective-permute-done.5 = bf16[2,2,192,128]{3,2,1,0:T(8,128)(2,1)S(1)} collective-permute-done((bf16[2,2,192,128]{3,2,1,0:T(8,128)(2,1)S(1)}, bf16[2,2,192,128]{3,2,1,0:T(8,128)(2,1)S(1)}, u32[]{:S(2)}, u32[]{:S(2)}) %collective-permute-start.5) | collective-permute-done | bytes 196640 | tf_op jit(solution)/shard_map/ppermute | solution.py:53
  72.6 0.2 broadcast_select_fusion.4
  72.8 0.3 fusion.13
  73.1 8.4 %collective-permute-start.6 = (f32[1,320,256]{2,1,0:T(8,128)S(1)}, f32[1,320,256]{2,1,0:T(8,128)S(1)}, u32[]{:S(2)}, u32[]{:S(2)}) collective-permute-start(f32[1,320,256]{2,1,0:T(8,128)S(1)} %dynamic-slice_bitcast_fusion), channel_id=1, source_target_pairs={{0,8},{8,0},{16,24},{24,16},{32,40},{40,32},{48,56},{56,48},{64,72... | collective-permute-start | bytes 983048 | tf_op jit(solution)/shard_map/ppermute | solution.py:45
  81.5 1.2 collective-permute-done.6
  82.8 3.0 %collective-permute-start.7 = (f32[1,320,128]{2,1,0:T(8,128)S(1)}, f32[1,320,128]{2,1,0:T(8,128)S(1)}, u32[]{:S(2)}, u32[]{:S(2)}) collective-permute-start(f32[1,320,128]{2,1,0:T(8,128)S(1)} %constant_dynamic-slice_fusion.4), channel_id=1, source_target_pairs={{0,16},{8,24},{16,0},{24,8},{32,48},{40,56},{48,32},{56,40},{64,80... | collective-permute-start | bytes 491528 | tf_op jit(solution)/shard_map/ppermute | solution.py:45
  85.8 4.2 %collective-permute-done.7 = f32[1,320,128]{2,1,0:T(8,128)S(1)} collective-permute-done((f32[1,320,128]{2,1,0:T(8,128)S(1)}, f32[1,320,128]{2,1,0:T(8,128)S(1)}, u32[]{:S(2)}, u32[]{:S(2)}) %collective-permute-start.7) | collective-permute-done | bytes 163872 | tf_op jit(solution)/shard_map/ppermute | solution.py:45
  90.1 3.1 %collective-permute-start.8 = (f32[1,160,128]{2,1,0:T(8,128)S(1)}, f32[1,160,128]{2,1,0:T(8,128)S(1)}, u32[]{:S(2)}, u32[]{:S(2)}) collective-permute-start(f32[1,160,128]{2,1,0:T(8,128)S(1)} %constant_dynamic-slice_fusion.3), channel_id=1, source_target_pairs={{0,64},{8,72},{16,80},{24,88},{32,96},{40,104},{48,112},{56,120},{... | collective-permute-start | bytes 245768 | tf_op jit(solution)/shard_map/ppermute | solution.py:45
  93.3 2.0 collective-permute-done.8
  95.3 4.5 %collective-permute-start.9 = (f32[1,80,128]{2,1,0:T(8,128)S(1)}, f32[1,80,128]{2,1,0:T(8,128)S(1)}, u32[]{:S(2)}, u32[]{:S(2)}) collective-permute-start(f32[1,80,128]{2,1,0:T(8,128)S(1)} %constant_dynamic-slice_fusion.2), channel_id=1, source_target_pairs={{0,32},{8,40},{16,48},{24,56},{32,0},{40,8},{48,16},{56,24},{64,96... | collective-permute-start | bytes 122888 | tf_op jit(solution)/shard_map/ppermute | solution.py:45
  99.9 1.7 collective-permute-done.9
  101.6 4.2 %collective-permute-start.10 = (f32[1,40,128]{2,1,0:T(8,128)S(1)}, f32[1,40,128]{2,1,0:T(8,128)S(1)}, u32[]{:S(2)}, u32[]{:S(2)}) collective-permute-start(f32[1,40,128]{2,1,0:T(8,128)S(1)} %constant_dynamic-slice_fusion.1), channel_id=1, source_target_pairs={{0,128},{8,136},{16,144},{24,152},{32,160},{40,168},{48,176},{56,1... | collective-permute-start | bytes 61448 | tf_op jit(solution)/shard_map/ppermute | solution.py:45
  105.8 1.3 collective-permute-done.10
  107.1 7.6 %collective-permute-start.11 = (f32[1,20,128]{2,1,0:T(8,128)S(1)}, f32[1,20,128]{2,1,0:T(8,128)S(1)}, u32[]{:S(2)}, u32[]{:S(2)}) collective-permute-start(f32[1,20,128]{2,1,0:T(8,128)S(1)} %constant_dynamic-slice_fusion), channel_id=1, source_target_pairs={{0,256},{8,264},{16,272},{24,280},{32,288},{40,296},{48,304},{56,3... | collective-permute-start | bytes 30728 | tf_op jit(solution)/shard_map/ppermute | solution.py:45
  114.7 1.1 collective-permute-done.11
  115.8 7.2 %collective-permute-start.12 = (f32[1,20,128]{2,1,0:T(8,128)S(1)}, f32[1,20,128]{2,1,0:T(8,128)S(1)}, u32[]{:S(2)}, u32[]{:S(2)}) collective-permute-start(f32[1,20,128]{2,1,0:T(8,128)S(1)} %dynamic-slice_add_fusion.7), channel_id=1, source_target_pairs={{0,256},{8,264},{16,272},{24,280},{32,288},{40,296},{48,304},{56,3... | collective-permute-start | bytes 30728 | tf_op jit(solution)/shard_map/ppermute | solution.py:53
  123.0 1.2 collective-permute-done.12
  124.2 3.8 %collective-permute-start.13 = (f32[1,40,128]{2,1,0:T(8,128)S(1)}, f32[1,40,128]{2,1,0:T(8,128)S(1)}, u32[]{:S(2)}, u32[]{:S(2)}) collective-permute-start(f32[1,40,128]{2,1,0:T(8,128)S(1)} %pad_maximum_fusion.11), channel_id=1, source_target_pairs={{0,128},{8,136},{16,144},{24,152},{32,160},{40,168},{48,176},{56,1... | collective-permute-start | bytes 61448 | tf_op jit(solution)/shard_map/ppermute | solution.py:53
  128.1 1.9 collective-permute-done.13
  130.0 4.5 %collective-permute-start.14 = (f32[1,80,128]{2,1,0:T(8,128)S(1)}, f32[1,80,128]{2,1,0:T(8,128)S(1)}, u32[]{:S(2)}, u32[]{:S(2)}) collective-permute-start(f32[1,80,128]{2,1,0:T(8,128)S(1)} %pad_maximum_fusion.10), channel_id=1, source_target_pairs={{0,32},{8,40},{16,48},{24,56},{32,0},{40,8},{48,16},{56,24},{64,96... | collective-permute-start | bytes 122888 | tf_op jit(solution)/shard_map/ppermute | solution.py:53
  134.4 1.8 collective-permute-done.14
  136.2 2.8 %collective-permute-start.15 = (f32[1,160,128]{2,1,0:T(8,128)S(1)}, f32[1,160,128]{2,1,0:T(8,128)S(1)}, u32[]{:S(2)}, u32[]{:S(2)}) collective-permute-start(f32[1,160,128]{2,1,0:T(8,128)S(1)} %pad_maximum_fusion.9), channel_id=1, source_target_pairs={{0,64},{8,72},{16,80},{24,88},{32,96},{40,104},{48,112},{56,120},{... | collective-permute-start | bytes 245768 | tf_op jit(solution)/shard_map/ppermute | solution.py:53
  139.0 2.4 collective-permute-done.15
  141.5 2.8 %collective-permute-start.16 = (f32[1,320,128]{2,1,0:T(8,128)S(1)}, f32[1,320,128]{2,1,0:T(8,128)S(1)}, u32[]{:S(2)}, u32[]{:S(2)}) collective-permute-start(f32[1,320,128]{2,1,0:T(8,128)S(1)} %pad_maximum_fusion.8), channel_id=1, source_target_pairs={{0,16},{8,24},{16,0},{24,8},{32,48},{40,56},{48,32},{56,40},{64,80... | collective-permute-start | bytes 491528 | tf_op jit(solution)/shard_map/ppermute | solution.py:53
  144.3 3.3 %collective-permute-done.16 = f32[1,320,128]{2,1,0:T(8,128)S(1)} collective-permute-done((f32[1,320,128]{2,1,0:T(8,128)S(1)}, f32[1,320,128]{2,1,0:T(8,128)S(1)}, u32[]{:S(2)}, u32[]{:S(2)}) %collective-permute-start.16) | collective-permute-done | bytes 163872 | tf_op jit(solution)/shard_map/ppermute | solution.py:53
  147.6 12.8 %collective-permute-start.17 = (f32[1,320,256]{2,1,0:T(8,128)S(1)}, f32[1,320,256]{2,1,0:T(8,128)S(1)}, u32[]{:S(2)}, u32[]{:S(2)}) collective-permute-start(f32[1,320,256]{2,1,0:T(8,128)S(1)} %pad_maximum_fusion.3), channel_id=1, source_target_pairs={{0,8},{8,0},{16,24},{24,16},{32,40},{40,32},{48,56},{56,48},{64,72... | collective-permute-start | bytes 983048 | tf_op jit(solution)/shard_map/ppermute | solution.py:53
  160.4 1.2 collective-permute-done.17
  161.7 1.6 fusion.4
  163.2 1.9 collective-permute-start.18
  165.2 13.1 %collective-permute-done.18 = f32[2,256,256]{2,1,0:T(8,128)S(1)} collective-permute-done((f32[2,256,256]{2,1,0:T(8,128)S(1)}, f32[2,256,256]{2,1,0:T(8,128)S(1)}, u32[]{:S(2)}, u32[]{:S(2)}) %collective-permute-start.18) | collective-permute-done | bytes 524320 | tf_op jit(solution)/shard_map/ppermute | solution.py:33
  178.3 2.7 %collective-permute-start.19 = (f32[2,256,256]{2,1,0:T(8,128)S(1)}, f32[2,256,256]{2,1,0:T(8,128)S(1)}, u32[]{:S(2)}, u32[]{:S(2)}) collective-permute-start(f32[2,256,256]{2,1,0:T(8,128)S(1)} %add.144), channel_id=1, source_target_pairs={{0,2},{1,3},{2,0},{3,1},{4,6},{5,7},{6,4},{7,5},{8,10},{9,11},{10,... | collective-permute-start | bytes 1572872 | tf_op jit(solution)/shard_map/ppermute | solution.py:33
  181.0 25.2 %collective-permute-done.19 = f32[2,256,256]{2,1,0:T(8,128)S(1)} collective-permute-done((f32[2,256,256]{2,1,0:T(8,128)S(1)}, f32[2,256,256]{2,1,0:T(8,128)S(1)}, u32[]{:S(2)}, u32[]{:S(2)}) %collective-permute-start.19) | collective-permute-done | bytes 524320 | tf_op jit(solution)/shard_map/ppermute | solution.py:33
  206.2 5.7 %collective-permute-start.20 = (f32[2,256,256]{2,1,0:T(8,128)S(1)}, f32[2,256,256]{2,1,0:T(8,128)}, u32[]{:S(2)}, u32[]{:S(2)}) collective-permute-start(f32[2,256,256]{2,1,0:T(8,128)S(1)} %add.145), channel_id=1, source_target_pairs={{0,4},{1,5},{2,6},{3,7},{4,0},{5,1},{6,2},{7,3},{8,12},{9,13},{10,... | collective-permute-start | bytes 1572872 | tf_op jit(solution)/shard_map/ppermute | solution.py:33
  212.0 0.7 copy.50
  212.7 0.7 copy.51
  213.4 1.1 fusion
  214.5 22.3 %collective-permute-done.20 = f32[2,256,256]{2,1,0:T(8,128)} collective-permute-done((f32[2,256,256]{2,1,0:T(8,128)S(1)}, f32[2,256,256]{2,1,0:T(8,128)}, u32[]{:S(2)}, u32[]{:S(2)}) %collective-permute-start.20) | collective-permute-done | bytes 524320 | tf_op jit(solution)/shard_map/ppermute | solution.py:33
  236.8 1.2 select_reduce_fusion
  238.0 0.9 multiply_convert_fusion
  238.9 0.2 copy.48
  239.2 1.1 copy.52
  (40 shorter events, 0.9 us)
Async XLA Ops:
  0.6 1.4 copy-start
  2.4 7.9 %collective-permute-start = (f32[2,192,128]{2,1,0:T(8,128)S(1)}, f32[2,192,128]{2,1,0:T(8,128)S(1)}, u32[]{:S(2)}, u32[]{:S(2)}) collective-permute-start(f32[2,192,128]{2,1,0:T(8,128)S(1)} %constant_dynamic-slice_fusion.7), channel_id=1, source_target_pairs={{0,1},{1,0},{2,3},{3,2},{4,5},{5,4},{6,7},{7,6},{8,9},{9,8},{10,11... | collective-permute-start | bytes 589832 | tf_op jit(solution)/shard_map/ppermute | solution.py:45
  10.4 15.8 %collective-permute-start.1 = (f32[2,192,64]{2,1,0:T(8,128)S(1)}, f32[2,192,64]{2,1,0:T(8,128)S(1)}, u32[]{:S(2)}, u32[]{:S(2)}) collective-permute-start(f32[2,192,64]{2,1,0:T(8,128)S(1)} %constant_dynamic-slice_fusion.6), channel_id=1, source_target_pairs={{0,2},{1,3},{2,0},{3,1},{4,6},{5,7},{6,4},{7,5},{8,10},{9,11},{10,... | collective-permute-start | bytes 294920 | tf_op jit(solution)/shard_map/ppermute | solution.py:45
  26.3 8.6 %copy-start.2 = (f32[2,192,32]{1,2,0:T(8,128)S(1)}, f32[2,192,32]{1,2,0:T(8,128)}, u32[]{:S(2)}) copy-start(f32[2,192,32]{1,2,0:T(8,128)} %param.8) | copy-start | bytes 147460
  26.5 15.2 %collective-permute-start.2 = (f32[2,192,32]{2,1,0:T(8,128)S(1)}, f32[2,192,32]{2,1,0:T(8,128)S(1)}, u32[]{:S(2)}, u32[]{:S(2)}) collective-permute-start(f32[2,192,32]{2,1,0:T(8,128)S(1)} %constant_dynamic-slice_fusion.5), channel_id=1, source_target_pairs={{0,4},{1,5},{2,6},{3,7},{4,0},{5,1},{6,2},{7,3},{8,12},{9,13},{10,... | collective-permute-start | bytes 147464 | tf_op jit(solution)/shard_map/ppermute | solution.py:45
  34.9 0.8 copy-start.3
  42.0 12.6 %collective-permute-start.3 = (bf16[2,2,192,32]{3,2,1,0:T(8,128)(2,1)S(1)}, bf16[2,2,192,32]{3,2,1,0:T(8,128)(2,1)S(1)}, u32[]{:S(2)}, u32[]{:S(2)}) collective-permute-start(bf16[2,2,192,32]{3,2,1,0:T(8,128)(2,1)S(1)} %pad_maximum_fusion.5), channel_id=1, source_target_pairs={{0,4},{1,5},{2,6},{3,7},{4,0},{5,1},{6,2},{7,3},{8,12},{9,13},{10,... | collective-permute-start | bytes 147464 | tf_op jit(solution)/shard_map/ppermute | solution.py:53
  54.8 7.3 %collective-permute-start.4 = (bf16[2,2,192,64]{3,2,1,0:T(8,128)(2,1)S(1)}, bf16[2,2,192,64]{3,2,1,0:T(8,128)(2,1)S(1)}, u32[]{:S(2)}, u32[]{:S(2)}) collective-permute-start(bf16[2,2,192,64]{3,2,1,0:T(8,128)(2,1)S(1)} %pad_maximum_fusion.6), channel_id=1, source_target_pairs={{0,2},{1,3},{2,0},{3,1},{4,6},{5,7},{6,4},{7,5},{8,10},{9,11},{10,... | collective-permute-start | bytes 294920 | tf_op jit(solution)/shard_map/ppermute | solution.py:53
  62.4 10.1 %collective-permute-start.5 = (bf16[2,2,192,128]{3,2,1,0:T(8,128)(2,1)S(1)}, bf16[2,2,192,128]{3,2,1,0:T(8,128)(2,1)S(1)}, u32[]{:S(2)}, u32[]{:S(2)}) collective-permute-start(bf16[2,2,192,128]{3,2,1,0:T(8,128)(2,1)S(1)} %pad_maximum_fusion.7), channel_id=1, source_target_pairs={{0,1},{1,0},{2,3},{3,2},{4,5},{5,4},{6,7},{7,6},{8,9},{9,8},{10,11... | collective-permute-start | bytes 589832 | tf_op jit(solution)/shard_map/ppermute | solution.py:53
  73.1 9.6 %collective-permute-start.6 = (f32[1,320,256]{2,1,0:T(8,128)S(1)}, f32[1,320,256]{2,1,0:T(8,128)S(1)}, u32[]{:S(2)}, u32[]{:S(2)}) collective-permute-start(f32[1,320,256]{2,1,0:T(8,128)S(1)} %dynamic-slice_bitcast_fusion), channel_id=1, source_target_pairs={{0,8},{8,0},{16,24},{24,16},{32,40},{40,32},{48,56},{56,48},{64,72... | collective-permute-start | bytes 983048 | tf_op jit(solution)/shard_map/ppermute | solution.py:45
  82.8 7.3 %collective-permute-start.7 = (f32[1,320,128]{2,1,0:T(8,128)S(1)}, f32[1,320,128]{2,1,0:T(8,128)S(1)}, u32[]{:S(2)}, u32[]{:S(2)}) collective-permute-start(f32[1,320,128]{2,1,0:T(8,128)S(1)} %constant_dynamic-slice_fusion.4), channel_id=1, source_target_pairs={{0,16},{8,24},{16,0},{24,8},{32,48},{40,56},{48,32},{56,40},{64,80... | collective-permute-start | bytes 491528 | tf_op jit(solution)/shard_map/ppermute | solution.py:45
  90.1 5.2 %collective-permute-start.8 = (f32[1,160,128]{2,1,0:T(8,128)S(1)}, f32[1,160,128]{2,1,0:T(8,128)S(1)}, u32[]{:S(2)}, u32[]{:S(2)}) collective-permute-start(f32[1,160,128]{2,1,0:T(8,128)S(1)} %constant_dynamic-slice_fusion.3), channel_id=1, source_target_pairs={{0,64},{8,72},{16,80},{24,88},{32,96},{40,104},{48,112},{56,120},{... | collective-permute-start | bytes 245768 | tf_op jit(solution)/shard_map/ppermute | solution.py:45
  95.3 6.3 %collective-permute-start.9 = (f32[1,80,128]{2,1,0:T(8,128)S(1)}, f32[1,80,128]{2,1,0:T(8,128)S(1)}, u32[]{:S(2)}, u32[]{:S(2)}) collective-permute-start(f32[1,80,128]{2,1,0:T(8,128)S(1)} %constant_dynamic-slice_fusion.2), channel_id=1, source_target_pairs={{0,32},{8,40},{16,48},{24,56},{32,0},{40,8},{48,16},{56,24},{64,96... | collective-permute-start | bytes 122888 | tf_op jit(solution)/shard_map/ppermute | solution.py:45
  101.6 5.4 %collective-permute-start.10 = (f32[1,40,128]{2,1,0:T(8,128)S(1)}, f32[1,40,128]{2,1,0:T(8,128)S(1)}, u32[]{:S(2)}, u32[]{:S(2)}) collective-permute-start(f32[1,40,128]{2,1,0:T(8,128)S(1)} %constant_dynamic-slice_fusion.1), channel_id=1, source_target_pairs={{0,128},{8,136},{16,144},{24,152},{32,160},{40,168},{48,176},{56,1... | collective-permute-start | bytes 61448 | tf_op jit(solution)/shard_map/ppermute | solution.py:45
  107.1 8.7 %collective-permute-start.11 = (f32[1,20,128]{2,1,0:T(8,128)S(1)}, f32[1,20,128]{2,1,0:T(8,128)S(1)}, u32[]{:S(2)}, u32[]{:S(2)}) collective-permute-start(f32[1,20,128]{2,1,0:T(8,128)S(1)} %constant_dynamic-slice_fusion), channel_id=1, source_target_pairs={{0,256},{8,264},{16,272},{24,280},{32,288},{40,296},{48,304},{56,3... | collective-permute-start | bytes 30728 | tf_op jit(solution)/shard_map/ppermute | solution.py:45
  115.8 8.4 %collective-permute-start.12 = (f32[1,20,128]{2,1,0:T(8,128)S(1)}, f32[1,20,128]{2,1,0:T(8,128)S(1)}, u32[]{:S(2)}, u32[]{:S(2)}) collective-permute-start(f32[1,20,128]{2,1,0:T(8,128)S(1)} %dynamic-slice_add_fusion.7), channel_id=1, source_target_pairs={{0,256},{8,264},{16,272},{24,280},{32,288},{40,296},{48,304},{56,3... | collective-permute-start | bytes 30728 | tf_op jit(solution)/shard_map/ppermute | solution.py:53
  124.2 5.7 %collective-permute-start.13 = (f32[1,40,128]{2,1,0:T(8,128)S(1)}, f32[1,40,128]{2,1,0:T(8,128)S(1)}, u32[]{:S(2)}, u32[]{:S(2)}) collective-permute-start(f32[1,40,128]{2,1,0:T(8,128)S(1)} %pad_maximum_fusion.11), channel_id=1, source_target_pairs={{0,128},{8,136},{16,144},{24,152},{32,160},{40,168},{48,176},{56,1... | collective-permute-start | bytes 61448 | tf_op jit(solution)/shard_map/ppermute | solution.py:53
  130.0 6.3 %collective-permute-start.14 = (f32[1,80,128]{2,1,0:T(8,128)S(1)}, f32[1,80,128]{2,1,0:T(8,128)S(1)}, u32[]{:S(2)}, u32[]{:S(2)}) collective-permute-start(f32[1,80,128]{2,1,0:T(8,128)S(1)} %pad_maximum_fusion.10), channel_id=1, source_target_pairs={{0,32},{8,40},{16,48},{24,56},{32,0},{40,8},{48,16},{56,24},{64,96... | collective-permute-start | bytes 122888 | tf_op jit(solution)/shard_map/ppermute | solution.py:53
  136.2 5.2 %collective-permute-start.15 = (f32[1,160,128]{2,1,0:T(8,128)S(1)}, f32[1,160,128]{2,1,0:T(8,128)S(1)}, u32[]{:S(2)}, u32[]{:S(2)}) collective-permute-start(f32[1,160,128]{2,1,0:T(8,128)S(1)} %pad_maximum_fusion.9), channel_id=1, source_target_pairs={{0,64},{8,72},{16,80},{24,88},{32,96},{40,104},{48,112},{56,120},{... | collective-permute-start | bytes 245768 | tf_op jit(solution)/shard_map/ppermute | solution.py:53
  141.5 6.1 %collective-permute-start.16 = (f32[1,320,128]{2,1,0:T(8,128)S(1)}, f32[1,320,128]{2,1,0:T(8,128)S(1)}, u32[]{:S(2)}, u32[]{:S(2)}) collective-permute-start(f32[1,320,128]{2,1,0:T(8,128)S(1)} %pad_maximum_fusion.8), channel_id=1, source_target_pairs={{0,16},{8,24},{16,0},{24,8},{32,48},{40,56},{48,32},{56,40},{64,80... | collective-permute-start | bytes 491528 | tf_op jit(solution)/shard_map/ppermute | solution.py:53
  147.6 14.0 %collective-permute-start.17 = (f32[1,320,256]{2,1,0:T(8,128)S(1)}, f32[1,320,256]{2,1,0:T(8,128)S(1)}, u32[]{:S(2)}, u32[]{:S(2)}) collective-permute-start(f32[1,320,256]{2,1,0:T(8,128)S(1)} %pad_maximum_fusion.3), channel_id=1, source_target_pairs={{0,8},{8,0},{16,24},{24,16},{32,40},{40,32},{48,56},{56,48},{64,72... | collective-permute-start | bytes 983048 | tf_op jit(solution)/shard_map/ppermute | solution.py:53
  163.2 15.0 %collective-permute-start.18 = (f32[2,256,256]{2,1,0:T(8,128)S(1)}, f32[2,256,256]{2,1,0:T(8,128)S(1)}, u32[]{:S(2)}, u32[]{:S(2)}) collective-permute-start(f32[2,256,256]{2,1,0:T(8,128)S(1)} %fusion.4), channel_id=1, source_target_pairs={{0,1},{1,0},{2,3},{3,2},{4,5},{5,4},{6,7},{7,6},{8,9},{9,8},{10,11... | collective-permute-start | bytes 1572872 | tf_op jit(solution)/shard_map/ppermute | solution.py:33
  178.3 27.9 %collective-permute-start.19 = (f32[2,256,256]{2,1,0:T(8,128)S(1)}, f32[2,256,256]{2,1,0:T(8,128)S(1)}, u32[]{:S(2)}, u32[]{:S(2)}) collective-permute-start(f32[2,256,256]{2,1,0:T(8,128)S(1)} %add.144), channel_id=1, source_target_pairs={{0,2},{1,3},{2,0},{3,1},{4,6},{5,7},{6,4},{7,5},{8,10},{9,11},{10,... | collective-permute-start | bytes 1572872 | tf_op jit(solution)/shard_map/ppermute | solution.py:33
  206.2 7.3 %copy-start.1 = (f32[2,192,320]{2,1,0:T(8,128)S(1)}, f32[2,192,320]{2,1,0:T(8,128)}, u32[]{:S(2)}) copy-start(f32[2,192,320]{2,1,0:T(8,128)} %param.6) | copy-start | bytes 1474564
  206.2 30.5 %collective-permute-start.20 = (f32[2,256,256]{2,1,0:T(8,128)S(1)}, f32[2,256,256]{2,1,0:T(8,128)}, u32[]{:S(2)}, u32[]{:S(2)}) collective-permute-start(f32[2,256,256]{2,1,0:T(8,128)S(1)} %add.145), channel_id=1, source_target_pairs={{0,4},{1,5},{2,6},{3,7},{4,0},{5,1},{6,2},{7,3},{8,12},{9,13},{10,... | collective-permute-start | bytes 1572872 | tf_op jit(solution)/shard_map/ppermute | solution.py:33

commit v3 on v2

--- a/solution.py
+++ b/solution.py
@@ -64,6 +64,33 @@
     return jnp.transpose(split, axes).reshape(value.shape)
 
 
+def block_masks(shape):
+    rows = lax.broadcasted_iota(jnp.int32, shape, 1)
+    cols = lax.broadcasted_iota(jnp.int32, shape, 2)
+    return rows < cols, rows == cols, rows > cols
+
+
+def pack_gram(gram):
+    h = gram.shape[1] // 2
+    top_left, top_right, bottom_right = gram[:, :h, :h], gram[:, :h, h:], gram[:, h:, h:]
+    upper, same, lower = block_masks(top_left.shape)
+    folded = jnp.where(upper | same, top_left, bottom_right)
+    corner = jnp.sum(jnp.where(same, bottom_right, 0.0), axis=1, keepdims=True)
+    return jnp.concatenate([folded, top_right, corner], axis=1)
+
+
+def unpack_gram(packed):
+    h = packed.shape[2]
+    folded, top_right, corner = packed[:, :h], packed[:, h : 2 * h], packed[:, 2 * h :]
+    upper, same, lower = block_masks(folded.shape)
+    flipped = jnp.transpose(folded, (0, 2, 1))
+    top_left = jnp.where(upper | same, folded, flipped)
+    bottom_right = jnp.where(lower, folded, jnp.where(same, corner, flipped))
+    top = jnp.concatenate([top_left, top_right], axis=2)
+    bottom = jnp.concatenate([jnp.transpose(top_right, (0, 2, 1)), bottom_right], axis=2)
+    return jnp.concatenate([top, bottom], axis=1)
+
+
 def shards(grads, weights, basis, first_moment, second_moment):
     highest = lax.Precision.HIGHEST
     fsdp = lax.axis_size("fsdp")
@@ -87,7 +114,7 @@
     update = jnp.einsum("mfr,dmr->mfd", normal_full, basis_order, preferred_element_type=jnp.float32)
     weight_next = weights - LEARNING_RATE * GALORE_SCALE * update
 
-    gram = butterfly_sum(jnp.einsum("mdr,mds->mrs", image, image, precision=highest), "tp", tp)
+    gram = unpack_gram(butterfly_sum(pack_gram(jnp.einsum("mdr,mds->mrs", image, image, precision=highest)), "tp", tp))
     diagonal = lax.broadcasted_iota(jnp.int32, gram.shape, 1) == lax.broadcasted_iota(jnp.int32, gram.shape, 2)
     total = jnp.sum(jnp.where(diagonal, gram, 0.0), axis=(1, 2)) + EPSILON_NORM
     factor = jnp.sqrt(rank_width / total)

time: 241 us -> 213 us (0.88)
  waiting for transfers between devices: 117 us -> 89.4 us
    ppermute x3, waiting for transfers between devices: 60.6 us -> 33.2 us  [butterfly_sum(): value = value + lax.ppermute(value, axis, partner_perm(size, bit))]
    unnamed x14 -> x17, local copies, waits for them, and re-layouts: 4.85 us -> 5.13 us
where the time goes in v3:
time: 213 us
  starting transfers between devices  110 us (52%)
  waiting for transfers between devices  89.4 us (42%)
  local copies, waits for them, and re-layouts  6.05 us (3%)
  matrix products  4.17 us (2%)
    ppermute x9, starting transfers between devices, halving_scatter(): value = keep + lax.ppermute(send, axis, partner_perm(size, bit))  51.4 us
    ppermute x9, starting transfers between devices, doubling_gather(): other = lax.ppermute(value, axis, partner_perm(size, bit))  48.3 us
    ppermute x3, waiting for transfers between devices, butterfly_sum(): value = value + lax.ppermute(value, axis, partner_perm(size, bit))  33.2 us
    ppermute x9, waiting for transfers between devices, halving_scatter(): value = keep + lax.ppermute(send, axis, partner_perm(size, bit))  28.9 us
    ppermute x9, waiting for transfers between devices, doubling_gather(): other = lax.ppermute(value, axis, partner_perm(size, bit))  27.3 us
    ppermute x3, starting transfers between devices, butterfly_sum(): value = value + lax.ppermute(value, axis, partner_perm(size, bit))  10.2 us
    unnamed x17, local copies, waits for them, and re-layouts  5.13 us
  transfers between devices with their start and end apart: 21, of which 21 were waited for; matrix products, arithmetic and copies ran while one was open for 1% of the time, Pallas kernels for 0%

profile of v3, /device:TPU:1, one launch (start us, length us, event | category | flops | bytes accessed | tf_op | source)
XLA Modules:
  0.0 212.6 jit_solution(4030874940889746892)
XLA Ops:
  0.7 1.3 copy.63
  2.1 0.3 fusion.32
  2.4 4.8 %collective-permute-start = (f32[2,192,128]{2,1,0:T(8,128)S(1)}, f32[2,192,128]{2,1,0:T(8,128)S(1)}, u32[]{:S(2)}, u32[]{:S(2)}) collective-permute-start(f32[2,192,128]{2,1,0:T(8,128)S(1)} %constant_dynamic-slice_fusion.7), channel_id=1, source_target_pairs={{0,1},{1,0},{2,3},{3,2},{4,5},{5,4},{6,7},{7,6},{8,9},{9,8},{10,11... | collective-permute-start | bytes 589832 | tf_op jit(solution)/shard_map/ppermute | solution.py:45
  7.3 3.0 %collective-permute-done = f32[2,192,128]{2,1,0:T(8,128)S(1)} collective-permute-done((f32[2,192,128]{2,1,0:T(8,128)S(1)}, f32[2,192,128]{2,1,0:T(8,128)S(1)}, u32[]{:S(2)}, u32[]{:S(2)}) %collective-permute-start) | collective-permute-done | bytes 196640 | tf_op jit(solution)/shard_map/ppermute | solution.py:45
  10.3 0.1 constant_dynamic-slice_fusion.6
  10.4 7.4 %collective-permute-start.1 = (f32[2,192,64]{2,1,0:T(8,128)S(1)}, f32[2,192,64]{2,1,0:T(8,128)S(1)}, u32[]{:S(2)}, u32[]{:S(2)}) collective-permute-start(f32[2,192,64]{2,1,0:T(8,128)S(1)} %constant_dynamic-slice_fusion.6), channel_id=1, source_target_pairs={{0,2},{1,3},{2,0},{3,1},{4,6},{5,7},{6,4},{7,5},{8,10},{9,11},{10,... | collective-permute-start | bytes 294920 | tf_op jit(solution)/shard_map/ppermute | solution.py:45
  17.8 8.4 %collective-permute-done.1 = f32[2,192,64]{2,1,0:T(8,128)S(1)} collective-permute-done((f32[2,192,64]{2,1,0:T(8,128)S(1)}, f32[2,192,64]{2,1,0:T(8,128)S(1)}, u32[]{:S(2)}, u32[]{:S(2)}) %collective-permute-start.1) | collective-permute-done | bytes 98336 | tf_op jit(solution)/shard_map/ppermute | solution.py:45
  26.2 0.1 dynamic-slice_add_fusion.1
  26.4 0.1 constant_dynamic-slice_fusion.5
  26.5 8.4 %collective-permute-start.2 = (f32[2,192,32]{2,1,0:T(8,128)S(1)}, f32[2,192,32]{2,1,0:T(8,128)S(1)}, u32[]{:S(2)}, u32[]{:S(2)}) collective-permute-start(f32[2,192,32]{2,1,0:T(8,128)S(1)} %constant_dynamic-slice_fusion.5), channel_id=1, source_target_pairs={{0,4},{1,5},{2,6},{3,7},{4,0},{5,1},{6,2},{7,3},{8,12},{9,13},{10,... | collective-permute-start | bytes 147464 | tf_op jit(solution)/shard_map/ppermute | solution.py:45
  34.9 0.1 copy.66
  35.0 0.7 copy-done.3
  35.9 5.8 %collective-permute-done.2 = f32[2,192,32]{2,1,0:T(8,128)S(1)} collective-permute-done((f32[2,192,32]{2,1,0:T(8,128)S(1)}, f32[2,192,32]{2,1,0:T(8,128)S(1)}, u32[]{:S(2)}, u32[]{:S(2)}) %collective-permute-start.2) | collective-permute-done | bytes 49184 | tf_op jit(solution)/shard_map/ppermute | solution.py:45
  41.7 0.1 convert_bitcast_fusion
  41.8 0.1 fusion.22
  42.0 5.5 %collective-permute-start.3 = (bf16[2,2,192,32]{3,2,1,0:T(8,128)(2,1)S(1)}, bf16[2,2,192,32]{3,2,1,0:T(8,128)(2,1)S(1)}, u32[]{:S(2)}, u32[]{:S(2)}) collective-permute-start(bf16[2,2,192,32]{3,2,1,0:T(8,128)(2,1)S(1)} %pad_maximum_fusion.6), channel_id=1, source_target_pairs={{0,4},{1,5},{2,6},{3,7},{4,0},{5,1},{6,2},{7,3},{8,12},{9,13},{10,... | collective-permute-start | bytes 147464 | tf_op jit(solution)/shard_map/ppermute | solution.py:53
  47.5 7.1 %collective-permute-done.3 = bf16[2,2,192,32]{3,2,1,0:T(8,128)(2,1)S(1)} collective-permute-done((bf16[2,2,192,32]{3,2,1,0:T(8,128)(2,1)S(1)}, bf16[2,2,192,32]{3,2,1,0:T(8,128)(2,1)S(1)}, u32[]{:S(2)}, u32[]{:S(2)}) %collective-permute-start.3) | collective-permute-done | bytes 49184 | tf_op jit(solution)/shard_map/ppermute | solution.py:53
  54.7 0.1 pad_maximum_fusion.7
  54.8 1.9 collective-permute-start.4
  56.7 5.4 %collective-permute-done.4 = bf16[2,2,192,64]{3,2,1,0:T(8,128)(2,1)S(1)} collective-permute-done((bf16[2,2,192,64]{3,2,1,0:T(8,128)(2,1)S(1)}, bf16[2,2,192,64]{3,2,1,0:T(8,128)(2,1)S(1)}, u32[]{:S(2)}, u32[]{:S(2)}) %collective-permute-start.4) | collective-permute-done | bytes 98336 | tf_op jit(solution)/shard_map/ppermute | solution.py:53
  62.1 0.2 broadcast_select_fusion.3
  62.3 0.1 pad_maximum_fusion.8
  62.4 7.0 %collective-permute-start.5 = (bf16[2,2,192,128]{3,2,1,0:T(8,128)(2,1)S(1)}, bf16[2,2,192,128]{3,2,1,0:T(8,128)(2,1)S(1)}, u32[]{:S(2)}, u32[]{:S(2)}) collective-permute-start(bf16[2,2,192,128]{3,2,1,0:T(8,128)(2,1)S(1)} %pad_maximum_fusion.8), channel_id=1, source_target_pairs={{0,1},{1,0},{2,3},{3,2},{4,5},{5,4},{6,7},{7,6},{8,9},{9,8},{10,11... | collective-permute-start | bytes 589832 | tf_op jit(solution)/shard_map/ppermute | solution.py:53
  69.5 3.1 %collective-permute-done.5 = bf16[2,2,192,128]{3,2,1,0:T(8,128)(2,1)S(1)} collective-permute-done((bf16[2,2,192,128]{3,2,1,0:T(8,128)(2,1)S(1)}, bf16[2,2,192,128]{3,2,1,0:T(8,128)(2,1)S(1)}, u32[]{:S(2)}, u32[]{:S(2)}) %collective-permute-start.5) | collective-permute-done | bytes 196640 | tf_op jit(solution)/shard_map/ppermute | solution.py:53
  72.6 0.2 broadcast_select_fusion.4
  72.8 0.3 fusion.13
  73.1 8.4 %collective-permute-start.6 = (f32[1,320,256]{2,1,0:T(8,128)S(1)}, f32[1,320,256]{2,1,0:T(8,128)S(1)}, u32[]{:S(2)}, u32[]{:S(2)}) collective-permute-start(f32[1,320,256]{2,1,0:T(8,128)S(1)} %dynamic-slice_bitcast_fusion), channel_id=1, source_target_pairs={{0,8},{8,0},{16,24},{24,16},{32,40},{40,32},{48,56},{56,48},{64,72... | collective-permute-start | bytes 983048 | tf_op jit(solution)/shard_map/ppermute | solution.py:45
  81.5 1.2 collective-permute-done.6
  82.8 3.0 %collective-permute-start.7 = (f32[1,320,128]{2,1,0:T(8,128)S(1)}, f32[1,320,128]{2,1,0:T(8,128)S(1)}, u32[]{:S(2)}, u32[]{:S(2)}) collective-permute-start(f32[1,320,128]{2,1,0:T(8,128)S(1)} %constant_dynamic-slice_fusion.4), channel_id=1, source_target_pairs={{0,16},{8,24},{16,0},{24,8},{32,48},{40,56},{48,32},{56,40},{64,80... | collective-permute-start | bytes 491528 | tf_op jit(solution)/shard_map/ppermute | solution.py:45
  85.8 4.2 %collective-permute-done.7 = f32[1,320,128]{2,1,0:T(8,128)S(1)} collective-permute-done((f32[1,320,128]{2,1,0:T(8,128)S(1)}, f32[1,320,128]{2,1,0:T(8,128)S(1)}, u32[]{:S(2)}, u32[]{:S(2)}) %collective-permute-start.7) | collective-permute-done | bytes 163872 | tf_op jit(solution)/shard_map/ppermute | solution.py:45
  90.1 3.1 %collective-permute-start.8 = (f32[1,160,128]{2,1,0:T(8,128)S(1)}, f32[1,160,128]{2,1,0:T(8,128)S(1)}, u32[]{:S(2)}, u32[]{:S(2)}) collective-permute-start(f32[1,160,128]{2,1,0:T(8,128)S(1)} %constant_dynamic-slice_fusion.3), channel_id=1, source_target_pairs={{0,64},{8,72},{16,80},{24,88},{32,96},{40,104},{48,112},{56,120},{... | collective-permute-start | bytes 245768 | tf_op jit(solution)/shard_map/ppermute | solution.py:45
  93.3 2.0 collective-permute-done.8
  95.3 4.5 %collective-permute-start.9 = (f32[1,80,128]{2,1,0:T(8,128)S(1)}, f32[1,80,128]{2,1,0:T(8,128)S(1)}, u32[]{:S(2)}, u32[]{:S(2)}) collective-permute-start(f32[1,80,128]{2,1,0:T(8,128)S(1)} %constant_dynamic-slice_fusion.2), channel_id=1, source_target_pairs={{0,32},{8,40},{16,48},{24,56},{32,0},{40,8},{48,16},{56,24},{64,96... | collective-permute-start | bytes 122888 | tf_op jit(solution)/shard_map/ppermute | solution.py:45
  99.9 1.7 collective-permute-done.9
  101.6 4.2 %collective-permute-start.10 = (f32[1,40,128]{2,1,0:T(8,128)S(1)}, f32[1,40,128]{2,1,0:T(8,128)S(1)}, u32[]{:S(2)}, u32[]{:S(2)}) collective-permute-start(f32[1,40,128]{2,1,0:T(8,128)S(1)} %constant_dynamic-slice_fusion.1), channel_id=1, source_target_pairs={{0,128},{8,136},{16,144},{24,152},{32,160},{40,168},{48,176},{56,1... | collective-permute-start | bytes 61448 | tf_op jit(solution)/shard_map/ppermute | solution.py:45
  105.8 1.3 collective-permute-done.10
  107.1 7.6 %collective-permute-start.11 = (f32[1,20,128]{2,1,0:T(8,128)S(1)}, f32[1,20,128]{2,1,0:T(8,128)S(1)}, u32[]{:S(2)}, u32[]{:S(2)}) collective-permute-start(f32[1,20,128]{2,1,0:T(8,128)S(1)} %constant_dynamic-slice_fusion), channel_id=1, source_target_pairs={{0,256},{8,264},{16,272},{24,280},{32,288},{40,296},{48,304},{56,3... | collective-permute-start | bytes 30728 | tf_op jit(solution)/shard_map/ppermute | solution.py:45
  114.7 1.1 collective-permute-done.11
  115.8 7.2 %collective-permute-start.12 = (f32[1,20,128]{2,1,0:T(8,128)S(1)}, f32[1,20,128]{2,1,0:T(8,128)S(1)}, u32[]{:S(2)}, u32[]{:S(2)}) collective-permute-start(f32[1,20,128]{2,1,0:T(8,128)S(1)} %dynamic-slice_add_fusion.7), channel_id=1, source_target_pairs={{0,256},{8,264},{16,272},{24,280},{32,288},{40,296},{48,304},{56,3... | collective-permute-start | bytes 30728 | tf_op jit(solution)/shard_map/ppermute | solution.py:53
  123.0 1.2 collective-permute-done.12
  124.2 3.8 %collective-permute-start.13 = (f32[1,40,128]{2,1,0:T(8,128)S(1)}, f32[1,40,128]{2,1,0:T(8,128)S(1)}, u32[]{:S(2)}, u32[]{:S(2)}) collective-permute-start(f32[1,40,128]{2,1,0:T(8,128)S(1)} %pad_maximum_fusion.12), channel_id=1, source_target_pairs={{0,128},{8,136},{16,144},{24,152},{32,160},{40,168},{48,176},{56,1... | collective-permute-start | bytes 61448 | tf_op jit(solution)/shard_map/ppermute | solution.py:53
  128.1 1.9 collective-permute-done.13
  130.0 4.5 %collective-permute-start.14 = (f32[1,80,128]{2,1,0:T(8,128)S(1)}, f32[1,80,128]{2,1,0:T(8,128)S(1)}, u32[]{:S(2)}, u32[]{:S(2)}) collective-permute-start(f32[1,80,128]{2,1,0:T(8,128)S(1)} %pad_maximum_fusion.11), channel_id=1, source_target_pairs={{0,32},{8,40},{16,48},{24,56},{32,0},{40,8},{48,16},{56,24},{64,96... | collective-permute-start | bytes 122888 | tf_op jit(solution)/shard_map/ppermute | solution.py:53
  134.4 1.8 collective-permute-done.14
  136.2 2.8 %collective-permute-start.15 = (f32[1,160,128]{2,1,0:T(8,128)S(1)}, f32[1,160,128]{2,1,0:T(8,128)S(1)}, u32[]{:S(2)}, u32[]{:S(2)}) collective-permute-start(f32[1,160,128]{2,1,0:T(8,128)S(1)} %pad_maximum_fusion.10), channel_id=1, source_target_pairs={{0,64},{8,72},{16,80},{24,88},{32,96},{40,104},{48,112},{56,120},{... | collective-permute-start | bytes 245768 | tf_op jit(solution)/shard_map/ppermute | solution.py:53
  139.0 2.4 %collective-permute-done.15 = f32[1,160,128]{2,1,0:T(8,128)S(1)} collective-permute-done((f32[1,160,128]{2,1,0:T(8,128)S(1)}, f32[1,160,128]{2,1,0:T(8,128)S(1)}, u32[]{:S(2)}, u32[]{:S(2)}) %collective-permute-start.15) | collective-permute-done | bytes 81952 | tf_op jit(solution)/shard_map/ppermute | solution.py:53
  141.5 2.8 %collective-permute-start.16 = (f32[1,320,128]{2,1,0:T(8,128)S(1)}, f32[1,320,128]{2,1,0:T(8,128)S(1)}, u32[]{:S(2)}, u32[]{:S(2)}) collective-permute-start(f32[1,320,128]{2,1,0:T(8,128)S(1)} %pad_maximum_fusion.9), channel_id=1, source_target_pairs={{0,16},{8,24},{16,0},{24,8},{32,48},{40,56},{48,32},{56,40},{64,80... | collective-permute-start | bytes 491528 | tf_op jit(solution)/shard_map/ppermute | solution.py:53
  144.3 3.3 %collective-permute-done.16 = f32[1,320,128]{2,1,0:T(8,128)S(1)} collective-permute-done((f32[1,320,128]{2,1,0:T(8,128)S(1)}, f32[1,320,128]{2,1,0:T(8,128)S(1)}, u32[]{:S(2)}, u32[]{:S(2)}) %collective-permute-start.16) | collective-permute-done | bytes 163872 | tf_op jit(solution)/shard_map/ppermute | solution.py:53
  147.6 12.8 %collective-permute-start.17 = (f32[1,320,256]{2,1,0:T(8,128)S(1)}, f32[1,320,256]{2,1,0:T(8,128)S(1)}, u32[]{:S(2)}, u32[]{:S(2)}) collective-permute-start(f32[1,320,256]{2,1,0:T(8,128)S(1)} %pad_maximum_fusion.3), channel_id=1, source_target_pairs={{0,8},{8,0},{16,24},{24,16},{32,40},{40,32},{48,56},{56,48},{64,72... | collective-permute-start | bytes 983048 | tf_op jit(solution)/shard_map/ppermute | solution.py:53
  160.4 1.2 collective-permute-done.17
  161.7 1.6 fusion.4
  163.7 1.9 collective-permute-start.18
  165.7 7.6 %collective-permute-done.18 = f32[2,257,128]{2,1,0:T(8,128)S(1)} collective-permute-done((f32[2,257,128]{2,1,0:T(8,128)S(1)}, f32[2,257,128]{2,1,0:T(8,128)S(1)}, u32[]{:S(2)}, u32[]{:S(2)}) %collective-permute-start.18) | collective-permute-done | bytes 263200 | tf_op jit(solution)/shard_map/ppermute | solution.py:33
  173.3 2.7 %collective-permute-start.19 = (f32[2,257,128]{2,1,0:T(8,128)S(1)}, f32[2,257,128]{2,1,0:T(8,128)S(1)}, u32[]{:S(2)}, u32[]{:S(2)}) collective-permute-start(f32[2,257,128]{2,1,0:T(8,128)S(1)} %fusion.27), channel_id=1, source_target_pairs={{0,2},{1,3},{2,0},{3,1},{4,6},{5,7},{6,4},{7,5},{8,10},{9,11},{10,... | collective-permute-start | bytes 789512 | tf_op jit(solution)/shard_map/ppermute | solution.py:33
  176.0 0.7 copy.78
  176.7 0.7 copy.79
  177.5 12.8 %collective-permute-done.19 = f32[2,257,128]{2,1,0:T(8,128)S(1)} collective-permute-done((f32[2,257,128]{2,1,0:T(8,128)S(1)}, f32[2,257,128]{2,1,0:T(8,128)S(1)}, u32[]{:S(2)}, u32[]{:S(2)}) %collective-permute-start.19) | collective-permute-done | bytes 263200 | tf_op jit(solution)/shard_map/ppermute | solution.py:33
  190.3 5.6 %collective-permute-start.20 = (f32[2,257,128]{2,1,0:T(8,128)S(1)}, f32[2,257,128]{2,1,0:T(8,128)S(1)}, u32[]{:S(2)}, u32[]{:S(2)}) collective-permute-start(f32[2,257,128]{2,1,0:T(8,128)S(1)} %add.145), channel_id=1, source_target_pairs={{0,4},{1,5},{2,6},{3,7},{4,0},{5,1},{6,2},{7,3},{8,12},{9,13},{10,... | collective-permute-start | bytes 789512 | tf_op jit(solution)/shard_map/ppermute | solution.py:33
  195.9 1.1 fusion
  197.0 12.8 %collective-permute-done.20 = f32[2,257,128]{2,1,0:T(8,128)S(1)} collective-permute-done((f32[2,257,128]{2,1,0:T(8,128)S(1)}, f32[2,257,128]{2,1,0:T(8,128)S(1)}, u32[]{:S(2)}, u32[]{:S(2)}) %collective-permute-start.20) | collective-permute-done | bytes 263200 | tf_op jit(solution)/shard_map/ppermute | solution.py:33
  210.2 0.1 select_reduce_fusion
  210.3 0.9 multiply_convert_fusion
  211.3 0.2 copy.76
  211.5 1.1 copy.80
  (52 shorter events, 1.6 us)
Async XLA Ops:
  0.6 1.4 copy-start
  2.4 7.9 %collective-permute-start = (f32[2,192,128]{2,1,0:T(8,128)S(1)}, f32[2,192,128]{2,1,0:T(8,128)S(1)}, u32[]{:S(2)}, u32[]{:S(2)}) collective-permute-start(f32[2,192,128]{2,1,0:T(8,128)S(1)} %constant_dynamic-slice_fusion.7), channel_id=1, source_target_pairs={{0,1},{1,0},{2,3},{3,2},{4,5},{5,4},{6,7},{7,6},{8,9},{9,8},{10,11... | collective-permute-start | bytes 589832 | tf_op jit(solution)/shard_map/ppermute | solution.py:45
  10.4 15.8 %collective-permute-start.1 = (f32[2,192,64]{2,1,0:T(8,128)S(1)}, f32[2,192,64]{2,1,0:T(8,128)S(1)}, u32[]{:S(2)}, u32[]{:S(2)}) collective-permute-start(f32[2,192,64]{2,1,0:T(8,128)S(1)} %constant_dynamic-slice_fusion.6), channel_id=1, source_target_pairs={{0,2},{1,3},{2,0},{3,1},{4,6},{5,7},{6,4},{7,5},{8,10},{9,11},{10,... | collective-permute-start | bytes 294920 | tf_op jit(solution)/shard_map/ppermute | solution.py:45
  26.3 8.6 %copy-start.2 = (f32[2,192,32]{1,2,0:T(8,128)S(1)}, f32[2,192,32]{1,2,0:T(8,128)}, u32[]{:S(2)}) copy-start(f32[2,192,32]{1,2,0:T(8,128)} %param.8) | copy-start | bytes 147460
  26.5 15.2 %collective-permute-start.2 = (f32[2,192,32]{2,1,0:T(8,128)S(1)}, f32[2,192,32]{2,1,0:T(8,128)S(1)}, u32[]{:S(2)}, u32[]{:S(2)}) collective-permute-start(f32[2,192,32]{2,1,0:T(8,128)S(1)} %constant_dynamic-slice_fusion.5), channel_id=1, source_target_pairs={{0,4},{1,5},{2,6},{3,7},{4,0},{5,1},{6,2},{7,3},{8,12},{9,13},{10,... | collective-permute-start | bytes 147464 | tf_op jit(solution)/shard_map/ppermute | solution.py:45
  34.9 0.8 copy-start.3
  42.0 12.6 %collective-permute-start.3 = (bf16[2,2,192,32]{3,2,1,0:T(8,128)(2,1)S(1)}, bf16[2,2,192,32]{3,2,1,0:T(8,128)(2,1)S(1)}, u32[]{:S(2)}, u32[]{:S(2)}) collective-permute-start(bf16[2,2,192,32]{3,2,1,0:T(8,128)(2,1)S(1)} %pad_maximum_fusion.6), channel_id=1, source_target_pairs={{0,4},{1,5},{2,6},{3,7},{4,0},{5,1},{6,2},{7,3},{8,12},{9,13},{10,... | collective-permute-start | bytes 147464 | tf_op jit(solution)/shard_map/ppermute | solution.py:53
  54.8 7.3 %collective-permute-start.4 = (bf16[2,2,192,64]{3,2,1,0:T(8,128)(2,1)S(1)}, bf16[2,2,192,64]{3,2,1,0:T(8,128)(2,1)S(1)}, u32[]{:S(2)}, u32[]{:S(2)}) collective-permute-start(bf16[2,2,192,64]{3,2,1,0:T(8,128)(2,1)S(1)} %pad_maximum_fusion.7), channel_id=1, source_target_pairs={{0,2},{1,3},{2,0},{3,1},{4,6},{5,7},{6,4},{7,5},{8,10},{9,11},{10,... | collective-permute-start | bytes 294920 | tf_op jit(solution)/shard_map/ppermute | solution.py:53
  62.4 10.1 %collective-permute-start.5 = (bf16[2,2,192,128]{3,2,1,0:T(8,128)(2,1)S(1)}, bf16[2,2,192,128]{3,2,1,0:T(8,128)(2,1)S(1)}, u32[]{:S(2)}, u32[]{:S(2)}) collective-permute-start(bf16[2,2,192,128]{3,2,1,0:T(8,128)(2,1)S(1)} %pad_maximum_fusion.8), channel_id=1, source_target_pairs={{0,1},{1,0},{2,3},{3,2},{4,5},{5,4},{6,7},{7,6},{8,9},{9,8},{10,11... | collective-permute-start | bytes 589832 | tf_op jit(solution)/shard_map/ppermute | solution.py:53
  73.1 9.6 %collective-permute-start.6 = (f32[1,320,256]{2,1,0:T(8,128)S(1)}, f32[1,320,256]{2,1,0:T(8,128)S(1)}, u32[]{:S(2)}, u32[]{:S(2)}) collective-permute-start(f32[1,320,256]{2,1,0:T(8,128)S(1)} %dynamic-slice_bitcast_fusion), channel_id=1, source_target_pairs={{0,8},{8,0},{16,24},{24,16},{32,40},{40,32},{48,56},{56,48},{64,72... | collective-permute-start | bytes 983048 | tf_op jit(solution)/shard_map/ppermute | solution.py:45
  82.8 7.3 %collective-permute-start.7 = (f32[1,320,128]{2,1,0:T(8,128)S(1)}, f32[1,320,128]{2,1,0:T(8,128)S(1)}, u32[]{:S(2)}, u32[]{:S(2)}) collective-permute-start(f32[1,320,128]{2,1,0:T(8,128)S(1)} %constant_dynamic-slice_fusion.4), channel_id=1, source_target_pairs={{0,16},{8,24},{16,0},{24,8},{32,48},{40,56},{48,32},{56,40},{64,80... | collective-permute-start | bytes 491528 | tf_op jit(solution)/shard_map/ppermute | solution.py:45
  90.1 5.2 %collective-permute-start.8 = (f32[1,160,128]{2,1,0:T(8,128)S(1)}, f32[1,160,128]{2,1,0:T(8,128)S(1)}, u32[]{:S(2)}, u32[]{:S(2)}) collective-permute-start(f32[1,160,128]{2,1,0:T(8,128)S(1)} %constant_dynamic-slice_fusion.3), channel_id=1, source_target_pairs={{0,64},{8,72},{16,80},{24,88},{32,96},{40,104},{48,112},{56,120},{... | collective-permute-start | bytes 245768 | tf_op jit(solution)/shard_map/ppermute | solution.py:45
  95.3 6.3 %collective-permute-start.9 = (f32[1,80,128]{2,1,0:T(8,128)S(1)}, f32[1,80,128]{2,1,0:T(8,128)S(1)}, u32[]{:S(2)}, u32[]{:S(2)}) collective-permute-start(f32[1,80,128]{2,1,0:T(8,128)S(1)} %constant_dynamic-slice_fusion.2), channel_id=1, source_target_pairs={{0,32},{8,40},{16,48},{24,56},{32,0},{40,8},{48,16},{56,24},{64,96... | collective-permute-start | bytes 122888 | tf_op jit(solution)/shard_map/ppermute | solution.py:45
  101.6 5.4 %collective-permute-start.10 = (f32[1,40,128]{2,1,0:T(8,128)S(1)}, f32[1,40,128]{2,1,0:T(8,128)S(1)}, u32[]{:S(2)}, u32[]{:S(2)}) collective-permute-start(f32[1,40,128]{2,1,0:T(8,128)S(1)} %constant_dynamic-slice_fusion.1), channel_id=1, source_target_pairs={{0,128},{8,136},{16,144},{24,152},{32,160},{40,168},{48,176},{56,1... | collective-permute-start | bytes 61448 | tf_op jit(solution)/shard_map/ppermute | solution.py:45
  107.1 8.7 %collective-permute-start.11 = (f32[1,20,128]{2,1,0:T(8,128)S(1)}, f32[1,20,128]{2,1,0:T(8,128)S(1)}, u32[]{:S(2)}, u32[]{:S(2)}) collective-permute-start(f32[1,20,128]{2,1,0:T(8,128)S(1)} %constant_dynamic-slice_fusion), channel_id=1, source_target_pairs={{0,256},{8,264},{16,272},{24,280},{32,288},{40,296},{48,304},{56,3... | collective-permute-start | bytes 30728 | tf_op jit(solution)/shard_map/ppermute | solution.py:45
  115.8 8.4 %collective-permute-start.12 = (f32[1,20,128]{2,1,0:T(8,128)S(1)}, f32[1,20,128]{2,1,0:T(8,128)S(1)}, u32[]{:S(2)}, u32[]{:S(2)}) collective-permute-start(f32[1,20,128]{2,1,0:T(8,128)S(1)} %dynamic-slice_add_fusion.7), channel_id=1, source_target_pairs={{0,256},{8,264},{16,272},{24,280},{32,288},{40,296},{48,304},{56,3... | collective-permute-start | bytes 30728 | tf_op jit(solution)/shard_map/ppermute | solution.py:53
  124.2 5.7 %collective-permute-start.13 = (f32[1,40,128]{2,1,0:T(8,128)S(1)}, f32[1,40,128]{2,1,0:T(8,128)S(1)}, u32[]{:S(2)}, u32[]{:S(2)}) collective-permute-start(f32[1,40,128]{2,1,0:T(8,128)S(1)} %pad_maximum_fusion.12), channel_id=1, source_target_pairs={{0,128},{8,136},{16,144},{24,152},{32,160},{40,168},{48,176},{56,1... | collective-permute-start | bytes 61448 | tf_op jit(solution)/shard_map/ppermute | solution.py:53
  130.0 6.3 %collective-permute-start.14 = (f32[1,80,128]{2,1,0:T(8,128)S(1)}, f32[1,80,128]{2,1,0:T(8,128)S(1)}, u32[]{:S(2)}, u32[]{:S(2)}) collective-permute-start(f32[1,80,128]{2,1,0:T(8,128)S(1)} %pad_maximum_fusion.11), channel_id=1, source_target_pairs={{0,32},{8,40},{16,48},{24,56},{32,0},{40,8},{48,16},{56,24},{64,96... | collective-permute-start | bytes 122888 | tf_op jit(solution)/shard_map/ppermute | solution.py:53
  136.2 5.2 %collective-permute-start.15 = (f32[1,160,128]{2,1,0:T(8,128)S(1)}, f32[1,160,128]{2,1,0:T(8,128)S(1)}, u32[]{:S(2)}, u32[]{:S(2)}) collective-permute-start(f32[1,160,128]{2,1,0:T(8,128)S(1)} %pad_maximum_fusion.10), channel_id=1, source_target_pairs={{0,64},{8,72},{16,80},{24,88},{32,96},{40,104},{48,112},{56,120},{... | collective-permute-start | bytes 245768 | tf_op jit(solution)/shard_map/ppermute | solution.py:53
  141.5 6.1 %collective-permute-start.16 = (f32[1,320,128]{2,1,0:T(8,128)S(1)}, f32[1,320,128]{2,1,0:T(8,128)S(1)}, u32[]{:S(2)}, u32[]{:S(2)}) collective-permute-start(f32[1,320,128]{2,1,0:T(8,128)S(1)} %pad_maximum_fusion.9), channel_id=1, source_target_pairs={{0,16},{8,24},{16,0},{24,8},{32,48},{40,56},{48,32},{56,40},{64,80... | collective-permute-start | bytes 491528 | tf_op jit(solution)/shard_map/ppermute | solution.py:53
  147.6 14.0 %collective-permute-start.17 = (f32[1,320,256]{2,1,0:T(8,128)S(1)}, f32[1,320,256]{2,1,0:T(8,128)S(1)}, u32[]{:S(2)}, u32[]{:S(2)}) collective-permute-start(f32[1,320,256]{2,1,0:T(8,128)S(1)} %pad_maximum_fusion.3), channel_id=1, source_target_pairs={{0,8},{8,0},{16,24},{24,16},{32,40},{40,32},{48,56},{56,48},{64,72... | collective-permute-start | bytes 983048 | tf_op jit(solution)/shard_map/ppermute | solution.py:53
  163.7 9.6 %collective-permute-start.18 = (f32[2,257,128]{2,1,0:T(8,128)S(1)}, f32[2,257,128]{2,1,0:T(8,128)S(1)}, u32[]{:S(2)}, u32[]{:S(2)}) collective-permute-start(f32[2,257,128]{2,1,0:T(8,128)S(1)} %pad_maximum_fusion.4), channel_id=1, source_target_pairs={{0,1},{1,0},{2,3},{3,2},{4,5},{5,4},{6,7},{7,6},{8,9},{9,8},{10,11... | collective-permute-start | bytes 789512 | tf_op jit(solution)/shard_map/ppermute | solution.py:33
  173.3 17.0 %collective-permute-start.19 = (f32[2,257,128]{2,1,0:T(8,128)S(1)}, f32[2,257,128]{2,1,0:T(8,128)S(1)}, u32[]{:S(2)}, u32[]{:S(2)}) collective-permute-start(f32[2,257,128]{2,1,0:T(8,128)S(1)} %fusion.27), channel_id=1, source_target_pairs={{0,2},{1,3},{2,0},{3,1},{4,6},{5,7},{6,4},{7,5},{8,10},{9,11},{10,... | collective-permute-start | bytes 789512 | tf_op jit(solution)/shard_map/ppermute | solution.py:33
  176.7 19.2 %copy-start.1 = (f32[2,192,320]{2,1,0:T(8,128)S(1)}, f32[2,192,320]{2,1,0:T(8,128)}, u32[]{:S(2)}) copy-start(f32[2,192,320]{2,1,0:T(8,128)} %param.6) | copy-start | bytes 1474564
  190.3 19.4 %collective-permute-start.20 = (f32[2,257,128]{2,1,0:T(8,128)S(1)}, f32[2,257,128]{2,1,0:T(8,128)S(1)}, u32[]{:S(2)}, u32[]{:S(2)}) collective-permute-start(f32[2,257,128]{2,1,0:T(8,128)S(1)} %add.145), channel_id=1, source_target_pairs={{0,4},{1,5},{2,6},{3,7},{4,0},{5,1},{6,2},{7,3},{8,12},{9,13},{10,... | collective-permute-start | bytes 789512 | tf_op jit(solution)/shard_map/ppermute | solution.py:33

commit v4 on v3

--- a/solution.py
+++ b/solution.py
@@ -27,11 +27,11 @@
     return [(i, i ^ (1 << bit)) for i in range(size)]
 
 
-def butterfly_sum(value, axis, size):
-    bit = 0
-    while (1 << bit) < size:
+def butterfly_sum(value, axis, size, bits=None):
+    if bits is None:
+        bits = range(size.bit_length() - 1)
+    for bit in bits:
         value = value + lax.ppermute(value, axis, partner_perm(size, bit))
-        bit += 1
     return value
 
 
@@ -108,8 +108,10 @@
     projected_half, normal_full = gathered[0], gathered[1]
 
     image_part = jnp.einsum("mfd,mfr->mdr", grads, projected_half, preferred_element_type=jnp.float32)
-    stages = [(0, 0), (1, 2), (3, 1), (2, 1), (4, 1), (5, 1)]
-    image = doubling_gather(halving_scatter(image_part, "fsdp", fsdp, stages), "fsdp", fsdp, stages)
+    stages = [(0, 0), (1, 2), (3, 1)]
+    chunk = halving_scatter(image_part, "fsdp", fsdp, stages)
+    chunk = butterfly_sum(chunk, "fsdp", fsdp, [b for b in range(fsdp.bit_length() - 1) if b not in (0, 1, 3)])
+    image = doubling_gather(chunk, "fsdp", fsdp, stages)
 
     update = jnp.einsum("mfr,dmr->mfd", normal_full, basis_order, preferred_element_type=jnp.float32)
     weight_next = weights - LEARNING_RATE * GALORE_SCALE * update

time: 213 us -> 193 us (0.906)
  starting transfers between devices: 110 us -> 91.9 us
  waiting for transfers between devices: 89.4 us -> 86.9 us
    ppermute x9 -> x6, starting transfers between devices: 48.3 us -> 29.7 us  [doubling_gather(): other = lax.ppermute(value, axis, partner_perm(size, bit))]
    ppermute x3 -> x6, starting transfers between devices: 10.2 us -> 27 us  [butterfly_sum(): value = value + lax.ppermute(value, axis, partner_perm(size, bit))]
    ppermute x9 -> x6, starting transfers between devices: 51.4 us -> 35.1 us  [halving_scatter(): value = keep + lax.ppermute(send, axis, partner_perm(size, bit))]
    ppermute x3 -> x6, waiting for transfers between devices: 33.2 us -> 39.2 us  [butterfly_sum(): value = value + lax.ppermute(value, axis, partner_perm(size, bit))]
    ppermute x9 -> x6, waiting for transfers between devices: 27.3 us -> 22.9 us  [doubling_gather(): other = lax.ppermute(value, axis, partner_perm(size, bit))]
    ppermute x9 -> x6, waiting for transfers between devices: 28.9 us -> 24.8 us  [halving_scatter(): value = keep + lax.ppermute(send, axis, partner_perm(size, bit))]
  transfers between devices with their start and end apart: 21 -> 18, of which waited for: 21 -> 18; matrix products, arithmetic and copies ran while one was open for 1% -> 1% of each run, Pallas kernels for 0% -> 0%
where the time goes in v4:
time: 193 us; the launch traced here: 192 us
  starting transfers between devices  91.9 us (48%)
  waiting for transfers between devices  86.9 us (45%)
  local copies, waits for them, and re-layouts  6.02 us (3%)
  matrix products  4.16 us (2%)
    ppermute x6, waiting for transfers between devices, butterfly_sum(): value = value + lax.ppermute(value, axis, partner_perm(size, bit))  39.2 us
    ppermute x6, starting transfers between devices, halving_scatter(): value = keep + lax.ppermute(send, axis, partner_perm(size, bit))  35.1 us
    ppermute x6, starting transfers between devices, doubling_gather(): other = lax.ppermute(value, axis, partner_perm(size, bit))  29.7 us
    ppermute x6, starting transfers between devices, butterfly_sum(): value = value + lax.ppermute(value, axis, partner_perm(size, bit))  27 us
    ppermute x6, waiting for transfers between devices, halving_scatter(): value = keep + lax.ppermute(send, axis, partner_perm(size, bit))  24.8 us
    ppermute x6, waiting for transfers between devices, doubling_gather(): other = lax.ppermute(value, axis, partner_perm(size, bit))  22.9 us
    unnamed x17, local copies, waits for them, and re-layouts  5.13 us
  transfers between devices with their start and end apart: 18, of which 18 were waited for; matrix products, arithmetic and copies ran while one was open for 1% of the time, Pallas kernels for 0%

profile of v4, /device:TPU:1, one launch (start us, length us, event | category | flops | bytes accessed | tf_op | source)
XLA Modules:
  0.0 192.0 jit_solution(11811407720567232933)
XLA Ops:
  0.7 1.3 copy.63
  2.1 0.3 fusion.32
  2.4 4.8 %collective-permute-start = (f32[2,192,128]{2,1,0:T(8,128)S(1)}, f32[2,192,128]{2,1,0:T(8,128)S(1)}, u32[]{:S(2)}, u32[]{:S(2)}) collective-permute-start(f32[2,192,128]{2,1,0:T(8,128)S(1)} %constant_dynamic-slice_fusion.4), channel_id=1, source_target_pairs={{0,1},{1,0},{2,3},{3,2},{4,5},{5,4},{6,7},{7,6},{8,9},{9,8},{10,11... | collective-permute-start | bytes 589832 | tf_op jit(solution)/shard_map/ppermute | solution.py:45
  7.3 3.0 %collective-permute-done = f32[2,192,128]{2,1,0:T(8,128)S(1)} collective-permute-done((f32[2,192,128]{2,1,0:T(8,128)S(1)}, f32[2,192,128]{2,1,0:T(8,128)S(1)}, u32[]{:S(2)}, u32[]{:S(2)}) %collective-permute-start) | collective-permute-done | bytes 196640 | tf_op jit(solution)/shard_map/ppermute | solution.py:45
  10.3 0.1 constant_dynamic-slice_fusion.3
  10.4 7.4 %collective-permute-start.1 = (f32[2,192,64]{2,1,0:T(8,128)S(1)}, f32[2,192,64]{2,1,0:T(8,128)S(1)}, u32[]{:S(2)}, u32[]{:S(2)}) collective-permute-start(f32[2,192,64]{2,1,0:T(8,128)S(1)} %constant_dynamic-slice_fusion.3), channel_id=1, source_target_pairs={{0,2},{1,3},{2,0},{3,1},{4,6},{5,7},{6,4},{7,5},{8,10},{9,11},{10,... | collective-permute-start | bytes 294920 | tf_op jit(solution)/shard_map/ppermute | solution.py:45
  17.8 8.4 %collective-permute-done.1 = f32[2,192,64]{2,1,0:T(8,128)S(1)} collective-permute-done((f32[2,192,64]{2,1,0:T(8,128)S(1)}, f32[2,192,64]{2,1,0:T(8,128)S(1)}, u32[]{:S(2)}, u32[]{:S(2)}) %collective-permute-start.1) | collective-permute-done | bytes 98336 | tf_op jit(solution)/shard_map/ppermute | solution.py:45
  26.2 0.1 dynamic-slice_add_fusion.1
  26.4 0.1 constant_dynamic-slice_fusion.2
  26.5 8.4 %collective-permute-start.2 = (f32[2,192,32]{2,1,0:T(8,128)S(1)}, f32[2,192,32]{2,1,0:T(8,128)S(1)}, u32[]{:S(2)}, u32[]{:S(2)}) collective-permute-start(f32[2,192,32]{2,1,0:T(8,128)S(1)} %constant_dynamic-slice_fusion.2), channel_id=1, source_target_pairs={{0,4},{1,5},{2,6},{3,7},{4,0},{5,1},{6,2},{7,3},{8,12},{9,13},{10,... | collective-permute-start | bytes 147464 | tf_op jit(solution)/shard_map/ppermute | solution.py:45
  34.9 0.1 copy.66
  35.0 0.7 copy-done.3
  35.8 0.1 copy.67
  35.9 5.8 %collective-permute-done.2 = f32[2,192,32]{2,1,0:T(8,128)S(1)} collective-permute-done((f32[2,192,32]{2,1,0:T(8,128)S(1)}, f32[2,192,32]{2,1,0:T(8,128)S(1)}, u32[]{:S(2)}, u32[]{:S(2)}) %collective-permute-start.2) | collective-permute-done | bytes 49184 | tf_op jit(solution)/shard_map/ppermute | solution.py:45
  41.7 0.1 convert_bitcast_fusion
  41.8 0.1 fusion.22
  42.0 5.5 %collective-permute-start.3 = (bf16[2,2,192,32]{3,2,1,0:T(8,128)(2,1)S(1)}, bf16[2,2,192,32]{3,2,1,0:T(8,128)(2,1)S(1)}, u32[]{:S(2)}, u32[]{:S(2)}) collective-permute-start(bf16[2,2,192,32]{3,2,1,0:T(8,128)(2,1)S(1)} %pad_maximum_fusion.6), channel_id=1, source_target_pairs={{0,4},{1,5},{2,6},{3,7},{4,0},{5,1},{6,2},{7,3},{8,12},{9,13},{10,... | collective-permute-start | bytes 147464 | tf_op jit(solution)/shard_map/ppermute | solution.py:53
  47.5 7.1 %collective-permute-done.3 = bf16[2,2,192,32]{3,2,1,0:T(8,128)(2,1)S(1)} collective-permute-done((bf16[2,2,192,32]{3,2,1,0:T(8,128)(2,1)S(1)}, bf16[2,2,192,32]{3,2,1,0:T(8,128)(2,1)S(1)}, u32[]{:S(2)}, u32[]{:S(2)}) %collective-permute-start.3) | collective-permute-done | bytes 49184 | tf_op jit(solution)/shard_map/ppermute | solution.py:53
  54.7 0.1 pad_maximum_fusion.7
  54.8 1.9 %collective-permute-start.4 = (bf16[2,2,192,64]{3,2,1,0:T(8,128)(2,1)S(1)}, bf16[2,2,192,64]{3,2,1,0:T(8,128)(2,1)S(1)}, u32[]{:S(2)}, u32[]{:S(2)}) collective-permute-start(bf16[2,2,192,64]{3,2,1,0:T(8,128)(2,1)S(1)} %pad_maximum_fusion.7), channel_id=1, source_target_pairs={{0,2},{1,3},{2,0},{3,1},{4,6},{5,7},{6,4},{7,5},{8,10},{9,11},{10,... | collective-permute-start | bytes 294920 | tf_op jit(solution)/shard_map/ppermute | solution.py:53
  56.7 5.4 %collective-permute-done.4 = bf16[2,2,192,64]{3,2,1,0:T(8,128)(2,1)S(1)} collective-permute-done((bf16[2,2,192,64]{3,2,1,0:T(8,128)(2,1)S(1)}, bf16[2,2,192,64]{3,2,1,0:T(8,128)(2,1)S(1)}, u32[]{:S(2)}, u32[]{:S(2)}) %collective-permute-start.4) | collective-permute-done | bytes 98336 | tf_op jit(solution)/shard_map/ppermute | solution.py:53
  62.1 0.2 broadcast_select_fusion.3
  62.3 0.1 pad_maximum_fusion.8
  62.4 7.0 %collective-permute-start.5 = (bf16[2,2,192,128]{3,2,1,0:T(8,128)(2,1)S(1)}, bf16[2,2,192,128]{3,2,1,0:T(8,128)(2,1)S(1)}, u32[]{:S(2)}, u32[]{:S(2)}) collective-permute-start(bf16[2,2,192,128]{3,2,1,0:T(8,128)(2,1)S(1)} %pad_maximum_fusion.8), channel_id=1, source_target_pairs={{0,1},{1,0},{2,3},{3,2},{4,5},{5,4},{6,7},{7,6},{8,9},{9,8},{10,11... | collective-permute-start | bytes 589832 | tf_op jit(solution)/shard_map/ppermute | solution.py:53
  69.5 3.1 %collective-permute-done.5 = bf16[2,2,192,128]{3,2,1,0:T(8,128)(2,1)S(1)} collective-permute-done((bf16[2,2,192,128]{3,2,1,0:T(8,128)(2,1)S(1)}, bf16[2,2,192,128]{3,2,1,0:T(8,128)(2,1)S(1)}, u32[]{:S(2)}, u32[]{:S(2)}) %collective-permute-start.5) | collective-permute-done | bytes 196640 | tf_op jit(solution)/shard_map/ppermute | solution.py:53
  72.6 0.2 broadcast_select_fusion.4
  72.8 0.3 fusion.13
  73.1 8.4 %collective-permute-start.6 = (f32[1,320,256]{2,1,0:T(8,128)S(1)}, f32[1,320,256]{2,1,0:T(8,128)S(1)}, u32[]{:S(2)}, u32[]{:S(2)}) collective-permute-start(f32[1,320,256]{2,1,0:T(8,128)S(1)} %dynamic-slice_bitcast_fusion), channel_id=1, source_target_pairs={{0,8},{8,0},{16,24},{24,16},{32,40},{40,32},{48,56},{56,48},{64,72... | collective-permute-start | bytes 983048 | tf_op jit(solution)/shard_map/ppermute | solution.py:45
  81.5 1.2 collective-permute-done.6
  82.8 3.0 %collective-permute-start.7 = (f32[1,320,128]{2,1,0:T(8,128)S(1)}, f32[1,320,128]{2,1,0:T(8,128)S(1)}, u32[]{:S(2)}, u32[]{:S(2)}) collective-permute-start(f32[1,320,128]{2,1,0:T(8,128)S(1)} %constant_dynamic-slice_fusion.1), channel_id=1, source_target_pairs={{0,16},{8,24},{16,0},{24,8},{32,48},{40,56},{48,32},{56,40},{64,80... | collective-permute-start | bytes 491528 | tf_op jit(solution)/shard_map/ppermute | solution.py:45
  85.8 4.2 %collective-permute-done.7 = f32[1,320,128]{2,1,0:T(8,128)S(1)} collective-permute-done((f32[1,320,128]{2,1,0:T(8,128)S(1)}, f32[1,320,128]{2,1,0:T(8,128)S(1)}, u32[]{:S(2)}, u32[]{:S(2)}) %collective-permute-start.7) | collective-permute-done | bytes 163872 | tf_op jit(solution)/shard_map/ppermute | solution.py:45
  90.1 3.1 %collective-permute-start.8 = (f32[1,160,128]{2,1,0:T(8,128)S(1)}, f32[1,160,128]{2,1,0:T(8,128)S(1)}, u32[]{:S(2)}, u32[]{:S(2)}) collective-permute-start(f32[1,160,128]{2,1,0:T(8,128)S(1)} %constant_dynamic-slice_fusion), channel_id=1, source_target_pairs={{0,64},{8,72},{16,80},{24,88},{32,96},{40,104},{48,112},{56,120},{... | collective-permute-start | bytes 245768 | tf_op jit(solution)/shard_map/ppermute | solution.py:45
  93.3 2.0 %collective-permute-done.8 = f32[1,160,128]{2,1,0:T(8,128)S(1)} collective-permute-done((f32[1,160,128]{2,1,0:T(8,128)S(1)}, f32[1,160,128]{2,1,0:T(8,128)S(1)}, u32[]{:S(2)}, u32[]{:S(2)}) %collective-permute-start.8) | collective-permute-done | bytes 81952 | tf_op jit(solution)/shard_map/ppermute | solution.py:45
  95.3 4.5 %collective-permute-start.9 = (f32[1,160,128]{2,1,0:T(8,128)S(1)}, f32[1,160,128]{2,1,0:T(8,128)S(1)}, u32[]{:S(2)}, u32[]{:S(2)}) collective-permute-start(f32[1,160,128]{2,1,0:T(8,128)S(1)} %dynamic-slice_add_fusion.4), channel_id=1, source_target_pairs={{0,32},{8,40},{16,48},{24,56},{32,0},{40,8},{48,16},{56,24},{64,96... | collective-permute-start | bytes 245768 | tf_op jit(solution)/shard_map/ppermute | solution.py:34
  99.8 2.2 %collective-permute-done.9 = f32[1,160,128]{2,1,0:T(8,128)S(1)} collective-permute-done((f32[1,160,128]{2,1,0:T(8,128)S(1)}, f32[1,160,128]{2,1,0:T(8,128)S(1)}, u32[]{:S(2)}, u32[]{:S(2)}) %collective-permute-start.9) | collective-permute-done | bytes 81952 | tf_op jit(solution)/shard_map/ppermute | solution.py:34
  102.0 4.2 %collective-permute-start.10 = (f32[1,160,128]{2,1,0:T(8,128)S(1)}, f32[1,160,128]{2,1,0:T(8,128)S(1)}, u32[]{:S(2)}, u32[]{:S(2)}) collective-permute-start(f32[1,160,128]{2,1,0:T(8,128)S(1)} %add.117), channel_id=1, source_target_pairs={{0,128},{8,136},{16,144},{24,152},{32,160},{40,168},{48,176},{56,1... | collective-permute-start | bytes 245768 | tf_op jit(solution)/shard_map/ppermute | solution.py:34
  106.2 1.9 %collective-permute-done.10 = f32[1,160,128]{2,1,0:T(8,128)S(1)} collective-permute-done((f32[1,160,128]{2,1,0:T(8,128)S(1)}, f32[1,160,128]{2,1,0:T(8,128)S(1)}, u32[]{:S(2)}, u32[]{:S(2)}) %collective-permute-start.10) | collective-permute-done | bytes 81952 | tf_op jit(solution)/shard_map/ppermute | solution.py:34
  108.1 8.2 %collective-permute-start.11 = (f32[1,160,128]{2,1,0:T(8,128)S(1)}, f32[1,160,128]{2,1,0:T(8,128)S(1)}, u32[]{:S(2)}, u32[]{:S(2)}) collective-permute-start(f32[1,160,128]{2,1,0:T(8,128)S(1)} %add.118), channel_id=1, source_target_pairs={{0,256},{8,264},{16,272},{24,280},{32,288},{40,296},{48,304},{56,3... | collective-permute-start | bytes 245768 | tf_op jit(solution)/shard_map/ppermute | solution.py:34
  116.4 1.9 collective-permute-done.11
  118.3 3.0 %collective-permute-start.12 = (f32[1,160,128]{2,1,0:T(8,128)S(1)}, f32[1,160,128]{2,1,0:T(8,128)S(1)}, u32[]{:S(2)}, u32[]{:S(2)}) collective-permute-start(f32[1,160,128]{2,1,0:T(8,128)S(1)} %add.119), channel_id=1, source_target_pairs={{0,64},{8,72},{16,80},{24,88},{32,96},{40,104},{48,112},{56,120},{... | collective-permute-start | bytes 245768 | tf_op jit(solution)/shard_map/ppermute | solution.py:53
  121.4 3.3 %collective-permute-done.12 = f32[1,160,128]{2,1,0:T(8,128)S(1)} collective-permute-done((f32[1,160,128]{2,1,0:T(8,128)S(1)}, f32[1,160,128]{2,1,0:T(8,128)S(1)}, u32[]{:S(2)}, u32[]{:S(2)}) %collective-permute-start.12) | collective-permute-done | bytes 81952 | tf_op jit(solution)/shard_map/ppermute | solution.py:53
  124.7 3.2 %collective-permute-start.13 = (f32[1,320,128]{2,1,0:T(8,128)S(1)}, f32[1,320,128]{2,1,0:T(8,128)S(1)}, u32[]{:S(2)}, u32[]{:S(2)}) collective-permute-start(f32[1,320,128]{2,1,0:T(8,128)S(1)} %pad_maximum_fusion.9), channel_id=1, source_target_pairs={{0,16},{8,24},{16,0},{24,8},{32,48},{40,56},{48,32},{56,40},{64,80... | collective-permute-start | bytes 491528 | tf_op jit(solution)/shard_map/ppermute | solution.py:53
  127.9 2.9 %collective-permute-done.13 = f32[1,320,128]{2,1,0:T(8,128)S(1)} collective-permute-done((f32[1,320,128]{2,1,0:T(8,128)S(1)}, f32[1,320,128]{2,1,0:T(8,128)S(1)}, u32[]{:S(2)}, u32[]{:S(2)}) %collective-permute-start.13) | collective-permute-done | bytes 163872 | tf_op jit(solution)/shard_map/ppermute | solution.py:53
  130.8 9.0 %collective-permute-start.14 = (f32[1,320,256]{2,1,0:T(8,128)S(1)}, f32[1,320,256]{2,1,0:T(8,128)S(1)}, u32[]{:S(2)}, u32[]{:S(2)}) collective-permute-start(f32[1,320,256]{2,1,0:T(8,128)S(1)} %pad_maximum_fusion.3), channel_id=1, source_target_pairs={{0,8},{8,0},{16,24},{24,16},{32,40},{40,32},{48,56},{56,48},{64,72... | collective-permute-start | bytes 983048 | tf_op jit(solution)/shard_map/ppermute | solution.py:53
  139.9 1.2 collective-permute-done.14
  141.1 1.5 fusion.4
  142.7 0.1 copy.84
  142.9 0.1 fusion.21
  143.0 0.1 copy.71
  143.2 1.9 %collective-permute-start.15 = (f32[2,257,128]{2,1,0:T(8,128)S(1)}, f32[2,257,128]{2,1,0:T(8,128)S(1)}, u32[]{:S(2)}, u32[]{:S(2)}) collective-permute-start(f32[2,257,128]{2,1,0:T(8,128)S(1)} %pad_maximum_fusion.4), channel_id=1, source_target_pairs={{0,1},{1,0},{2,3},{3,2},{4,5},{5,4},{6,7},{7,6},{8,9},{9,8},{10,11... | collective-permute-start | bytes 789512 | tf_op jit(solution)/shard_map/ppermute | solution.py:34
  145.1 7.6 %collective-permute-done.15 = f32[2,257,128]{2,1,0:T(8,128)S(1)} collective-permute-done((f32[2,257,128]{2,1,0:T(8,128)S(1)}, f32[2,257,128]{2,1,0:T(8,128)S(1)}, u32[]{:S(2)}, u32[]{:S(2)}) %collective-permute-start.15) | collective-permute-done | bytes 263200 | tf_op jit(solution)/shard_map/ppermute | solution.py:34
  152.8 2.6 %collective-permute-start.16 = (f32[2,257,128]{2,1,0:T(8,128)S(1)}, f32[2,257,128]{2,1,0:T(8,128)S(1)}, u32[]{:S(2)}, u32[]{:S(2)}) collective-permute-start(f32[2,257,128]{2,1,0:T(8,128)S(1)} %fusion.27), channel_id=1, source_target_pairs={{0,2},{1,3},{2,0},{3,1},{4,6},{5,7},{6,4},{7,5},{8,10},{9,11},{10,... | collective-permute-start | bytes 789512 | tf_op jit(solution)/shard_map/ppermute | solution.py:34
  155.4 0.7 copy.78
  156.1 0.7 copy.79
  156.9 12.9 %collective-permute-done.16 = f32[2,257,128]{2,1,0:T(8,128)S(1)} collective-permute-done((f32[2,257,128]{2,1,0:T(8,128)S(1)}, f32[2,257,128]{2,1,0:T(8,128)S(1)}, u32[]{:S(2)}, u32[]{:S(2)}) %collective-permute-start.16) | collective-permute-done | bytes 263200 | tf_op jit(solution)/shard_map/ppermute | solution.py:34
  169.8 5.6 %collective-permute-start.17 = (f32[2,257,128]{2,1,0:T(8,128)S(1)}, f32[2,257,128]{2,1,0:T(8,128)S(1)}, u32[]{:S(2)}, u32[]{:S(2)}) collective-permute-start(f32[2,257,128]{2,1,0:T(8,128)S(1)} %add.121), channel_id=1, source_target_pairs={{0,4},{1,5},{2,6},{3,7},{4,0},{5,1},{6,2},{7,3},{8,12},{9,13},{10,... | collective-permute-start | bytes 789512 | tf_op jit(solution)/shard_map/ppermute | solution.py:34
  175.4 1.1 fusion
  176.5 12.7 %collective-permute-done.17 = f32[2,257,128]{2,1,0:T(8,128)S(1)} collective-permute-done((f32[2,257,128]{2,1,0:T(8,128)S(1)}, f32[2,257,128]{2,1,0:T(8,128)S(1)}, u32[]{:S(2)}, u32[]{:S(2)}) %collective-permute-start.17) | collective-permute-done | bytes 263200 | tf_op jit(solution)/shard_map/ppermute | solution.py:34
  189.3 0.1 copy.74
  189.5 0.1 bitcast_select_fusion
  189.6 0.1 select_reduce_fusion
  189.7 0.9 multiply_convert_fusion
  190.7 0.2 copy.76
  191.0 1.1 copy.80
  (37 shorter events, 0.9 us)
Async XLA Ops:
  0.6 1.4 copy-start
  2.4 7.9 %collective-permute-start = (f32[2,192,128]{2,1,0:T(8,128)S(1)}, f32[2,192,128]{2,1,0:T(8,128)S(1)}, u32[]{:S(2)}, u32[]{:S(2)}) collective-permute-start(f32[2,192,128]{2,1,0:T(8,128)S(1)} %constant_dynamic-slice_fusion.4), channel_id=1, source_target_pairs={{0,1},{1,0},{2,3},{3,2},{4,5},{5,4},{6,7},{7,6},{8,9},{9,8},{10,11... | collective-permute-start | bytes 589832 | tf_op jit(solution)/shard_map/ppermute | solution.py:45
  10.4 15.8 %collective-permute-start.1 = (f32[2,192,64]{2,1,0:T(8,128)S(1)}, f32[2,192,64]{2,1,0:T(8,128)S(1)}, u32[]{:S(2)}, u32[]{:S(2)}) collective-permute-start(f32[2,192,64]{2,1,0:T(8,128)S(1)} %constant_dynamic-slice_fusion.3), channel_id=1, source_target_pairs={{0,2},{1,3},{2,0},{3,1},{4,6},{5,7},{6,4},{7,5},{8,10},{9,11},{10,... | collective-permute-start | bytes 294920 | tf_op jit(solution)/shard_map/ppermute | solution.py:45
  26.3 8.6 %copy-start.2 = (f32[2,192,32]{1,2,0:T(8,128)S(1)}, f32[2,192,32]{1,2,0:T(8,128)}, u32[]{:S(2)}) copy-start(f32[2,192,32]{1,2,0:T(8,128)} %param.8) | copy-start | bytes 147460
  26.5 15.2 %collective-permute-start.2 = (f32[2,192,32]{2,1,0:T(8,128)S(1)}, f32[2,192,32]{2,1,0:T(8,128)S(1)}, u32[]{:S(2)}, u32[]{:S(2)}) collective-permute-start(f32[2,192,32]{2,1,0:T(8,128)S(1)} %constant_dynamic-slice_fusion.2), channel_id=1, source_target_pairs={{0,4},{1,5},{2,6},{3,7},{4,0},{5,1},{6,2},{7,3},{8,12},{9,13},{10,... | collective-permute-start | bytes 147464 | tf_op jit(solution)/shard_map/ppermute | solution.py:45
  34.9 0.8 copy-start.3
  42.0 12.6 %collective-permute-start.3 = (bf16[2,2,192,32]{3,2,1,0:T(8,128)(2,1)S(1)}, bf16[2,2,192,32]{3,2,1,0:T(8,128)(2,1)S(1)}, u32[]{:S(2)}, u32[]{:S(2)}) collective-permute-start(bf16[2,2,192,32]{3,2,1,0:T(8,128)(2,1)S(1)} %pad_maximum_fusion.6), channel_id=1, source_target_pairs={{0,4},{1,5},{2,6},{3,7},{4,0},{5,1},{6,2},{7,3},{8,12},{9,13},{10,... | collective-permute-start | bytes 147464 | tf_op jit(solution)/shard_map/ppermute | solution.py:53
  54.8 7.3 %collective-permute-start.4 = (bf16[2,2,192,64]{3,2,1,0:T(8,128)(2,1)S(1)}, bf16[2,2,192,64]{3,2,1,0:T(8,128)(2,1)S(1)}, u32[]{:S(2)}, u32[]{:S(2)}) collective-permute-start(bf16[2,2,192,64]{3,2,1,0:T(8,128)(2,1)S(1)} %pad_maximum_fusion.7), channel_id=1, source_target_pairs={{0,2},{1,3},{2,0},{3,1},{4,6},{5,7},{6,4},{7,5},{8,10},{9,11},{10,... | collective-permute-start | bytes 294920 | tf_op jit(solution)/shard_map/ppermute | solution.py:53
  62.4 10.1 %collective-permute-start.5 = (bf16[2,2,192,128]{3,2,1,0:T(8,128)(2,1)S(1)}, bf16[2,2,192,128]{3,2,1,0:T(8,128)(2,1)S(1)}, u32[]{:S(2)}, u32[]{:S(2)}) collective-permute-start(bf16[2,2,192,128]{3,2,1,0:T(8,128)(2,1)S(1)} %pad_maximum_fusion.8), channel_id=1, source_target_pairs={{0,1},{1,0},{2,3},{3,2},{4,5},{5,4},{6,7},{7,6},{8,9},{9,8},{10,11... | collective-permute-start | bytes 589832 | tf_op jit(solution)/shard_map/ppermute | solution.py:53
  73.1 9.6 %collective-permute-start.6 = (f32[1,320,256]{2,1,0:T(8,128)S(1)}, f32[1,320,256]{2,1,0:T(8,128)S(1)}, u32[]{:S(2)}, u32[]{:S(2)}) collective-permute-start(f32[1,320,256]{2,1,0:T(8,128)S(1)} %dynamic-slice_bitcast_fusion), channel_id=1, source_target_pairs={{0,8},{8,0},{16,24},{24,16},{32,40},{40,32},{48,56},{56,48},{64,72... | collective-permute-start | bytes 983048 | tf_op jit(solution)/shard_map/ppermute | solution.py:45
  82.8 7.3 %collective-permute-start.7 = (f32[1,320,128]{2,1,0:T(8,128)S(1)}, f32[1,320,128]{2,1,0:T(8,128)S(1)}, u32[]{:S(2)}, u32[]{:S(2)}) collective-permute-start(f32[1,320,128]{2,1,0:T(8,128)S(1)} %constant_dynamic-slice_fusion.1), channel_id=1, source_target_pairs={{0,16},{8,24},{16,0},{24,8},{32,48},{40,56},{48,32},{56,40},{64,80... | collective-permute-start | bytes 491528 | tf_op jit(solution)/shard_map/ppermute | solution.py:45
  90.1 5.2 %collective-permute-start.8 = (f32[1,160,128]{2,1,0:T(8,128)S(1)}, f32[1,160,128]{2,1,0:T(8,128)S(1)}, u32[]{:S(2)}, u32[]{:S(2)}) collective-permute-start(f32[1,160,128]{2,1,0:T(8,128)S(1)} %constant_dynamic-slice_fusion), channel_id=1, source_target_pairs={{0,64},{8,72},{16,80},{24,88},{32,96},{40,104},{48,112},{56,120},{... | collective-permute-start | bytes 245768 | tf_op jit(solution)/shard_map/ppermute | solution.py:45
  95.3 6.7 %collective-permute-start.9 = (f32[1,160,128]{2,1,0:T(8,128)S(1)}, f32[1,160,128]{2,1,0:T(8,128)S(1)}, u32[]{:S(2)}, u32[]{:S(2)}) collective-permute-start(f32[1,160,128]{2,1,0:T(8,128)S(1)} %dynamic-slice_add_fusion.4), channel_id=1, source_target_pairs={{0,32},{8,40},{16,48},{24,56},{32,0},{40,8},{48,16},{56,24},{64,96... | collective-permute-start | bytes 245768 | tf_op jit(solution)/shard_map/ppermute | solution.py:34
  102.0 6.1 %collective-permute-start.10 = (f32[1,160,128]{2,1,0:T(8,128)S(1)}, f32[1,160,128]{2,1,0:T(8,128)S(1)}, u32[]{:S(2)}, u32[]{:S(2)}) collective-permute-start(f32[1,160,128]{2,1,0:T(8,128)S(1)} %add.117), channel_id=1, source_target_pairs={{0,128},{8,136},{16,144},{24,152},{32,160},{40,168},{48,176},{56,1... | collective-permute-start | bytes 245768 | tf_op jit(solution)/shard_map/ppermute | solution.py:34
  108.1 10.2 %collective-permute-start.11 = (f32[1,160,128]{2,1,0:T(8,128)S(1)}, f32[1,160,128]{2,1,0:T(8,128)S(1)}, u32[]{:S(2)}, u32[]{:S(2)}) collective-permute-start(f32[1,160,128]{2,1,0:T(8,128)S(1)} %add.118), channel_id=1, source_target_pairs={{0,256},{8,264},{16,272},{24,280},{32,288},{40,296},{48,304},{56,3... | collective-permute-start | bytes 245768 | tf_op jit(solution)/shard_map/ppermute | solution.py:34
  118.3 6.3 %collective-permute-start.12 = (f32[1,160,128]{2,1,0:T(8,128)S(1)}, f32[1,160,128]{2,1,0:T(8,128)S(1)}, u32[]{:S(2)}, u32[]{:S(2)}) collective-permute-start(f32[1,160,128]{2,1,0:T(8,128)S(1)} %add.119), channel_id=1, source_target_pairs={{0,64},{8,72},{16,80},{24,88},{32,96},{40,104},{48,112},{56,120},{... | collective-permute-start | bytes 245768 | tf_op jit(solution)/shard_map/ppermute | solution.py:53
  124.7 6.1 %collective-permute-start.13 = (f32[1,320,128]{2,1,0:T(8,128)S(1)}, f32[1,320,128]{2,1,0:T(8,128)S(1)}, u32[]{:S(2)}, u32[]{:S(2)}) collective-permute-start(f32[1,320,128]{2,1,0:T(8,128)S(1)} %pad_maximum_fusion.9), channel_id=1, source_target_pairs={{0,16},{8,24},{16,0},{24,8},{32,48},{40,56},{48,32},{56,40},{64,80... | collective-permute-start | bytes 491528 | tf_op jit(solution)/shard_map/ppermute | solution.py:53
  130.8 10.3 %collective-permute-start.14 = (f32[1,320,256]{2,1,0:T(8,128)S(1)}, f32[1,320,256]{2,1,0:T(8,128)S(1)}, u32[]{:S(2)}, u32[]{:S(2)}) collective-permute-start(f32[1,320,256]{2,1,0:T(8,128)S(1)} %pad_maximum_fusion.3), channel_id=1, source_target_pairs={{0,8},{8,0},{16,24},{24,16},{32,40},{40,32},{48,56},{56,48},{64,72... | collective-permute-start | bytes 983048 | tf_op jit(solution)/shard_map/ppermute | solution.py:53
  143.2 9.6 %collective-permute-start.15 = (f32[2,257,128]{2,1,0:T(8,128)S(1)}, f32[2,257,128]{2,1,0:T(8,128)S(1)}, u32[]{:S(2)}, u32[]{:S(2)}) collective-permute-start(f32[2,257,128]{2,1,0:T(8,128)S(1)} %pad_maximum_fusion.4), channel_id=1, source_target_pairs={{0,1},{1,0},{2,3},{3,2},{4,5},{5,4},{6,7},{7,6},{8,9},{9,8},{10,11... | collective-permute-start | bytes 789512 | tf_op jit(solution)/shard_map/ppermute | solution.py:34
  152.8 17.0 %collective-permute-start.16 = (f32[2,257,128]{2,1,0:T(8,128)S(1)}, f32[2,257,128]{2,1,0:T(8,128)S(1)}, u32[]{:S(2)}, u32[]{:S(2)}) collective-permute-start(f32[2,257,128]{2,1,0:T(8,128)S(1)} %fusion.27), channel_id=1, source_target_pairs={{0,2},{1,3},{2,0},{3,1},{4,6},{5,7},{6,4},{7,5},{8,10},{9,11},{10,... | collective-permute-start | bytes 789512 | tf_op jit(solution)/shard_map/ppermute | solution.py:34
  156.1 19.3 %copy-start.1 = (f32[2,192,320]{2,1,0:T(8,128)S(1)}, f32[2,192,320]{2,1,0:T(8,128)}, u32[]{:S(2)}) copy-start(f32[2,192,320]{2,1,0:T(8,128)} %param.6) | copy-start | bytes 1474564
  169.8 19.4 %collective-permute-start.17 = (f32[2,257,128]{2,1,0:T(8,128)S(1)}, f32[2,257,128]{2,1,0:T(8,128)S(1)}, u32[]{:S(2)}, u32[]{:S(2)}) collective-permute-start(f32[2,257,128]{2,1,0:T(8,128)S(1)} %add.121), channel_id=1, source_target_pairs={{0,4},{1,5},{2,6},{3,7},{4,0},{5,1},{6,2},{7,3},{8,12},{9,13},{10,... | collective-permute-start | bytes 789512 | tf_op jit(solution)/shard_map/ppermute | solution.py:34

commit v5 on v4

--- a/solution.py
+++ b/solution.py
@@ -101,10 +101,24 @@
     basis_order = reverse_blocks(basis, len(tp_bits), width)
 
     projected_part = jnp.einsum("mfd,dmr->mfr", grads, basis_order, preferred_element_type=jnp.float32)
-    own = halving_scatter(projected_part, "tp", tp, tp_bits)
-    first_next, second_next, normal_half = adam_share(own, first_moment, second_moment)
-    halves = jnp.stack([own.astype(jnp.bfloat16), normal_half], axis=0)
-    gathered = doubling_gather(halves, "tp", tp, [(b, 3) for b, _ in tp_bits])
+    half = halving_scatter(projected_part, "tp", tp, [(0, 2)])
+    moments = jnp.stack([first_moment, second_moment], axis=0)
+    member = lax.axis_index("tp")
+    own_place = 0
+    for step, bit in enumerate(reversed(range(1, len(tp_bits)))):
+        half_rows = half.size // 128
+        message = jnp.concatenate([half.reshape(half_rows, 128), moments.reshape(-1, 128)], axis=0)
+        arrived = lax.ppermute(message, "tp", partner_perm(tp, bit))
+        half = half + arrived[:half_rows].reshape(half.shape)
+        other = arrived[half_rows:].reshape(moments.shape)
+        mine = (member >> bit) & 1
+        moments = jnp.concatenate([jnp.where(mine == 0, moments, other), jnp.where(mine == 0, other, moments)], axis=3)
+        own_place = own_place + (mine << step)
+    first_half, second_half, normal_half = adam_share(half, moments[0], moments[1])
+    first_next = lax.dynamic_slice_in_dim(first_half, own_place * width, width, 2)
+    second_next = lax.dynamic_slice_in_dim(second_half, own_place * width, width, 2)
+    halves = jnp.stack([half.astype(jnp.bfloat16), normal_half], axis=0)
+    gathered = doubling_gather(halves, "tp", tp, [(0, 3)])
     projected_half, normal_full = gathered[0], gathered[1]
 
     image_part = jnp.einsum("mfd,mfr->mdr", grads, projected_half, preferred_element_type=jnp.float32)

time: 193 us -> 181 us (0.938)
  starting transfers between devices: 91.9 us -> 83.2 us
  waiting for transfers between devices: 86.9 us -> 83.8 us
    ppermute x0 -> x2, starting transfers between devices: none -> 24.1 us  [shards(): arrived = lax.ppermute(message, 'tp', partner_perm(tp, bit))]
    ppermute x0 -> x2, waiting for transfers between devices: none -> 22.5 us  [shards(): arrived = lax.ppermute(message, 'tp', partner_perm(tp, bit))]
    ppermute x6 -> x4, starting transfers between devices: 35.1 us -> 14.4 us  [halving_scatter(): value = keep + lax.ppermute(send, axis, partner_perm(size, bit))]
    ppermute x6 -> x4, waiting for transfers between devices: 24.8 us -> 10 us  [halving_scatter(): value = keep + lax.ppermute(send, axis, partner_perm(size, bit))]
    ppermute x6 -> x4, starting transfers between devices: 29.7 us -> 16.8 us  [doubling_gather(): other = lax.ppermute(value, axis, partner_perm(size, bit))]
    ppermute x6 -> x4, waiting for transfers between devices: 22.9 us -> 13.5 us  [doubling_gather(): other = lax.ppermute(value, axis, partner_perm(size, bit))]
    unnamed x17 -> x15, local copies, waits for them, and re-layouts: 5.13 us -> 4.21 us
  transfers between devices with their start and end apart: 18 -> 16, of which waited for: 18 -> 16; matrix products, arithmetic and copies ran while one was open for 1% -> 2% of each run, Pallas kernels for 0% -> 0%
where the time goes in v5:
time: 181 us; the launch traced here: 180 us
  waiting for transfers between devices  83.8 us (46%)
  starting transfers between devices  83.2 us (46%)
  local copies, waits for them, and re-layouts  5.78 us (3%)
  matrix products  4.17 us (2%)
    ppermute x6, waiting for transfers between devices, butterfly_sum(): value = value + lax.ppermute(value, axis, partner_perm(size, bit))  37.7 us
    ppermute x6, starting transfers between devices, butterfly_sum(): value = value + lax.ppermute(value, axis, partner_perm(size, bit))  28 us
    ppermute x2, starting transfers between devices, shards(): arrived = lax.ppermute(message, 'tp', partner_perm(tp, bit))  24.1 us
    ppermute x2, waiting for transfers between devices, shards(): arrived = lax.ppermute(message, 'tp', partner_perm(tp, bit))  22.5 us
    ppermute x4, starting transfers between devices, doubling_gather(): other = lax.ppermute(value, axis, partner_perm(size, bit))  16.8 us
    ppermute x4, starting transfers between devices, halving_scatter(): value = keep + lax.ppermute(send, axis, partner_perm(size, bit))  14.4 us
    ppermute x4, waiting for transfers between devices, doubling_gather(): other = lax.ppermute(value, axis, partner_perm(size, bit))  13.5 us
    ppermute x4, waiting for transfers between devices, halving_scatter(): value = keep + lax.ppermute(send, axis, partner_perm(size, bit))  10 us
  transfers between devices with their start and end apart: 16, of which 16 were waited for; matrix products, arithmetic and copies ran while one was open for 2% of the time, Pallas kernels for 0%

profile of v5, /device:TPU:1, one launch (start us, length us, event | category | flops | bytes accessed | tf_op | source)
XLA Modules:
  0.0 179.7 jit_solution(4448156473581693547)
XLA Ops:
  0.6 0.0 copy-start
  0.6 1.3 copy.40
  2.0 0.1 copy.41
  2.1 0.3 fusion.40
  2.4 0.0 copy-start.2
  2.4 4.8 %collective-permute-start = (f32[2,192,128]{2,1,0:T(8,128)S(1)}, f32[2,192,128]{2,1,0:T(8,128)S(1)}, u32[]{:S(2)}, u32[]{:S(2)}) collective-permute-start(f32[2,192,128]{2,1,0:T(8,128)S(1)} %constant_dynamic-slice_fusion.4), channel_id=1, source_target_pairs={{0,1},{1,0},{2,3},{3,2},{4,5},{5,4},{6,7},{7,6},{8,9},{9,8},{10,11... | collective-permute-start | bytes 589832 | tf_op jit(solution)/shard_map/ppermute | solution.py:45
  7.3 0.2 copy.43
  7.5 0.1 reshape.59
  7.6 2.7 %collective-permute-done = f32[2,192,128]{2,1,0:T(8,128)S(1)} collective-permute-done((f32[2,192,128]{2,1,0:T(8,128)S(1)}, f32[2,192,128]{2,1,0:T(8,128)S(1)}, u32[]{:S(2)}, u32[]{:S(2)}) %collective-permute-start) | collective-permute-done | bytes 196640 | tf_op jit(solution)/shard_map/ppermute | solution.py:45
  10.4 11.3 %collective-permute-start.1 = (f32[576,128]{1,0:T(8,128)S(1)}, f32[576,128]{1,0:T(8,128)S(1)}, u32[]{:S(2)}, u32[]{:S(2)}) collective-permute-start(f32[576,128]{1,0:T(8,128)S(1)} %pad_maximum_fusion.6), channel_id=1, source_target_pairs={{0,4},{1,5},{2,6},{3,7},{4,0},{5,1},{6,2},{7,3},{8,12},{9,13},{10,... | collective-permute-start | bytes 884744 | tf_op jit(solution)/shard_map/ppermute | solution.py:111
  21.7 5.0 %collective-permute-done.1 = f32[576,128]{1,0:T(8,128)S(1)} collective-permute-done((f32[576,128]{1,0:T(8,128)S(1)}, f32[576,128]{1,0:T(8,128)S(1)}, u32[]{:S(2)}, u32[]{:S(2)}) %collective-permute-start.1) | collective-permute-done | bytes 294944 | tf_op jit(solution)/shard_map/ppermute | solution.py:111
  26.7 0.1 reshape.62
  26.8 0.1 broadcast_select_fusion.3
  26.9 0.2 pad_maximum_fusion.3
  27.1 0.1 reshape.63
  27.2 12.8 %collective-permute-start.2 = (f32[768,128]{1,0:T(8,128)S(1)}, f32[768,128]{1,0:T(8,128)S(1)}, u32[]{:S(2)}, u32[]{:S(2)}) collective-permute-start(f32[768,128]{1,0:T(8,128)S(1)} %pad_maximum_fusion.4), channel_id=1, source_target_pairs={{0,2},{1,3},{2,0},{3,1},{4,6},{5,7},{6,4},{7,5},{8,10},{9,11},{10,... | collective-permute-start | bytes 1179656 | tf_op jit(solution)/shard_map/ppermute | solution.py:111
  40.0 17.6 %collective-permute-done.2 = f32[768,128]{1,0:T(8,128)S(1)} collective-permute-done((f32[768,128]{1,0:T(8,128)S(1)}, f32[768,128]{1,0:T(8,128)S(1)}, u32[]{:S(2)}, u32[]{:S(2)}) %collective-permute-start.2) | collective-permute-done | bytes 393248 | tf_op jit(solution)/shard_map/ppermute | solution.py:111
  57.6 0.1 reshape.65
  57.8 0.2 broadcast_select_fusion.1
  57.9 0.3 fusion.28
  58.2 1.9 %collective-permute-start.3 = (bf16[2,2,192,128]{3,2,1,0:T(8,128)(2,1)S(1)}, bf16[2,2,192,128]{3,2,1,0:T(8,128)(2,1)S(1)}, u32[]{:S(2)}, u32[]{:S(2)}) collective-permute-start(bf16[2,2,192,128]{3,2,1,0:T(8,128)(2,1)S(1)} %pad_maximum_fusion.10), channel_id=1, source_target_pairs={{0,1},{1,0},{2,3},{3,2},{4,5},{5,4},{6,7},{7,6},{8,9},{9,8},{10,11... | collective-permute-start | bytes 589832 | tf_op jit(solution)/shard_map/ppermute | solution.py:53
  60.2 5.9 %collective-permute-done.3 = bf16[2,2,192,128]{3,2,1,0:T(8,128)(2,1)S(1)} collective-permute-done((bf16[2,2,192,128]{3,2,1,0:T(8,128)(2,1)S(1)}, bf16[2,2,192,128]{3,2,1,0:T(8,128)(2,1)S(1)}, u32[]{:S(2)}, u32[]{:S(2)}) %collective-permute-start.3) | collective-permute-done | bytes 196640 | tf_op jit(solution)/shard_map/ppermute | solution.py:53
  66.2 0.3 fusion.17
  66.5 3.2 %collective-permute-start.4 = (f32[1,320,256]{2,1,0:T(8,128)S(1)}, f32[1,320,256]{2,1,0:T(8,128)S(1)}, u32[]{:S(2)}, u32[]{:S(2)}) collective-permute-start(f32[1,320,256]{2,1,0:T(8,128)S(1)} %dynamic-slice_bitcast_fusion), channel_id=1, source_target_pairs={{0,8},{8,0},{16,24},{24,16},{32,40},{40,32},{48,56},{56,48},{64,72... | collective-permute-start | bytes 983048 | tf_op jit(solution)/shard_map/ppermute | solution.py:45
  69.7 1.2 collective-permute-done.4
  71.0 3.1 %collective-permute-start.5 = (f32[1,320,128]{2,1,0:T(8,128)S(1)}, f32[1,320,128]{2,1,0:T(8,128)S(1)}, u32[]{:S(2)}, u32[]{:S(2)}) collective-permute-start(f32[1,320,128]{2,1,0:T(8,128)S(1)} %constant_dynamic-slice_fusion.1), channel_id=1, source_target_pairs={{0,16},{8,24},{16,0},{24,8},{32,48},{40,56},{48,32},{56,40},{64,80... | collective-permute-start | bytes 491528 | tf_op jit(solution)/shard_map/ppermute | solution.py:45
  74.2 4.1 %collective-permute-done.5 = f32[1,320,128]{2,1,0:T(8,128)S(1)} collective-permute-done((f32[1,320,128]{2,1,0:T(8,128)S(1)}, f32[1,320,128]{2,1,0:T(8,128)S(1)}, u32[]{:S(2)}, u32[]{:S(2)}) %collective-permute-start.5) | collective-permute-done | bytes 163872 | tf_op jit(solution)/shard_map/ppermute | solution.py:45
  78.4 3.2 %collective-permute-start.6 = (f32[1,160,128]{2,1,0:T(8,128)S(1)}, f32[1,160,128]{2,1,0:T(8,128)S(1)}, u32[]{:S(2)}, u32[]{:S(2)}) collective-permute-start(f32[1,160,128]{2,1,0:T(8,128)S(1)} %constant_dynamic-slice_fusion), channel_id=1, source_target_pairs={{0,64},{8,72},{16,80},{24,88},{32,96},{40,104},{48,112},{56,120},{... | collective-permute-start | bytes 245768 | tf_op jit(solution)/shard_map/ppermute | solution.py:45
  81.6 2.0 %collective-permute-done.6 = f32[1,160,128]{2,1,0:T(8,128)S(1)} collective-permute-done((f32[1,160,128]{2,1,0:T(8,128)S(1)}, f32[1,160,128]{2,1,0:T(8,128)S(1)}, u32[]{:S(2)}, u32[]{:S(2)}) %collective-permute-start.6) | collective-permute-done | bytes 81952 | tf_op jit(solution)/shard_map/ppermute | solution.py:45
  83.6 4.6 %collective-permute-start.7 = (f32[1,160,128]{2,1,0:T(8,128)S(1)}, f32[1,160,128]{2,1,0:T(8,128)S(1)}, u32[]{:S(2)}, u32[]{:S(2)}) collective-permute-start(f32[1,160,128]{2,1,0:T(8,128)S(1)} %dynamic-slice_add_fusion.2), channel_id=1, source_target_pairs={{0,32},{8,40},{16,48},{24,56},{32,0},{40,8},{48,16},{56,24},{64,96... | collective-permute-start | bytes 245768 | tf_op jit(solution)/shard_map/ppermute | solution.py:34
  88.2 2.0 %collective-permute-done.7 = f32[1,160,128]{2,1,0:T(8,128)S(1)} collective-permute-done((f32[1,160,128]{2,1,0:T(8,128)S(1)}, f32[1,160,128]{2,1,0:T(8,128)S(1)}, u32[]{:S(2)}, u32[]{:S(2)}) %collective-permute-start.7) | collective-permute-done | bytes 81952 | tf_op jit(solution)/shard_map/ppermute | solution.py:34
  90.3 4.2 %collective-permute-start.8 = (f32[1,160,128]{2,1,0:T(8,128)S(1)}, f32[1,160,128]{2,1,0:T(8,128)S(1)}, u32[]{:S(2)}, u32[]{:S(2)}) collective-permute-start(f32[1,160,128]{2,1,0:T(8,128)S(1)} %add.110), channel_id=1, source_target_pairs={{0,128},{8,136},{16,144},{24,152},{32,160},{40,168},{48,176},{56,1... | collective-permute-start | bytes 245768 | tf_op jit(solution)/shard_map/ppermute | solution.py:34
  94.5 1.9 %collective-permute-done.8 = f32[1,160,128]{2,1,0:T(8,128)S(1)} collective-permute-done((f32[1,160,128]{2,1,0:T(8,128)S(1)}, f32[1,160,128]{2,1,0:T(8,128)S(1)}, u32[]{:S(2)}, u32[]{:S(2)}) %collective-permute-start.8) | collective-permute-done | bytes 81952 | tf_op jit(solution)/shard_map/ppermute | solution.py:34
  96.4 8.3 %collective-permute-start.9 = (f32[1,160,128]{2,1,0:T(8,128)S(1)}, f32[1,160,128]{2,1,0:T(8,128)S(1)}, u32[]{:S(2)}, u32[]{:S(2)}) collective-permute-start(f32[1,160,128]{2,1,0:T(8,128)S(1)} %add.111), channel_id=1, source_target_pairs={{0,256},{8,264},{16,272},{24,280},{32,288},{40,296},{48,304},{56,3... | collective-permute-start | bytes 245768 | tf_op jit(solution)/shard_map/ppermute | solution.py:34
  104.7 1.9 %collective-permute-done.9 = f32[1,160,128]{2,1,0:T(8,128)S(1)} collective-permute-done((f32[1,160,128]{2,1,0:T(8,128)S(1)}, f32[1,160,128]{2,1,0:T(8,128)S(1)}, u32[]{:S(2)}, u32[]{:S(2)}) %collective-permute-start.9) | collective-permute-done | bytes 81952 | tf_op jit(solution)/shard_map/ppermute | solution.py:34
  106.6 2.9 %collective-permute-start.10 = (f32[1,160,128]{2,1,0:T(8,128)S(1)}, f32[1,160,128]{2,1,0:T(8,128)S(1)}, u32[]{:S(2)}, u32[]{:S(2)}) collective-permute-start(f32[1,160,128]{2,1,0:T(8,128)S(1)} %add.112), channel_id=1, source_target_pairs={{0,64},{8,72},{16,80},{24,88},{32,96},{40,104},{48,112},{56,120},{... | collective-permute-start | bytes 245768 | tf_op jit(solution)/shard_map/ppermute | solution.py:53
  109.6 3.4 %collective-permute-done.10 = f32[1,160,128]{2,1,0:T(8,128)S(1)} collective-permute-done((f32[1,160,128]{2,1,0:T(8,128)S(1)}, f32[1,160,128]{2,1,0:T(8,128)S(1)}, u32[]{:S(2)}, u32[]{:S(2)}) %collective-permute-start.10) | collective-permute-done | bytes 81952 | tf_op jit(solution)/shard_map/ppermute | solution.py:53
  113.1 3.1 %collective-permute-start.11 = (f32[1,320,128]{2,1,0:T(8,128)S(1)}, f32[1,320,128]{2,1,0:T(8,128)S(1)}, u32[]{:S(2)}, u32[]{:S(2)}) collective-permute-start(f32[1,320,128]{2,1,0:T(8,128)S(1)} %pad_maximum_fusion.11), channel_id=1, source_target_pairs={{0,16},{8,24},{16,0},{24,8},{32,48},{40,56},{48,32},{56,40},{64,80... | collective-permute-start | bytes 491528 | tf_op jit(solution)/shard_map/ppermute | solution.py:53
  116.2 2.9 %collective-permute-done.11 = f32[1,320,128]{2,1,0:T(8,128)S(1)} collective-permute-done((f32[1,320,128]{2,1,0:T(8,128)S(1)}, f32[1,320,128]{2,1,0:T(8,128)S(1)}, u32[]{:S(2)}, u32[]{:S(2)}) %collective-permute-start.11) | collective-permute-done | bytes 163872 | tf_op jit(solution)/shard_map/ppermute | solution.py:53
  119.2 8.8 %collective-permute-start.12 = (f32[1,320,256]{2,1,0:T(8,128)S(1)}, f32[1,320,256]{2,1,0:T(8,128)S(1)}, u32[]{:S(2)}, u32[]{:S(2)}) collective-permute-start(f32[1,320,256]{2,1,0:T(8,128)S(1)} %pad_maximum_fusion.5), channel_id=1, source_target_pairs={{0,8},{8,0},{16,24},{24,16},{32,40},{40,32},{48,56},{56,48},{64,72... | collective-permute-start | bytes 983048 | tf_op jit(solution)/shard_map/ppermute | solution.py:53
  128.0 1.2 collective-permute-done.12
  129.3 1.6 fusion.4
  130.9 0.1 copy.62
  131.0 0.1 copy.63
  131.1 0.1 fusion.27
  131.2 0.1 copy.49
  131.4 1.9 %collective-permute-start.13 = (f32[2,257,128]{2,1,0:T(8,128)S(1)}, f32[2,257,128]{2,1,0:T(8,128)S(1)}, u32[]{:S(2)}, u32[]{:S(2)}) collective-permute-start(f32[2,257,128]{2,1,0:T(8,128)S(1)} %pad_maximum_fusion.7), channel_id=1, source_target_pairs={{0,1},{1,0},{2,3},{3,2},{4,5},{5,4},{6,7},{7,6},{8,9},{9,8},{10,11... | collective-permute-start | bytes 789512 | tf_op jit(solution)/shard_map/ppermute | solution.py:34
  133.3 7.6 %collective-permute-done.13 = f32[2,257,128]{2,1,0:T(8,128)S(1)} collective-permute-done((f32[2,257,128]{2,1,0:T(8,128)S(1)}, f32[2,257,128]{2,1,0:T(8,128)S(1)}, u32[]{:S(2)}, u32[]{:S(2)}) %collective-permute-start.13) | collective-permute-done | bytes 263200 | tf_op jit(solution)/shard_map/ppermute | solution.py:34
  141.0 1.9 %collective-permute-start.14 = (f32[2,257,128]{2,1,0:T(8,128)S(1)}, f32[2,257,128]{2,1,0:T(8,128)S(1)}, u32[]{:S(2)}, u32[]{:S(2)}) collective-permute-start(f32[2,257,128]{2,1,0:T(8,128)S(1)} %fusion.33), channel_id=1, source_target_pairs={{0,2},{1,3},{2,0},{3,1},{4,6},{5,7},{6,4},{7,5},{8,10},{9,11},{10,... | collective-permute-start | bytes 789512 | tf_op jit(solution)/shard_map/ppermute | solution.py:34
  142.9 0.2 constant_dynamic-slice_fusion.2
  143.1 0.7 copy.56
  143.8 0.7 copy.57
  144.6 13.1 %collective-permute-done.14 = f32[2,257,128]{2,1,0:T(8,128)S(1)} collective-permute-done((f32[2,257,128]{2,1,0:T(8,128)S(1)}, f32[2,257,128]{2,1,0:T(8,128)S(1)}, u32[]{:S(2)}, u32[]{:S(2)}) %collective-permute-start.14) | collective-permute-done | bytes 263200 | tf_op jit(solution)/shard_map/ppermute | solution.py:34
  157.7 6.9 %collective-permute-start.15 = (f32[2,257,128]{2,1,0:T(8,128)S(1)}, f32[2,257,128]{2,1,0:T(8,128)S(1)}, u32[]{:S(2)}, u32[]{:S(2)}) collective-permute-start(f32[2,257,128]{2,1,0:T(8,128)S(1)} %add.114), channel_id=1, source_target_pairs={{0,4},{1,5},{2,6},{3,7},{4,0},{5,1},{6,2},{7,3},{8,12},{9,13},{10,... | collective-permute-start | bytes 789512 | tf_op jit(solution)/shard_map/ppermute | solution.py:34
  164.7 1.1 fusion
  165.8 11.1 %collective-permute-done.15 = f32[2,257,128]{2,1,0:T(8,128)S(1)} collective-permute-done((f32[2,257,128]{2,1,0:T(8,128)S(1)}, f32[2,257,128]{2,1,0:T(8,128)S(1)}, u32[]{:S(2)}, u32[]{:S(2)}) %collective-permute-start.15) | collective-permute-done | bytes 263200 | tf_op jit(solution)/shard_map/ppermute | solution.py:34
  177.0 0.1 copy.64
  177.1 0.1 copy.52
  177.2 0.1 bitcast_select_fusion
  177.3 0.1 select_reduce_fusion
  177.4 0.9 multiply_convert_fusion
  178.4 0.2 copy.54
  178.6 0.1 copy.55
  178.6 1.1 copy.58
  (39 shorter events, 0.7 us)
Async XLA Ops:
  0.6 1.4 copy-start
  2.4 4.9 %copy-start.2 = (f32[2,192,32]{1,2,0:T(8,128)S(1)}, f32[2,192,32]{1,2,0:T(8,128)}, u32[]{:S(2)}) copy-start(f32[2,192,32]{1,2,0:T(8,128)} %param.9) | copy-start | bytes 147460
  2.4 4.9 %copy-start.3 = (f32[2,192,32]{1,2,0:T(8,128)S(1)}, f32[2,192,32]{1,2,0:T(8,128)}, u32[]{:S(2)}) copy-start(f32[2,192,32]{1,2,0:T(8,128)} %param.8) | copy-start | bytes 147460
  2.4 7.9 %collective-permute-start = (f32[2,192,128]{2,1,0:T(8,128)S(1)}, f32[2,192,128]{2,1,0:T(8,128)S(1)}, u32[]{:S(2)}, u32[]{:S(2)}) collective-permute-start(f32[2,192,128]{2,1,0:T(8,128)S(1)} %constant_dynamic-slice_fusion.4), channel_id=1, source_target_pairs={{0,1},{1,0},{2,3},{3,2},{4,5},{5,4},{6,7},{7,6},{8,9},{9,8},{10,11... | collective-permute-start | bytes 589832 | tf_op jit(solution)/shard_map/ppermute | solution.py:45
  10.4 16.2 %collective-permute-start.1 = (f32[576,128]{1,0:T(8,128)S(1)}, f32[576,128]{1,0:T(8,128)S(1)}, u32[]{:S(2)}, u32[]{:S(2)}) collective-permute-start(f32[576,128]{1,0:T(8,128)S(1)} %pad_maximum_fusion.6), channel_id=1, source_target_pairs={{0,4},{1,5},{2,6},{3,7},{4,0},{5,1},{6,2},{7,3},{8,12},{9,13},{10,... | collective-permute-start | bytes 884744 | tf_op jit(solution)/shard_map/ppermute | solution.py:111
  27.2 30.4 %collective-permute-start.2 = (f32[768,128]{1,0:T(8,128)S(1)}, f32[768,128]{1,0:T(8,128)S(1)}, u32[]{:S(2)}, u32[]{:S(2)}) collective-permute-start(f32[768,128]{1,0:T(8,128)S(1)} %pad_maximum_fusion.4), channel_id=1, source_target_pairs={{0,2},{1,3},{2,0},{3,1},{4,6},{5,7},{6,4},{7,5},{8,10},{9,11},{10,... | collective-permute-start | bytes 1179656 | tf_op jit(solution)/shard_map/ppermute | solution.py:111
  58.2 7.9 %collective-permute-start.3 = (bf16[2,2,192,128]{3,2,1,0:T(8,128)(2,1)S(1)}, bf16[2,2,192,128]{3,2,1,0:T(8,128)(2,1)S(1)}, u32[]{:S(2)}, u32[]{:S(2)}) collective-permute-start(bf16[2,2,192,128]{3,2,1,0:T(8,128)(2,1)S(1)} %pad_maximum_fusion.10), channel_id=1, source_target_pairs={{0,1},{1,0},{2,3},{3,2},{4,5},{5,4},{6,7},{7,6},{8,9},{9,8},{10,11... | collective-permute-start | bytes 589832 | tf_op jit(solution)/shard_map/ppermute | solution.py:53
  66.5 4.5 %collective-permute-start.4 = (f32[1,320,256]{2,1,0:T(8,128)S(1)}, f32[1,320,256]{2,1,0:T(8,128)S(1)}, u32[]{:S(2)}, u32[]{:S(2)}) collective-permute-start(f32[1,320,256]{2,1,0:T(8,128)S(1)} %dynamic-slice_bitcast_fusion), channel_id=1, source_target_pairs={{0,8},{8,0},{16,24},{24,16},{32,40},{40,32},{48,56},{56,48},{64,72... | collective-permute-start | bytes 983048 | tf_op jit(solution)/shard_map/ppermute | solution.py:45
  71.0 7.3 %collective-permute-start.5 = (f32[1,320,128]{2,1,0:T(8,128)S(1)}, f32[1,320,128]{2,1,0:T(8,128)S(1)}, u32[]{:S(2)}, u32[]{:S(2)}) collective-permute-start(f32[1,320,128]{2,1,0:T(8,128)S(1)} %constant_dynamic-slice_fusion.1), channel_id=1, source_target_pairs={{0,16},{8,24},{16,0},{24,8},{32,48},{40,56},{48,32},{56,40},{64,80... | collective-permute-start | bytes 491528 | tf_op jit(solution)/shard_map/ppermute | solution.py:45
  78.4 5.2 %collective-permute-start.6 = (f32[1,160,128]{2,1,0:T(8,128)S(1)}, f32[1,160,128]{2,1,0:T(8,128)S(1)}, u32[]{:S(2)}, u32[]{:S(2)}) collective-permute-start(f32[1,160,128]{2,1,0:T(8,128)S(1)} %constant_dynamic-slice_fusion), channel_id=1, source_target_pairs={{0,64},{8,72},{16,80},{24,88},{32,96},{40,104},{48,112},{56,120},{... | collective-permute-start | bytes 245768 | tf_op jit(solution)/shard_map/ppermute | solution.py:45
  83.6 6.7 %collective-permute-start.7 = (f32[1,160,128]{2,1,0:T(8,128)S(1)}, f32[1,160,128]{2,1,0:T(8,128)S(1)}, u32[]{:S(2)}, u32[]{:S(2)}) collective-permute-start(f32[1,160,128]{2,1,0:T(8,128)S(1)} %dynamic-slice_add_fusion.2), channel_id=1, source_target_pairs={{0,32},{8,40},{16,48},{24,56},{32,0},{40,8},{48,16},{56,24},{64,96... | collective-permute-start | bytes 245768 | tf_op jit(solution)/shard_map/ppermute | solution.py:34
  90.3 6.1 %collective-permute-start.8 = (f32[1,160,128]{2,1,0:T(8,128)S(1)}, f32[1,160,128]{2,1,0:T(8,128)S(1)}, u32[]{:S(2)}, u32[]{:S(2)}) collective-permute-start(f32[1,160,128]{2,1,0:T(8,128)S(1)} %add.110), channel_id=1, source_target_pairs={{0,128},{8,136},{16,144},{24,152},{32,160},{40,168},{48,176},{56,1... | collective-permute-start | bytes 245768 | tf_op jit(solution)/shard_map/ppermute | solution.py:34
  96.4 10.3 %collective-permute-start.9 = (f32[1,160,128]{2,1,0:T(8,128)S(1)}, f32[1,160,128]{2,1,0:T(8,128)S(1)}, u32[]{:S(2)}, u32[]{:S(2)}) collective-permute-start(f32[1,160,128]{2,1,0:T(8,128)S(1)} %add.111), channel_id=1, source_target_pairs={{0,256},{8,264},{16,272},{24,280},{32,288},{40,296},{48,304},{56,3... | collective-permute-start | bytes 245768 | tf_op jit(solution)/shard_map/ppermute | solution.py:34
  106.6 6.4 %collective-permute-start.10 = (f32[1,160,128]{2,1,0:T(8,128)S(1)}, f32[1,160,128]{2,1,0:T(8,128)S(1)}, u32[]{:S(2)}, u32[]{:S(2)}) collective-permute-start(f32[1,160,128]{2,1,0:T(8,128)S(1)} %add.112), channel_id=1, source_target_pairs={{0,64},{8,72},{16,80},{24,88},{32,96},{40,104},{48,112},{56,120},{... | collective-permute-start | bytes 245768 | tf_op jit(solution)/shard_map/ppermute | solution.py:53
  113.1 6.1 %collective-permute-start.11 = (f32[1,320,128]{2,1,0:T(8,128)S(1)}, f32[1,320,128]{2,1,0:T(8,128)S(1)}, u32[]{:S(2)}, u32[]{:S(2)}) collective-permute-start(f32[1,320,128]{2,1,0:T(8,128)S(1)} %pad_maximum_fusion.11), channel_id=1, source_target_pairs={{0,16},{8,24},{16,0},{24,8},{32,48},{40,56},{48,32},{56,40},{64,80... | collective-permute-start | bytes 491528 | tf_op jit(solution)/shard_map/ppermute | solution.py:53
  119.2 10.1 %collective-permute-start.12 = (f32[1,320,256]{2,1,0:T(8,128)S(1)}, f32[1,320,256]{2,1,0:T(8,128)S(1)}, u32[]{:S(2)}, u32[]{:S(2)}) collective-permute-start(f32[1,320,256]{2,1,0:T(8,128)S(1)} %pad_maximum_fusion.5), channel_id=1, source_target_pairs={{0,8},{8,0},{16,24},{24,16},{32,40},{40,32},{48,56},{56,48},{64,72... | collective-permute-start | bytes 983048 | tf_op jit(solution)/shard_map/ppermute | solution.py:53
  131.4 9.6 %collective-permute-start.13 = (f32[2,257,128]{2,1,0:T(8,128)S(1)}, f32[2,257,128]{2,1,0:T(8,128)S(1)}, u32[]{:S(2)}, u32[]{:S(2)}) collective-permute-start(f32[2,257,128]{2,1,0:T(8,128)S(1)} %pad_maximum_fusion.7), channel_id=1, source_target_pairs={{0,1},{1,0},{2,3},{3,2},{4,5},{5,4},{6,7},{7,6},{8,9},{9,8},{10,11... | collective-permute-start | bytes 789512 | tf_op jit(solution)/shard_map/ppermute | solution.py:34
  141.0 16.7 %collective-permute-start.14 = (f32[2,257,128]{2,1,0:T(8,128)S(1)}, f32[2,257,128]{2,1,0:T(8,128)S(1)}, u32[]{:S(2)}, u32[]{:S(2)}) collective-permute-start(f32[2,257,128]{2,1,0:T(8,128)S(1)} %fusion.33), channel_id=1, source_target_pairs={{0,2},{1,3},{2,0},{3,1},{4,6},{5,7},{6,4},{7,5},{8,10},{9,11},{10,... | collective-permute-start | bytes 789512 | tf_op jit(solution)/shard_map/ppermute | solution.py:34
  143.8 20.9 %copy-start.1 = (f32[2,192,320]{2,1,0:T(8,128)S(1)}, f32[2,192,320]{2,1,0:T(8,128)}, u32[]{:S(2)}) copy-start(f32[2,192,320]{2,1,0:T(8,128)} %param.6) | copy-start | bytes 1474564
  157.7 19.1 %collective-permute-start.15 = (f32[2,257,128]{2,1,0:T(8,128)S(1)}, f32[2,257,128]{2,1,0:T(8,128)S(1)}, u32[]{:S(2)}, u32[]{:S(2)}) collective-permute-start(f32[2,257,128]{2,1,0:T(8,128)S(1)} %add.114), channel_id=1, source_target_pairs={{0,4},{1,5},{2,6},{3,7},{4,0},{5,1},{6,2},{7,3},{8,12},{9,13},{10,... | collective-permute-start | bytes 789512 | tf_op jit(solution)/shard_map/ppermute | solution.py:34

commit v6 on v5

--- a/solution.py
+++ b/solution.py
@@ -130,7 +130,9 @@
     update = jnp.einsum("mfr,dmr->mfd", normal_full, basis_order, preferred_element_type=jnp.float32)
     weight_next = weights - LEARNING_RATE * GALORE_SCALE * update
 
-    gram = unpack_gram(butterfly_sum(pack_gram(jnp.einsum("mdr,mds->mrs", image, image, precision=highest)), "tp", tp))
+    packed = halving_scatter(pack_gram(jnp.einsum("mdr,mds->mrs", image, image, precision=highest)), "tp", tp, [(0, 0)])
+    packed = butterfly_sum(packed, "tp", tp, range(1, len(tp_bits)))
+    gram = unpack_gram(doubling_gather(packed, "tp", tp, [(0, 0)]))
     diagonal = lax.broadcasted_iota(jnp.int32, gram.shape, 1) == lax.broadcasted_iota(jnp.int32, gram.shape, 2)
     total = jnp.sum(jnp.where(diagonal, gram, 0.0), axis=(1, 2)) + EPSILON_NORM
     factor = jnp.sqrt(rank_width / total)

time: 181 us -> 173 us (0.956)
  the two profiles are of different devices: /device:TPU:1 before, /device:TPU:38 now
where the time goes in v6:
time: 173 us
  waiting for transfers between devices  97.8 us (57%)
  starting transfers between devices  62 us (36%)
  local copies, waits for them, and re-layouts  5.76 us (3%)
  matrix products  4.17 us (2%)
    ppermute x5, waiting for transfers between devices, butterfly_sum(): value = value + lax.ppermute(value, axis, partner_perm(size, bit))  32.6 us
    ppermute x2, waiting for transfers between devices, shards(): arrived = lax.ppermute(message, 'tp', partner_perm(tp, bit))  23.4 us
    ppermute x5, waiting for transfers between devices, doubling_gather(): other = lax.ppermute(value, axis, partner_perm(size, bit))  21.3 us
    ppermute x2, starting transfers between devices, shards(): arrived = lax.ppermute(message, 'tp', partner_perm(tp, bit))  20.8 us
    ppermute x5, waiting for transfers between devices, halving_scatter(): value = keep + lax.ppermute(send, axis, partner_perm(size, bit))  20.5 us
    ppermute x5, starting transfers between devices, butterfly_sum(): value = value + lax.ppermute(value, axis, partner_perm(size, bit))  17.1 us
    ppermute x5, starting transfers between devices, halving_scatter(): value = keep + lax.ppermute(send, axis, partner_perm(size, bit))  13.7 us
    ppermute x5, starting transfers between devices, doubling_gather(): other = lax.ppermute(value, axis, partner_perm(size, bit))  10.3 us
  transfers between devices with their start and end apart: 17, of which 17 were waited for; matrix products, arithmetic and copies ran while one was open for 2% of the time, Pallas kernels for 0%

profile of v6, /device:TPU:38, one launch (start us, length us, event | category | flops | bytes accessed | tf_op | source)
XLA Modules:
  0.0 172.5 jit_solution(5990024690743291119)
XLA Ops:
  0.6 1.3 copy.40
  2.0 0.1 copy.41
  2.1 0.3 fusion.40
  2.4 4.3 %collective-permute-start = (f32[2,192,128]{2,1,0:T(8,128)S(1)}, f32[2,192,128]{2,1,0:T(8,128)S(1)}, u32[]{:S(2)}, u32[]{:S(2)}) collective-permute-start(f32[2,192,128]{2,1,0:T(8,128)S(1)} %constant_dynamic-slice_fusion.5), channel_id=1, source_target_pairs={{0,1},{1,0},{2,3},{3,2},{4,5},{5,4},{6,7},{7,6},{8,9},{9,8},{10,11... | collective-permute-start | bytes 589832 | tf_op jit(solution)/shard_map/ppermute | solution.py:45
  6.8 0.2 copy.43
  7.0 0.1 reshape.59
  7.1 4.5 %collective-permute-done = f32[2,192,128]{2,1,0:T(8,128)S(1)} collective-permute-done((f32[2,192,128]{2,1,0:T(8,128)S(1)}, f32[2,192,128]{2,1,0:T(8,128)S(1)}, u32[]{:S(2)}, u32[]{:S(2)}) %collective-permute-start) | collective-permute-done | bytes 196640 | tf_op jit(solution)/shard_map/ppermute | solution.py:45
  11.7 10.3 %collective-permute-start.1 = (f32[576,128]{1,0:T(8,128)S(1)}, f32[576,128]{1,0:T(8,128)S(1)}, u32[]{:S(2)}, u32[]{:S(2)}) collective-permute-start(f32[576,128]{1,0:T(8,128)S(1)} %pad_maximum_fusion.6), channel_id=1, source_target_pairs={{0,4},{1,5},{2,6},{3,7},{4,0},{5,1},{6,2},{7,3},{8,12},{9,13},{10,... | collective-permute-start | bytes 884744 | tf_op jit(solution)/shard_map/ppermute | solution.py:111
  22.0 6.3 %collective-permute-done.1 = f32[576,128]{1,0:T(8,128)S(1)} collective-permute-done((f32[576,128]{1,0:T(8,128)S(1)}, f32[576,128]{1,0:T(8,128)S(1)}, u32[]{:S(2)}, u32[]{:S(2)}) %collective-permute-start.1) | collective-permute-done | bytes 294944 | tf_op jit(solution)/shard_map/ppermute | solution.py:111
  28.3 0.1 reshape.62
  28.5 0.1 broadcast_select_fusion.3
  28.5 0.2 pad_maximum_fusion.3
  28.7 0.1 reshape.63
  28.9 10.5 %collective-permute-start.2 = (f32[768,128]{1,0:T(8,128)S(1)}, f32[768,128]{1,0:T(8,128)S(1)}, u32[]{:S(2)}, u32[]{:S(2)}) collective-permute-start(f32[768,128]{1,0:T(8,128)S(1)} %pad_maximum_fusion.4), channel_id=1, source_target_pairs={{0,2},{1,3},{2,0},{3,1},{4,6},{5,7},{6,4},{7,5},{8,10},{9,11},{10,... | collective-permute-start | bytes 1179656 | tf_op jit(solution)/shard_map/ppermute | solution.py:111
  39.4 17.2 %collective-permute-done.2 = f32[768,128]{1,0:T(8,128)S(1)} collective-permute-done((f32[768,128]{1,0:T(8,128)S(1)}, f32[768,128]{1,0:T(8,128)S(1)}, u32[]{:S(2)}, u32[]{:S(2)}) %collective-permute-start.2) | collective-permute-done | bytes 393248 | tf_op jit(solution)/shard_map/ppermute | solution.py:111
  56.6 0.1 reshape.65
  56.7 0.2 broadcast_select_fusion.1
  56.9 0.3 fusion.30
  57.2 1.9 %collective-permute-start.3 = (bf16[2,2,192,128]{3,2,1,0:T(8,128)(2,1)S(1)}, bf16[2,2,192,128]{3,2,1,0:T(8,128)(2,1)S(1)}, u32[]{:S(2)}, u32[]{:S(2)}) collective-permute-start(bf16[2,2,192,128]{3,2,1,0:T(8,128)(2,1)S(1)} %pad_maximum_fusion.10), channel_id=1, source_target_pairs={{0,1},{1,0},{2,3},{3,2},{4,5},{5,4},{6,7},{7,6},{8,9},{9,8},{10,11... | collective-permute-start | bytes 589832 | tf_op jit(solution)/shard_map/ppermute | solution.py:53
  59.1 6.8 %collective-permute-done.3 = bf16[2,2,192,128]{3,2,1,0:T(8,128)(2,1)S(1)} collective-permute-done((bf16[2,2,192,128]{3,2,1,0:T(8,128)(2,1)S(1)}, bf16[2,2,192,128]{3,2,1,0:T(8,128)(2,1)S(1)}, u32[]{:S(2)}, u32[]{:S(2)}) %collective-permute-start.3) | collective-permute-done | bytes 196640 | tf_op jit(solution)/shard_map/ppermute | solution.py:53
  66.0 0.3 fusion.17
  66.3 1.9 %collective-permute-start.4 = (f32[1,320,256]{2,1,0:T(8,128)S(1)}, f32[1,320,256]{2,1,0:T(8,128)S(1)}, u32[]{:S(2)}, u32[]{:S(2)}) collective-permute-start(f32[1,320,256]{2,1,0:T(8,128)S(1)} %dynamic-slice_bitcast_fusion), channel_id=1, source_target_pairs={{0,8},{8,0},{16,24},{24,16},{32,40},{40,32},{48,56},{56,48},{64,72... | collective-permute-start | bytes 983048 | tf_op jit(solution)/shard_map/ppermute | solution.py:45
  68.3 1.6 collective-permute-done.4
  69.9 2.7 %collective-permute-start.5 = (f32[1,320,128]{2,1,0:T(8,128)S(1)}, f32[1,320,128]{2,1,0:T(8,128)S(1)}, u32[]{:S(2)}, u32[]{:S(2)}) collective-permute-start(f32[1,320,128]{2,1,0:T(8,128)S(1)} %constant_dynamic-slice_fusion.2), channel_id=1, source_target_pairs={{0,16},{8,24},{16,0},{24,8},{32,48},{40,56},{48,32},{56,40},{64,80... | collective-permute-start | bytes 491528 | tf_op jit(solution)/shard_map/ppermute | solution.py:45
  72.7 5.4 %collective-permute-done.5 = f32[1,320,128]{2,1,0:T(8,128)S(1)} collective-permute-done((f32[1,320,128]{2,1,0:T(8,128)S(1)}, f32[1,320,128]{2,1,0:T(8,128)S(1)}, u32[]{:S(2)}, u32[]{:S(2)}) %collective-permute-start.5) | collective-permute-done | bytes 163872 | tf_op jit(solution)/shard_map/ppermute | solution.py:45
  78.1 2.6 %collective-permute-start.6 = (f32[1,160,128]{2,1,0:T(8,128)S(1)}, f32[1,160,128]{2,1,0:T(8,128)S(1)}, u32[]{:S(2)}, u32[]{:S(2)}) collective-permute-start(f32[1,160,128]{2,1,0:T(8,128)S(1)} %constant_dynamic-slice_fusion.1), channel_id=1, source_target_pairs={{0,64},{8,72},{16,80},{24,88},{32,96},{40,104},{48,112},{56,120},{... | collective-permute-start | bytes 245768 | tf_op jit(solution)/shard_map/ppermute | solution.py:45
  80.7 3.7 %collective-permute-done.6 = f32[1,160,128]{2,1,0:T(8,128)S(1)} collective-permute-done((f32[1,160,128]{2,1,0:T(8,128)S(1)}, f32[1,160,128]{2,1,0:T(8,128)S(1)}, u32[]{:S(2)}, u32[]{:S(2)}) %collective-permute-start.6) | collective-permute-done | bytes 81952 | tf_op jit(solution)/shard_map/ppermute | solution.py:45
  84.5 3.3 %collective-permute-start.7 = (f32[1,160,128]{2,1,0:T(8,128)S(1)}, f32[1,160,128]{2,1,0:T(8,128)S(1)}, u32[]{:S(2)}, u32[]{:S(2)}) collective-permute-start(f32[1,160,128]{2,1,0:T(8,128)S(1)} %dynamic-slice_add_fusion.3), channel_id=1, source_target_pairs={{0,32},{8,40},{16,48},{24,56},{32,0},{40,8},{48,16},{56,24},{64,96... | collective-permute-start | bytes 245768 | tf_op jit(solution)/shard_map/ppermute | solution.py:34
  87.8 4.5 %collective-permute-done.7 = f32[1,160,128]{2,1,0:T(8,128)S(1)} collective-permute-done((f32[1,160,128]{2,1,0:T(8,128)S(1)}, f32[1,160,128]{2,1,0:T(8,128)S(1)}, u32[]{:S(2)}, u32[]{:S(2)}) %collective-permute-start.7) | collective-permute-done | bytes 81952 | tf_op jit(solution)/shard_map/ppermute | solution.py:34
  92.3 2.7 %collective-permute-start.8 = (f32[1,160,128]{2,1,0:T(8,128)S(1)}, f32[1,160,128]{2,1,0:T(8,128)S(1)}, u32[]{:S(2)}, u32[]{:S(2)}) collective-permute-start(f32[1,160,128]{2,1,0:T(8,128)S(1)} %add.117), channel_id=1, source_target_pairs={{0,128},{8,136},{16,144},{24,152},{32,160},{40,168},{48,176},{56,1... | collective-permute-start | bytes 245768 | tf_op jit(solution)/shard_map/ppermute | solution.py:34
  95.0 5.5 %collective-permute-done.8 = f32[1,160,128]{2,1,0:T(8,128)S(1)} collective-permute-done((f32[1,160,128]{2,1,0:T(8,128)S(1)}, f32[1,160,128]{2,1,0:T(8,128)S(1)}, u32[]{:S(2)}, u32[]{:S(2)}) %collective-permute-start.8) | collective-permute-done | bytes 81952 | tf_op jit(solution)/shard_map/ppermute | solution.py:34
  100.5 1.9 %collective-permute-start.9 = (f32[1,160,128]{2,1,0:T(8,128)S(1)}, f32[1,160,128]{2,1,0:T(8,128)S(1)}, u32[]{:S(2)}, u32[]{:S(2)}) collective-permute-start(f32[1,160,128]{2,1,0:T(8,128)S(1)} %add.118), channel_id=1, source_target_pairs={{0,256},{8,264},{16,272},{24,280},{32,288},{40,296},{48,304},{56,3... | collective-permute-start | bytes 245768 | tf_op jit(solution)/shard_map/ppermute | solution.py:34
  102.4 9.2 %collective-permute-done.9 = f32[1,160,128]{2,1,0:T(8,128)S(1)} collective-permute-done((f32[1,160,128]{2,1,0:T(8,128)S(1)}, f32[1,160,128]{2,1,0:T(8,128)S(1)}, u32[]{:S(2)}, u32[]{:S(2)}) %collective-permute-start.9) | collective-permute-done | bytes 81952 | tf_op jit(solution)/shard_map/ppermute | solution.py:34
  111.6 1.9 %collective-permute-start.10 = (f32[1,160,128]{2,1,0:T(8,128)S(1)}, f32[1,160,128]{2,1,0:T(8,128)S(1)}, u32[]{:S(2)}, u32[]{:S(2)}) collective-permute-start(f32[1,160,128]{2,1,0:T(8,128)S(1)} %add.119), channel_id=1, source_target_pairs={{0,64},{8,72},{16,80},{24,88},{32,96},{40,104},{48,112},{56,120},{... | collective-permute-start | bytes 245768 | tf_op jit(solution)/shard_map/ppermute | solution.py:53
  113.6 4.4 %collective-permute-done.10 = f32[1,160,128]{2,1,0:T(8,128)S(1)} collective-permute-done((f32[1,160,128]{2,1,0:T(8,128)S(1)}, f32[1,160,128]{2,1,0:T(8,128)S(1)}, u32[]{:S(2)}, u32[]{:S(2)}) %collective-permute-start.10) | collective-permute-done | bytes 81952 | tf_op jit(solution)/shard_map/ppermute | solution.py:53
  118.0 2.6 %collective-permute-start.11 = (f32[1,320,128]{2,1,0:T(8,128)S(1)}, f32[1,320,128]{2,1,0:T(8,128)S(1)}, u32[]{:S(2)}, u32[]{:S(2)}) collective-permute-start(f32[1,320,128]{2,1,0:T(8,128)S(1)} %pad_maximum_fusion.11), channel_id=1, source_target_pairs={{0,16},{8,24},{16,0},{24,8},{32,48},{40,56},{48,32},{56,40},{64,80... | collective-permute-start | bytes 491528 | tf_op jit(solution)/shard_map/ppermute | solution.py:53
  120.7 4.6 %collective-permute-done.11 = f32[1,320,128]{2,1,0:T(8,128)S(1)} collective-permute-done((f32[1,320,128]{2,1,0:T(8,128)S(1)}, f32[1,320,128]{2,1,0:T(8,128)S(1)}, u32[]{:S(2)}, u32[]{:S(2)}) %collective-permute-start.11) | collective-permute-done | bytes 163872 | tf_op jit(solution)/shard_map/ppermute | solution.py:53
  125.3 1.9 %collective-permute-start.12 = (f32[1,320,256]{2,1,0:T(8,128)S(1)}, f32[1,320,256]{2,1,0:T(8,128)S(1)}, u32[]{:S(2)}, u32[]{:S(2)}) collective-permute-start(f32[1,320,256]{2,1,0:T(8,128)S(1)} %pad_maximum_fusion.5), channel_id=1, source_target_pairs={{0,8},{8,0},{16,24},{24,16},{32,40},{40,32},{48,56},{56,48},{64,72... | collective-permute-start | bytes 983048 | tf_op jit(solution)/shard_map/ppermute | solution.py:53
  127.2 1.6 collective-permute-done.12
  128.9 1.6 fusion.4
  130.5 0.1 copy.62
  130.6 0.1 copy.63
  130.7 0.1 fusion.29
  130.8 0.1 copy.49
  130.9 2.2 %collective-permute-start.13 = (f32[1,257,128]{2,1,0:T(8,128)S(1)}, f32[1,257,128]{2,1,0:T(8,128)S(1)}, u32[]{:S(2)}, u32[]{:S(2)}) collective-permute-start(f32[1,257,128]{2,1,0:T(8,128)S(1)} %constant_dynamic-slice_fusion), channel_id=1, source_target_pairs={{0,1},{1,0},{2,3},{3,2},{4,5},{5,4},{6,7},{7,6},{8,9},{9,8},{10,11... | collective-permute-start | bytes 394760 | tf_op jit(solution)/shard_map/ppermute | solution.py:45
  133.2 5.3 %collective-permute-done.13 = f32[1,257,128]{2,1,0:T(8,128)S(1)} collective-permute-done((f32[1,257,128]{2,1,0:T(8,128)S(1)}, f32[1,257,128]{2,1,0:T(8,128)S(1)}, u32[]{:S(2)}, u32[]{:S(2)}) %collective-permute-start.13) | collective-permute-done | bytes 131616 | tf_op jit(solution)/shard_map/ppermute | solution.py:45
  138.5 1.9 %collective-permute-start.14 = (f32[1,257,128]{2,1,0:T(8,128)S(1)}, f32[1,257,128]{2,1,0:T(8,128)S(1)}, u32[]{:S(2)}, u32[]{:S(2)}) collective-permute-start(f32[1,257,128]{2,1,0:T(8,128)S(1)} %dynamic-slice_add_fusion.2), channel_id=1, source_target_pairs={{0,2},{1,3},{2,0},{3,1},{4,6},{5,7},{6,4},{7,5},{8,10},{9,11},{10,... | collective-permute-start | bytes 394760 | tf_op jit(solution)/shard_map/ppermute | solution.py:34
  140.4 8.3 %collective-permute-done.14 = f32[1,257,128]{2,1,0:T(8,128)S(1)} collective-permute-done((f32[1,257,128]{2,1,0:T(8,128)S(1)}, f32[1,257,128]{2,1,0:T(8,128)S(1)}, u32[]{:S(2)}, u32[]{:S(2)}) %collective-permute-start.14) | collective-permute-done | bytes 131616 | tf_op jit(solution)/shard_map/ppermute | solution.py:34
  148.7 7.3 %collective-permute-start.15 = (f32[1,257,128]{2,1,0:T(8,128)S(1)}, f32[1,257,128]{2,1,0:T(8,128)S(1)}, u32[]{:S(2)}, u32[]{:S(2)}) collective-permute-start(f32[1,257,128]{2,1,0:T(8,128)S(1)} %add.123), channel_id=1, source_target_pairs={{0,4},{1,5},{2,6},{3,7},{4,0},{5,1},{6,2},{7,3},{8,12},{9,13},{10,... | collective-permute-start | bytes 394760 | tf_op jit(solution)/shard_map/ppermute | solution.py:34
  156.0 0.2 constant_dynamic-slice_fusion.3
  156.2 0.7 copy.56
  156.9 0.7 copy.57
  157.7 5.1 %collective-permute-done.15 = f32[1,257,128]{2,1,0:T(8,128)S(1)} collective-permute-done((f32[1,257,128]{2,1,0:T(8,128)S(1)}, f32[1,257,128]{2,1,0:T(8,128)S(1)}, u32[]{:S(2)}, u32[]{:S(2)}) %collective-permute-start.15) | collective-permute-done | bytes 131616 | tf_op jit(solution)/shard_map/ppermute | solution.py:34
  162.8 1.9 %collective-permute-start.16 = (f32[1,257,128]{2,1,0:T(8,128)S(1)}, f32[1,257,128]{2,1,0:T(8,128)S(1)}, u32[]{:S(2)}, u32[]{:S(2)}) collective-permute-start(f32[1,257,128]{2,1,0:T(8,128)S(1)} %add.124), channel_id=1, source_target_pairs={{0,1},{1,0},{2,3},{3,2},{4,5},{5,4},{6,7},{7,6},{8,9},{9,8},{10,11... | collective-permute-start | bytes 394760 | tf_op jit(solution)/shard_map/ppermute | solution.py:53
  164.7 1.1 fusion
  165.8 3.9 %collective-permute-done.16 = f32[1,257,128]{2,1,0:T(8,128)S(1)} collective-permute-done((f32[1,257,128]{2,1,0:T(8,128)S(1)}, f32[1,257,128]{2,1,0:T(8,128)S(1)}, u32[]{:S(2)}, u32[]{:S(2)}) %collective-permute-start.16) | collective-permute-done | bytes 131616 | tf_op jit(solution)/shard_map/ppermute | solution.py:53
  169.8 0.1 copy.64
  169.9 0.1 copy.52
  170.0 0.1 bitcast_select_fusion
  170.1 0.1 select_reduce_fusion
  170.2 0.9 multiply_convert_fusion
  171.2 0.2 copy.54
  171.4 0.1 copy.55
  171.5 1.1 copy.58
  (43 shorter events, 0.7 us)
Async XLA Ops:
  0.6 1.4 copy-start
  2.4 4.3 %copy-start.2 = (f32[2,192,32]{1,2,0:T(8,128)S(1)}, f32[2,192,32]{1,2,0:T(8,128)}, u32[]{:S(2)}) copy-start(f32[2,192,32]{1,2,0:T(8,128)} %param.9) | copy-start | bytes 147460
  2.4 4.3 %copy-start.3 = (f32[2,192,32]{1,2,0:T(8,128)S(1)}, f32[2,192,32]{1,2,0:T(8,128)}, u32[]{:S(2)}) copy-start(f32[2,192,32]{1,2,0:T(8,128)} %param.8) | copy-start | bytes 147460
  2.4 9.2 %collective-permute-start = (f32[2,192,128]{2,1,0:T(8,128)S(1)}, f32[2,192,128]{2,1,0:T(8,128)S(1)}, u32[]{:S(2)}, u32[]{:S(2)}) collective-permute-start(f32[2,192,128]{2,1,0:T(8,128)S(1)} %constant_dynamic-slice_fusion.5), channel_id=1, source_target_pairs={{0,1},{1,0},{2,3},{3,2},{4,5},{5,4},{6,7},{7,6},{8,9},{9,8},{10,11... | collective-permute-start | bytes 589832 | tf_op jit(solution)/shard_map/ppermute | solution.py:45
  11.7 16.6 %collective-permute-start.1 = (f32[576,128]{1,0:T(8,128)S(1)}, f32[576,128]{1,0:T(8,128)S(1)}, u32[]{:S(2)}, u32[]{:S(2)}) collective-permute-start(f32[576,128]{1,0:T(8,128)S(1)} %pad_maximum_fusion.6), channel_id=1, source_target_pairs={{0,4},{1,5},{2,6},{3,7},{4,0},{5,1},{6,2},{7,3},{8,12},{9,13},{10,... | collective-permute-start | bytes 884744 | tf_op jit(solution)/shard_map/ppermute | solution.py:111
  28.9 27.7 %collective-permute-start.2 = (f32[768,128]{1,0:T(8,128)S(1)}, f32[768,128]{1,0:T(8,128)S(1)}, u32[]{:S(2)}, u32[]{:S(2)}) collective-permute-start(f32[768,128]{1,0:T(8,128)S(1)} %pad_maximum_fusion.4), channel_id=1, source_target_pairs={{0,2},{1,3},{2,0},{3,1},{4,6},{5,7},{6,4},{7,5},{8,10},{9,11},{10,... | collective-permute-start | bytes 1179656 | tf_op jit(solution)/shard_map/ppermute | solution.py:111
  57.2 8.7 %collective-permute-start.3 = (bf16[2,2,192,128]{3,2,1,0:T(8,128)(2,1)S(1)}, bf16[2,2,192,128]{3,2,1,0:T(8,128)(2,1)S(1)}, u32[]{:S(2)}, u32[]{:S(2)}) collective-permute-start(bf16[2,2,192,128]{3,2,1,0:T(8,128)(2,1)S(1)} %pad_maximum_fusion.10), channel_id=1, source_target_pairs={{0,1},{1,0},{2,3},{3,2},{4,5},{5,4},{6,7},{7,6},{8,9},{9,8},{10,11... | collective-permute-start | bytes 589832 | tf_op jit(solution)/shard_map/ppermute | solution.py:53
  66.3 3.5 %collective-permute-start.4 = (f32[1,320,256]{2,1,0:T(8,128)S(1)}, f32[1,320,256]{2,1,0:T(8,128)S(1)}, u32[]{:S(2)}, u32[]{:S(2)}) collective-permute-start(f32[1,320,256]{2,1,0:T(8,128)S(1)} %dynamic-slice_bitcast_fusion), channel_id=1, source_target_pairs={{0,8},{8,0},{16,24},{24,16},{32,40},{40,32},{48,56},{56,48},{64,72... | collective-permute-start | bytes 983048 | tf_op jit(solution)/shard_map/ppermute | solution.py:45
  69.9 8.1 %collective-permute-start.5 = (f32[1,320,128]{2,1,0:T(8,128)S(1)}, f32[1,320,128]{2,1,0:T(8,128)S(1)}, u32[]{:S(2)}, u32[]{:S(2)}) collective-permute-start(f32[1,320,128]{2,1,0:T(8,128)S(1)} %constant_dynamic-slice_fusion.2), channel_id=1, source_target_pairs={{0,16},{8,24},{16,0},{24,8},{32,48},{40,56},{48,32},{56,40},{64,80... | collective-permute-start | bytes 491528 | tf_op jit(solution)/shard_map/ppermute | solution.py:45
  78.1 6.3 %collective-permute-start.6 = (f32[1,160,128]{2,1,0:T(8,128)S(1)}, f32[1,160,128]{2,1,0:T(8,128)S(1)}, u32[]{:S(2)}, u32[]{:S(2)}) collective-permute-start(f32[1,160,128]{2,1,0:T(8,128)S(1)} %constant_dynamic-slice_fusion.1), channel_id=1, source_target_pairs={{0,64},{8,72},{16,80},{24,88},{32,96},{40,104},{48,112},{56,120},{... | collective-permute-start | bytes 245768 | tf_op jit(solution)/shard_map/ppermute | solution.py:45
  84.5 7.8 %collective-permute-start.7 = (f32[1,160,128]{2,1,0:T(8,128)S(1)}, f32[1,160,128]{2,1,0:T(8,128)S(1)}, u32[]{:S(2)}, u32[]{:S(2)}) collective-permute-start(f32[1,160,128]{2,1,0:T(8,128)S(1)} %dynamic-slice_add_fusion.3), channel_id=1, source_target_pairs={{0,32},{8,40},{16,48},{24,56},{32,0},{40,8},{48,16},{56,24},{64,96... | collective-permute-start | bytes 245768 | tf_op jit(solution)/shard_map/ppermute | solution.py:34
  92.3 8.2 %collective-permute-start.8 = (f32[1,160,128]{2,1,0:T(8,128)S(1)}, f32[1,160,128]{2,1,0:T(8,128)S(1)}, u32[]{:S(2)}, u32[]{:S(2)}) collective-permute-start(f32[1,160,128]{2,1,0:T(8,128)S(1)} %add.117), channel_id=1, source_target_pairs={{0,128},{8,136},{16,144},{24,152},{32,160},{40,168},{48,176},{56,1... | collective-permute-start | bytes 245768 | tf_op jit(solution)/shard_map/ppermute | solution.py:34
  100.5 11.1 %collective-permute-start.9 = (f32[1,160,128]{2,1,0:T(8,128)S(1)}, f32[1,160,128]{2,1,0:T(8,128)S(1)}, u32[]{:S(2)}, u32[]{:S(2)}) collective-permute-start(f32[1,160,128]{2,1,0:T(8,128)S(1)} %add.118), channel_id=1, source_target_pairs={{0,256},{8,264},{16,272},{24,280},{32,288},{40,296},{48,304},{56,3... | collective-permute-start | bytes 245768 | tf_op jit(solution)/shard_map/ppermute | solution.py:34
  111.6 6.3 %collective-permute-start.10 = (f32[1,160,128]{2,1,0:T(8,128)S(1)}, f32[1,160,128]{2,1,0:T(8,128)S(1)}, u32[]{:S(2)}, u32[]{:S(2)}) collective-permute-start(f32[1,160,128]{2,1,0:T(8,128)S(1)} %add.119), channel_id=1, source_target_pairs={{0,64},{8,72},{16,80},{24,88},{32,96},{40,104},{48,112},{56,120},{... | collective-permute-start | bytes 245768 | tf_op jit(solution)/shard_map/ppermute | solution.py:53
  118.0 7.2 %collective-permute-start.11 = (f32[1,320,128]{2,1,0:T(8,128)S(1)}, f32[1,320,128]{2,1,0:T(8,128)S(1)}, u32[]{:S(2)}, u32[]{:S(2)}) collective-permute-start(f32[1,320,128]{2,1,0:T(8,128)S(1)} %pad_maximum_fusion.11), channel_id=1, source_target_pairs={{0,16},{8,24},{16,0},{24,8},{32,48},{40,56},{48,32},{56,40},{64,80... | collective-permute-start | bytes 491528 | tf_op jit(solution)/shard_map/ppermute | solution.py:53
  125.3 3.5 %collective-permute-start.12 = (f32[1,320,256]{2,1,0:T(8,128)S(1)}, f32[1,320,256]{2,1,0:T(8,128)S(1)}, u32[]{:S(2)}, u32[]{:S(2)}) collective-permute-start(f32[1,320,256]{2,1,0:T(8,128)S(1)} %pad_maximum_fusion.5), channel_id=1, source_target_pairs={{0,8},{8,0},{16,24},{24,16},{32,40},{40,32},{48,56},{56,48},{64,72... | collective-permute-start | bytes 983048 | tf_op jit(solution)/shard_map/ppermute | solution.py:53
  130.9 7.5 %collective-permute-start.13 = (f32[1,257,128]{2,1,0:T(8,128)S(1)}, f32[1,257,128]{2,1,0:T(8,128)S(1)}, u32[]{:S(2)}, u32[]{:S(2)}) collective-permute-start(f32[1,257,128]{2,1,0:T(8,128)S(1)} %constant_dynamic-slice_fusion), channel_id=1, source_target_pairs={{0,1},{1,0},{2,3},{3,2},{4,5},{5,4},{6,7},{7,6},{8,9},{9,8},{10,11... | collective-permute-start | bytes 394760 | tf_op jit(solution)/shard_map/ppermute | solution.py:45
  138.5 10.2 %collective-permute-start.14 = (f32[1,257,128]{2,1,0:T(8,128)S(1)}, f32[1,257,128]{2,1,0:T(8,128)S(1)}, u32[]{:S(2)}, u32[]{:S(2)}) collective-permute-start(f32[1,257,128]{2,1,0:T(8,128)S(1)} %dynamic-slice_add_fusion.2), channel_id=1, source_target_pairs={{0,2},{1,3},{2,0},{3,1},{4,6},{5,7},{6,4},{7,5},{8,10},{9,11},{10,... | collective-permute-start | bytes 394760 | tf_op jit(solution)/shard_map/ppermute | solution.py:34
  148.7 14.1 %collective-permute-start.15 = (f32[1,257,128]{2,1,0:T(8,128)S(1)}, f32[1,257,128]{2,1,0:T(8,128)S(1)}, u32[]{:S(2)}, u32[]{:S(2)}) collective-permute-start(f32[1,257,128]{2,1,0:T(8,128)S(1)} %add.123), channel_id=1, source_target_pairs={{0,4},{1,5},{2,6},{3,7},{4,0},{5,1},{6,2},{7,3},{8,12},{9,13},{10,... | collective-permute-start | bytes 394760 | tf_op jit(solution)/shard_map/ppermute | solution.py:34
  156.2 8.6 %copy-start.1 = (f32[2,192,320]{2,1,0:T(8,128)S(1)}, f32[2,192,320]{2,1,0:T(8,128)}, u32[]{:S(2)}) copy-start(f32[2,192,320]{2,1,0:T(8,128)} %param.6) | copy-start | bytes 1474564
  162.8 6.9 %collective-permute-start.16 = (f32[1,257,128]{2,1,0:T(8,128)S(1)}, f32[1,257,128]{2,1,0:T(8,128)S(1)}, u32[]{:S(2)}, u32[]{:S(2)}) collective-permute-start(f32[1,257,128]{2,1,0:T(8,128)S(1)} %add.124), channel_id=1, source_target_pairs={{0,1},{1,0},{2,3},{3,2},{4,5},{5,4},{6,7},{7,6},{8,9},{9,8},{10,11... | collective-permute-start | bytes 394760 | tf_op jit(solution)/shard_map/ppermute | solution.py:53

commit v7 on v4

--- a/solution.py
+++ b/solution.py
@@ -101,11 +101,16 @@
     basis_order = reverse_blocks(basis, len(tp_bits), width)
 
     projected_part = jnp.einsum("mfd,dmr->mfr", grads, basis_order, preferred_element_type=jnp.float32)
-    own = halving_scatter(projected_part, "tp", tp, tp_bits)
+    half = halving_scatter(projected_part, "tp", tp, [(0, 2)])
+    half = butterfly_sum(half, "tp", tp, reversed(range(1, len(tp_bits))))
+    member = lax.axis_index("tp")
+    own_place = 0
+    for step, bit in enumerate(reversed(range(1, len(tp_bits)))):
+        own_place = own_place + (((member >> bit) & 1) << step)
+    own = lax.dynamic_slice_in_dim(half, own_place * width, width, 2)
     first_next, second_next, normal_half = adam_share(own, first_moment, second_moment)
-    halves = jnp.stack([own.astype(jnp.bfloat16), normal_half], axis=0)
-    gathered = doubling_gather(halves, "tp", tp, [(b, 3) for b, _ in tp_bits])
-    projected_half, normal_full = gathered[0], gathered[1]
+    projected_half = doubling_gather(half.astype(jnp.bfloat16), "tp", tp, [(0, 2)])
+    normal_full = doubling_gather(normal_half, "tp", tp, tp_bits)
 
     image_part = jnp.einsum("mfd,mfr->mdr", grads, projected_half, preferred_element_type=jnp.float32)
     stages = [(0, 0), (1, 2), (3, 1)]
@@ -116,7 +121,9 @@
     update = jnp.einsum("mfr,dmr->mfd", normal_full, basis_order, preferred_element_type=jnp.float32)
     weight_next = weights - LEARNING_RATE * GALORE_SCALE * update
 
-    gram = unpack_gram(butterfly_sum(pack_gram(jnp.einsum("mdr,mds->mrs", image, image, precision=highest)), "tp", tp))
+    packed = halving_scatter(pack_gram(jnp.einsum("mdr,mds->mrs", image, image, precision=highest)), "tp", tp, [(0, 0)])
+    packed = butterfly_sum(packed, "tp", tp, range(1, len(tp_bits)))
+    gram = unpack_gram(doubling_gather(packed, "tp", tp, [(0, 0)]))
     diagonal = lax.broadcasted_iota(jnp.int32, gram.shape, 1) == lax.broadcasted_iota(jnp.int32, gram.shape, 2)
     total = jnp.sum(jnp.where(diagonal, gram, 0.0), axis=(1, 2)) + EPSILON_NORM
     factor = jnp.sqrt(rank_width / total)

time: 193 us -> 158 us (0.82)
  the two profiles are of different devices: /device:TPU:1 before, /device:TPU:32 now
where the time goes in v7:
time: 158 us
  starting transfers between devices  79.9 us (51%)
  waiting for transfers between devices  65.2 us (41%)
  local copies, waits for them, and re-layouts  5.78 us (4%)
  matrix products  4.17 us (3%)
    ppermute x7, starting transfers between devices, butterfly_sum(): value = value + lax.ppermute(value, axis, partner_perm(size, bit))  38.4 us
    ppermute x7, waiting for transfers between devices, butterfly_sum(): value = value + lax.ppermute(value, axis, partner_perm(size, bit))  36.1 us
    ppermute x8, starting transfers between devices, doubling_gather(): other = lax.ppermute(value, axis, partner_perm(size, bit))  25.3 us
    ppermute x5, waiting for transfers between devices, halving_scatter(): value = keep + lax.ppermute(send, axis, partner_perm(size, bit))  17.8 us
    ppermute x5, starting transfers between devices, halving_scatter(): value = keep + lax.ppermute(send, axis, partner_perm(size, bit))  16.2 us
    ppermute x8, waiting for transfers between devices, doubling_gather(): other = lax.ppermute(value, axis, partner_perm(size, bit))  11.2 us
    unnamed x17, local copies, waits for them, and re-layouts  5.13 us
  transfers between devices with their start and end apart: 20, of which 17 were waited for; matrix products, arithmetic and copies ran while one was open for 4% of the time, Pallas kernels for 0%

profile of v7, /device:TPU:32, one launch (start us, length us, event | category | flops | bytes accessed | tf_op | source)
XLA Modules:
  0.0 157.7 jit_solution(17722644671532052151)
XLA Ops:
  0.7 1.3 copy.23
  2.0 0.1 copy.24
  2.1 0.3 fusion.32
  2.4 4.3 %collective-permute-start = (f32[2,192,128]{2,1,0:T(8,128)S(1)}, f32[2,192,128]{2,1,0:T(8,128)S(1)}, u32[]{:S(2)}, u32[]{:S(2)}) collective-permute-start(f32[2,192,128]{2,1,0:T(8,128)S(1)} %constant_dynamic-slice_fusion.3), channel_id=1, source_target_pairs={{0,1},{1,0},{2,3},{3,2},{4,5},{5,4},{6,7},{7,6},{8,9},{9,8},{10,11... | collective-permute-start | bytes 589832 | tf_op jit(solution)/shard_map/ppermute | solution.py:45
  6.7 4.9 %collective-permute-done = f32[2,192,128]{2,1,0:T(8,128)S(1)} collective-permute-done((f32[2,192,128]{2,1,0:T(8,128)S(1)}, f32[2,192,128]{2,1,0:T(8,128)S(1)}, u32[]{:S(2)}, u32[]{:S(2)}) %collective-permute-start) | collective-permute-done | bytes 196640 | tf_op jit(solution)/shard_map/ppermute | solution.py:45
  11.6 10.3 %collective-permute-start.1 = (f32[2,192,128]{2,1,0:T(8,128)S(1)}, f32[2,192,128]{2,1,0:T(8,128)S(1)}, u32[]{:S(2)}, u32[]{:S(2)}) collective-permute-start(f32[2,192,128]{2,1,0:T(8,128)S(1)} %dynamic-slice_add_fusion), channel_id=1, source_target_pairs={{0,4},{1,5},{2,6},{3,7},{4,0},{5,1},{6,2},{7,3},{8,12},{9,13},{10,... | collective-permute-start | bytes 589832 | tf_op jit(solution)/shard_map/ppermute | solution.py:34
  21.9 4.1 %collective-permute-done.1 = f32[2,192,128]{2,1,0:T(8,128)S(1)} collective-permute-done((f32[2,192,128]{2,1,0:T(8,128)S(1)}, f32[2,192,128]{2,1,0:T(8,128)S(1)}, u32[]{:S(2)}, u32[]{:S(2)}) %collective-permute-start.1) | collective-permute-done | bytes 196640 | tf_op jit(solution)/shard_map/ppermute | solution.py:34
  26.1 8.5 %collective-permute-start.2 = (f32[2,192,128]{2,1,0:T(8,128)S(1)}, f32[2,192,128]{2,1,0:T(8,128)S(1)}, u32[]{:S(2)}, u32[]{:S(2)}) collective-permute-start(f32[2,192,128]{2,1,0:T(8,128)S(1)} %add.99), channel_id=1, source_target_pairs={{0,2},{1,3},{2,0},{3,1},{4,6},{5,7},{6,4},{7,5},{8,10},{9,11},{10,... | collective-permute-start | bytes 589832 | tf_op jit(solution)/shard_map/ppermute | solution.py:34
  34.6 7.9 %collective-permute-done.2 = f32[2,192,128]{2,1,0:T(8,128)S(1)} collective-permute-done((f32[2,192,128]{2,1,0:T(8,128)S(1)}, f32[2,192,128]{2,1,0:T(8,128)S(1)}, u32[]{:S(2)}, u32[]{:S(2)}) %collective-permute-start.2) | collective-permute-done | bytes 196640 | tf_op jit(solution)/shard_map/ppermute | solution.py:34
  42.5 1.9 %collective-permute-start.6 = (bf16[2,192,128]{2,1,0:T(8,128)(2,1)S(1)}, bf16[2,192,128]{2,1,0:T(8,128)(2,1)S(1)}, u32[]{:S(2)}, u32[]{:S(2)}) collective-permute-start(bf16[2,192,128]{2,1,0:T(8,128)(2,1)S(1)} %get-tuple-element.14), channel_id=1, source_target_pairs={{0,1},{1,0},{2,3},{3,2},{4,5},{5,4},{6,7},{7,6},{8,9},{9,8},{10,11... | collective-permute-start | bytes 294920 | tf_op jit(solution)/shard_map/ppermute | solution.py:53
  44.4 4.7 %collective-permute-done.6 = bf16[2,192,128]{2,1,0:T(8,128)(2,1)S(1)} collective-permute-done((bf16[2,192,128]{2,1,0:T(8,128)(2,1)S(1)}, bf16[2,192,128]{2,1,0:T(8,128)(2,1)S(1)}, u32[]{:S(2)}, u32[]{:S(2)}) %collective-permute-start.6) | collective-permute-done | bytes 98336 | tf_op jit(solution)/shard_map/ppermute | solution.py:53
  49.1 0.3 fusion.12
  49.5 1.9 %collective-permute-start.7 = (f32[1,320,256]{2,1,0:T(8,128)S(1)}, f32[1,320,256]{2,1,0:T(8,128)S(1)}, u32[]{:S(2)}, u32[]{:S(2)}) collective-permute-start(f32[1,320,256]{2,1,0:T(8,128)S(1)} %dynamic-slice_bitcast_fusion), channel_id=1, source_target_pairs={{0,8},{8,0},{16,24},{24,16},{32,40},{40,32},{48,56},{56,48},{64,72... | collective-permute-start | bytes 983048 | tf_op jit(solution)/shard_map/ppermute | solution.py:45
  51.4 1.6 %collective-permute-done.7 = f32[1,320,256]{2,1,0:T(8,128)S(1)} collective-permute-done((f32[1,320,256]{2,1,0:T(8,128)S(1)}, f32[1,320,256]{2,1,0:T(8,128)S(1)}, u32[]{:S(2)}, u32[]{:S(2)}) %collective-permute-start.7) | collective-permute-done | bytes 327712 | tf_op jit(solution)/shard_map/ppermute | solution.py:45
  53.1 3.4 %collective-permute-start.8 = (f32[1,320,128]{2,1,0:T(8,128)S(1)}, f32[1,320,128]{2,1,0:T(8,128)S(1)}, u32[]{:S(2)}, u32[]{:S(2)}) collective-permute-start(f32[1,320,128]{2,1,0:T(8,128)S(1)} %constant_dynamic-slice_fusion.2), channel_id=1, source_target_pairs={{0,16},{8,24},{16,0},{24,8},{32,48},{40,56},{48,32},{56,40},{64,80... | collective-permute-start | bytes 491528 | tf_op jit(solution)/shard_map/ppermute | solution.py:45
  56.5 4.7 %collective-permute-done.8 = f32[1,320,128]{2,1,0:T(8,128)S(1)} collective-permute-done((f32[1,320,128]{2,1,0:T(8,128)S(1)}, f32[1,320,128]{2,1,0:T(8,128)S(1)}, u32[]{:S(2)}, u32[]{:S(2)}) %collective-permute-start.8) | collective-permute-done | bytes 163872 | tf_op jit(solution)/shard_map/ppermute | solution.py:45
  61.3 2.6 %collective-permute-start.9 = (f32[1,160,128]{2,1,0:T(8,128)S(1)}, f32[1,160,128]{2,1,0:T(8,128)S(1)}, u32[]{:S(2)}, u32[]{:S(2)}) collective-permute-start(f32[1,160,128]{2,1,0:T(8,128)S(1)} %constant_dynamic-slice_fusion.1), channel_id=1, source_target_pairs={{0,64},{8,72},{16,80},{24,88},{32,96},{40,104},{48,112},{56,120},{... | collective-permute-start | bytes 245768 | tf_op jit(solution)/shard_map/ppermute | solution.py:45
  63.9 3.7 %collective-permute-done.9 = f32[1,160,128]{2,1,0:T(8,128)S(1)} collective-permute-done((f32[1,160,128]{2,1,0:T(8,128)S(1)}, f32[1,160,128]{2,1,0:T(8,128)S(1)}, u32[]{:S(2)}, u32[]{:S(2)}) %collective-permute-start.9) | collective-permute-done | bytes 81952 | tf_op jit(solution)/shard_map/ppermute | solution.py:45
  67.6 4.9 %collective-permute-start.10 = (f32[1,160,128]{2,1,0:T(8,128)S(1)}, f32[1,160,128]{2,1,0:T(8,128)S(1)}, u32[]{:S(2)}, u32[]{:S(2)}) collective-permute-start(f32[1,160,128]{2,1,0:T(8,128)S(1)} %dynamic-slice_add_fusion.3), channel_id=1, source_target_pairs={{0,32},{8,40},{16,48},{24,56},{32,0},{40,8},{48,16},{56,24},{64,96... | collective-permute-start | bytes 245768 | tf_op jit(solution)/shard_map/ppermute | solution.py:34
  72.5 2.9 %collective-permute-done.10 = f32[1,160,128]{2,1,0:T(8,128)S(1)} collective-permute-done((f32[1,160,128]{2,1,0:T(8,128)S(1)}, f32[1,160,128]{2,1,0:T(8,128)S(1)}, u32[]{:S(2)}, u32[]{:S(2)}) %collective-permute-start.10) | collective-permute-done | bytes 81952 | tf_op jit(solution)/shard_map/ppermute | solution.py:34
  75.5 2.7 %collective-permute-start.11 = (f32[1,160,128]{2,1,0:T(8,128)S(1)}, f32[1,160,128]{2,1,0:T(8,128)S(1)}, u32[]{:S(2)}, u32[]{:S(2)}) collective-permute-start(f32[1,160,128]{2,1,0:T(8,128)S(1)} %add.116), channel_id=1, source_target_pairs={{0,128},{8,136},{16,144},{24,152},{32,160},{40,168},{48,176},{56,1... | collective-permute-start | bytes 245768 | tf_op jit(solution)/shard_map/ppermute | solution.py:34
  78.2 5.5 %collective-permute-done.11 = f32[1,160,128]{2,1,0:T(8,128)S(1)} collective-permute-done((f32[1,160,128]{2,1,0:T(8,128)S(1)}, f32[1,160,128]{2,1,0:T(8,128)S(1)}, u32[]{:S(2)}, u32[]{:S(2)}) %collective-permute-start.11) | collective-permute-done | bytes 81952 | tf_op jit(solution)/shard_map/ppermute | solution.py:34
  83.7 1.9 %collective-permute-start.12 = (f32[1,160,128]{2,1,0:T(8,128)S(1)}, f32[1,160,128]{2,1,0:T(8,128)S(1)}, u32[]{:S(2)}, u32[]{:S(2)}) collective-permute-start(f32[1,160,128]{2,1,0:T(8,128)S(1)} %add.117), channel_id=1, source_target_pairs={{0,256},{8,264},{16,272},{24,280},{32,288},{40,296},{48,304},{56,3... | collective-permute-start | bytes 245768 | tf_op jit(solution)/shard_map/ppermute | solution.py:34
  85.6 9.2 %collective-permute-done.12 = f32[1,160,128]{2,1,0:T(8,128)S(1)} collective-permute-done((f32[1,160,128]{2,1,0:T(8,128)S(1)}, f32[1,160,128]{2,1,0:T(8,128)S(1)}, u32[]{:S(2)}, u32[]{:S(2)}) %collective-permute-start.12) | collective-permute-done | bytes 81952 | tf_op jit(solution)/shard_map/ppermute | solution.py:34
  94.8 2.3 %collective-permute-start.13 = (f32[1,160,128]{2,1,0:T(8,128)S(1)}, f32[1,160,128]{2,1,0:T(8,128)S(1)}, u32[]{:S(2)}, u32[]{:S(2)}) collective-permute-start(f32[1,160,128]{2,1,0:T(8,128)S(1)} %add.118), channel_id=1, source_target_pairs={{0,64},{8,72},{16,80},{24,88},{32,96},{40,104},{48,112},{56,120},{... | collective-permute-start | bytes 245768 | tf_op jit(solution)/shard_map/ppermute | solution.py:53
  97.2 0.1 copy.22
  97.3 0.7 copy-done.3
  98.0 0.1 copy.26
  98.1 3.2 %collective-permute-done.13 = f32[1,160,128]{2,1,0:T(8,128)S(1)} collective-permute-done((f32[1,160,128]{2,1,0:T(8,128)S(1)}, f32[1,160,128]{2,1,0:T(8,128)S(1)}, u32[]{:S(2)}, u32[]{:S(2)}) %collective-permute-start.13) | collective-permute-done | bytes 81952 | tf_op jit(solution)/shard_map/ppermute | solution.py:53
  101.3 3.3 %collective-permute-start.14 = (f32[1,320,128]{2,1,0:T(8,128)S(1)}, f32[1,320,128]{2,1,0:T(8,128)S(1)}, u32[]{:S(2)}, u32[]{:S(2)}) collective-permute-start(f32[1,320,128]{2,1,0:T(8,128)S(1)} %pad_maximum_fusion.5), channel_id=1, source_target_pairs={{0,16},{8,24},{16,0},{24,8},{32,48},{40,56},{48,32},{56,40},{64,80... | collective-permute-start | bytes 491528 | tf_op jit(solution)/shard_map/ppermute | solution.py:53
  104.6 0.2 divide_convert_fusion
  104.9 7.1 %collective-permute-start.3 = (bf16[2,192,32]{2,1,0:T(8,128)(2,1)S(1)}, bf16[2,192,32]{2,1,0:T(8,128)(2,1)S(1)}, u32[]{:S(2)}, u32[]{:S(2)}) collective-permute-start(bf16[2,192,32]{2,1,0:T(8,128)(2,1)S(1)} %get-tuple-element.16), channel_id=1, source_target_pairs={{0,4},{1,5},{2,6},{3,7},{4,0},{5,1},{6,2},{7,3},{8,12},{9,13},{10,... | collective-permute-start | bytes 73736 | tf_op jit(solution)/shard_map/ppermute | solution.py:53
  112.1 1.9 %collective-permute-start.15 = (f32[1,320,256]{2,1,0:T(8,128)S(1)}, f32[1,320,256]{2,1,0:T(8,128)S(1)}, u32[]{:S(2)}, u32[]{:S(2)}) collective-permute-start(f32[1,320,256]{2,1,0:T(8,128)S(1)} %pad_maximum_fusion.3), channel_id=1, source_target_pairs={{0,8},{8,0},{16,24},{24,16},{32,40},{40,32},{48,56},{56,48},{64,72... | collective-permute-start | bytes 983048 | tf_op jit(solution)/shard_map/ppermute | solution.py:53
  114.0 1.3 collective-permute-done.3
  115.3 0.1 pad_maximum_fusion.6
  115.4 2.0 %collective-permute-start.4 = (bf16[2,192,64]{2,1,0:T(8,128)(2,1)S(1)}, bf16[2,192,64]{2,1,0:T(8,128)(2,1)S(1)}, u32[]{:S(2)}, u32[]{:S(2)}) collective-permute-start(bf16[2,192,64]{2,1,0:T(8,128)(2,1)S(1)} %pad_maximum_fusion.6), channel_id=1, source_target_pairs={{0,2},{1,3},{2,0},{3,1},{4,6},{5,7},{6,4},{7,5},{8,10},{9,11},{10,... | collective-permute-start | bytes 147464 | tf_op jit(solution)/shard_map/ppermute | solution.py:53
  117.5 1.6 fusion.4
  119.1 0.1 copy.43
  119.2 0.1 copy.44
  119.3 0.1 fusion.23
  119.4 0.1 copy.30
  119.6 4.0 %collective-permute-start.16 = (f32[1,257,128]{2,1,0:T(8,128)S(1)}, f32[1,257,128]{2,1,0:T(8,128)S(1)}, u32[]{:S(2)}, u32[]{:S(2)}) collective-permute-start(f32[1,257,128]{2,1,0:T(8,128)S(1)} %constant_dynamic-slice_fusion), channel_id=1, source_target_pairs={{0,1},{1,0},{2,3},{3,2},{4,5},{5,4},{6,7},{7,6},{8,9},{9,8},{10,11... | collective-permute-start | bytes 394760 | tf_op jit(solution)/shard_map/ppermute | solution.py:45
  123.6 0.2 collective-permute-done.4
  123.8 0.1 broadcast_select_fusion.5
  124.0 2.9 %collective-permute-done.16 = f32[1,257,128]{2,1,0:T(8,128)S(1)} collective-permute-done((f32[1,257,128]{2,1,0:T(8,128)S(1)}, f32[1,257,128]{2,1,0:T(8,128)S(1)}, u32[]{:S(2)}, u32[]{:S(2)}) %collective-permute-start.16) | collective-permute-done | bytes 131616 | tf_op jit(solution)/shard_map/ppermute | solution.py:45
  126.9 4.4 %collective-permute-start.17 = (f32[1,257,128]{2,1,0:T(8,128)S(1)}, f32[1,257,128]{2,1,0:T(8,128)S(1)}, u32[]{:S(2)}, u32[]{:S(2)}) collective-permute-start(f32[1,257,128]{2,1,0:T(8,128)S(1)} %dynamic-slice_add_fusion.2), channel_id=1, source_target_pairs={{0,2},{1,3},{2,0},{3,1},{4,6},{5,7},{6,4},{7,5},{8,10},{9,11},{10,... | collective-permute-start | bytes 394760 | tf_op jit(solution)/shard_map/ppermute | solution.py:34
  131.2 0.1 pad_maximum_fusion.7
  131.3 2.2 %collective-permute-start.5 = (bf16[2,192,128]{2,1,0:T(8,128)(2,1)S(1)}, bf16[2,192,128]{2,1,0:T(8,128)(2,1)S(1)}, u32[]{:S(2)}, u32[]{:S(2)}) collective-permute-start(bf16[2,192,128]{2,1,0:T(8,128)(2,1)S(1)} %pad_maximum_fusion.7), channel_id=1, source_target_pairs={{0,1},{1,0},{2,3},{3,2},{4,5},{5,4},{6,7},{7,6},{8,9},{9,8},{10,11... | collective-permute-start | bytes 294920 | tf_op jit(solution)/shard_map/ppermute | solution.py:53
  133.6 0.7 copy.37
  134.3 0.7 copy.38
  135.0 1.5 collective-permute-done.17
  136.6 5.7 %collective-permute-start.18 = (f32[1,257,128]{2,1,0:T(8,128)S(1)}, f32[1,257,128]{2,1,0:T(8,128)S(1)}, u32[]{:S(2)}, u32[]{:S(2)}) collective-permute-start(f32[1,257,128]{2,1,0:T(8,128)S(1)} %add.122), channel_id=1, source_target_pairs={{0,4},{1,5},{2,6},{3,7},{4,0},{5,1},{6,2},{7,3},{8,12},{9,13},{10,... | collective-permute-start | bytes 394760 | tf_op jit(solution)/shard_map/ppermute | solution.py:34
  142.3 0.1 broadcast_select_fusion.9
  142.4 4.9 %collective-permute-done.18 = f32[1,257,128]{2,1,0:T(8,128)S(1)} collective-permute-done((f32[1,257,128]{2,1,0:T(8,128)S(1)}, f32[1,257,128]{2,1,0:T(8,128)S(1)}, u32[]{:S(2)}, u32[]{:S(2)}) %collective-permute-start.18) | collective-permute-done | bytes 131616 | tf_op jit(solution)/shard_map/ppermute | solution.py:34
  147.4 4.5 %collective-permute-start.19 = (f32[1,257,128]{2,1,0:T(8,128)S(1)}, f32[1,257,128]{2,1,0:T(8,128)S(1)}, u32[]{:S(2)}, u32[]{:S(2)}) collective-permute-start(f32[1,257,128]{2,1,0:T(8,128)S(1)} %add.123), channel_id=1, source_target_pairs={{0,1},{1,0},{2,3},{3,2},{4,5},{5,4},{6,7},{7,6},{8,9},{9,8},{10,11... | collective-permute-start | bytes 394760 | tf_op jit(solution)/shard_map/ppermute | solution.py:53
  151.9 1.1 fusion
  153.0 1.9 %collective-permute-done.19 = f32[1,257,128]{2,1,0:T(8,128)S(1)} collective-permute-done((f32[1,257,128]{2,1,0:T(8,128)S(1)}, f32[1,257,128]{2,1,0:T(8,128)S(1)}, u32[]{:S(2)}, u32[]{:S(2)}) %collective-permute-start.19) | collective-permute-done | bytes 131616 | tf_op jit(solution)/shard_map/ppermute | solution.py:53
  154.9 0.1 copy.45
  155.0 0.1 copy.33
  155.1 0.1 bitcast_select_fusion
  155.3 0.1 select_reduce_fusion
  155.4 0.9 multiply_convert_fusion
  156.4 0.2 copy.35
  156.6 1.1 copy.39
  (41 shorter events, 0.7 us)
Async XLA Ops:
  0.6 1.4 copy-start
  2.4 9.2 %collective-permute-start = (f32[2,192,128]{2,1,0:T(8,128)S(1)}, f32[2,192,128]{2,1,0:T(8,128)S(1)}, u32[]{:S(2)}, u32[]{:S(2)}) collective-permute-start(f32[2,192,128]{2,1,0:T(8,128)S(1)} %constant_dynamic-slice_fusion.3), channel_id=1, source_target_pairs={{0,1},{1,0},{2,3},{3,2},{4,5},{5,4},{6,7},{7,6},{8,9},{9,8},{10,11... | collective-permute-start | bytes 589832 | tf_op jit(solution)/shard_map/ppermute | solution.py:45
  11.6 14.4 %collective-permute-start.1 = (f32[2,192,128]{2,1,0:T(8,128)S(1)}, f32[2,192,128]{2,1,0:T(8,128)S(1)}, u32[]{:S(2)}, u32[]{:S(2)}) collective-permute-start(f32[2,192,128]{2,1,0:T(8,128)S(1)} %dynamic-slice_add_fusion), channel_id=1, source_target_pairs={{0,4},{1,5},{2,6},{3,7},{4,0},{5,1},{6,2},{7,3},{8,12},{9,13},{10,... | collective-permute-start | bytes 589832 | tf_op jit(solution)/shard_map/ppermute | solution.py:34
  26.1 16.4 %collective-permute-start.2 = (f32[2,192,128]{2,1,0:T(8,128)S(1)}, f32[2,192,128]{2,1,0:T(8,128)S(1)}, u32[]{:S(2)}, u32[]{:S(2)}) collective-permute-start(f32[2,192,128]{2,1,0:T(8,128)S(1)} %add.99), channel_id=1, source_target_pairs={{0,2},{1,3},{2,0},{3,1},{4,6},{5,7},{6,4},{7,5},{8,10},{9,11},{10,... | collective-permute-start | bytes 589832 | tf_op jit(solution)/shard_map/ppermute | solution.py:34
  42.5 6.6 %collective-permute-start.6 = (bf16[2,192,128]{2,1,0:T(8,128)(2,1)S(1)}, bf16[2,192,128]{2,1,0:T(8,128)(2,1)S(1)}, u32[]{:S(2)}, u32[]{:S(2)}) collective-permute-start(bf16[2,192,128]{2,1,0:T(8,128)(2,1)S(1)} %get-tuple-element.14), channel_id=1, source_target_pairs={{0,1},{1,0},{2,3},{3,2},{4,5},{5,4},{6,7},{7,6},{8,9},{9,8},{10,11... | collective-permute-start | bytes 294920 | tf_op jit(solution)/shard_map/ppermute | solution.py:53
  49.5 3.5 %collective-permute-start.7 = (f32[1,320,256]{2,1,0:T(8,128)S(1)}, f32[1,320,256]{2,1,0:T(8,128)S(1)}, u32[]{:S(2)}, u32[]{:S(2)}) collective-permute-start(f32[1,320,256]{2,1,0:T(8,128)S(1)} %dynamic-slice_bitcast_fusion), channel_id=1, source_target_pairs={{0,8},{8,0},{16,24},{24,16},{32,40},{40,32},{48,56},{56,48},{64,72... | collective-permute-start | bytes 983048 | tf_op jit(solution)/shard_map/ppermute | solution.py:45
  53.1 8.1 %collective-permute-start.8 = (f32[1,320,128]{2,1,0:T(8,128)S(1)}, f32[1,320,128]{2,1,0:T(8,128)S(1)}, u32[]{:S(2)}, u32[]{:S(2)}) collective-permute-start(f32[1,320,128]{2,1,0:T(8,128)S(1)} %constant_dynamic-slice_fusion.2), channel_id=1, source_target_pairs={{0,16},{8,24},{16,0},{24,8},{32,48},{40,56},{48,32},{56,40},{64,80... | collective-permute-start | bytes 491528 | tf_op jit(solution)/shard_map/ppermute | solution.py:45
  61.3 6.3 %collective-permute-start.9 = (f32[1,160,128]{2,1,0:T(8,128)S(1)}, f32[1,160,128]{2,1,0:T(8,128)S(1)}, u32[]{:S(2)}, u32[]{:S(2)}) collective-permute-start(f32[1,160,128]{2,1,0:T(8,128)S(1)} %constant_dynamic-slice_fusion.1), channel_id=1, source_target_pairs={{0,64},{8,72},{16,80},{24,88},{32,96},{40,104},{48,112},{56,120},{... | collective-permute-start | bytes 245768 | tf_op jit(solution)/shard_map/ppermute | solution.py:45
  67.6 7.8 %collective-permute-start.10 = (f32[1,160,128]{2,1,0:T(8,128)S(1)}, f32[1,160,128]{2,1,0:T(8,128)S(1)}, u32[]{:S(2)}, u32[]{:S(2)}) collective-permute-start(f32[1,160,128]{2,1,0:T(8,128)S(1)} %dynamic-slice_add_fusion.3), channel_id=1, source_target_pairs={{0,32},{8,40},{16,48},{24,56},{32,0},{40,8},{48,16},{56,24},{64,96... | collective-permute-start | bytes 245768 | tf_op jit(solution)/shard_map/ppermute | solution.py:34
  75.5 8.2 %collective-permute-start.11 = (f32[1,160,128]{2,1,0:T(8,128)S(1)}, f32[1,160,128]{2,1,0:T(8,128)S(1)}, u32[]{:S(2)}, u32[]{:S(2)}) collective-permute-start(f32[1,160,128]{2,1,0:T(8,128)S(1)} %add.116), channel_id=1, source_target_pairs={{0,128},{8,136},{16,144},{24,152},{32,160},{40,168},{48,176},{56,1... | collective-permute-start | bytes 245768 | tf_op jit(solution)/shard_map/ppermute | solution.py:34
  83.7 11.2 %collective-permute-start.12 = (f32[1,160,128]{2,1,0:T(8,128)S(1)}, f32[1,160,128]{2,1,0:T(8,128)S(1)}, u32[]{:S(2)}, u32[]{:S(2)}) collective-permute-start(f32[1,160,128]{2,1,0:T(8,128)S(1)} %add.117), channel_id=1, source_target_pairs={{0,256},{8,264},{16,272},{24,280},{32,288},{40,296},{48,304},{56,3... | collective-permute-start | bytes 245768 | tf_op jit(solution)/shard_map/ppermute | solution.py:34
  94.8 2.4 %copy-start.2 = (f32[2,192,32]{1,2,0:T(8,128)S(1)}, f32[2,192,32]{1,2,0:T(8,128)}, u32[]{:S(2)}) copy-start(f32[2,192,32]{1,2,0:T(8,128)} %param.8) | copy-start | bytes 147460
  94.8 6.5 %collective-permute-start.13 = (f32[1,160,128]{2,1,0:T(8,128)S(1)}, f32[1,160,128]{2,1,0:T(8,128)S(1)}, u32[]{:S(2)}, u32[]{:S(2)}) collective-permute-start(f32[1,160,128]{2,1,0:T(8,128)S(1)} %add.118), channel_id=1, source_target_pairs={{0,64},{8,72},{16,80},{24,88},{32,96},{40,104},{48,112},{56,120},{... | collective-permute-start | bytes 245768 | tf_op jit(solution)/shard_map/ppermute | solution.py:53
  97.2 0.8 copy-start.3
  101.3 10.6 %collective-permute-start.14 = (f32[1,320,128]{2,1,0:T(8,128)S(1)}, f32[1,320,128]{2,1,0:T(8,128)S(1)}, u32[]{:S(2)}, u32[]{:S(2)}) collective-permute-start(f32[1,320,128]{2,1,0:T(8,128)S(1)} %pad_maximum_fusion.5), channel_id=1, source_target_pairs={{0,16},{8,24},{16,0},{24,8},{32,48},{40,56},{48,32},{56,40},{64,80... | collective-permute-start | bytes 491528 | tf_op jit(solution)/shard_map/ppermute | solution.py:53
  104.9 10.4 %collective-permute-start.3 = (bf16[2,192,32]{2,1,0:T(8,128)(2,1)S(1)}, bf16[2,192,32]{2,1,0:T(8,128)(2,1)S(1)}, u32[]{:S(2)}, u32[]{:S(2)}) collective-permute-start(bf16[2,192,32]{2,1,0:T(8,128)(2,1)S(1)} %get-tuple-element.16), channel_id=1, source_target_pairs={{0,4},{1,5},{2,6},{3,7},{4,0},{5,1},{6,2},{7,3},{8,12},{9,13},{10,... | collective-permute-start | bytes 73736 | tf_op jit(solution)/shard_map/ppermute | solution.py:53
  112.1 5.4 %collective-permute-start.15 = (f32[1,320,256]{2,1,0:T(8,128)S(1)}, f32[1,320,256]{2,1,0:T(8,128)S(1)}, u32[]{:S(2)}, u32[]{:S(2)}) collective-permute-start(f32[1,320,256]{2,1,0:T(8,128)S(1)} %pad_maximum_fusion.3), channel_id=1, source_target_pairs={{0,8},{8,0},{16,24},{24,16},{32,40},{40,32},{48,56},{56,48},{64,72... | collective-permute-start | bytes 983048 | tf_op jit(solution)/shard_map/ppermute | solution.py:53
  115.4 8.4 %collective-permute-start.4 = (bf16[2,192,64]{2,1,0:T(8,128)(2,1)S(1)}, bf16[2,192,64]{2,1,0:T(8,128)(2,1)S(1)}, u32[]{:S(2)}, u32[]{:S(2)}) collective-permute-start(bf16[2,192,64]{2,1,0:T(8,128)(2,1)S(1)} %pad_maximum_fusion.6), channel_id=1, source_target_pairs={{0,2},{1,3},{2,0},{3,1},{4,6},{5,7},{6,4},{7,5},{8,10},{9,11},{10,... | collective-permute-start | bytes 147464 | tf_op jit(solution)/shard_map/ppermute | solution.py:53
  119.6 7.3 %collective-permute-start.16 = (f32[1,257,128]{2,1,0:T(8,128)S(1)}, f32[1,257,128]{2,1,0:T(8,128)S(1)}, u32[]{:S(2)}, u32[]{:S(2)}) collective-permute-start(f32[1,257,128]{2,1,0:T(8,128)S(1)} %constant_dynamic-slice_fusion), channel_id=1, source_target_pairs={{0,1},{1,0},{2,3},{3,2},{4,5},{5,4},{6,7},{7,6},{8,9},{9,8},{10,11... | collective-permute-start | bytes 394760 | tf_op jit(solution)/shard_map/ppermute | solution.py:45
  126.9 9.7 %collective-permute-start.17 = (f32[1,257,128]{2,1,0:T(8,128)S(1)}, f32[1,257,128]{2,1,0:T(8,128)S(1)}, u32[]{:S(2)}, u32[]{:S(2)}) collective-permute-start(f32[1,257,128]{2,1,0:T(8,128)S(1)} %dynamic-slice_add_fusion.2), channel_id=1, source_target_pairs={{0,2},{1,3},{2,0},{3,1},{4,6},{5,7},{6,4},{7,5},{8,10},{9,11},{10,... | collective-permute-start | bytes 394760 | tf_op jit(solution)/shard_map/ppermute | solution.py:34
  131.3 11.0 %collective-permute-start.5 = (bf16[2,192,128]{2,1,0:T(8,128)(2,1)S(1)}, bf16[2,192,128]{2,1,0:T(8,128)(2,1)S(1)}, u32[]{:S(2)}, u32[]{:S(2)}) collective-permute-start(bf16[2,192,128]{2,1,0:T(8,128)(2,1)S(1)} %pad_maximum_fusion.7), channel_id=1, source_target_pairs={{0,1},{1,0},{2,3},{3,2},{4,5},{5,4},{6,7},{7,6},{8,9},{9,8},{10,11... | collective-permute-start | bytes 294920 | tf_op jit(solution)/shard_map/ppermute | solution.py:53
  135.0 16.9 %copy-start.1 = (f32[2,192,320]{2,1,0:T(8,128)S(1)}, f32[2,192,320]{2,1,0:T(8,128)}, u32[]{:S(2)}) copy-start(f32[2,192,320]{2,1,0:T(8,128)} %param.6) | copy-start | bytes 1474564
  136.6 10.8 %collective-permute-start.18 = (f32[1,257,128]{2,1,0:T(8,128)S(1)}, f32[1,257,128]{2,1,0:T(8,128)S(1)}, u32[]{:S(2)}, u32[]{:S(2)}) collective-permute-start(f32[1,257,128]{2,1,0:T(8,128)S(1)} %add.122), channel_id=1, source_target_pairs={{0,4},{1,5},{2,6},{3,7},{4,0},{5,1},{6,2},{7,3},{8,12},{9,13},{10,... | collective-permute-start | bytes 394760 | tf_op jit(solution)/shard_map/ppermute | solution.py:34
  147.4 7.5 %collective-permute-start.19 = (f32[1,257,128]{2,1,0:T(8,128)S(1)}, f32[1,257,128]{2,1,0:T(8,128)S(1)}, u32[]{:S(2)}, u32[]{:S(2)}) collective-permute-start(f32[1,257,128]{2,1,0:T(8,128)S(1)} %add.123), channel_id=1, source_target_pairs={{0,1},{1,0},{2,3},{3,2},{4,5},{5,4},{6,7},{7,6},{8,9},{9,8},{10,11... | collective-permute-start | bytes 394760 | tf_op jit(solution)/shard_map/ppermute | solution.py:53

commit v8 on v7

--- a/solution.py
+++ b/solution.py
@@ -116,21 +116,21 @@
     stages = [(0, 0), (1, 2), (3, 1)]
     chunk = halving_scatter(image_part, "fsdp", fsdp, stages)
     chunk = butterfly_sum(chunk, "fsdp", fsdp, [b for b in range(fsdp.bit_length() - 1) if b not in (0, 1, 3)])
-    image = doubling_gather(chunk, "fsdp", fsdp, stages)
+    image = doubling_gather(chunk, "fsdp", fsdp, stages[1:])
 
     update = jnp.einsum("mfr,dmr->mfd", normal_full, basis_order, preferred_element_type=jnp.float32)
     weight_next = weights - LEARNING_RATE * GALORE_SCALE * update
 
-    packed = halving_scatter(pack_gram(jnp.einsum("mdr,mds->mrs", image, image, precision=highest)), "tp", tp, [(0, 0)])
-    packed = butterfly_sum(packed, "tp", tp, range(1, len(tp_bits)))
-    gram = unpack_gram(doubling_gather(packed, "tp", tp, [(0, 0)]))
+    packed = pack_gram(jnp.einsum("mdr,mds->mrs", image, image, precision=highest))
+    gram = unpack_gram(butterfly_sum(packed, "tp", tp))
     diagonal = lax.broadcasted_iota(jnp.int32, gram.shape, 1) == lax.broadcasted_iota(jnp.int32, gram.shape, 2)
     total = jnp.sum(jnp.where(diagonal, gram, 0.0), axis=(1, 2)) + EPSILON_NORM
     factor = jnp.sqrt(rank_width / total)
     scaled = image * factor[:, None, None]
     cross = gram * (factor * factor)[:, None, None]
     shaped = 1.5 * scaled - 0.5 * jnp.einsum("mdr,mrs->mds", scaled, cross, precision=highest)
-    basis_next = reverse_blocks((jnp.sqrt(D / rank_width) * shaped).astype(jnp.bfloat16), len(tp_bits), width)
+    basis_own = (jnp.sqrt(D / rank_width) * shaped).astype(jnp.bfloat16)
+    basis_next = reverse_blocks(doubling_gather(basis_own, "fsdp", fsdp, stages[:1]), len(tp_bits), width)
     return (weight_next, first_next, second_next, jnp.transpose(basis_next, (1, 0, 2)))
 
 

time: 158 us -> 155 us (0.981)
  the two profiles are of different devices: /device:TPU:32 before, /device:TPU:1 now
where the time goes in v8:
time: 155 us; the launch traced here: 153 us
  starting transfers between devices  103 us (66%)
  waiting for transfers between devices  37.7 us (24%)
  local copies, waits for them, and re-layouts  5.74 us (4%)
  matrix products  3 us (2%)
  other arithmetic  1.96 us (1%)
  between operations  1.95 us (1%)
    ppermute x8, starting transfers between devices, butterfly_sum(): value = value + lax.ppermute(value, axis, partner_perm(size, bit))  51.6 us
    ppermute x7, starting transfers between devices, doubling_gather(): other = lax.ppermute(value, axis, partner_perm(size, bit))  37 us
    ppermute x8, waiting for transfers between devices, butterfly_sum(): value = value + lax.ppermute(value, axis, partner_perm(size, bit))  22.4 us
    ppermute x4, starting transfers between devices, halving_scatter(): value = keep + lax.ppermute(send, axis, partner_perm(size, bit))  14.5 us
    ppermute x4, waiting for transfers between devices, halving_scatter(): value = keep + lax.ppermute(send, axis, partner_perm(size, bit))  10.3 us
    unnamed x17, local copies, waits for them, and re-layouts  5.12 us
    ppermute x7, waiting for transfers between devices, doubling_gather(): other = lax.ppermute(value, axis, partner_perm(size, bit))  5.01 us
  transfers between devices with their start and end apart: 19, of which 14 were waited for; matrix products, arithmetic and copies ran while one was open for 3% of the time, Pallas kernels for 0%

profile of v8, /device:TPU:1, one launch (start us, length us, event | category | flops | bytes accessed | tf_op | source)
XLA Modules:
  0.0 153.4 jit_solution(16761105026893768748)
XLA Ops:
  0.6 0.0 copy-start
  0.7 1.3 copy.22
  2.0 0.1 copy.23
  2.1 0.3 fusion.35
  2.4 4.8 %collective-permute-start = (f32[2,192,128]{2,1,0:T(8,128)S(1)}, f32[2,192,128]{2,1,0:T(8,128)S(1)}, u32[]{:S(2)}, u32[]{:S(2)}) collective-permute-start(f32[2,192,128]{2,1,0:T(8,128)S(1)} %constant_dynamic-slice_fusion.2), channel_id=1, source_target_pairs={{0,1},{1,0},{2,3},{3,2},{4,5},{5,4},{6,7},{7,6},{8,9},{9,8},{10,11... | collective-permute-start | bytes 589832 | tf_op jit(solution)/shard_map/ppermute | solution.py:45
  7.3 3.0 %collective-permute-done = f32[2,192,128]{2,1,0:T(8,128)S(1)} collective-permute-done((f32[2,192,128]{2,1,0:T(8,128)S(1)}, f32[2,192,128]{2,1,0:T(8,128)S(1)}, u32[]{:S(2)}, u32[]{:S(2)}) %collective-permute-start) | collective-permute-done | bytes 196640 | tf_op jit(solution)/shard_map/ppermute | solution.py:45
  10.3 11.3 %collective-permute-start.1 = (f32[2,192,128]{2,1,0:T(8,128)S(1)}, f32[2,192,128]{2,1,0:T(8,128)S(1)}, u32[]{:S(2)}, u32[]{:S(2)}) collective-permute-start(f32[2,192,128]{2,1,0:T(8,128)S(1)} %dynamic-slice_add_fusion), channel_id=1, source_target_pairs={{0,4},{1,5},{2,6},{3,7},{4,0},{5,1},{6,2},{7,3},{8,12},{9,13},{10,... | collective-permute-start | bytes 589832 | tf_op jit(solution)/shard_map/ppermute | solution.py:34
  21.6 3.1 %collective-permute-done.1 = f32[2,192,128]{2,1,0:T(8,128)S(1)} collective-permute-done((f32[2,192,128]{2,1,0:T(8,128)S(1)}, f32[2,192,128]{2,1,0:T(8,128)S(1)}, u32[]{:S(2)}, u32[]{:S(2)}) %collective-permute-start.1) | collective-permute-done | bytes 196640 | tf_op jit(solution)/shard_map/ppermute | solution.py:34
  24.8 10.4 %collective-permute-start.2 = (f32[2,192,128]{2,1,0:T(8,128)S(1)}, f32[2,192,128]{2,1,0:T(8,128)S(1)}, u32[]{:S(2)}, u32[]{:S(2)}) collective-permute-start(f32[2,192,128]{2,1,0:T(8,128)S(1)} %add.86), channel_id=1, source_target_pairs={{0,2},{1,3},{2,0},{3,1},{4,6},{5,7},{6,4},{7,5},{8,10},{9,11},{10,... | collective-permute-start | bytes 589832 | tf_op jit(solution)/shard_map/ppermute | solution.py:34
  35.2 8.2 %collective-permute-done.2 = f32[2,192,128]{2,1,0:T(8,128)S(1)} collective-permute-done((f32[2,192,128]{2,1,0:T(8,128)S(1)}, f32[2,192,128]{2,1,0:T(8,128)S(1)}, u32[]{:S(2)}, u32[]{:S(2)}) %collective-permute-start.2) | collective-permute-done | bytes 196640 | tf_op jit(solution)/shard_map/ppermute | solution.py:34
  43.5 1.9 %collective-permute-start.6 = (bf16[2,192,128]{2,1,0:T(8,128)(2,1)S(1)}, bf16[2,192,128]{2,1,0:T(8,128)(2,1)S(1)}, u32[]{:S(2)}, u32[]{:S(2)}) collective-permute-start(bf16[2,192,128]{2,1,0:T(8,128)(2,1)S(1)} %get-tuple-element.12), channel_id=1, source_target_pairs={{0,1},{1,0},{2,3},{3,2},{4,5},{5,4},{6,7},{7,6},{8,9},{9,8},{10,11... | collective-permute-start | bytes 294920 | tf_op jit(solution)/shard_map/ppermute | solution.py:53
  45.4 3.8 %collective-permute-done.6 = bf16[2,192,128]{2,1,0:T(8,128)(2,1)S(1)} collective-permute-done((bf16[2,192,128]{2,1,0:T(8,128)(2,1)S(1)}, bf16[2,192,128]{2,1,0:T(8,128)(2,1)S(1)}, u32[]{:S(2)}, u32[]{:S(2)}) %collective-permute-start.6) | collective-permute-done | bytes 98336 | tf_op jit(solution)/shard_map/ppermute | solution.py:53
  49.3 0.3 fusion.14
  49.6 3.2 %collective-permute-start.7 = (f32[1,320,256]{2,1,0:T(8,128)S(1)}, f32[1,320,256]{2,1,0:T(8,128)S(1)}, u32[]{:S(2)}, u32[]{:S(2)}) collective-permute-start(f32[1,320,256]{2,1,0:T(8,128)S(1)} %dynamic-slice_bitcast_fusion), channel_id=1, source_target_pairs={{0,8},{8,0},{16,24},{24,16},{32,40},{40,32},{48,56},{56,48},{64,72... | collective-permute-start | bytes 983048 | tf_op jit(solution)/shard_map/ppermute | solution.py:45
  52.9 1.2 collective-permute-done.7
  54.2 3.2 %collective-permute-start.8 = (f32[1,320,128]{2,1,0:T(8,128)S(1)}, f32[1,320,128]{2,1,0:T(8,128)S(1)}, u32[]{:S(2)}, u32[]{:S(2)}) collective-permute-start(f32[1,320,128]{2,1,0:T(8,128)S(1)} %constant_dynamic-slice_fusion.1), channel_id=1, source_target_pairs={{0,16},{8,24},{16,0},{24,8},{32,48},{40,56},{48,32},{56,40},{64,80... | collective-permute-start | bytes 491528 | tf_op jit(solution)/shard_map/ppermute | solution.py:45
  57.3 4.1 %collective-permute-done.8 = f32[1,320,128]{2,1,0:T(8,128)S(1)} collective-permute-done((f32[1,320,128]{2,1,0:T(8,128)S(1)}, f32[1,320,128]{2,1,0:T(8,128)S(1)}, u32[]{:S(2)}, u32[]{:S(2)}) %collective-permute-start.8) | collective-permute-done | bytes 163872 | tf_op jit(solution)/shard_map/ppermute | solution.py:45
  61.5 3.2 %collective-permute-start.9 = (f32[1,160,128]{2,1,0:T(8,128)S(1)}, f32[1,160,128]{2,1,0:T(8,128)S(1)}, u32[]{:S(2)}, u32[]{:S(2)}) collective-permute-start(f32[1,160,128]{2,1,0:T(8,128)S(1)} %constant_dynamic-slice_fusion), channel_id=1, source_target_pairs={{0,64},{8,72},{16,80},{24,88},{32,96},{40,104},{48,112},{56,120},{... | collective-permute-start | bytes 245768 | tf_op jit(solution)/shard_map/ppermute | solution.py:45
  64.7 1.9 %collective-permute-done.9 = f32[1,160,128]{2,1,0:T(8,128)S(1)} collective-permute-done((f32[1,160,128]{2,1,0:T(8,128)S(1)}, f32[1,160,128]{2,1,0:T(8,128)S(1)}, u32[]{:S(2)}, u32[]{:S(2)}) %collective-permute-start.9) | collective-permute-done | bytes 81952 | tf_op jit(solution)/shard_map/ppermute | solution.py:45
  66.7 4.7 %collective-permute-start.10 = (f32[1,160,128]{2,1,0:T(8,128)S(1)}, f32[1,160,128]{2,1,0:T(8,128)S(1)}, u32[]{:S(2)}, u32[]{:S(2)}) collective-permute-start(f32[1,160,128]{2,1,0:T(8,128)S(1)} %dynamic-slice_add_fusion.2), channel_id=1, source_target_pairs={{0,32},{8,40},{16,48},{24,56},{32,0},{40,8},{48,16},{56,24},{64,96... | collective-permute-start | bytes 245768 | tf_op jit(solution)/shard_map/ppermute | solution.py:34
  71.4 2.0 %collective-permute-done.10 = f32[1,160,128]{2,1,0:T(8,128)S(1)} collective-permute-done((f32[1,160,128]{2,1,0:T(8,128)S(1)}, f32[1,160,128]{2,1,0:T(8,128)S(1)}, u32[]{:S(2)}, u32[]{:S(2)}) %collective-permute-start.10) | collective-permute-done | bytes 81952 | tf_op jit(solution)/shard_map/ppermute | solution.py:34
  73.4 4.3 %collective-permute-start.11 = (f32[1,160,128]{2,1,0:T(8,128)S(1)}, f32[1,160,128]{2,1,0:T(8,128)S(1)}, u32[]{:S(2)}, u32[]{:S(2)}) collective-permute-start(f32[1,160,128]{2,1,0:T(8,128)S(1)} %add.103), channel_id=1, source_target_pairs={{0,128},{8,136},{16,144},{24,152},{32,160},{40,168},{48,176},{56,1... | collective-permute-start | bytes 245768 | tf_op jit(solution)/shard_map/ppermute | solution.py:34
  77.7 1.8 %collective-permute-done.11 = f32[1,160,128]{2,1,0:T(8,128)S(1)} collective-permute-done((f32[1,160,128]{2,1,0:T(8,128)S(1)}, f32[1,160,128]{2,1,0:T(8,128)S(1)}, u32[]{:S(2)}, u32[]{:S(2)}) %collective-permute-start.11) | collective-permute-done | bytes 81952 | tf_op jit(solution)/shard_map/ppermute | solution.py:34
  79.5 8.5 %collective-permute-start.12 = (f32[1,160,128]{2,1,0:T(8,128)S(1)}, f32[1,160,128]{2,1,0:T(8,128)S(1)}, u32[]{:S(2)}, u32[]{:S(2)}) collective-permute-start(f32[1,160,128]{2,1,0:T(8,128)S(1)} %add.104), channel_id=1, source_target_pairs={{0,256},{8,264},{16,272},{24,280},{32,288},{40,296},{48,304},{56,3... | collective-permute-start | bytes 245768 | tf_op jit(solution)/shard_map/ppermute | solution.py:34
  88.0 0.0 copy-start.3
  88.0 0.1 copy.21
  88.2 0.7 copy-done.3
  88.9 0.1 copy.25
  89.0 0.9 collective-permute-done.12
  89.9 2.8 %collective-permute-start.13 = (f32[1,160,128]{2,1,0:T(8,128)S(1)}, f32[1,160,128]{2,1,0:T(8,128)S(1)}, u32[]{:S(2)}, u32[]{:S(2)}) collective-permute-start(f32[1,160,128]{2,1,0:T(8,128)S(1)} %add.105), channel_id=1, source_target_pairs={{0,64},{8,72},{16,80},{24,88},{32,96},{40,104},{48,112},{56,120},{... | collective-permute-start | bytes 245768 | tf_op jit(solution)/shard_map/ppermute | solution.py:53
  92.7 0.2 divide_convert_fusion
  93.0 7.0 %collective-permute-start.3 = (bf16[2,192,32]{2,1,0:T(8,128)(2,1)S(1)}, bf16[2,192,32]{2,1,0:T(8,128)(2,1)S(1)}, u32[]{:S(2)}, u32[]{:S(2)}) collective-permute-start(bf16[2,192,32]{2,1,0:T(8,128)(2,1)S(1)} %get-tuple-element.14), channel_id=1, source_target_pairs={{0,4},{1,5},{2,6},{3,7},{4,0},{5,1},{6,2},{7,3},{8,12},{9,13},{10,... | collective-permute-start | bytes 73736 | tf_op jit(solution)/shard_map/ppermute | solution.py:53
  100.0 3.0 %collective-permute-start.14 = (f32[1,320,128]{2,1,0:T(8,128)S(1)}, f32[1,320,128]{2,1,0:T(8,128)S(1)}, u32[]{:S(2)}, u32[]{:S(2)}) collective-permute-start(f32[1,320,128]{2,1,0:T(8,128)S(1)} %pad_maximum_fusion.1), channel_id=1, source_target_pairs={{0,16},{8,24},{16,0},{24,8},{32,48},{40,56},{48,32},{56,40},{64,80... | collective-permute-start | bytes 491528 | tf_op jit(solution)/shard_map/ppermute | solution.py:53
  103.1 0.1 pad_maximum_fusion.3
  103.2 2.3 %collective-permute-start.4 = (bf16[2,192,64]{2,1,0:T(8,128)(2,1)S(1)}, bf16[2,192,64]{2,1,0:T(8,128)(2,1)S(1)}, u32[]{:S(2)}, u32[]{:S(2)}) collective-permute-start(bf16[2,192,64]{2,1,0:T(8,128)(2,1)S(1)} %pad_maximum_fusion.3), channel_id=1, source_target_pairs={{0,2},{1,3},{2,0},{3,1},{4,6},{5,7},{6,4},{7,5},{8,10},{9,11},{10,... | collective-permute-start | bytes 147464 | tf_op jit(solution)/shard_map/ppermute | solution.py:53
  105.4 0.6 collective-permute-done.14
  106.1 0.9 convolution_bitcast_fusion
  107.0 0.1 copy.40
  107.1 0.1 copy.41
  107.2 0.1 fusion.25
  107.3 0.1 copy.29
  107.4 3.0 %collective-permute-start.15 = (f32[1,257,128]{2,1,0:T(8,128)S(1)}, f32[1,257,128]{2,1,0:T(8,128)S(1)}, u32[]{:S(2)}, u32[]{:S(2)}) collective-permute-start(f32[1,257,128]{2,1,0:T(8,128)S(1)} %pad_maximum_fusion.2), channel_id=1, source_target_pairs={{0,1},{1,0},{2,3},{3,2},{4,5},{5,4},{6,7},{7,6},{8,9},{9,8},{10,11... | collective-permute-start | bytes 394760 | tf_op jit(solution)/shard_map/ppermute | solution.py:34
  110.5 0.5 collective-permute-done.4
  111.0 0.1 broadcast_select_fusion.5
  111.2 2.0 %collective-permute-done.15 = f32[1,257,128]{2,1,0:T(8,128)S(1)} collective-permute-done((f32[1,257,128]{2,1,0:T(8,128)S(1)}, f32[1,257,128]{2,1,0:T(8,128)S(1)}, u32[]{:S(2)}, u32[]{:S(2)}) %collective-permute-start.15) | collective-permute-done | bytes 131616 | tf_op jit(solution)/shard_map/ppermute | solution.py:34
  113.2 3.3 %collective-permute-start.16 = (f32[1,257,128]{2,1,0:T(8,128)S(1)}, f32[1,257,128]{2,1,0:T(8,128)S(1)}, u32[]{:S(2)}, u32[]{:S(2)}) collective-permute-start(f32[1,257,128]{2,1,0:T(8,128)S(1)} %fusion.30), channel_id=1, source_target_pairs={{0,2},{1,3},{2,0},{3,1},{4,6},{5,7},{6,4},{7,5},{8,10},{9,11},{10,... | collective-permute-start | bytes 394760 | tf_op jit(solution)/shard_map/ppermute | solution.py:34
  116.5 0.1 pad_maximum_fusion.4
  116.6 2.8 %collective-permute-start.5 = (bf16[2,192,128]{2,1,0:T(8,128)(2,1)S(1)}, bf16[2,192,128]{2,1,0:T(8,128)(2,1)S(1)}, u32[]{:S(2)}, u32[]{:S(2)}) collective-permute-start(bf16[2,192,128]{2,1,0:T(8,128)(2,1)S(1)} %pad_maximum_fusion.4), channel_id=1, source_target_pairs={{0,1},{1,0},{2,3},{3,2},{4,5},{5,4},{6,7},{7,6},{8,9},{9,8},{10,11... | collective-permute-start | bytes 294920 | tf_op jit(solution)/shard_map/ppermute | solution.py:53
  119.4 0.7 copy.35
  120.2 0.7 copy.36
  120.9 6.1 %collective-permute-start.17 = (f32[1,257,128]{2,1,0:T(8,128)S(1)}, f32[1,257,128]{2,1,0:T(8,128)S(1)}, u32[]{:S(2)}, u32[]{:S(2)}) collective-permute-start(f32[1,257,128]{2,1,0:T(8,128)S(1)} %add.107), channel_id=1, source_target_pairs={{0,4},{1,5},{2,6},{3,7},{4,0},{5,1},{6,2},{7,3},{8,12},{9,13},{10,... | collective-permute-start | bytes 394760 | tf_op jit(solution)/shard_map/ppermute | solution.py:34
  127.1 0.1 broadcast_select_fusion.9
  127.2 4.2 %collective-permute-done.17 = f32[1,257,128]{2,1,0:T(8,128)S(1)} collective-permute-done((f32[1,257,128]{2,1,0:T(8,128)S(1)}, f32[1,257,128]{2,1,0:T(8,128)S(1)}, u32[]{:S(2)}, u32[]{:S(2)}) %collective-permute-start.17) | collective-permute-done | bytes 131616 | tf_op jit(solution)/shard_map/ppermute | solution.py:34
  131.5 0.1 copy.42
  131.6 0.1 copy.32
  131.7 0.1 bitcast_select_fusion
  131.8 0.6 fusion.7
  133.2 0.0 copy-start.1
  133.2 0.5 fusion.4
  133.7 17.2 %collective-permute-start.18 = (bf16[1,320,256]{2,1,0:T(8,128)(2,1)S(1)}, bf16[1,320,256]{2,1,0:T(8,128)(2,1)S(1)}, u32[]{:S(2)}, u32[]{:S(2)}) collective-permute-start(bf16[1,320,256]{2,1,0:T(8,128)(2,1)S(1)} %fusion.4), channel_id=1, source_target_pairs={{0,8},{8,0},{16,24},{24,16},{32,40},{40,32},{48,56},{56,48},{64,72... | collective-permute-start | bytes 491528 | tf_op jit(solution)/shard_map/ppermute | solution.py:53
  150.9 1.1 fusion
  152.1 0.2 copy.33
  152.3 0.1 copy.34
  152.3 1.1 copy.37
  (37 shorter events, 0.6 us)
Async XLA Ops:
  0.6 1.4 copy-start
  2.4 7.9 %collective-permute-start = (f32[2,192,128]{2,1,0:T(8,128)S(1)}, f32[2,192,128]{2,1,0:T(8,128)S(1)}, u32[]{:S(2)}, u32[]{:S(2)}) collective-permute-start(f32[2,192,128]{2,1,0:T(8,128)S(1)} %constant_dynamic-slice_fusion.2), channel_id=1, source_target_pairs={{0,1},{1,0},{2,3},{3,2},{4,5},{5,4},{6,7},{7,6},{8,9},{9,8},{10,11... | collective-permute-start | bytes 589832 | tf_op jit(solution)/shard_map/ppermute | solution.py:45
  10.3 14.4 %collective-permute-start.1 = (f32[2,192,128]{2,1,0:T(8,128)S(1)}, f32[2,192,128]{2,1,0:T(8,128)S(1)}, u32[]{:S(2)}, u32[]{:S(2)}) collective-permute-start(f32[2,192,128]{2,1,0:T(8,128)S(1)} %dynamic-slice_add_fusion), channel_id=1, source_target_pairs={{0,4},{1,5},{2,6},{3,7},{4,0},{5,1},{6,2},{7,3},{8,12},{9,13},{10,... | collective-permute-start | bytes 589832 | tf_op jit(solution)/shard_map/ppermute | solution.py:34
  24.8 18.7 %collective-permute-start.2 = (f32[2,192,128]{2,1,0:T(8,128)S(1)}, f32[2,192,128]{2,1,0:T(8,128)S(1)}, u32[]{:S(2)}, u32[]{:S(2)}) collective-permute-start(f32[2,192,128]{2,1,0:T(8,128)S(1)} %add.86), channel_id=1, source_target_pairs={{0,2},{1,3},{2,0},{3,1},{4,6},{5,7},{6,4},{7,5},{8,10},{9,11},{10,... | collective-permute-start | bytes 589832 | tf_op jit(solution)/shard_map/ppermute | solution.py:34
  43.5 5.8 %collective-permute-start.6 = (bf16[2,192,128]{2,1,0:T(8,128)(2,1)S(1)}, bf16[2,192,128]{2,1,0:T(8,128)(2,1)S(1)}, u32[]{:S(2)}, u32[]{:S(2)}) collective-permute-start(bf16[2,192,128]{2,1,0:T(8,128)(2,1)S(1)} %get-tuple-element.12), channel_id=1, source_target_pairs={{0,1},{1,0},{2,3},{3,2},{4,5},{5,4},{6,7},{7,6},{8,9},{9,8},{10,11... | collective-permute-start | bytes 294920 | tf_op jit(solution)/shard_map/ppermute | solution.py:53
  49.6 4.5 %collective-permute-start.7 = (f32[1,320,256]{2,1,0:T(8,128)S(1)}, f32[1,320,256]{2,1,0:T(8,128)S(1)}, u32[]{:S(2)}, u32[]{:S(2)}) collective-permute-start(f32[1,320,256]{2,1,0:T(8,128)S(1)} %dynamic-slice_bitcast_fusion), channel_id=1, source_target_pairs={{0,8},{8,0},{16,24},{24,16},{32,40},{40,32},{48,56},{56,48},{64,72... | collective-permute-start | bytes 983048 | tf_op jit(solution)/shard_map/ppermute | solution.py:45
  54.2 7.3 %collective-permute-start.8 = (f32[1,320,128]{2,1,0:T(8,128)S(1)}, f32[1,320,128]{2,1,0:T(8,128)S(1)}, u32[]{:S(2)}, u32[]{:S(2)}) collective-permute-start(f32[1,320,128]{2,1,0:T(8,128)S(1)} %constant_dynamic-slice_fusion.1), channel_id=1, source_target_pairs={{0,16},{8,24},{16,0},{24,8},{32,48},{40,56},{48,32},{56,40},{64,80... | collective-permute-start | bytes 491528 | tf_op jit(solution)/shard_map/ppermute | solution.py:45
  61.5 5.2 %collective-permute-start.9 = (f32[1,160,128]{2,1,0:T(8,128)S(1)}, f32[1,160,128]{2,1,0:T(8,128)S(1)}, u32[]{:S(2)}, u32[]{:S(2)}) collective-permute-start(f32[1,160,128]{2,1,0:T(8,128)S(1)} %constant_dynamic-slice_fusion), channel_id=1, source_target_pairs={{0,64},{8,72},{16,80},{24,88},{32,96},{40,104},{48,112},{56,120},{... | collective-permute-start | bytes 245768 | tf_op jit(solution)/shard_map/ppermute | solution.py:45
  66.7 6.7 %collective-permute-start.10 = (f32[1,160,128]{2,1,0:T(8,128)S(1)}, f32[1,160,128]{2,1,0:T(8,128)S(1)}, u32[]{:S(2)}, u32[]{:S(2)}) collective-permute-start(f32[1,160,128]{2,1,0:T(8,128)S(1)} %dynamic-slice_add_fusion.2), channel_id=1, source_target_pairs={{0,32},{8,40},{16,48},{24,56},{32,0},{40,8},{48,16},{56,24},{64,96... | collective-permute-start | bytes 245768 | tf_op jit(solution)/shard_map/ppermute | solution.py:34
  73.4 6.1 %collective-permute-start.11 = (f32[1,160,128]{2,1,0:T(8,128)S(1)}, f32[1,160,128]{2,1,0:T(8,128)S(1)}, u32[]{:S(2)}, u32[]{:S(2)}) collective-permute-start(f32[1,160,128]{2,1,0:T(8,128)S(1)} %add.103), channel_id=1, source_target_pairs={{0,128},{8,136},{16,144},{24,152},{32,160},{40,168},{48,176},{56,1... | collective-permute-start | bytes 245768 | tf_op jit(solution)/shard_map/ppermute | solution.py:34
  79.5 8.5 %copy-start.2 = (f32[2,192,32]{1,2,0:T(8,128)S(1)}, f32[2,192,32]{1,2,0:T(8,128)}, u32[]{:S(2)}) copy-start(f32[2,192,32]{1,2,0:T(8,128)} %param.8) | copy-start | bytes 147460
  79.5 10.4 %collective-permute-start.12 = (f32[1,160,128]{2,1,0:T(8,128)S(1)}, f32[1,160,128]{2,1,0:T(8,128)S(1)}, u32[]{:S(2)}, u32[]{:S(2)}) collective-permute-start(f32[1,160,128]{2,1,0:T(8,128)S(1)} %add.104), channel_id=1, source_target_pairs={{0,256},{8,264},{16,272},{24,280},{32,288},{40,296},{48,304},{56,3... | collective-permute-start | bytes 245768 | tf_op jit(solution)/shard_map/ppermute | solution.py:34
  88.0 0.8 copy-start.3
  89.9 10.0 %collective-permute-start.13 = (f32[1,160,128]{2,1,0:T(8,128)S(1)}, f32[1,160,128]{2,1,0:T(8,128)S(1)}, u32[]{:S(2)}, u32[]{:S(2)}) collective-permute-start(f32[1,160,128]{2,1,0:T(8,128)S(1)} %add.105), channel_id=1, source_target_pairs={{0,64},{8,72},{16,80},{24,88},{32,96},{40,104},{48,112},{56,120},{... | collective-permute-start | bytes 245768 | tf_op jit(solution)/shard_map/ppermute | solution.py:53
  93.0 10.1 %collective-permute-start.3 = (bf16[2,192,32]{2,1,0:T(8,128)(2,1)S(1)}, bf16[2,192,32]{2,1,0:T(8,128)(2,1)S(1)}, u32[]{:S(2)}, u32[]{:S(2)}) collective-permute-start(bf16[2,192,32]{2,1,0:T(8,128)(2,1)S(1)} %get-tuple-element.14), channel_id=1, source_target_pairs={{0,4},{1,5},{2,6},{3,7},{4,0},{5,1},{6,2},{7,3},{8,12},{9,13},{10,... | collective-permute-start | bytes 73736 | tf_op jit(solution)/shard_map/ppermute | solution.py:53
  100.0 6.1 %collective-permute-start.14 = (f32[1,320,128]{2,1,0:T(8,128)S(1)}, f32[1,320,128]{2,1,0:T(8,128)S(1)}, u32[]{:S(2)}, u32[]{:S(2)}) collective-permute-start(f32[1,320,128]{2,1,0:T(8,128)S(1)} %pad_maximum_fusion.1), channel_id=1, source_target_pairs={{0,16},{8,24},{16,0},{24,8},{32,48},{40,56},{48,32},{56,40},{64,80... | collective-permute-start | bytes 491528 | tf_op jit(solution)/shard_map/ppermute | solution.py:53
  103.2 7.8 %collective-permute-start.4 = (bf16[2,192,64]{2,1,0:T(8,128)(2,1)S(1)}, bf16[2,192,64]{2,1,0:T(8,128)(2,1)S(1)}, u32[]{:S(2)}, u32[]{:S(2)}) collective-permute-start(bf16[2,192,64]{2,1,0:T(8,128)(2,1)S(1)} %pad_maximum_fusion.3), channel_id=1, source_target_pairs={{0,2},{1,3},{2,0},{3,1},{4,6},{5,7},{6,4},{7,5},{8,10},{9,11},{10,... | collective-permute-start | bytes 147464 | tf_op jit(solution)/shard_map/ppermute | solution.py:53
  107.4 5.8 %collective-permute-start.15 = (f32[1,257,128]{2,1,0:T(8,128)S(1)}, f32[1,257,128]{2,1,0:T(8,128)S(1)}, u32[]{:S(2)}, u32[]{:S(2)}) collective-permute-start(f32[1,257,128]{2,1,0:T(8,128)S(1)} %pad_maximum_fusion.2), channel_id=1, source_target_pairs={{0,1},{1,0},{2,3},{3,2},{4,5},{5,4},{6,7},{7,6},{8,9},{9,8},{10,11... | collective-permute-start | bytes 394760 | tf_op jit(solution)/shard_map/ppermute | solution.py:34
  113.2 7.7 %collective-permute-start.16 = (f32[1,257,128]{2,1,0:T(8,128)S(1)}, f32[1,257,128]{2,1,0:T(8,128)S(1)}, u32[]{:S(2)}, u32[]{:S(2)}) collective-permute-start(f32[1,257,128]{2,1,0:T(8,128)S(1)} %fusion.30), channel_id=1, source_target_pairs={{0,2},{1,3},{2,0},{3,1},{4,6},{5,7},{6,4},{7,5},{8,10},{9,11},{10,... | collective-permute-start | bytes 394760 | tf_op jit(solution)/shard_map/ppermute | solution.py:34
  116.6 10.4 %collective-permute-start.5 = (bf16[2,192,128]{2,1,0:T(8,128)(2,1)S(1)}, bf16[2,192,128]{2,1,0:T(8,128)(2,1)S(1)}, u32[]{:S(2)}, u32[]{:S(2)}) collective-permute-start(bf16[2,192,128]{2,1,0:T(8,128)(2,1)S(1)} %pad_maximum_fusion.4), channel_id=1, source_target_pairs={{0,1},{1,0},{2,3},{3,2},{4,5},{5,4},{6,7},{7,6},{8,9},{9,8},{10,11... | collective-permute-start | bytes 294920 | tf_op jit(solution)/shard_map/ppermute | solution.py:53
  120.9 10.5 %collective-permute-start.17 = (f32[1,257,128]{2,1,0:T(8,128)S(1)}, f32[1,257,128]{2,1,0:T(8,128)S(1)}, u32[]{:S(2)}, u32[]{:S(2)}) collective-permute-start(f32[1,257,128]{2,1,0:T(8,128)S(1)} %add.107), channel_id=1, source_target_pairs={{0,4},{1,5},{2,6},{3,7},{4,0},{5,1},{6,2},{7,3},{8,12},{9,13},{10,... | collective-permute-start | bytes 394760 | tf_op jit(solution)/shard_map/ppermute | solution.py:34
  133.2 17.7 %copy-start.1 = (f32[2,192,320]{2,1,0:T(8,128)S(1)}, f32[2,192,320]{2,1,0:T(8,128)}, u32[]{:S(2)}) copy-start(f32[2,192,320]{2,1,0:T(8,128)} %param.6) | copy-start | bytes 1474564
  133.7 18.3 %collective-permute-start.18 = (bf16[1,320,256]{2,1,0:T(8,128)(2,1)S(1)}, bf16[1,320,256]{2,1,0:T(8,128)(2,1)S(1)}, u32[]{:S(2)}, u32[]{:S(2)}) collective-permute-start(bf16[1,320,256]{2,1,0:T(8,128)(2,1)S(1)} %fusion.4), channel_id=1, source_target_pairs={{0,8},{8,0},{16,24},{24,16},{32,40},{40,32},{48,56},{56,48},{64,72... | collective-permute-start | bytes 491528 | tf_op jit(solution)/shard_map/ppermute | solution.py:53

commit v9 on v8

--- a/solution.py
+++ b/solution.py
@@ -101,16 +101,22 @@
     basis_order = reverse_blocks(basis, len(tp_bits), width)
 
     projected_part = jnp.einsum("mfd,dmr->mfr", grads, basis_order, preferred_element_type=jnp.float32)
-    half = halving_scatter(projected_part, "tp", tp, [(0, 2)])
-    half = butterfly_sum(half, "tp", tp, reversed(range(1, len(tp_bits))))
-    member = lax.axis_index("tp")
-    own_place = 0
-    for step, bit in enumerate(reversed(range(1, len(tp_bits)))):
-        own_place = own_place + (((member >> bit) & 1) << step)
-    own = lax.dynamic_slice_in_dim(half, own_place * width, width, 2)
-    first_next, second_next, normal_half = adam_share(own, first_moment, second_moment)
-    projected_half = doubling_gather(half.astype(jnp.bfloat16), "tp", tp, [(0, 2)])
-    normal_full = doubling_gather(normal_half, "tp", tp, tp_bits)
+    last = len(tp_bits) - 1
+    quarter = halving_scatter(projected_part, "tp", tp, tp_bits[:last])
+    moments = jnp.stack([first_moment, second_moment], axis=0)
+    rows = quarter.size // 128
+    message = jnp.concatenate([quarter.reshape(rows, 128), moments.reshape(-1, 128)], axis=0)
+    arrived = lax.ppermute(message, "tp", partner_perm(tp, last))
+    quarter = quarter + arrived[:rows].reshape(quarter.shape)
+    other = arrived[rows:].reshape(moments.shape)
+    mine = (lax.axis_index("tp") >> last) & 1
+    moments = jnp.concatenate([jnp.where(mine == 0, moments, other), jnp.where(mine == 0, other, moments)], axis=3)
+    first_pair, second_pair, normal_pair = adam_share(quarter, moments[0], moments[1])
+    first_next = lax.dynamic_slice_in_dim(first_pair, mine * width, width, 2)
+    second_next = lax.dynamic_slice_in_dim(second_pair, mine * width, width, 2)
+    halves = jnp.stack([quarter.astype(jnp.bfloat16), normal_pair], axis=0)
+    gathered = doubling_gather(halves, "tp", tp, [(b, 3) for b, _ in tp_bits[:last]])
+    projected_half, normal_full = gathered[0], gathered[1]
 
     image_part = jnp.einsum("mfd,mfr->mdr", grads, projected_half, preferred_element_type=jnp.float32)
     stages = [(0, 0), (1, 2), (3, 1)]

time: 155 us -> 164 us (1.058)
  waiting for transfers between devices: 37.7 us -> 61 us
  starting transfers between devices: 103 us -> 89.1 us
    ppermute x8 -> x6, starting transfers between devices: 51.6 us -> 26.6 us  [butterfly_sum(): value = value + lax.ppermute(value, axis, partner_perm(size, bit))]
    ppermute x4 -> x5, starting transfers between devices: 14.5 us -> 26.5 us  [halving_scatter(): value = keep + lax.ppermute(send, axis, partner_perm(size, bit))]
    ppermute x7 -> x5, waiting for transfers between devices: 5.01 us -> 14.8 us  [doubling_gather(): other = lax.ppermute(value, axis, partner_perm(size, bit))]
    ppermute x7 -> x5, starting transfers between devices: 37 us -> 27.6 us  [doubling_gather(): other = lax.ppermute(value, axis, partner_perm(size, bit))]
    ppermute x0 -> x1, starting transfers between devices: none -> 8.41 us  [shards(): arrived = lax.ppermute(message, 'tp', partner_perm(tp, last))]
    ppermute x4 -> x5, waiting for transfers between devices: 10.3 us -> 18.4 us  [halving_scatter(): value = keep + lax.ppermute(send, axis, partner_perm(size, bit))]
    ppermute x0 -> x1, waiting for transfers between devices: none -> 6.77 us  [shards(): arrived = lax.ppermute(message, 'tp', partner_perm(tp, last))]
    ppermute x8 -> x6, waiting for transfers between devices: 22.4 us -> 21.1 us  [butterfly_sum(): value = value + lax.ppermute(value, axis, partner_perm(size, bit))]
  transfers between devices with their start and end apart: 19 -> 17, of which waited for: 14 -> 16; matrix products, arithmetic and copies ran while one was open for 3% -> 2% of each run, Pallas kernels for 0% -> 0%
where the time goes in v9:
time: 164 us; the launch traced here: 163 us
  starting transfers between devices  89.1 us (54%)
  waiting for transfers between devices  61 us (37%)
  local copies, waits for them, and re-layouts  5.75 us (4%)
  matrix products  3.01 us (2%)
  other arithmetic  2.03 us (1%)
  between operations  2 us (1%)
    ppermute x5, starting transfers between devices, doubling_gather(): other = lax.ppermute(value, axis, partner_perm(size, bit))  27.6 us
    ppermute x6, starting transfers between devices, butterfly_sum(): value = value + lax.ppermute(value, axis, partner_perm(size, bit))  26.6 us
    ppermute x5, starting transfers between devices, halving_scatter(): value = keep + lax.ppermute(send, axis, partner_perm(size, bit))  26.5 us
    ppermute x6, waiting for transfers between devices, butterfly_sum(): value = value + lax.ppermute(value, axis, partner_perm(size, bit))  21.1 us
    ppermute x5, waiting for transfers between devices, halving_scatter(): value = keep + lax.ppermute(send, axis, partner_perm(size, bit))  18.4 us
    ppermute x5, waiting for transfers between devices, doubling_gather(): other = lax.ppermute(value, axis, partner_perm(size, bit))  14.8 us
    ppermute x1, starting transfers between devices, shards(): arrived = lax.ppermute(message, 'tp', partner_perm(tp, last))  8.41 us
    ppermute x1, waiting for transfers between devices, shards(): arrived = lax.ppermute(message, 'tp', partner_perm(tp, last))  6.77 us
  transfers between devices with their start and end apart: 17, of which 16 were waited for; matrix products, arithmetic and copies ran while one was open for 2% of the time, Pallas kernels for 0%

profile of v9, /device:TPU:1, one launch (start us, length us, event | category | flops | bytes accessed | tf_op | source)
XLA Modules:
  0.0 163.0 jit_solution(3829623392473577214)
XLA Ops:
  0.6 1.3 copy.38
  2.1 0.3 fusion.43
  2.4 4.8 %collective-permute-start = (f32[2,192,128]{2,1,0:T(8,128)S(1)}, f32[2,192,128]{2,1,0:T(8,128)S(1)}, u32[]{:S(2)}, u32[]{:S(2)}) collective-permute-start(f32[2,192,128]{2,1,0:T(8,128)S(1)} %constant_dynamic-slice_fusion.5), channel_id=1, source_target_pairs={{0,1},{1,0},{2,3},{3,2},{4,5},{5,4},{6,7},{7,6},{8,9},{9,8},{10,11... | collective-permute-start | bytes 589832 | tf_op jit(solution)/shard_map/ppermute | solution.py:45
  7.3 3.0 %collective-permute-done = f32[2,192,128]{2,1,0:T(8,128)S(1)} collective-permute-done((f32[2,192,128]{2,1,0:T(8,128)S(1)}, f32[2,192,128]{2,1,0:T(8,128)S(1)}, u32[]{:S(2)}, u32[]{:S(2)}) %collective-permute-start) | collective-permute-done | bytes 196640 | tf_op jit(solution)/shard_map/ppermute | solution.py:45
  10.3 0.1 constant_dynamic-slice_fusion.4
  10.5 7.4 %collective-permute-start.1 = (f32[2,192,64]{2,1,0:T(8,128)S(1)}, f32[2,192,64]{2,1,0:T(8,128)S(1)}, u32[]{:S(2)}, u32[]{:S(2)}) collective-permute-start(f32[2,192,64]{2,1,0:T(8,128)S(1)} %constant_dynamic-slice_fusion.4), channel_id=1, source_target_pairs={{0,2},{1,3},{2,0},{3,1},{4,6},{5,7},{6,4},{7,5},{8,10},{9,11},{10,... | collective-permute-start | bytes 294920 | tf_op jit(solution)/shard_map/ppermute | solution.py:45
  17.9 0.2 copy.41
  18.1 0.1 reshape.173
  18.2 8.0 %collective-permute-done.1 = f32[2,192,64]{2,1,0:T(8,128)S(1)} collective-permute-done((f32[2,192,64]{2,1,0:T(8,128)S(1)}, f32[2,192,64]{2,1,0:T(8,128)S(1)}, u32[]{:S(2)}, u32[]{:S(2)}) %collective-permute-start.1) | collective-permute-done | bytes 98336 | tf_op jit(solution)/shard_map/ppermute | solution.py:45
  26.2 0.1 dynamic-slice_add_fusion
  26.4 0.1 reshape.172
  26.5 8.4 %collective-permute-start.2 = (f32[384,128]{1,0:T(8,128)S(1)}, f32[384,128]{1,0:T(8,128)S(1)}, u32[]{:S(2)}, u32[]{:S(2)}) collective-permute-start(f32[384,128]{1,0:T(8,128)S(1)} %pad_maximum_fusion.3), channel_id=1, source_target_pairs={{0,4},{1,5},{2,6},{3,7},{4,0},{5,1},{6,2},{7,3},{8,12},{9,13},{10,... | collective-permute-start | bytes 589832 | tf_op jit(solution)/shard_map/ppermute | solution.py:109
  34.9 6.8 %collective-permute-done.2 = f32[384,128]{1,0:T(8,128)S(1)} collective-permute-done((f32[384,128]{1,0:T(8,128)S(1)}, f32[384,128]{1,0:T(8,128)S(1)}, u32[]{:S(2)}, u32[]{:S(2)}) %collective-permute-start.2) | collective-permute-done | bytes 196640 | tf_op jit(solution)/shard_map/ppermute | solution.py:109
  41.7 0.1 reshape.174
  41.8 0.1 reshape.175
  41.9 0.1 broadcast_select_fusion.1
  42.0 0.3 fusion.29
  42.3 1.9 %collective-permute-start.3 = (bf16[2,2,192,64]{3,2,1,0:T(8,128)(2,1)S(1)}, bf16[2,2,192,64]{3,2,1,0:T(8,128)(2,1)S(1)}, u32[]{:S(2)}, u32[]{:S(2)}) collective-permute-start(bf16[2,2,192,64]{3,2,1,0:T(8,128)(2,1)S(1)} %pad_maximum_fusion.4), channel_id=1, source_target_pairs={{0,2},{1,3},{2,0},{3,1},{4,6},{5,7},{6,4},{7,5},{8,10},{9,11},{10,... | collective-permute-start | bytes 294920 | tf_op jit(solution)/shard_map/ppermute | solution.py:53
  44.2 5.4 %collective-permute-done.3 = bf16[2,2,192,64]{3,2,1,0:T(8,128)(2,1)S(1)} collective-permute-done((bf16[2,2,192,64]{3,2,1,0:T(8,128)(2,1)S(1)}, bf16[2,2,192,64]{3,2,1,0:T(8,128)(2,1)S(1)}, u32[]{:S(2)}, u32[]{:S(2)}) %collective-permute-start.3) | collective-permute-done | bytes 98336 | tf_op jit(solution)/shard_map/ppermute | solution.py:53
  49.6 0.1 broadcast_select_fusion.3
  49.7 0.1 pad_maximum_fusion.5
  49.8 5.8 %collective-permute-start.4 = (bf16[2,2,192,128]{3,2,1,0:T(8,128)(2,1)S(1)}, bf16[2,2,192,128]{3,2,1,0:T(8,128)(2,1)S(1)}, u32[]{:S(2)}, u32[]{:S(2)}) collective-permute-start(bf16[2,2,192,128]{3,2,1,0:T(8,128)(2,1)S(1)} %pad_maximum_fusion.5), channel_id=1, source_target_pairs={{0,1},{1,0},{2,3},{3,2},{4,5},{5,4},{6,7},{7,6},{8,9},{9,8},{10,11... | collective-permute-start | bytes 589832 | tf_op jit(solution)/shard_map/ppermute | solution.py:53
  55.6 3.0 %collective-permute-done.4 = bf16[2,2,192,128]{3,2,1,0:T(8,128)(2,1)S(1)} collective-permute-done((bf16[2,2,192,128]{3,2,1,0:T(8,128)(2,1)S(1)}, bf16[2,2,192,128]{3,2,1,0:T(8,128)(2,1)S(1)}, u32[]{:S(2)}, u32[]{:S(2)}) %collective-permute-start.4) | collective-permute-done | bytes 196640 | tf_op jit(solution)/shard_map/ppermute | solution.py:53
  58.7 0.2 broadcast_select_fusion.4
  58.8 0.3 fusion.19
  59.2 8.0 %collective-permute-start.5 = (f32[1,320,256]{2,1,0:T(8,128)S(1)}, f32[1,320,256]{2,1,0:T(8,128)S(1)}, u32[]{:S(2)}, u32[]{:S(2)}) collective-permute-start(f32[1,320,256]{2,1,0:T(8,128)S(1)} %dynamic-slice_bitcast_fusion), channel_id=1, source_target_pairs={{0,8},{8,0},{16,24},{24,16},{32,40},{40,32},{48,56},{56,48},{64,72... | collective-permute-start | bytes 983048 | tf_op jit(solution)/shard_map/ppermute | solution.py:45
  67.2 1.2 collective-permute-done.5
  68.5 3.1 %collective-permute-start.6 = (f32[1,320,128]{2,1,0:T(8,128)S(1)}, f32[1,320,128]{2,1,0:T(8,128)S(1)}, u32[]{:S(2)}, u32[]{:S(2)}) collective-permute-start(f32[1,320,128]{2,1,0:T(8,128)S(1)} %constant_dynamic-slice_fusion.1), channel_id=1, source_target_pairs={{0,16},{8,24},{16,0},{24,8},{32,48},{40,56},{48,32},{56,40},{64,80... | collective-permute-start | bytes 491528 | tf_op jit(solution)/shard_map/ppermute | solution.py:45
  71.6 4.1 %collective-permute-done.6 = f32[1,320,128]{2,1,0:T(8,128)S(1)} collective-permute-done((f32[1,320,128]{2,1,0:T(8,128)S(1)}, f32[1,320,128]{2,1,0:T(8,128)S(1)}, u32[]{:S(2)}, u32[]{:S(2)}) %collective-permute-start.6) | collective-permute-done | bytes 163872 | tf_op jit(solution)/shard_map/ppermute | solution.py:45
  75.8 3.2 %collective-permute-start.7 = (f32[1,160,128]{2,1,0:T(8,128)S(1)}, f32[1,160,128]{2,1,0:T(8,128)S(1)}, u32[]{:S(2)}, u32[]{:S(2)}) collective-permute-start(f32[1,160,128]{2,1,0:T(8,128)S(1)} %constant_dynamic-slice_fusion), channel_id=1, source_target_pairs={{0,64},{8,72},{16,80},{24,88},{32,96},{40,104},{48,112},{56,120},{... | collective-permute-start | bytes 245768 | tf_op jit(solution)/shard_map/ppermute | solution.py:45
  79.0 2.0 %collective-permute-done.7 = f32[1,160,128]{2,1,0:T(8,128)S(1)} collective-permute-done((f32[1,160,128]{2,1,0:T(8,128)S(1)}, f32[1,160,128]{2,1,0:T(8,128)S(1)}, u32[]{:S(2)}, u32[]{:S(2)}) %collective-permute-start.7) | collective-permute-done | bytes 81952 | tf_op jit(solution)/shard_map/ppermute | solution.py:45
  81.0 4.6 %collective-permute-start.8 = (f32[1,160,128]{2,1,0:T(8,128)S(1)}, f32[1,160,128]{2,1,0:T(8,128)S(1)}, u32[]{:S(2)}, u32[]{:S(2)}) collective-permute-start(f32[1,160,128]{2,1,0:T(8,128)S(1)} %dynamic-slice_add_fusion.3), channel_id=1, source_target_pairs={{0,32},{8,40},{16,48},{24,56},{32,0},{40,8},{48,16},{56,24},{64,96... | collective-permute-start | bytes 245768 | tf_op jit(solution)/shard_map/ppermute | solution.py:34
  85.7 2.0 %collective-permute-done.8 = f32[1,160,128]{2,1,0:T(8,128)S(1)} collective-permute-done((f32[1,160,128]{2,1,0:T(8,128)S(1)}, f32[1,160,128]{2,1,0:T(8,128)S(1)}, u32[]{:S(2)}, u32[]{:S(2)}) %collective-permute-start.8) | collective-permute-done | bytes 81952 | tf_op jit(solution)/shard_map/ppermute | solution.py:34
  87.7 4.2 %collective-permute-start.9 = (f32[1,160,128]{2,1,0:T(8,128)S(1)}, f32[1,160,128]{2,1,0:T(8,128)S(1)}, u32[]{:S(2)}, u32[]{:S(2)}) collective-permute-start(f32[1,160,128]{2,1,0:T(8,128)S(1)} %add.108), channel_id=1, source_target_pairs={{0,128},{8,136},{16,144},{24,152},{32,160},{40,168},{48,176},{56,1... | collective-permute-start | bytes 245768 | tf_op jit(solution)/shard_map/ppermute | solution.py:34
  92.0 1.9 %collective-permute-done.9 = f32[1,160,128]{2,1,0:T(8,128)S(1)} collective-permute-done((f32[1,160,128]{2,1,0:T(8,128)S(1)}, f32[1,160,128]{2,1,0:T(8,128)S(1)}, u32[]{:S(2)}, u32[]{:S(2)}) %collective-permute-start.9) | collective-permute-done | bytes 81952 | tf_op jit(solution)/shard_map/ppermute | solution.py:34
  93.8 8.3 %collective-permute-start.10 = (f32[1,160,128]{2,1,0:T(8,128)S(1)}, f32[1,160,128]{2,1,0:T(8,128)S(1)}, u32[]{:S(2)}, u32[]{:S(2)}) collective-permute-start(f32[1,160,128]{2,1,0:T(8,128)S(1)} %add.109), channel_id=1, source_target_pairs={{0,256},{8,264},{16,272},{24,280},{32,288},{40,296},{48,304},{56,3... | collective-permute-start | bytes 245768 | tf_op jit(solution)/shard_map/ppermute | solution.py:34
  102.2 1.9 %collective-permute-done.10 = f32[1,160,128]{2,1,0:T(8,128)S(1)} collective-permute-done((f32[1,160,128]{2,1,0:T(8,128)S(1)}, f32[1,160,128]{2,1,0:T(8,128)S(1)}, u32[]{:S(2)}, u32[]{:S(2)}) %collective-permute-start.10) | collective-permute-done | bytes 81952 | tf_op jit(solution)/shard_map/ppermute | solution.py:34
  104.1 2.9 %collective-permute-start.11 = (f32[1,160,128]{2,1,0:T(8,128)S(1)}, f32[1,160,128]{2,1,0:T(8,128)S(1)}, u32[]{:S(2)}, u32[]{:S(2)}) collective-permute-start(f32[1,160,128]{2,1,0:T(8,128)S(1)} %add.110), channel_id=1, source_target_pairs={{0,64},{8,72},{16,80},{24,88},{32,96},{40,104},{48,112},{56,120},{... | collective-permute-start | bytes 245768 | tf_op jit(solution)/shard_map/ppermute | solution.py:53
  107.0 3.4 %collective-permute-done.11 = f32[1,160,128]{2,1,0:T(8,128)S(1)} collective-permute-done((f32[1,160,128]{2,1,0:T(8,128)S(1)}, f32[1,160,128]{2,1,0:T(8,128)S(1)}, u32[]{:S(2)}, u32[]{:S(2)}) %collective-permute-start.11) | collective-permute-done | bytes 81952 | tf_op jit(solution)/shard_map/ppermute | solution.py:53
  110.5 3.1 %collective-permute-start.12 = (f32[1,320,128]{2,1,0:T(8,128)S(1)}, f32[1,320,128]{2,1,0:T(8,128)S(1)}, u32[]{:S(2)}, u32[]{:S(2)}) collective-permute-start(f32[1,320,128]{2,1,0:T(8,128)S(1)} %pad_maximum_fusion.6), channel_id=1, source_target_pairs={{0,16},{8,24},{16,0},{24,8},{32,48},{40,56},{48,32},{56,40},{64,80... | collective-permute-start | bytes 491528 | tf_op jit(solution)/shard_map/ppermute | solution.py:53
  113.7 2.9 %collective-permute-done.12 = f32[1,320,128]{2,1,0:T(8,128)S(1)} collective-permute-done((f32[1,320,128]{2,1,0:T(8,128)S(1)}, f32[1,320,128]{2,1,0:T(8,128)S(1)}, u32[]{:S(2)}, u32[]{:S(2)}) %collective-permute-start.12) | collective-permute-done | bytes 163872 | tf_op jit(solution)/shard_map/ppermute | solution.py:53
  116.6 0.9 convolution_bitcast_fusion
  117.5 0.1 copy.58
  117.6 0.1 copy.59
  117.7 0.1 fusion.32
  117.8 0.1 copy.47
  117.9 1.9 %collective-permute-start.13 = (f32[1,257,128]{2,1,0:T(8,128)S(1)}, f32[1,257,128]{2,1,0:T(8,128)S(1)}, u32[]{:S(2)}, u32[]{:S(2)}) collective-permute-start(f32[1,257,128]{2,1,0:T(8,128)S(1)} %pad_maximum_fusion.7), channel_id=1, source_target_pairs={{0,1},{1,0},{2,3},{3,2},{4,5},{5,4},{6,7},{7,6},{8,9},{9,8},{10,11... | collective-permute-start | bytes 394760 | tf_op jit(solution)/shard_map/ppermute | solution.py:34
  119.9 3.8 %collective-permute-done.13 = f32[1,257,128]{2,1,0:T(8,128)S(1)} collective-permute-done((f32[1,257,128]{2,1,0:T(8,128)S(1)}, f32[1,257,128]{2,1,0:T(8,128)S(1)}, u32[]{:S(2)}, u32[]{:S(2)}) %collective-permute-start.13) | collective-permute-done | bytes 131616 | tf_op jit(solution)/shard_map/ppermute | solution.py:34
  123.7 1.9 %collective-permute-start.14 = (f32[1,257,128]{2,1,0:T(8,128)S(1)}, f32[1,257,128]{2,1,0:T(8,128)S(1)}, u32[]{:S(2)}, u32[]{:S(2)}) collective-permute-start(f32[1,257,128]{2,1,0:T(8,128)S(1)} %fusion.37), channel_id=1, source_target_pairs={{0,2},{1,3},{2,0},{3,1},{4,6},{5,7},{6,4},{7,5},{8,10},{9,11},{10,... | collective-permute-start | bytes 394760 | tf_op jit(solution)/shard_map/ppermute | solution.py:34
  125.6 6.1 %collective-permute-done.14 = f32[1,257,128]{2,1,0:T(8,128)S(1)} collective-permute-done((f32[1,257,128]{2,1,0:T(8,128)S(1)}, f32[1,257,128]{2,1,0:T(8,128)S(1)}, u32[]{:S(2)}, u32[]{:S(2)}) %collective-permute-start.14) | collective-permute-done | bytes 131616 | tf_op jit(solution)/shard_map/ppermute | solution.py:34
  131.7 5.6 %collective-permute-start.15 = (f32[1,257,128]{2,1,0:T(8,128)S(1)}, f32[1,257,128]{2,1,0:T(8,128)S(1)}, u32[]{:S(2)}, u32[]{:S(2)}) collective-permute-start(f32[1,257,128]{2,1,0:T(8,128)S(1)} %add.112), channel_id=1, source_target_pairs={{0,4},{1,5},{2,6},{3,7},{4,0},{5,1},{6,2},{7,3},{8,12},{9,13},{10,... | collective-permute-start | bytes 394760 | tf_op jit(solution)/shard_map/ppermute | solution.py:34
  137.3 0.2 constant_dynamic-slice_fusion.2
  137.5 0.7 copy.53
  138.2 0.7 copy.54
  139.0 5.4 %collective-permute-done.15 = f32[1,257,128]{2,1,0:T(8,128)S(1)} collective-permute-done((f32[1,257,128]{2,1,0:T(8,128)S(1)}, f32[1,257,128]{2,1,0:T(8,128)S(1)}, u32[]{:S(2)}, u32[]{:S(2)}) %collective-permute-start.15) | collective-permute-done | bytes 131616 | tf_op jit(solution)/shard_map/ppermute | solution.py:34
  144.4 0.1 copy.50
  144.5 0.1 copy.60
  144.6 0.1 bitcast_select_fusion
  144.7 0.6 fusion.7
  146.1 0.5 fusion.4
  146.6 13.9 %collective-permute-start.16 = (bf16[1,320,256]{2,1,0:T(8,128)(2,1)S(1)}, bf16[1,320,256]{2,1,0:T(8,128)(2,1)S(1)}, u32[]{:S(2)}, u32[]{:S(2)}) collective-permute-start(bf16[1,320,256]{2,1,0:T(8,128)(2,1)S(1)} %fusion.4), channel_id=1, source_target_pairs={{0,8},{8,0},{16,24},{24,16},{32,40},{40,32},{48,56},{56,48},{64,72... | collective-permute-start | bytes 491528 | tf_op jit(solution)/shard_map/ppermute | solution.py:53
  160.5 1.1 fusion
  161.6 0.2 copy.51
  161.9 1.1 copy.55
  (39 shorter events, 0.7 us)
Async XLA Ops:
  0.6 1.4 copy-start
  2.4 7.9 %collective-permute-start = (f32[2,192,128]{2,1,0:T(8,128)S(1)}, f32[2,192,128]{2,1,0:T(8,128)S(1)}, u32[]{:S(2)}, u32[]{:S(2)}) collective-permute-start(f32[2,192,128]{2,1,0:T(8,128)S(1)} %constant_dynamic-slice_fusion.5), channel_id=1, source_target_pairs={{0,1},{1,0},{2,3},{3,2},{4,5},{5,4},{6,7},{7,6},{8,9},{9,8},{10,11... | collective-permute-start | bytes 589832 | tf_op jit(solution)/shard_map/ppermute | solution.py:45
  10.3 7.5 %copy-start.2 = (f32[2,192,32]{1,2,0:T(8,128)S(1)}, f32[2,192,32]{1,2,0:T(8,128)}, u32[]{:S(2)}) copy-start(f32[2,192,32]{1,2,0:T(8,128)} %param.9) | copy-start | bytes 147460
  10.3 7.5 %copy-start.3 = (f32[2,192,32]{1,2,0:T(8,128)S(1)}, f32[2,192,32]{1,2,0:T(8,128)}, u32[]{:S(2)}) copy-start(f32[2,192,32]{1,2,0:T(8,128)} %param.8) | copy-start | bytes 147460
  10.5 15.8 %collective-permute-start.1 = (f32[2,192,64]{2,1,0:T(8,128)S(1)}, f32[2,192,64]{2,1,0:T(8,128)S(1)}, u32[]{:S(2)}, u32[]{:S(2)}) collective-permute-start(f32[2,192,64]{2,1,0:T(8,128)S(1)} %constant_dynamic-slice_fusion.4), channel_id=1, source_target_pairs={{0,2},{1,3},{2,0},{3,1},{4,6},{5,7},{6,4},{7,5},{8,10},{9,11},{10,... | collective-permute-start | bytes 294920 | tf_op jit(solution)/shard_map/ppermute | solution.py:45
  26.5 15.2 %collective-permute-start.2 = (f32[384,128]{1,0:T(8,128)S(1)}, f32[384,128]{1,0:T(8,128)S(1)}, u32[]{:S(2)}, u32[]{:S(2)}) collective-permute-start(f32[384,128]{1,0:T(8,128)S(1)} %pad_maximum_fusion.3), channel_id=1, source_target_pairs={{0,4},{1,5},{2,6},{3,7},{4,0},{5,1},{6,2},{7,3},{8,12},{9,13},{10,... | collective-permute-start | bytes 589832 | tf_op jit(solution)/shard_map/ppermute | solution.py:109
  42.3 7.3 %collective-permute-start.3 = (bf16[2,2,192,64]{3,2,1,0:T(8,128)(2,1)S(1)}, bf16[2,2,192,64]{3,2,1,0:T(8,128)(2,1)S(1)}, u32[]{:S(2)}, u32[]{:S(2)}) collective-permute-start(bf16[2,2,192,64]{3,2,1,0:T(8,128)(2,1)S(1)} %pad_maximum_fusion.4), channel_id=1, source_target_pairs={{0,2},{1,3},{2,0},{3,1},{4,6},{5,7},{6,4},{7,5},{8,10},{9,11},{10,... | collective-permute-start | bytes 294920 | tf_op jit(solution)/shard_map/ppermute | solution.py:53
  49.8 8.8 %collective-permute-start.4 = (bf16[2,2,192,128]{3,2,1,0:T(8,128)(2,1)S(1)}, bf16[2,2,192,128]{3,2,1,0:T(8,128)(2,1)S(1)}, u32[]{:S(2)}, u32[]{:S(2)}) collective-permute-start(bf16[2,2,192,128]{3,2,1,0:T(8,128)(2,1)S(1)} %pad_maximum_fusion.5), channel_id=1, source_target_pairs={{0,1},{1,0},{2,3},{3,2},{4,5},{5,4},{6,7},{7,6},{8,9},{9,8},{10,11... | collective-permute-start | bytes 589832 | tf_op jit(solution)/shard_map/ppermute | solution.py:53
  59.2 9.2 %collective-permute-start.5 = (f32[1,320,256]{2,1,0:T(8,128)S(1)}, f32[1,320,256]{2,1,0:T(8,128)S(1)}, u32[]{:S(2)}, u32[]{:S(2)}) collective-permute-start(f32[1,320,256]{2,1,0:T(8,128)S(1)} %dynamic-slice_bitcast_fusion), channel_id=1, source_target_pairs={{0,8},{8,0},{16,24},{24,16},{32,40},{40,32},{48,56},{56,48},{64,72... | collective-permute-start | bytes 983048 | tf_op jit(solution)/shard_map/ppermute | solution.py:45
  68.5 7.3 %collective-permute-start.6 = (f32[1,320,128]{2,1,0:T(8,128)S(1)}, f32[1,320,128]{2,1,0:T(8,128)S(1)}, u32[]{:S(2)}, u32[]{:S(2)}) collective-permute-start(f32[1,320,128]{2,1,0:T(8,128)S(1)} %constant_dynamic-slice_fusion.1), channel_id=1, source_target_pairs={{0,16},{8,24},{16,0},{24,8},{32,48},{40,56},{48,32},{56,40},{64,80... | collective-permute-start | bytes 491528 | tf_op jit(solution)/shard_map/ppermute | solution.py:45
  75.8 5.2 %collective-permute-start.7 = (f32[1,160,128]{2,1,0:T(8,128)S(1)}, f32[1,160,128]{2,1,0:T(8,128)S(1)}, u32[]{:S(2)}, u32[]{:S(2)}) collective-permute-start(f32[1,160,128]{2,1,0:T(8,128)S(1)} %constant_dynamic-slice_fusion), channel_id=1, source_target_pairs={{0,64},{8,72},{16,80},{24,88},{32,96},{40,104},{48,112},{56,120},{... | collective-permute-start | bytes 245768 | tf_op jit(solution)/shard_map/ppermute | solution.py:45
  81.0 6.7 %collective-permute-start.8 = (f32[1,160,128]{2,1,0:T(8,128)S(1)}, f32[1,160,128]{2,1,0:T(8,128)S(1)}, u32[]{:S(2)}, u32[]{:S(2)}) collective-permute-start(f32[1,160,128]{2,1,0:T(8,128)S(1)} %dynamic-slice_add_fusion.3), channel_id=1, source_target_pairs={{0,32},{8,40},{16,48},{24,56},{32,0},{40,8},{48,16},{56,24},{64,96... | collective-permute-start | bytes 245768 | tf_op jit(solution)/shard_map/ppermute | solution.py:34
  87.7 6.1 %collective-permute-start.9 = (f32[1,160,128]{2,1,0:T(8,128)S(1)}, f32[1,160,128]{2,1,0:T(8,128)S(1)}, u32[]{:S(2)}, u32[]{:S(2)}) collective-permute-start(f32[1,160,128]{2,1,0:T(8,128)S(1)} %add.108), channel_id=1, source_target_pairs={{0,128},{8,136},{16,144},{24,152},{32,160},{40,168},{48,176},{56,1... | collective-permute-start | bytes 245768 | tf_op jit(solution)/shard_map/ppermute | solution.py:34
  93.8 10.3 %collective-permute-start.10 = (f32[1,160,128]{2,1,0:T(8,128)S(1)}, f32[1,160,128]{2,1,0:T(8,128)S(1)}, u32[]{:S(2)}, u32[]{:S(2)}) collective-permute-start(f32[1,160,128]{2,1,0:T(8,128)S(1)} %add.109), channel_id=1, source_target_pairs={{0,256},{8,264},{16,272},{24,280},{32,288},{40,296},{48,304},{56,3... | collective-permute-start | bytes 245768 | tf_op jit(solution)/shard_map/ppermute | solution.py:34
  104.1 6.4 %collective-permute-start.11 = (f32[1,160,128]{2,1,0:T(8,128)S(1)}, f32[1,160,128]{2,1,0:T(8,128)S(1)}, u32[]{:S(2)}, u32[]{:S(2)}) collective-permute-start(f32[1,160,128]{2,1,0:T(8,128)S(1)} %add.110), channel_id=1, source_target_pairs={{0,64},{8,72},{16,80},{24,88},{32,96},{40,104},{48,112},{56,120},{... | collective-permute-start | bytes 245768 | tf_op jit(solution)/shard_map/ppermute | solution.py:53
  110.5 6.1 %collective-permute-start.12 = (f32[1,320,128]{2,1,0:T(8,128)S(1)}, f32[1,320,128]{2,1,0:T(8,128)S(1)}, u32[]{:S(2)}, u32[]{:S(2)}) collective-permute-start(f32[1,320,128]{2,1,0:T(8,128)S(1)} %pad_maximum_fusion.6), channel_id=1, source_target_pairs={{0,16},{8,24},{16,0},{24,8},{32,48},{40,56},{48,32},{56,40},{64,80... | collective-permute-start | bytes 491528 | tf_op jit(solution)/shard_map/ppermute | solution.py:53
  117.9 5.8 %collective-permute-start.13 = (f32[1,257,128]{2,1,0:T(8,128)S(1)}, f32[1,257,128]{2,1,0:T(8,128)S(1)}, u32[]{:S(2)}, u32[]{:S(2)}) collective-permute-start(f32[1,257,128]{2,1,0:T(8,128)S(1)} %pad_maximum_fusion.7), channel_id=1, source_target_pairs={{0,1},{1,0},{2,3},{3,2},{4,5},{5,4},{6,7},{7,6},{8,9},{9,8},{10,11... | collective-permute-start | bytes 394760 | tf_op jit(solution)/shard_map/ppermute | solution.py:34
  123.7 8.0 %collective-permute-start.14 = (f32[1,257,128]{2,1,0:T(8,128)S(1)}, f32[1,257,128]{2,1,0:T(8,128)S(1)}, u32[]{:S(2)}, u32[]{:S(2)}) collective-permute-start(f32[1,257,128]{2,1,0:T(8,128)S(1)} %fusion.37), channel_id=1, source_target_pairs={{0,2},{1,3},{2,0},{3,1},{4,6},{5,7},{6,4},{7,5},{8,10},{9,11},{10,... | collective-permute-start | bytes 394760 | tf_op jit(solution)/shard_map/ppermute | solution.py:34
  131.7 12.6 %collective-permute-start.15 = (f32[1,257,128]{2,1,0:T(8,128)S(1)}, f32[1,257,128]{2,1,0:T(8,128)S(1)}, u32[]{:S(2)}, u32[]{:S(2)}) collective-permute-start(f32[1,257,128]{2,1,0:T(8,128)S(1)} %add.112), channel_id=1, source_target_pairs={{0,4},{1,5},{2,6},{3,7},{4,0},{5,1},{6,2},{7,3},{8,12},{9,13},{10,... | collective-permute-start | bytes 394760 | tf_op jit(solution)/shard_map/ppermute | solution.py:34
  146.1 14.4 %copy-start.1 = (f32[2,192,320]{2,1,0:T(8,128)S(1)}, f32[2,192,320]{2,1,0:T(8,128)}, u32[]{:S(2)}) copy-start(f32[2,192,320]{2,1,0:T(8,128)} %param.6) | copy-start | bytes 1474564
  146.6 15.0 %collective-permute-start.16 = (bf16[1,320,256]{2,1,0:T(8,128)(2,1)S(1)}, bf16[1,320,256]{2,1,0:T(8,128)(2,1)S(1)}, u32[]{:S(2)}, u32[]{:S(2)}) collective-permute-start(bf16[1,320,256]{2,1,0:T(8,128)(2,1)S(1)} %fusion.4), channel_id=1, source_target_pairs={{0,8},{8,0},{16,24},{24,16},{32,40},{40,32},{48,56},{56,48},{64,72... | collective-permute-start | bytes 491528 | tf_op jit(solution)/shard_map/ppermute | solution.py:53

commit v10 on v8

--- a/solution.py
+++ b/solution.py
@@ -110,7 +110,7 @@
     own = lax.dynamic_slice_in_dim(half, own_place * width, width, 2)
     first_next, second_next, normal_half = adam_share(own, first_moment, second_moment)
     projected_half = doubling_gather(half.astype(jnp.bfloat16), "tp", tp, [(0, 2)])
-    normal_full = doubling_gather(normal_half, "tp", tp, tp_bits)
+    normal_full = doubling_gather(normal_half, "tp", tp, list(reversed(tp_bits)))
 
     image_part = jnp.einsum("mfd,mfr->mdr", grads, projected_half, preferred_element_type=jnp.float32)
     stages = [(0, 0), (1, 2), (3, 1)]
@@ -118,7 +118,7 @@
     chunk = butterfly_sum(chunk, "fsdp", fsdp, [b for b in range(fsdp.bit_length() - 1) if b not in (0, 1, 3)])
     image = doubling_gather(chunk, "fsdp", fsdp, stages[1:])
 
-    update = jnp.einsum("mfr,dmr->mfd", normal_full, basis_order, preferred_element_type=jnp.float32)
+    update = jnp.einsum("mfr,dmr->mfd", normal_full, basis, preferred_element_type=jnp.float32)
     weight_next = weights - LEARNING_RATE * GALORE_SCALE * update
 
     packed = pack_gram(jnp.einsum("mdr,mds->mrs", image, image, precision=highest))

time: 155 us -> 151 us (0.974)
  starting transfers between devices: 103 us -> 92.5 us
  waiting for transfers between devices: 37.7 us -> 44.2 us
    ppermute x7, starting transfers between devices: 37 us -> 30.7 us  [doubling_gather(): other = lax.ppermute(value, axis, partner_perm(size, bit))]
    ppermute x8, waiting for transfers between devices: 22.4 us -> 27.4 us  [butterfly_sum(): value = value + lax.ppermute(value, axis, partner_perm(size, bit))]
    ppermute x8, starting transfers between devices: 51.6 us -> 47.3 us  [butterfly_sum(): value = value + lax.ppermute(value, axis, partner_perm(size, bit))]
  transfers between devices with their start and end apart: 19 -> 19, of which waited for: 14 -> 15; matrix products, arithmetic and copies ran while one was open for 3% -> 3% of each run, Pallas kernels for 0% -> 0%
where the time goes in v10:
time: 151 us; the launch traced here: 149 us
  starting transfers between devices  92.5 us (61%)
  waiting for transfers between devices  44.2 us (29%)
  local copies, waits for them, and re-layouts  5.75 us (4%)
  matrix products  3 us (2%)
  other arithmetic  1.95 us (1%)
  between operations  1.94 us (1%)
    ppermute x8, starting transfers between devices, butterfly_sum(): value = value + lax.ppermute(value, axis, partner_perm(size, bit))  47.3 us
    ppermute x7, starting transfers between devices, doubling_gather(): other = lax.ppermute(value, axis, partner_perm(size, bit))  30.7 us
    ppermute x8, waiting for transfers between devices, butterfly_sum(): value = value + lax.ppermute(value, axis, partner_perm(size, bit))  27.4 us
    ppermute x4, starting transfers between devices, halving_scatter(): value = keep + lax.ppermute(send, axis, partner_perm(size, bit))  14.5 us
    ppermute x4, waiting for transfers between devices, halving_scatter(): value = keep + lax.ppermute(send, axis, partner_perm(size, bit))  10.3 us
    ppermute x7, waiting for transfers between devices, doubling_gather(): other = lax.ppermute(value, axis, partner_perm(size, bit))  6.55 us
    unnamed x17, local copies, waits for them, and re-layouts  5.12 us
  transfers between devices with their start and end apart: 19, of which 15 were waited for; matrix products, arithmetic and copies ran while one was open for 3% of the time, Pallas kernels for 0%

profile of v10, /device:TPU:1, one launch (start us, length us, event | category | flops | bytes accessed | tf_op | source)
XLA Modules:
  0.0 149.4 jit_solution(10385856378336749114)
XLA Ops:
  0.6 0.0 copy-start
  0.7 1.3 copy.23
  2.0 0.1 copy.24
  2.1 0.3 fusion.35
  2.4 4.8 %collective-permute-start = (f32[2,192,128]{2,1,0:T(8,128)S(1)}, f32[2,192,128]{2,1,0:T(8,128)S(1)}, u32[]{:S(2)}, u32[]{:S(2)}) collective-permute-start(f32[2,192,128]{2,1,0:T(8,128)S(1)} %constant_dynamic-slice_fusion.2), channel_id=1, source_target_pairs={{0,1},{1,0},{2,3},{3,2},{4,5},{5,4},{6,7},{7,6},{8,9},{9,8},{10,11... | collective-permute-start | bytes 589832 | tf_op jit(solution)/shard_map/ppermute | solution.py:45
  7.3 3.0 %collective-permute-done = f32[2,192,128]{2,1,0:T(8,128)S(1)} collective-permute-done((f32[2,192,128]{2,1,0:T(8,128)S(1)}, f32[2,192,128]{2,1,0:T(8,128)S(1)}, u32[]{:S(2)}, u32[]{:S(2)}) %collective-permute-start) | collective-permute-done | bytes 196640 | tf_op jit(solution)/shard_map/ppermute | solution.py:45
  10.3 11.3 %collective-permute-start.1 = (f32[2,192,128]{2,1,0:T(8,128)S(1)}, f32[2,192,128]{2,1,0:T(8,128)S(1)}, u32[]{:S(2)}, u32[]{:S(2)}) collective-permute-start(f32[2,192,128]{2,1,0:T(8,128)S(1)} %dynamic-slice_add_fusion), channel_id=1, source_target_pairs={{0,4},{1,5},{2,6},{3,7},{4,0},{5,1},{6,2},{7,3},{8,12},{9,13},{10,... | collective-permute-start | bytes 589832 | tf_op jit(solution)/shard_map/ppermute | solution.py:34
  21.6 3.1 %collective-permute-done.1 = f32[2,192,128]{2,1,0:T(8,128)S(1)} collective-permute-done((f32[2,192,128]{2,1,0:T(8,128)S(1)}, f32[2,192,128]{2,1,0:T(8,128)S(1)}, u32[]{:S(2)}, u32[]{:S(2)}) %collective-permute-start.1) | collective-permute-done | bytes 196640 | tf_op jit(solution)/shard_map/ppermute | solution.py:34
  24.8 10.4 %collective-permute-start.2 = (f32[2,192,128]{2,1,0:T(8,128)S(1)}, f32[2,192,128]{2,1,0:T(8,128)S(1)}, u32[]{:S(2)}, u32[]{:S(2)}) collective-permute-start(f32[2,192,128]{2,1,0:T(8,128)S(1)} %add.86), channel_id=1, source_target_pairs={{0,2},{1,3},{2,0},{3,1},{4,6},{5,7},{6,4},{7,5},{8,10},{9,11},{10,... | collective-permute-start | bytes 589832 | tf_op jit(solution)/shard_map/ppermute | solution.py:34
  35.2 8.2 %collective-permute-done.2 = f32[2,192,128]{2,1,0:T(8,128)S(1)} collective-permute-done((f32[2,192,128]{2,1,0:T(8,128)S(1)}, f32[2,192,128]{2,1,0:T(8,128)S(1)}, u32[]{:S(2)}, u32[]{:S(2)}) %collective-permute-start.2) | collective-permute-done | bytes 196640 | tf_op jit(solution)/shard_map/ppermute | solution.py:34
  43.5 1.9 %collective-permute-start.6 = (bf16[2,192,128]{2,1,0:T(8,128)(2,1)S(1)}, bf16[2,192,128]{2,1,0:T(8,128)(2,1)S(1)}, u32[]{:S(2)}, u32[]{:S(2)}) collective-permute-start(bf16[2,192,128]{2,1,0:T(8,128)(2,1)S(1)} %get-tuple-element.12), channel_id=1, source_target_pairs={{0,1},{1,0},{2,3},{3,2},{4,5},{5,4},{6,7},{7,6},{8,9},{9,8},{10,11... | collective-permute-start | bytes 294920 | tf_op jit(solution)/shard_map/ppermute | solution.py:53
  45.4 3.8 %collective-permute-done.6 = bf16[2,192,128]{2,1,0:T(8,128)(2,1)S(1)} collective-permute-done((bf16[2,192,128]{2,1,0:T(8,128)(2,1)S(1)}, bf16[2,192,128]{2,1,0:T(8,128)(2,1)S(1)}, u32[]{:S(2)}, u32[]{:S(2)}) %collective-permute-start.6) | collective-permute-done | bytes 98336 | tf_op jit(solution)/shard_map/ppermute | solution.py:53
  49.3 0.3 fusion.14
  49.6 3.2 %collective-permute-start.7 = (f32[1,320,256]{2,1,0:T(8,128)S(1)}, f32[1,320,256]{2,1,0:T(8,128)S(1)}, u32[]{:S(2)}, u32[]{:S(2)}) collective-permute-start(f32[1,320,256]{2,1,0:T(8,128)S(1)} %dynamic-slice_bitcast_fusion), channel_id=1, source_target_pairs={{0,8},{8,0},{16,24},{24,16},{32,40},{40,32},{48,56},{56,48},{64,72... | collective-permute-start | bytes 983048 | tf_op jit(solution)/shard_map/ppermute | solution.py:45
  52.9 1.2 collective-permute-done.7
  54.2 3.2 %collective-permute-start.8 = (f32[1,320,128]{2,1,0:T(8,128)S(1)}, f32[1,320,128]{2,1,0:T(8,128)S(1)}, u32[]{:S(2)}, u32[]{:S(2)}) collective-permute-start(f32[1,320,128]{2,1,0:T(8,128)S(1)} %constant_dynamic-slice_fusion.1), channel_id=1, source_target_pairs={{0,16},{8,24},{16,0},{24,8},{32,48},{40,56},{48,32},{56,40},{64,80... | collective-permute-start | bytes 491528 | tf_op jit(solution)/shard_map/ppermute | solution.py:45
  57.3 4.1 %collective-permute-done.8 = f32[1,320,128]{2,1,0:T(8,128)S(1)} collective-permute-done((f32[1,320,128]{2,1,0:T(8,128)S(1)}, f32[1,320,128]{2,1,0:T(8,128)S(1)}, u32[]{:S(2)}, u32[]{:S(2)}) %collective-permute-start.8) | collective-permute-done | bytes 163872 | tf_op jit(solution)/shard_map/ppermute | solution.py:45
  61.5 3.2 %collective-permute-start.9 = (f32[1,160,128]{2,1,0:T(8,128)S(1)}, f32[1,160,128]{2,1,0:T(8,128)S(1)}, u32[]{:S(2)}, u32[]{:S(2)}) collective-permute-start(f32[1,160,128]{2,1,0:T(8,128)S(1)} %constant_dynamic-slice_fusion), channel_id=1, source_target_pairs={{0,64},{8,72},{16,80},{24,88},{32,96},{40,104},{48,112},{56,120},{... | collective-permute-start | bytes 245768 | tf_op jit(solution)/shard_map/ppermute | solution.py:45
  64.7 1.9 %collective-permute-done.9 = f32[1,160,128]{2,1,0:T(8,128)S(1)} collective-permute-done((f32[1,160,128]{2,1,0:T(8,128)S(1)}, f32[1,160,128]{2,1,0:T(8,128)S(1)}, u32[]{:S(2)}, u32[]{:S(2)}) %collective-permute-start.9) | collective-permute-done | bytes 81952 | tf_op jit(solution)/shard_map/ppermute | solution.py:45
  66.7 4.7 %collective-permute-start.10 = (f32[1,160,128]{2,1,0:T(8,128)S(1)}, f32[1,160,128]{2,1,0:T(8,128)S(1)}, u32[]{:S(2)}, u32[]{:S(2)}) collective-permute-start(f32[1,160,128]{2,1,0:T(8,128)S(1)} %dynamic-slice_add_fusion.2), channel_id=1, source_target_pairs={{0,32},{8,40},{16,48},{24,56},{32,0},{40,8},{48,16},{56,24},{64,96... | collective-permute-start | bytes 245768 | tf_op jit(solution)/shard_map/ppermute | solution.py:34
  71.4 2.0 %collective-permute-done.10 = f32[1,160,128]{2,1,0:T(8,128)S(1)} collective-permute-done((f32[1,160,128]{2,1,0:T(8,128)S(1)}, f32[1,160,128]{2,1,0:T(8,128)S(1)}, u32[]{:S(2)}, u32[]{:S(2)}) %collective-permute-start.10) | collective-permute-done | bytes 81952 | tf_op jit(solution)/shard_map/ppermute | solution.py:34
  73.4 4.3 %collective-permute-start.11 = (f32[1,160,128]{2,1,0:T(8,128)S(1)}, f32[1,160,128]{2,1,0:T(8,128)S(1)}, u32[]{:S(2)}, u32[]{:S(2)}) collective-permute-start(f32[1,160,128]{2,1,0:T(8,128)S(1)} %add.103), channel_id=1, source_target_pairs={{0,128},{8,136},{16,144},{24,152},{32,160},{40,168},{48,176},{56,1... | collective-permute-start | bytes 245768 | tf_op jit(solution)/shard_map/ppermute | solution.py:34
  77.7 1.8 %collective-permute-done.11 = f32[1,160,128]{2,1,0:T(8,128)S(1)} collective-permute-done((f32[1,160,128]{2,1,0:T(8,128)S(1)}, f32[1,160,128]{2,1,0:T(8,128)S(1)}, u32[]{:S(2)}, u32[]{:S(2)}) %collective-permute-start.11) | collective-permute-done | bytes 81952 | tf_op jit(solution)/shard_map/ppermute | solution.py:34
  79.5 8.5 %collective-permute-start.12 = (f32[1,160,128]{2,1,0:T(8,128)S(1)}, f32[1,160,128]{2,1,0:T(8,128)S(1)}, u32[]{:S(2)}, u32[]{:S(2)}) collective-permute-start(f32[1,160,128]{2,1,0:T(8,128)S(1)} %add.104), channel_id=1, source_target_pairs={{0,256},{8,264},{16,272},{24,280},{32,288},{40,296},{48,304},{56,3... | collective-permute-start | bytes 245768 | tf_op jit(solution)/shard_map/ppermute | solution.py:34
  88.0 0.0 copy-start.3
  88.0 0.1 copy.22
  88.2 0.7 copy-done.3
  88.9 0.1 copy.26
  89.0 0.9 collective-permute-done.12
  89.9 2.8 %collective-permute-start.13 = (f32[1,160,128]{2,1,0:T(8,128)S(1)}, f32[1,160,128]{2,1,0:T(8,128)S(1)}, u32[]{:S(2)}, u32[]{:S(2)}) collective-permute-start(f32[1,160,128]{2,1,0:T(8,128)S(1)} %add.105), channel_id=1, source_target_pairs={{0,64},{8,72},{16,80},{24,88},{32,96},{40,104},{48,112},{56,120},{... | collective-permute-start | bytes 245768 | tf_op jit(solution)/shard_map/ppermute | solution.py:53
  92.7 0.2 divide_convert_fusion
  93.0 1.9 %collective-permute-start.3 = (bf16[2,192,32]{2,1,0:T(8,128)(2,1)S(1)}, bf16[2,192,32]{2,1,0:T(8,128)(2,1)S(1)}, u32[]{:S(2)}, u32[]{:S(2)}) collective-permute-start(bf16[2,192,32]{2,1,0:T(8,128)(2,1)S(1)} %get-tuple-element.14), channel_id=1, source_target_pairs={{0,1},{1,0},{2,3},{3,2},{4,5},{5,4},{6,7},{7,6},{8,9},{9,8},{10,11... | collective-permute-start | bytes 73736 | tf_op jit(solution)/shard_map/ppermute | solution.py:53
  94.9 1.4 collective-permute-done.13
  96.4 3.1 %collective-permute-start.14 = (f32[1,320,128]{2,1,0:T(8,128)S(1)}, f32[1,320,128]{2,1,0:T(8,128)S(1)}, u32[]{:S(2)}, u32[]{:S(2)}) collective-permute-start(f32[1,320,128]{2,1,0:T(8,128)S(1)} %pad_maximum_fusion.1), channel_id=1, source_target_pairs={{0,16},{8,24},{16,0},{24,8},{32,48},{40,56},{48,32},{56,40},{64,80... | collective-permute-start | bytes 491528 | tf_op jit(solution)/shard_map/ppermute | solution.py:53
  99.5 0.1 pad_maximum_fusion.3
  99.6 2.0 %collective-permute-start.4 = (bf16[2,192,64]{2,1,0:T(8,128)(2,1)S(1)}, bf16[2,192,64]{2,1,0:T(8,128)(2,1)S(1)}, u32[]{:S(2)}, u32[]{:S(2)}) collective-permute-start(bf16[2,192,64]{2,1,0:T(8,128)(2,1)S(1)} %pad_maximum_fusion.3), channel_id=1, source_target_pairs={{0,2},{1,3},{2,0},{3,1},{4,6},{5,7},{6,4},{7,5},{8,10},{9,11},{10,... | collective-permute-start | bytes 147464 | tf_op jit(solution)/shard_map/ppermute | solution.py:53
  101.6 0.8 collective-permute-done.14
  102.5 0.9 convolution_bitcast_fusion
  103.4 0.1 copy.40
  103.5 0.1 copy.41
  103.6 0.1 fusion.25
  103.7 0.1 copy.30
  103.8 2.4 %collective-permute-start.15 = (f32[1,257,128]{2,1,0:T(8,128)S(1)}, f32[1,257,128]{2,1,0:T(8,128)S(1)}, u32[]{:S(2)}, u32[]{:S(2)}) collective-permute-start(f32[1,257,128]{2,1,0:T(8,128)S(1)} %pad_maximum_fusion.2), channel_id=1, source_target_pairs={{0,1},{1,0},{2,3},{3,2},{4,5},{5,4},{6,7},{7,6},{8,9},{9,8},{10,11... | collective-permute-start | bytes 394760 | tf_op jit(solution)/shard_map/ppermute | solution.py:34
  106.2 0.5 collective-permute-done.4
  106.7 0.1 broadcast_select_fusion.7
  106.8 2.7 %collective-permute-done.15 = f32[1,257,128]{2,1,0:T(8,128)S(1)} collective-permute-done((f32[1,257,128]{2,1,0:T(8,128)S(1)}, f32[1,257,128]{2,1,0:T(8,128)S(1)}, u32[]{:S(2)}, u32[]{:S(2)}) %collective-permute-start.15) | collective-permute-done | bytes 131616 | tf_op jit(solution)/shard_map/ppermute | solution.py:34
  109.6 3.4 %collective-permute-start.16 = (f32[1,257,128]{2,1,0:T(8,128)S(1)}, f32[1,257,128]{2,1,0:T(8,128)S(1)}, u32[]{:S(2)}, u32[]{:S(2)}) collective-permute-start(f32[1,257,128]{2,1,0:T(8,128)S(1)} %fusion.30), channel_id=1, source_target_pairs={{0,2},{1,3},{2,0},{3,1},{4,6},{5,7},{6,4},{7,5},{8,10},{9,11},{10,... | collective-permute-start | bytes 394760 | tf_op jit(solution)/shard_map/ppermute | solution.py:34
  113.0 0.1 pad_maximum_fusion.4
  113.1 6.9 %collective-permute-start.5 = (bf16[2,192,128]{2,1,0:T(8,128)(2,1)S(1)}, bf16[2,192,128]{2,1,0:T(8,128)(2,1)S(1)}, u32[]{:S(2)}, u32[]{:S(2)}) collective-permute-start(bf16[2,192,128]{2,1,0:T(8,128)(2,1)S(1)} %pad_maximum_fusion.4), channel_id=1, source_target_pairs={{0,4},{1,5},{2,6},{3,7},{4,0},{5,1},{6,2},{7,3},{8,12},{9,13},{10,... | collective-permute-start | bytes 294920 | tf_op jit(solution)/shard_map/ppermute | solution.py:53
  120.0 0.7 copy.36
  120.7 0.7 copy.37
  121.5 2.3 %collective-permute-start.17 = (f32[1,257,128]{2,1,0:T(8,128)S(1)}, f32[1,257,128]{2,1,0:T(8,128)S(1)}, u32[]{:S(2)}, u32[]{:S(2)}) collective-permute-start(f32[1,257,128]{2,1,0:T(8,128)S(1)} %add.107), channel_id=1, source_target_pairs={{0,4},{1,5},{2,6},{3,7},{4,0},{5,1},{6,2},{7,3},{8,12},{9,13},{10,... | collective-permute-start | bytes 394760 | tf_op jit(solution)/shard_map/ppermute | solution.py:34
  123.8 0.1 broadcast_select_fusion.9
  124.0 8.6 %collective-permute-done.17 = f32[1,257,128]{2,1,0:T(8,128)S(1)} collective-permute-done((f32[1,257,128]{2,1,0:T(8,128)S(1)}, f32[1,257,128]{2,1,0:T(8,128)S(1)}, u32[]{:S(2)}, u32[]{:S(2)}) %collective-permute-start.17) | collective-permute-done | bytes 131616 | tf_op jit(solution)/shard_map/ppermute | solution.py:34
  132.6 0.1 copy.42
  132.7 0.1 copy.33
  132.8 0.1 bitcast_select_fusion
  132.9 0.6 fusion.7
  134.3 0.5 fusion.4
  134.8 12.1 %collective-permute-start.18 = (bf16[1,320,256]{2,1,0:T(8,128)(2,1)S(1)}, bf16[1,320,256]{2,1,0:T(8,128)(2,1)S(1)}, u32[]{:S(2)}, u32[]{:S(2)}) collective-permute-start(bf16[1,320,256]{2,1,0:T(8,128)(2,1)S(1)} %fusion.4), channel_id=1, source_target_pairs={{0,8},{8,0},{16,24},{24,16},{32,40},{40,32},{48,56},{56,48},{64,72... | collective-permute-start | bytes 491528 | tf_op jit(solution)/shard_map/ppermute | solution.py:53
  146.9 1.1 fusion
  148.0 0.2 copy.34
  148.2 0.1 copy.35
  148.3 1.1 copy.38
  (37 shorter events, 0.6 us)
Async XLA Ops:
  0.6 1.4 copy-start
  2.4 7.9 %collective-permute-start = (f32[2,192,128]{2,1,0:T(8,128)S(1)}, f32[2,192,128]{2,1,0:T(8,128)S(1)}, u32[]{:S(2)}, u32[]{:S(2)}) collective-permute-start(f32[2,192,128]{2,1,0:T(8,128)S(1)} %constant_dynamic-slice_fusion.2), channel_id=1, source_target_pairs={{0,1},{1,0},{2,3},{3,2},{4,5},{5,4},{6,7},{7,6},{8,9},{9,8},{10,11... | collective-permute-start | bytes 589832 | tf_op jit(solution)/shard_map/ppermute | solution.py:45
  10.3 14.4 %collective-permute-start.1 = (f32[2,192,128]{2,1,0:T(8,128)S(1)}, f32[2,192,128]{2,1,0:T(8,128)S(1)}, u32[]{:S(2)}, u32[]{:S(2)}) collective-permute-start(f32[2,192,128]{2,1,0:T(8,128)S(1)} %dynamic-slice_add_fusion), channel_id=1, source_target_pairs={{0,4},{1,5},{2,6},{3,7},{4,0},{5,1},{6,2},{7,3},{8,12},{9,13},{10,... | collective-permute-start | bytes 589832 | tf_op jit(solution)/shard_map/ppermute | solution.py:34
  24.8 18.7 %collective-permute-start.2 = (f32[2,192,128]{2,1,0:T(8,128)S(1)}, f32[2,192,128]{2,1,0:T(8,128)S(1)}, u32[]{:S(2)}, u32[]{:S(2)}) collective-permute-start(f32[2,192,128]{2,1,0:T(8,128)S(1)} %add.86), channel_id=1, source_target_pairs={{0,2},{1,3},{2,0},{3,1},{4,6},{5,7},{6,4},{7,5},{8,10},{9,11},{10,... | collective-permute-start | bytes 589832 | tf_op jit(solution)/shard_map/ppermute | solution.py:34
  43.5 5.8 %collective-permute-start.6 = (bf16[2,192,128]{2,1,0:T(8,128)(2,1)S(1)}, bf16[2,192,128]{2,1,0:T(8,128)(2,1)S(1)}, u32[]{:S(2)}, u32[]{:S(2)}) collective-permute-start(bf16[2,192,128]{2,1,0:T(8,128)(2,1)S(1)} %get-tuple-element.12), channel_id=1, source_target_pairs={{0,1},{1,0},{2,3},{3,2},{4,5},{5,4},{6,7},{7,6},{8,9},{9,8},{10,11... | collective-permute-start | bytes 294920 | tf_op jit(solution)/shard_map/ppermute | solution.py:53
  49.6 4.5 %collective-permute-start.7 = (f32[1,320,256]{2,1,0:T(8,128)S(1)}, f32[1,320,256]{2,1,0:T(8,128)S(1)}, u32[]{:S(2)}, u32[]{:S(2)}) collective-permute-start(f32[1,320,256]{2,1,0:T(8,128)S(1)} %dynamic-slice_bitcast_fusion), channel_id=1, source_target_pairs={{0,8},{8,0},{16,24},{24,16},{32,40},{40,32},{48,56},{56,48},{64,72... | collective-permute-start | bytes 983048 | tf_op jit(solution)/shard_map/ppermute | solution.py:45
  54.2 7.3 %collective-permute-start.8 = (f32[1,320,128]{2,1,0:T(8,128)S(1)}, f32[1,320,128]{2,1,0:T(8,128)S(1)}, u32[]{:S(2)}, u32[]{:S(2)}) collective-permute-start(f32[1,320,128]{2,1,0:T(8,128)S(1)} %constant_dynamic-slice_fusion.1), channel_id=1, source_target_pairs={{0,16},{8,24},{16,0},{24,8},{32,48},{40,56},{48,32},{56,40},{64,80... | collective-permute-start | bytes 491528 | tf_op jit(solution)/shard_map/ppermute | solution.py:45
  61.5 5.2 %collective-permute-start.9 = (f32[1,160,128]{2,1,0:T(8,128)S(1)}, f32[1,160,128]{2,1,0:T(8,128)S(1)}, u32[]{:S(2)}, u32[]{:S(2)}) collective-permute-start(f32[1,160,128]{2,1,0:T(8,128)S(1)} %constant_dynamic-slice_fusion), channel_id=1, source_target_pairs={{0,64},{8,72},{16,80},{24,88},{32,96},{40,104},{48,112},{56,120},{... | collective-permute-start | bytes 245768 | tf_op jit(solution)/shard_map/ppermute | solution.py:45
  66.7 6.7 %collective-permute-start.10 = (f32[1,160,128]{2,1,0:T(8,128)S(1)}, f32[1,160,128]{2,1,0:T(8,128)S(1)}, u32[]{:S(2)}, u32[]{:S(2)}) collective-permute-start(f32[1,160,128]{2,1,0:T(8,128)S(1)} %dynamic-slice_add_fusion.2), channel_id=1, source_target_pairs={{0,32},{8,40},{16,48},{24,56},{32,0},{40,8},{48,16},{56,24},{64,96... | collective-permute-start | bytes 245768 | tf_op jit(solution)/shard_map/ppermute | solution.py:34
  73.4 6.1 %collective-permute-start.11 = (f32[1,160,128]{2,1,0:T(8,128)S(1)}, f32[1,160,128]{2,1,0:T(8,128)S(1)}, u32[]{:S(2)}, u32[]{:S(2)}) collective-permute-start(f32[1,160,128]{2,1,0:T(8,128)S(1)} %add.103), channel_id=1, source_target_pairs={{0,128},{8,136},{16,144},{24,152},{32,160},{40,168},{48,176},{56,1... | collective-permute-start | bytes 245768 | tf_op jit(solution)/shard_map/ppermute | solution.py:34
  79.5 8.5 %copy-start.2 = (f32[2,192,32]{1,2,0:T(8,128)S(1)}, f32[2,192,32]{1,2,0:T(8,128)}, u32[]{:S(2)}) copy-start(f32[2,192,32]{1,2,0:T(8,128)} %param.8) | copy-start | bytes 147460
  79.5 10.4 %collective-permute-start.12 = (f32[1,160,128]{2,1,0:T(8,128)S(1)}, f32[1,160,128]{2,1,0:T(8,128)S(1)}, u32[]{:S(2)}, u32[]{:S(2)}) collective-permute-start(f32[1,160,128]{2,1,0:T(8,128)S(1)} %add.104), channel_id=1, source_target_pairs={{0,256},{8,264},{16,272},{24,280},{32,288},{40,296},{48,304},{56,3... | collective-permute-start | bytes 245768 | tf_op jit(solution)/shard_map/ppermute | solution.py:34
  88.0 0.8 copy-start.3
  89.9 6.4 %collective-permute-start.13 = (f32[1,160,128]{2,1,0:T(8,128)S(1)}, f32[1,160,128]{2,1,0:T(8,128)S(1)}, u32[]{:S(2)}, u32[]{:S(2)}) collective-permute-start(f32[1,160,128]{2,1,0:T(8,128)S(1)} %add.105), channel_id=1, source_target_pairs={{0,64},{8,72},{16,80},{24,88},{32,96},{40,104},{48,112},{56,120},{... | collective-permute-start | bytes 245768 | tf_op jit(solution)/shard_map/ppermute | solution.py:53
  93.0 6.5 %collective-permute-start.3 = (bf16[2,192,32]{2,1,0:T(8,128)(2,1)S(1)}, bf16[2,192,32]{2,1,0:T(8,128)(2,1)S(1)}, u32[]{:S(2)}, u32[]{:S(2)}) collective-permute-start(bf16[2,192,32]{2,1,0:T(8,128)(2,1)S(1)} %get-tuple-element.14), channel_id=1, source_target_pairs={{0,1},{1,0},{2,3},{3,2},{4,5},{5,4},{6,7},{7,6},{8,9},{9,8},{10,11... | collective-permute-start | bytes 73736 | tf_op jit(solution)/shard_map/ppermute | solution.py:53
  96.4 6.1 %collective-permute-start.14 = (f32[1,320,128]{2,1,0:T(8,128)S(1)}, f32[1,320,128]{2,1,0:T(8,128)S(1)}, u32[]{:S(2)}, u32[]{:S(2)}) collective-permute-start(f32[1,320,128]{2,1,0:T(8,128)S(1)} %pad_maximum_fusion.1), channel_id=1, source_target_pairs={{0,16},{8,24},{16,0},{24,8},{32,48},{40,56},{48,32},{56,40},{64,80... | collective-permute-start | bytes 491528 | tf_op jit(solution)/shard_map/ppermute | solution.py:53
  99.6 7.1 %collective-permute-start.4 = (bf16[2,192,64]{2,1,0:T(8,128)(2,1)S(1)}, bf16[2,192,64]{2,1,0:T(8,128)(2,1)S(1)}, u32[]{:S(2)}, u32[]{:S(2)}) collective-permute-start(bf16[2,192,64]{2,1,0:T(8,128)(2,1)S(1)} %pad_maximum_fusion.3), channel_id=1, source_target_pairs={{0,2},{1,3},{2,0},{3,1},{4,6},{5,7},{6,4},{7,5},{8,10},{9,11},{10,... | collective-permute-start | bytes 147464 | tf_op jit(solution)/shard_map/ppermute | solution.py:53
  103.8 5.8 %collective-permute-start.15 = (f32[1,257,128]{2,1,0:T(8,128)S(1)}, f32[1,257,128]{2,1,0:T(8,128)S(1)}, u32[]{:S(2)}, u32[]{:S(2)}) collective-permute-start(f32[1,257,128]{2,1,0:T(8,128)S(1)} %pad_maximum_fusion.2), channel_id=1, source_target_pairs={{0,1},{1,0},{2,3},{3,2},{4,5},{5,4},{6,7},{7,6},{8,9},{9,8},{10,11... | collective-permute-start | bytes 394760 | tf_op jit(solution)/shard_map/ppermute | solution.py:34
  109.6 11.9 %collective-permute-start.16 = (f32[1,257,128]{2,1,0:T(8,128)S(1)}, f32[1,257,128]{2,1,0:T(8,128)S(1)}, u32[]{:S(2)}, u32[]{:S(2)}) collective-permute-start(f32[1,257,128]{2,1,0:T(8,128)S(1)} %fusion.30), channel_id=1, source_target_pairs={{0,2},{1,3},{2,0},{3,1},{4,6},{5,7},{6,4},{7,5},{8,10},{9,11},{10,... | collective-permute-start | bytes 394760 | tf_op jit(solution)/shard_map/ppermute | solution.py:34
  113.1 10.7 %collective-permute-start.5 = (bf16[2,192,128]{2,1,0:T(8,128)(2,1)S(1)}, bf16[2,192,128]{2,1,0:T(8,128)(2,1)S(1)}, u32[]{:S(2)}, u32[]{:S(2)}) collective-permute-start(bf16[2,192,128]{2,1,0:T(8,128)(2,1)S(1)} %pad_maximum_fusion.4), channel_id=1, source_target_pairs={{0,4},{1,5},{2,6},{3,7},{4,0},{5,1},{6,2},{7,3},{8,12},{9,13},{10,... | collective-permute-start | bytes 294920 | tf_op jit(solution)/shard_map/ppermute | solution.py:53
  121.5 11.1 %collective-permute-start.17 = (f32[1,257,128]{2,1,0:T(8,128)S(1)}, f32[1,257,128]{2,1,0:T(8,128)S(1)}, u32[]{:S(2)}, u32[]{:S(2)}) collective-permute-start(f32[1,257,128]{2,1,0:T(8,128)S(1)} %add.107), channel_id=1, source_target_pairs={{0,4},{1,5},{2,6},{3,7},{4,0},{5,1},{6,2},{7,3},{8,12},{9,13},{10,... | collective-permute-start | bytes 394760 | tf_op jit(solution)/shard_map/ppermute | solution.py:34
  134.3 12.6 %copy-start.1 = (f32[2,192,320]{2,1,0:T(8,128)S(1)}, f32[2,192,320]{2,1,0:T(8,128)}, u32[]{:S(2)}) copy-start(f32[2,192,320]{2,1,0:T(8,128)} %param.6) | copy-start | bytes 1474564
  134.8 13.2 %collective-permute-start.18 = (bf16[1,320,256]{2,1,0:T(8,128)(2,1)S(1)}, bf16[1,320,256]{2,1,0:T(8,128)(2,1)S(1)}, u32[]{:S(2)}, u32[]{:S(2)}) collective-permute-start(bf16[1,320,256]{2,1,0:T(8,128)(2,1)S(1)} %fusion.4), channel_id=1, source_target_pairs={{0,8},{8,0},{16,24},{24,16},{32,40},{40,32},{48,56},{56,48},{64,72... | collective-permute-start | bytes 491528 | tf_op jit(solution)/shard_map/ppermute | solution.py:53

commit v11 on v10

--- a/solution.py
+++ b/solution.py
@@ -110,7 +110,8 @@
     own = lax.dynamic_slice_in_dim(half, own_place * width, width, 2)
     first_next, second_next, normal_half = adam_share(own, first_moment, second_moment)
     projected_half = doubling_gather(half.astype(jnp.bfloat16), "tp", tp, [(0, 2)])
-    normal_full = doubling_gather(normal_half, "tp", tp, list(reversed(tp_bits)))
+    last = len(tp_bits) - 1
+    normal_part = doubling_gather(normal_half, "tp", tp, list(reversed(tp_bits[:last])))
 
     image_part = jnp.einsum("mfd,mfr->mdr", grads, projected_half, preferred_element_type=jnp.float32)
     stages = [(0, 0), (1, 2), (3, 1)]
@@ -118,11 +119,17 @@
     chunk = butterfly_sum(chunk, "fsdp", fsdp, [b for b in range(fsdp.bit_length() - 1) if b not in (0, 1, 3)])
     image = doubling_gather(chunk, "fsdp", fsdp, stages[1:])
 
+    packed = pack_gram(jnp.einsum("mdr,mds->mrs", image, image, precision=highest))
+    packed = butterfly_sum(packed, "tp", tp, range(last))
+    packed_rows = packed.size // 128
+    message = jnp.concatenate([packed.reshape(packed_rows, 128), normal_part.astype(jnp.float32).reshape(-1, 128)], axis=0)
+    arrived = lax.ppermute(message, "tp", partner_perm(tp, last))
+    gram = unpack_gram(packed + arrived[:packed_rows].reshape(packed.shape))
+    other = arrived[packed_rows:].reshape(normal_part.shape).astype(jnp.bfloat16)
+    high = (lax.axis_index("tp") >> last) & 1
+    normal_full = jnp.concatenate([jnp.where(high == 0, normal_part, other), jnp.where(high == 0, other, normal_part)], axis=2)
     update = jnp.einsum("mfr,dmr->mfd", normal_full, basis, preferred_element_type=jnp.float32)
     weight_next = weights - LEARNING_RATE * GALORE_SCALE * update
-
-    packed = pack_gram(jnp.einsum("mdr,mds->mrs", image, image, precision=highest))
-    gram = unpack_gram(butterfly_sum(packed, "tp", tp))
     diagonal = lax.broadcasted_iota(jnp.int32, gram.shape, 1) == lax.broadcasted_iota(jnp.int32, gram.shape, 2)
     total = jnp.sum(jnp.where(diagonal, gram, 0.0), axis=(1, 2)) + EPSILON_NORM
     factor = jnp.sqrt(rank_width / total)

time: 151 us -> 159 us (1.053)
  starting transfers between devices: 92.5 us -> 99.6 us
  waiting for transfers between devices: 44.2 us -> 45.9 us
    ppermute x0 -> x1, starting transfers between devices: none -> 7.21 us  [shards(): arrived = lax.ppermute(message, 'tp', partner_perm(tp, last))]
    ppermute x0 -> x1, waiting for transfers between devices: none -> 6.38 us  [shards(): arrived = lax.ppermute(message, 'tp', partner_perm(tp, last))]
    ppermute x8 -> x7, waiting for transfers between devices: 27.4 us -> 21.1 us  [butterfly_sum(): value = value + lax.ppermute(value, axis, partner_perm(size, bit))]
    ppermute x8 -> x7, starting transfers between devices: 47.3 us -> 44.8 us  [butterfly_sum(): value = value + lax.ppermute(value, axis, partner_perm(size, bit))]
    ppermute x7 -> x6, starting transfers between devices: 30.7 us -> 33.2 us  [doubling_gather(): other = lax.ppermute(value, axis, partner_perm(size, bit))]
    ppermute x7 -> x6, waiting for transfers between devices: 6.55 us -> 8.03 us  [doubling_gather(): other = lax.ppermute(value, axis, partner_perm(size, bit))]
  transfers between devices with their start and end apart: 19 -> 18, of which waited for: 15 -> 16; matrix products, arithmetic and copies ran while one was open for 3% -> 3% of each run, Pallas kernels for 0% -> 0%
where the time goes in v11:
time: 159 us; the launch traced here: 158 us
  starting transfers between devices  99.6 us (63%)
  waiting for transfers between devices  45.9 us (29%)
  local copies, waits for them, and re-layouts  5.77 us (4%)
  matrix products  3.02 us (2%)
  other arithmetic  1.98 us (1%)
  between operations  1.94 us (1%)
    ppermute x7, starting transfers between devices, butterfly_sum(): value = value + lax.ppermute(value, axis, partner_perm(size, bit))  44.8 us
    ppermute x6, starting transfers between devices, doubling_gather(): other = lax.ppermute(value, axis, partner_perm(size, bit))  33.2 us
    ppermute x7, waiting for transfers between devices, butterfly_sum(): value = value + lax.ppermute(value, axis, partner_perm(size, bit))  21.1 us
    ppermute x4, starting transfers between devices, halving_scatter(): value = keep + lax.ppermute(send, axis, partner_perm(size, bit))  14.5 us
    ppermute x4, waiting for transfers between devices, halving_scatter(): value = keep + lax.ppermute(send, axis, partner_perm(size, bit))  10.3 us
    ppermute x6, waiting for transfers between devices, doubling_gather(): other = lax.ppermute(value, axis, partner_perm(size, bit))  8.03 us
    ppermute x1, starting transfers between devices, shards(): arrived = lax.ppermute(message, 'tp', partner_perm(tp, last))  7.21 us
    ppermute x1, waiting for transfers between devices, shards(): arrived = lax.ppermute(message, 'tp', partner_perm(tp, last))  6.38 us
  transfers between devices with their start and end apart: 18, of which 16 were waited for; matrix products, arithmetic and copies ran while one was open for 3% of the time, Pallas kernels for 0%

profile of v11, /device:TPU:1, one launch (start us, length us, event | category | flops | bytes accessed | tf_op | source)
XLA Modules:
  0.0 158.2 jit_solution(7265611637408494490)
XLA Ops:
  0.6 0.0 copy-start
  0.7 1.3 copy.23
  2.0 0.1 copy.24
  2.1 0.3 fusion.36
  2.4 4.8 %collective-permute-start = (f32[2,192,128]{2,1,0:T(8,128)S(1)}, f32[2,192,128]{2,1,0:T(8,128)S(1)}, u32[]{:S(2)}, u32[]{:S(2)}) collective-permute-start(f32[2,192,128]{2,1,0:T(8,128)S(1)} %constant_dynamic-slice_fusion.2), channel_id=1, source_target_pairs={{0,1},{1,0},{2,3},{3,2},{4,5},{5,4},{6,7},{7,6},{8,9},{9,8},{10,11... | collective-permute-start | bytes 589832 | tf_op jit(solution)/shard_map/ppermute | solution.py:45
  7.3 3.0 %collective-permute-done = f32[2,192,128]{2,1,0:T(8,128)S(1)} collective-permute-done((f32[2,192,128]{2,1,0:T(8,128)S(1)}, f32[2,192,128]{2,1,0:T(8,128)S(1)}, u32[]{:S(2)}, u32[]{:S(2)}) %collective-permute-start) | collective-permute-done | bytes 196640 | tf_op jit(solution)/shard_map/ppermute | solution.py:45
  10.3 11.3 %collective-permute-start.1 = (f32[2,192,128]{2,1,0:T(8,128)S(1)}, f32[2,192,128]{2,1,0:T(8,128)S(1)}, u32[]{:S(2)}, u32[]{:S(2)}) collective-permute-start(f32[2,192,128]{2,1,0:T(8,128)S(1)} %dynamic-slice_add_fusion), channel_id=1, source_target_pairs={{0,4},{1,5},{2,6},{3,7},{4,0},{5,1},{6,2},{7,3},{8,12},{9,13},{10,... | collective-permute-start | bytes 589832 | tf_op jit(solution)/shard_map/ppermute | solution.py:34
  21.6 3.1 %collective-permute-done.1 = f32[2,192,128]{2,1,0:T(8,128)S(1)} collective-permute-done((f32[2,192,128]{2,1,0:T(8,128)S(1)}, f32[2,192,128]{2,1,0:T(8,128)S(1)}, u32[]{:S(2)}, u32[]{:S(2)}) %collective-permute-start.1) | collective-permute-done | bytes 196640 | tf_op jit(solution)/shard_map/ppermute | solution.py:34
  24.8 10.4 %collective-permute-start.2 = (f32[2,192,128]{2,1,0:T(8,128)S(1)}, f32[2,192,128]{2,1,0:T(8,128)S(1)}, u32[]{:S(2)}, u32[]{:S(2)}) collective-permute-start(f32[2,192,128]{2,1,0:T(8,128)S(1)} %add.86), channel_id=1, source_target_pairs={{0,2},{1,3},{2,0},{3,1},{4,6},{5,7},{6,4},{7,5},{8,10},{9,11},{10,... | collective-permute-start | bytes 589832 | tf_op jit(solution)/shard_map/ppermute | solution.py:34
  35.2 8.2 %collective-permute-done.2 = f32[2,192,128]{2,1,0:T(8,128)S(1)} collective-permute-done((f32[2,192,128]{2,1,0:T(8,128)S(1)}, f32[2,192,128]{2,1,0:T(8,128)S(1)}, u32[]{:S(2)}, u32[]{:S(2)}) %collective-permute-start.2) | collective-permute-done | bytes 196640 | tf_op jit(solution)/shard_map/ppermute | solution.py:34
  43.5 1.9 %collective-permute-start.5 = (bf16[2,192,128]{2,1,0:T(8,128)(2,1)S(1)}, bf16[2,192,128]{2,1,0:T(8,128)(2,1)S(1)}, u32[]{:S(2)}, u32[]{:S(2)}) collective-permute-start(bf16[2,192,128]{2,1,0:T(8,128)(2,1)S(1)} %get-tuple-element.12), channel_id=1, source_target_pairs={{0,1},{1,0},{2,3},{3,2},{4,5},{5,4},{6,7},{7,6},{8,9},{9,8},{10,11... | collective-permute-start | bytes 294920 | tf_op jit(solution)/shard_map/ppermute | solution.py:53
  45.4 3.8 %collective-permute-done.5 = bf16[2,192,128]{2,1,0:T(8,128)(2,1)S(1)} collective-permute-done((bf16[2,192,128]{2,1,0:T(8,128)(2,1)S(1)}, bf16[2,192,128]{2,1,0:T(8,128)(2,1)S(1)}, u32[]{:S(2)}, u32[]{:S(2)}) %collective-permute-start.5) | collective-permute-done | bytes 98336 | tf_op jit(solution)/shard_map/ppermute | solution.py:53
  49.3 0.3 fusion.11
  49.6 3.2 %collective-permute-start.6 = (f32[1,320,256]{2,1,0:T(8,128)S(1)}, f32[1,320,256]{2,1,0:T(8,128)S(1)}, u32[]{:S(2)}, u32[]{:S(2)}) collective-permute-start(f32[1,320,256]{2,1,0:T(8,128)S(1)} %dynamic-slice_bitcast_fusion), channel_id=1, source_target_pairs={{0,8},{8,0},{16,24},{24,16},{32,40},{40,32},{48,56},{56,48},{64,72... | collective-permute-start | bytes 983048 | tf_op jit(solution)/shard_map/ppermute | solution.py:45
  52.9 1.2 collective-permute-done.6
  54.2 3.2 %collective-permute-start.7 = (f32[1,320,128]{2,1,0:T(8,128)S(1)}, f32[1,320,128]{2,1,0:T(8,128)S(1)}, u32[]{:S(2)}, u32[]{:S(2)}) collective-permute-start(f32[1,320,128]{2,1,0:T(8,128)S(1)} %constant_dynamic-slice_fusion.1), channel_id=1, source_target_pairs={{0,16},{8,24},{16,0},{24,8},{32,48},{40,56},{48,32},{56,40},{64,80... | collective-permute-start | bytes 491528 | tf_op jit(solution)/shard_map/ppermute | solution.py:45
  57.3 4.1 %collective-permute-done.7 = f32[1,320,128]{2,1,0:T(8,128)S(1)} collective-permute-done((f32[1,320,128]{2,1,0:T(8,128)S(1)}, f32[1,320,128]{2,1,0:T(8,128)S(1)}, u32[]{:S(2)}, u32[]{:S(2)}) %collective-permute-start.7) | collective-permute-done | bytes 163872 | tf_op jit(solution)/shard_map/ppermute | solution.py:45
  61.5 3.2 %collective-permute-start.8 = (f32[1,160,128]{2,1,0:T(8,128)S(1)}, f32[1,160,128]{2,1,0:T(8,128)S(1)}, u32[]{:S(2)}, u32[]{:S(2)}) collective-permute-start(f32[1,160,128]{2,1,0:T(8,128)S(1)} %constant_dynamic-slice_fusion), channel_id=1, source_target_pairs={{0,64},{8,72},{16,80},{24,88},{32,96},{40,104},{48,112},{56,120},{... | collective-permute-start | bytes 245768 | tf_op jit(solution)/shard_map/ppermute | solution.py:45
  64.7 1.9 %collective-permute-done.8 = f32[1,160,128]{2,1,0:T(8,128)S(1)} collective-permute-done((f32[1,160,128]{2,1,0:T(8,128)S(1)}, f32[1,160,128]{2,1,0:T(8,128)S(1)}, u32[]{:S(2)}, u32[]{:S(2)}) %collective-permute-start.8) | collective-permute-done | bytes 81952 | tf_op jit(solution)/shard_map/ppermute | solution.py:45
  66.7 4.7 %collective-permute-start.9 = (f32[1,160,128]{2,1,0:T(8,128)S(1)}, f32[1,160,128]{2,1,0:T(8,128)S(1)}, u32[]{:S(2)}, u32[]{:S(2)}) collective-permute-start(f32[1,160,128]{2,1,0:T(8,128)S(1)} %dynamic-slice_add_fusion.2), channel_id=1, source_target_pairs={{0,32},{8,40},{16,48},{24,56},{32,0},{40,8},{48,16},{56,24},{64,96... | collective-permute-start | bytes 245768 | tf_op jit(solution)/shard_map/ppermute | solution.py:34
  71.4 2.0 %collective-permute-done.9 = f32[1,160,128]{2,1,0:T(8,128)S(1)} collective-permute-done((f32[1,160,128]{2,1,0:T(8,128)S(1)}, f32[1,160,128]{2,1,0:T(8,128)S(1)}, u32[]{:S(2)}, u32[]{:S(2)}) %collective-permute-start.9) | collective-permute-done | bytes 81952 | tf_op jit(solution)/shard_map/ppermute | solution.py:34
  73.4 4.3 %collective-permute-start.10 = (f32[1,160,128]{2,1,0:T(8,128)S(1)}, f32[1,160,128]{2,1,0:T(8,128)S(1)}, u32[]{:S(2)}, u32[]{:S(2)}) collective-permute-start(f32[1,160,128]{2,1,0:T(8,128)S(1)} %add.103), channel_id=1, source_target_pairs={{0,128},{8,136},{16,144},{24,152},{32,160},{40,168},{48,176},{56,1... | collective-permute-start | bytes 245768 | tf_op jit(solution)/shard_map/ppermute | solution.py:34
  77.7 1.8 %collective-permute-done.10 = f32[1,160,128]{2,1,0:T(8,128)S(1)} collective-permute-done((f32[1,160,128]{2,1,0:T(8,128)S(1)}, f32[1,160,128]{2,1,0:T(8,128)S(1)}, u32[]{:S(2)}, u32[]{:S(2)}) %collective-permute-start.10) | collective-permute-done | bytes 81952 | tf_op jit(solution)/shard_map/ppermute | solution.py:34
  79.5 8.4 %collective-permute-start.11 = (f32[1,160,128]{2,1,0:T(8,128)S(1)}, f32[1,160,128]{2,1,0:T(8,128)S(1)}, u32[]{:S(2)}, u32[]{:S(2)}) collective-permute-start(f32[1,160,128]{2,1,0:T(8,128)S(1)} %add.104), channel_id=1, source_target_pairs={{0,256},{8,264},{16,272},{24,280},{32,288},{40,296},{48,304},{56,3... | collective-permute-start | bytes 245768 | tf_op jit(solution)/shard_map/ppermute | solution.py:34
  87.9 1.9 %collective-permute-done.11 = f32[1,160,128]{2,1,0:T(8,128)S(1)} collective-permute-done((f32[1,160,128]{2,1,0:T(8,128)S(1)}, f32[1,160,128]{2,1,0:T(8,128)S(1)}, u32[]{:S(2)}, u32[]{:S(2)}) %collective-permute-start.11) | collective-permute-done | bytes 81952 | tf_op jit(solution)/shard_map/ppermute | solution.py:34
  89.8 3.1 %collective-permute-start.12 = (f32[1,160,128]{2,1,0:T(8,128)S(1)}, f32[1,160,128]{2,1,0:T(8,128)S(1)}, u32[]{:S(2)}, u32[]{:S(2)}) collective-permute-start(f32[1,160,128]{2,1,0:T(8,128)S(1)} %add.105), channel_id=1, source_target_pairs={{0,64},{8,72},{16,80},{24,88},{32,96},{40,104},{48,112},{56,120},{... | collective-permute-start | bytes 245768 | tf_op jit(solution)/shard_map/ppermute | solution.py:53
  92.9 0.0 copy-start.3
  92.9 0.1 copy.22
  93.0 0.7 copy-done.3
  93.7 0.1 copy.26
  93.9 2.3 %collective-permute-done.12 = f32[1,160,128]{2,1,0:T(8,128)S(1)} collective-permute-done((f32[1,160,128]{2,1,0:T(8,128)S(1)}, f32[1,160,128]{2,1,0:T(8,128)S(1)}, u32[]{:S(2)}, u32[]{:S(2)}) %collective-permute-start.12) | collective-permute-done | bytes 81952 | tf_op jit(solution)/shard_map/ppermute | solution.py:53
  96.2 3.1 %collective-permute-start.13 = (f32[1,320,128]{2,1,0:T(8,128)S(1)}, f32[1,320,128]{2,1,0:T(8,128)S(1)}, u32[]{:S(2)}, u32[]{:S(2)}) collective-permute-start(f32[1,320,128]{2,1,0:T(8,128)S(1)} %pad_maximum_fusion.2), channel_id=1, source_target_pairs={{0,16},{8,24},{16,0},{24,8},{32,48},{40,56},{48,32},{56,40},{64,80... | collective-permute-start | bytes 491528 | tf_op jit(solution)/shard_map/ppermute | solution.py:53
  99.4 0.2 divide_convert_fusion
  99.6 1.9 %collective-permute-start.3 = (bf16[2,192,32]{2,1,0:T(8,128)(2,1)S(1)}, bf16[2,192,32]{2,1,0:T(8,128)(2,1)S(1)}, u32[]{:S(2)}, u32[]{:S(2)}) collective-permute-start(bf16[2,192,32]{2,1,0:T(8,128)(2,1)S(1)} %get-tuple-element.14), channel_id=1, source_target_pairs={{0,1},{1,0},{2,3},{3,2},{4,5},{5,4},{6,7},{7,6},{8,9},{9,8},{10,11... | collective-permute-start | bytes 73736 | tf_op jit(solution)/shard_map/ppermute | solution.py:53
  101.5 0.8 collective-permute-done.13
  102.3 0.9 convolution_bitcast_fusion
  103.2 0.1 copy.40
  103.3 0.1 copy.41
  103.4 0.1 fusion.26
  103.5 0.1 copy.29
  103.7 2.6 %collective-permute-start.14 = (f32[1,257,128]{2,1,0:T(8,128)S(1)}, f32[1,257,128]{2,1,0:T(8,128)S(1)}, u32[]{:S(2)}, u32[]{:S(2)}) collective-permute-start(f32[1,257,128]{2,1,0:T(8,128)S(1)} %pad_maximum_fusion.3), channel_id=1, source_target_pairs={{0,1},{1,0},{2,3},{3,2},{4,5},{5,4},{6,7},{7,6},{8,9},{9,8},{10,11... | collective-permute-start | bytes 394760 | tf_op jit(solution)/shard_map/ppermute | solution.py:34
  106.3 0.1 pad_maximum_fusion.4
  106.4 2.6 %collective-permute-start.4 = (bf16[2,192,64]{2,1,0:T(8,128)(2,1)S(1)}, bf16[2,192,64]{2,1,0:T(8,128)(2,1)S(1)}, u32[]{:S(2)}, u32[]{:S(2)}) collective-permute-start(bf16[2,192,64]{2,1,0:T(8,128)(2,1)S(1)} %pad_maximum_fusion.4), channel_id=1, source_target_pairs={{0,2},{1,3},{2,0},{3,1},{4,6},{5,7},{6,4},{7,5},{8,10},{9,11},{10,... | collective-permute-start | bytes 147464 | tf_op jit(solution)/shard_map/ppermute | solution.py:53
  109.1 0.4 collective-permute-done.14
  109.4 3.2 %collective-permute-start.15 = (f32[1,257,128]{2,1,0:T(8,128)S(1)}, f32[1,257,128]{2,1,0:T(8,128)S(1)}, u32[]{:S(2)}, u32[]{:S(2)}) collective-permute-start(f32[1,257,128]{2,1,0:T(8,128)S(1)} %fusion.31), channel_id=1, source_target_pairs={{0,2},{1,3},{2,0},{3,1},{4,6},{5,7},{6,4},{7,5},{8,10},{9,11},{10,... | collective-permute-start | bytes 394760 | tf_op jit(solution)/shard_map/ppermute | solution.py:34
  112.6 1.1 collective-permute-done.4
  113.7 0.1 broadcast_select_fusion.7
  113.9 0.1 maximum_convert_fusion
  114.0 3.7 %collective-permute-done.15 = f32[1,257,128]{2,1,0:T(8,128)S(1)} collective-permute-done((f32[1,257,128]{2,1,0:T(8,128)S(1)}, f32[1,257,128]{2,1,0:T(8,128)S(1)}, u32[]{:S(2)}, u32[]{:S(2)}) %collective-permute-start.15) | collective-permute-done | bytes 131616 | tf_op jit(solution)/shard_map/ppermute | solution.py:34
  117.7 7.2 %collective-permute-start.16 = (f32[641,128]{1,0:T(8,128)S(1)}, f32[641,128]{1,0:T(8,128)S(1)}, u32[]{:S(2)}, u32[]{:S(2)}) collective-permute-start(f32[641,128]{1,0:T(8,128)S(1)} %pad_maximum_fusion), channel_id=1, source_target_pairs={{0,4},{1,5},{2,6},{3,7},{4,0},{5,1},{6,2},{7,3},{8,12},{9,13},{10,... | collective-permute-start | bytes 984584 | tf_op jit(solution)/shard_map/ppermute | solution.py:126
  124.9 0.7 copy.36
  125.7 0.7 copy.37
  126.4 6.4 %collective-permute-done.16 = f32[641,128]{1,0:T(8,128)S(1)} collective-permute-done((f32[641,128]{1,0:T(8,128)S(1)}, f32[641,128]{1,0:T(8,128)S(1)}, u32[]{:S(2)}, u32[]{:S(2)}) %collective-permute-start.16) | collective-permute-done | bytes 328224 | tf_op jit(solution)/shard_map/ppermute | solution.py:126
  132.8 0.1 copy.42
  132.9 0.1 copy.33
  133.0 0.1 bitcast_select_fusion
  133.1 0.6 fusion.7
  134.5 0.5 fusion.4
  135.0 20.5 %collective-permute-start.17 = (bf16[1,320,256]{2,1,0:T(8,128)(2,1)S(1)}, bf16[1,320,256]{2,1,0:T(8,128)(2,1)S(1)}, u32[]{:S(2)}, u32[]{:S(2)}) collective-permute-start(bf16[1,320,256]{2,1,0:T(8,128)(2,1)S(1)} %fusion.4), channel_id=1, source_target_pairs={{0,8},{8,0},{16,24},{24,16},{32,40},{40,32},{48,56},{56,48},{64,72... | collective-permute-start | bytes 491528 | tf_op jit(solution)/shard_map/ppermute | solution.py:53
  155.6 0.1 broadcast_select_fusion.9
  155.7 1.1 fusion
  156.9 0.2 copy.34
  157.1 0.1 copy.35
  157.1 1.1 copy.38
  (37 shorter events, 0.6 us)
Async XLA Ops:
  0.6 1.4 copy-start
  2.4 7.9 %collective-permute-start = (f32[2,192,128]{2,1,0:T(8,128)S(1)}, f32[2,192,128]{2,1,0:T(8,128)S(1)}, u32[]{:S(2)}, u32[]{:S(2)}) collective-permute-start(f32[2,192,128]{2,1,0:T(8,128)S(1)} %constant_dynamic-slice_fusion.2), channel_id=1, source_target_pairs={{0,1},{1,0},{2,3},{3,2},{4,5},{5,4},{6,7},{7,6},{8,9},{9,8},{10,11... | collective-permute-start | bytes 589832 | tf_op jit(solution)/shard_map/ppermute | solution.py:45
  10.3 14.4 %collective-permute-start.1 = (f32[2,192,128]{2,1,0:T(8,128)S(1)}, f32[2,192,128]{2,1,0:T(8,128)S(1)}, u32[]{:S(2)}, u32[]{:S(2)}) collective-permute-start(f32[2,192,128]{2,1,0:T(8,128)S(1)} %dynamic-slice_add_fusion), channel_id=1, source_target_pairs={{0,4},{1,5},{2,6},{3,7},{4,0},{5,1},{6,2},{7,3},{8,12},{9,13},{10,... | collective-permute-start | bytes 589832 | tf_op jit(solution)/shard_map/ppermute | solution.py:34
  24.8 18.7 %collective-permute-start.2 = (f32[2,192,128]{2,1,0:T(8,128)S(1)}, f32[2,192,128]{2,1,0:T(8,128)S(1)}, u32[]{:S(2)}, u32[]{:S(2)}) collective-permute-start(f32[2,192,128]{2,1,0:T(8,128)S(1)} %add.86), channel_id=1, source_target_pairs={{0,2},{1,3},{2,0},{3,1},{4,6},{5,7},{6,4},{7,5},{8,10},{9,11},{10,... | collective-permute-start | bytes 589832 | tf_op jit(solution)/shard_map/ppermute | solution.py:34
  43.5 5.8 %collective-permute-start.5 = (bf16[2,192,128]{2,1,0:T(8,128)(2,1)S(1)}, bf16[2,192,128]{2,1,0:T(8,128)(2,1)S(1)}, u32[]{:S(2)}, u32[]{:S(2)}) collective-permute-start(bf16[2,192,128]{2,1,0:T(8,128)(2,1)S(1)} %get-tuple-element.12), channel_id=1, source_target_pairs={{0,1},{1,0},{2,3},{3,2},{4,5},{5,4},{6,7},{7,6},{8,9},{9,8},{10,11... | collective-permute-start | bytes 294920 | tf_op jit(solution)/shard_map/ppermute | solution.py:53
  49.6 4.5 %collective-permute-start.6 = (f32[1,320,256]{2,1,0:T(8,128)S(1)}, f32[1,320,256]{2,1,0:T(8,128)S(1)}, u32[]{:S(2)}, u32[]{:S(2)}) collective-permute-start(f32[1,320,256]{2,1,0:T(8,128)S(1)} %dynamic-slice_bitcast_fusion), channel_id=1, source_target_pairs={{0,8},{8,0},{16,24},{24,16},{32,40},{40,32},{48,56},{56,48},{64,72... | collective-permute-start | bytes 983048 | tf_op jit(solution)/shard_map/ppermute | solution.py:45
  54.2 7.3 %collective-permute-start.7 = (f32[1,320,128]{2,1,0:T(8,128)S(1)}, f32[1,320,128]{2,1,0:T(8,128)S(1)}, u32[]{:S(2)}, u32[]{:S(2)}) collective-permute-start(f32[1,320,128]{2,1,0:T(8,128)S(1)} %constant_dynamic-slice_fusion.1), channel_id=1, source_target_pairs={{0,16},{8,24},{16,0},{24,8},{32,48},{40,56},{48,32},{56,40},{64,80... | collective-permute-start | bytes 491528 | tf_op jit(solution)/shard_map/ppermute | solution.py:45
  61.5 5.2 %collective-permute-start.8 = (f32[1,160,128]{2,1,0:T(8,128)S(1)}, f32[1,160,128]{2,1,0:T(8,128)S(1)}, u32[]{:S(2)}, u32[]{:S(2)}) collective-permute-start(f32[1,160,128]{2,1,0:T(8,128)S(1)} %constant_dynamic-slice_fusion), channel_id=1, source_target_pairs={{0,64},{8,72},{16,80},{24,88},{32,96},{40,104},{48,112},{56,120},{... | collective-permute-start | bytes 245768 | tf_op jit(solution)/shard_map/ppermute | solution.py:45
  66.7 6.7 %collective-permute-start.9 = (f32[1,160,128]{2,1,0:T(8,128)S(1)}, f32[1,160,128]{2,1,0:T(8,128)S(1)}, u32[]{:S(2)}, u32[]{:S(2)}) collective-permute-start(f32[1,160,128]{2,1,0:T(8,128)S(1)} %dynamic-slice_add_fusion.2), channel_id=1, source_target_pairs={{0,32},{8,40},{16,48},{24,56},{32,0},{40,8},{48,16},{56,24},{64,96... | collective-permute-start | bytes 245768 | tf_op jit(solution)/shard_map/ppermute | solution.py:34
  73.4 6.1 %collective-permute-start.10 = (f32[1,160,128]{2,1,0:T(8,128)S(1)}, f32[1,160,128]{2,1,0:T(8,128)S(1)}, u32[]{:S(2)}, u32[]{:S(2)}) collective-permute-start(f32[1,160,128]{2,1,0:T(8,128)S(1)} %add.103), channel_id=1, source_target_pairs={{0,128},{8,136},{16,144},{24,152},{32,160},{40,168},{48,176},{56,1... | collective-permute-start | bytes 245768 | tf_op jit(solution)/shard_map/ppermute | solution.py:34
  79.5 10.3 %collective-permute-start.11 = (f32[1,160,128]{2,1,0:T(8,128)S(1)}, f32[1,160,128]{2,1,0:T(8,128)S(1)}, u32[]{:S(2)}, u32[]{:S(2)}) collective-permute-start(f32[1,160,128]{2,1,0:T(8,128)S(1)} %add.104), channel_id=1, source_target_pairs={{0,256},{8,264},{16,272},{24,280},{32,288},{40,296},{48,304},{56,3... | collective-permute-start | bytes 245768 | tf_op jit(solution)/shard_map/ppermute | solution.py:34
  89.8 3.1 %copy-start.2 = (f32[2,192,32]{1,2,0:T(8,128)S(1)}, f32[2,192,32]{1,2,0:T(8,128)}, u32[]{:S(2)}) copy-start(f32[2,192,32]{1,2,0:T(8,128)} %param.8) | copy-start | bytes 147460
  89.8 6.4 %collective-permute-start.12 = (f32[1,160,128]{2,1,0:T(8,128)S(1)}, f32[1,160,128]{2,1,0:T(8,128)S(1)}, u32[]{:S(2)}, u32[]{:S(2)}) collective-permute-start(f32[1,160,128]{2,1,0:T(8,128)S(1)} %add.105), channel_id=1, source_target_pairs={{0,64},{8,72},{16,80},{24,88},{32,96},{40,104},{48,112},{56,120},{... | collective-permute-start | bytes 245768 | tf_op jit(solution)/shard_map/ppermute | solution.py:53
  92.9 0.8 copy-start.3
  96.2 6.1 %collective-permute-start.13 = (f32[1,320,128]{2,1,0:T(8,128)S(1)}, f32[1,320,128]{2,1,0:T(8,128)S(1)}, u32[]{:S(2)}, u32[]{:S(2)}) collective-permute-start(f32[1,320,128]{2,1,0:T(8,128)S(1)} %pad_maximum_fusion.2), channel_id=1, source_target_pairs={{0,16},{8,24},{16,0},{24,8},{32,48},{40,56},{48,32},{56,40},{64,80... | collective-permute-start | bytes 491528 | tf_op jit(solution)/shard_map/ppermute | solution.py:53
  99.6 6.7 %collective-permute-start.3 = (bf16[2,192,32]{2,1,0:T(8,128)(2,1)S(1)}, bf16[2,192,32]{2,1,0:T(8,128)(2,1)S(1)}, u32[]{:S(2)}, u32[]{:S(2)}) collective-permute-start(bf16[2,192,32]{2,1,0:T(8,128)(2,1)S(1)} %get-tuple-element.14), channel_id=1, source_target_pairs={{0,1},{1,0},{2,3},{3,2},{4,5},{5,4},{6,7},{7,6},{8,9},{9,8},{10,11... | collective-permute-start | bytes 73736 | tf_op jit(solution)/shard_map/ppermute | solution.py:53
  103.7 5.8 %collective-permute-start.14 = (f32[1,257,128]{2,1,0:T(8,128)S(1)}, f32[1,257,128]{2,1,0:T(8,128)S(1)}, u32[]{:S(2)}, u32[]{:S(2)}) collective-permute-start(f32[1,257,128]{2,1,0:T(8,128)S(1)} %pad_maximum_fusion.3), channel_id=1, source_target_pairs={{0,1},{1,0},{2,3},{3,2},{4,5},{5,4},{6,7},{7,6},{8,9},{9,8},{10,11... | collective-permute-start | bytes 394760 | tf_op jit(solution)/shard_map/ppermute | solution.py:34
  106.4 7.3 %collective-permute-start.4 = (bf16[2,192,64]{2,1,0:T(8,128)(2,1)S(1)}, bf16[2,192,64]{2,1,0:T(8,128)(2,1)S(1)}, u32[]{:S(2)}, u32[]{:S(2)}) collective-permute-start(bf16[2,192,64]{2,1,0:T(8,128)(2,1)S(1)} %pad_maximum_fusion.4), channel_id=1, source_target_pairs={{0,2},{1,3},{2,0},{3,1},{4,6},{5,7},{6,4},{7,5},{8,10},{9,11},{10,... | collective-permute-start | bytes 147464 | tf_op jit(solution)/shard_map/ppermute | solution.py:53
  109.4 8.2 %collective-permute-start.15 = (f32[1,257,128]{2,1,0:T(8,128)S(1)}, f32[1,257,128]{2,1,0:T(8,128)S(1)}, u32[]{:S(2)}, u32[]{:S(2)}) collective-permute-start(f32[1,257,128]{2,1,0:T(8,128)S(1)} %fusion.31), channel_id=1, source_target_pairs={{0,2},{1,3},{2,0},{3,1},{4,6},{5,7},{6,4},{7,5},{8,10},{9,11},{10,... | collective-permute-start | bytes 394760 | tf_op jit(solution)/shard_map/ppermute | solution.py:34
  117.7 15.1 %collective-permute-start.16 = (f32[641,128]{1,0:T(8,128)S(1)}, f32[641,128]{1,0:T(8,128)S(1)}, u32[]{:S(2)}, u32[]{:S(2)}) collective-permute-start(f32[641,128]{1,0:T(8,128)S(1)} %pad_maximum_fusion), channel_id=1, source_target_pairs={{0,4},{1,5},{2,6},{3,7},{4,0},{5,1},{6,2},{7,3},{8,12},{9,13},{10,... | collective-permute-start | bytes 984584 | tf_op jit(solution)/shard_map/ppermute | solution.py:126
  135.0 20.7 %copy-start.1 = (f32[2,192,320]{2,1,0:T(8,128)S(1)}, f32[2,192,320]{2,1,0:T(8,128)}, u32[]{:S(2)}) copy-start(f32[2,192,320]{2,1,0:T(8,128)} %param.6) | copy-start | bytes 1474564
  135.0 21.8 %collective-permute-start.17 = (bf16[1,320,256]{2,1,0:T(8,128)(2,1)S(1)}, bf16[1,320,256]{2,1,0:T(8,128)(2,1)S(1)}, u32[]{:S(2)}, u32[]{:S(2)}) collective-permute-start(bf16[1,320,256]{2,1,0:T(8,128)(2,1)S(1)} %fusion.4), channel_id=1, source_target_pairs={{0,8},{8,0},{16,24},{24,16},{32,40},{40,32},{48,56},{56,48},{64,72... | collective-permute-start | bytes 491528 | tf_op jit(solution)/shard_map/ppermute | solution.py:53

commit v12 on v10

--- a/solution.py
+++ b/solution.py
@@ -102,7 +102,7 @@
 
     projected_part = jnp.einsum("mfd,dmr->mfr", grads, basis_order, preferred_element_type=jnp.float32)
     half = halving_scatter(projected_part, "tp", tp, [(0, 2)])
-    half = butterfly_sum(half, "tp", tp, reversed(range(1, len(tp_bits))))
+    half = butterfly_sum(half, "tp", tp, range(1, len(tp_bits)))
     member = lax.axis_index("tp")
     own_place = 0
     for step, bit in enumerate(reversed(range(1, len(tp_bits)))):

time: 151 us -> 152 us (level); the launches traced: 149 us -> 149 us
    ppermute x8, starting transfers between devices: 47.3 us -> 42.2 us  [butterfly_sum(): value = value + lax.ppermute(value, axis, partner_perm(size, bit))]
    ppermute x7, waiting for transfers between devices: 6.55 us -> 2.83 us  [doubling_gather(): other = lax.ppermute(value, axis, partner_perm(size, bit))]
    ppermute x8, waiting for transfers between devices: 27.4 us -> 31.1 us  [butterfly_sum(): value = value + lax.ppermute(value, axis, partner_perm(size, bit))]
    ppermute x7, starting transfers between devices: 30.7 us -> 33.4 us  [doubling_gather(): other = lax.ppermute(value, axis, partner_perm(size, bit))]
    ppermute x4, starting transfers between devices: 14.5 us -> 16.2 us  [halving_scatter(): value = keep + lax.ppermute(send, axis, partner_perm(size, bit))]
  transfers between devices with their start and end apart: 19 -> 19, of which waited for: 15 -> 13; matrix products, arithmetic and copies ran while one was open for 3% -> 3% of each run, Pallas kernels for 0% -> 0%
where the time goes in v12:
time: 152 us; the launch traced here: 149 us
  starting transfers between devices  91.8 us (60%)
  waiting for transfers between devices  44.4 us (29%)
  local copies, waits for them, and re-layouts  5.75 us (4%)
  matrix products  3 us (2%)
  other arithmetic  1.96 us (1%)
  between operations  1.96 us (1%)
    ppermute x8, starting transfers between devices, butterfly_sum(): value = value + lax.ppermute(value, axis, partner_perm(size, bit))  42.2 us
    ppermute x7, starting transfers between devices, doubling_gather(): other = lax.ppermute(value, axis, partner_perm(size, bit))  33.4 us
    ppermute x8, waiting for transfers between devices, butterfly_sum(): value = value + lax.ppermute(value, axis, partner_perm(size, bit))  31.1 us
    ppermute x4, starting transfers between devices, halving_scatter(): value = keep + lax.ppermute(send, axis, partner_perm(size, bit))  16.2 us
    ppermute x4, waiting for transfers between devices, halving_scatter(): value = keep + lax.ppermute(send, axis, partner_perm(size, bit))  10.4 us
    unnamed x17, local copies, waits for them, and re-layouts  5.12 us
  transfers between devices with their start and end apart: 19, of which 13 were waited for; matrix products, arithmetic and copies ran while one was open for 3% of the time, Pallas kernels for 0%

profile of v12, /device:TPU:1, one launch (start us, length us, event | category | flops | bytes accessed | tf_op | source)
XLA Modules:
  0.0 148.8 jit_solution(15530746182943998517)
XLA Ops:
  0.6 0.0 copy-start
  0.7 1.3 copy.23
  2.0 0.1 copy.24
  2.1 0.3 fusion.35
  2.4 4.8 %collective-permute-start = (f32[2,192,128]{2,1,0:T(8,128)S(1)}, f32[2,192,128]{2,1,0:T(8,128)S(1)}, u32[]{:S(2)}, u32[]{:S(2)}) collective-permute-start(f32[2,192,128]{2,1,0:T(8,128)S(1)} %constant_dynamic-slice_fusion.2), channel_id=1, source_target_pairs={{0,1},{1,0},{2,3},{3,2},{4,5},{5,4},{6,7},{7,6},{8,9},{9,8},{10,11... | collective-permute-start | bytes 589832 | tf_op jit(solution)/shard_map/ppermute | solution.py:45
  7.3 3.0 %collective-permute-done = f32[2,192,128]{2,1,0:T(8,128)S(1)} collective-permute-done((f32[2,192,128]{2,1,0:T(8,128)S(1)}, f32[2,192,128]{2,1,0:T(8,128)S(1)}, u32[]{:S(2)}, u32[]{:S(2)}) %collective-permute-start) | collective-permute-done | bytes 196640 | tf_op jit(solution)/shard_map/ppermute | solution.py:45
  10.3 7.4 %collective-permute-start.1 = (f32[2,192,128]{2,1,0:T(8,128)S(1)}, f32[2,192,128]{2,1,0:T(8,128)S(1)}, u32[]{:S(2)}, u32[]{:S(2)}) collective-permute-start(f32[2,192,128]{2,1,0:T(8,128)S(1)} %dynamic-slice_add_fusion), channel_id=1, source_target_pairs={{0,2},{1,3},{2,0},{3,1},{4,6},{5,7},{6,4},{7,5},{8,10},{9,11},{10,... | collective-permute-start | bytes 589832 | tf_op jit(solution)/shard_map/ppermute | solution.py:34
  17.7 8.4 %collective-permute-done.1 = f32[2,192,128]{2,1,0:T(8,128)S(1)} collective-permute-done((f32[2,192,128]{2,1,0:T(8,128)S(1)}, f32[2,192,128]{2,1,0:T(8,128)S(1)}, u32[]{:S(2)}, u32[]{:S(2)}) %collective-permute-start.1) | collective-permute-done | bytes 196640 | tf_op jit(solution)/shard_map/ppermute | solution.py:34
  26.1 8.4 %collective-permute-start.2 = (f32[2,192,128]{2,1,0:T(8,128)S(1)}, f32[2,192,128]{2,1,0:T(8,128)S(1)}, u32[]{:S(2)}, u32[]{:S(2)}) collective-permute-start(f32[2,192,128]{2,1,0:T(8,128)S(1)} %add.86), channel_id=1, source_target_pairs={{0,4},{1,5},{2,6},{3,7},{4,0},{5,1},{6,2},{7,3},{8,12},{9,13},{10,... | collective-permute-start | bytes 589832 | tf_op jit(solution)/shard_map/ppermute | solution.py:34
  34.6 6.8 %collective-permute-done.2 = f32[2,192,128]{2,1,0:T(8,128)S(1)} collective-permute-done((f32[2,192,128]{2,1,0:T(8,128)S(1)}, f32[2,192,128]{2,1,0:T(8,128)S(1)}, u32[]{:S(2)}, u32[]{:S(2)}) %collective-permute-start.2) | collective-permute-done | bytes 196640 | tf_op jit(solution)/shard_map/ppermute | solution.py:34
  41.4 3.3 %collective-permute-start.6 = (bf16[2,192,128]{2,1,0:T(8,128)(2,1)S(1)}, bf16[2,192,128]{2,1,0:T(8,128)(2,1)S(1)}, u32[]{:S(2)}, u32[]{:S(2)}) collective-permute-start(bf16[2,192,128]{2,1,0:T(8,128)(2,1)S(1)} %get-tuple-element.12), channel_id=1, source_target_pairs={{0,1},{1,0},{2,3},{3,2},{4,5},{5,4},{6,7},{7,6},{8,9},{9,8},{10,11... | collective-permute-start | bytes 294920 | tf_op jit(solution)/shard_map/ppermute | solution.py:53
  44.7 2.0 %collective-permute-done.6 = bf16[2,192,128]{2,1,0:T(8,128)(2,1)S(1)} collective-permute-done((bf16[2,192,128]{2,1,0:T(8,128)(2,1)S(1)}, bf16[2,192,128]{2,1,0:T(8,128)(2,1)S(1)}, u32[]{:S(2)}, u32[]{:S(2)}) %collective-permute-start.6) | collective-permute-done | bytes 98336 | tf_op jit(solution)/shard_map/ppermute | solution.py:53
  46.8 0.3 fusion.14
  47.1 5.1 %collective-permute-start.7 = (f32[1,320,256]{2,1,0:T(8,128)S(1)}, f32[1,320,256]{2,1,0:T(8,128)S(1)}, u32[]{:S(2)}, u32[]{:S(2)}) collective-permute-start(f32[1,320,256]{2,1,0:T(8,128)S(1)} %dynamic-slice_bitcast_fusion), channel_id=1, source_target_pairs={{0,8},{8,0},{16,24},{24,16},{32,40},{40,32},{48,56},{56,48},{64,72... | collective-permute-start | bytes 983048 | tf_op jit(solution)/shard_map/ppermute | solution.py:45
  52.2 1.2 collective-permute-done.7
  53.5 3.1 %collective-permute-start.8 = (f32[1,320,128]{2,1,0:T(8,128)S(1)}, f32[1,320,128]{2,1,0:T(8,128)S(1)}, u32[]{:S(2)}, u32[]{:S(2)}) collective-permute-start(f32[1,320,128]{2,1,0:T(8,128)S(1)} %constant_dynamic-slice_fusion.1), channel_id=1, source_target_pairs={{0,16},{8,24},{16,0},{24,8},{32,48},{40,56},{48,32},{56,40},{64,80... | collective-permute-start | bytes 491528 | tf_op jit(solution)/shard_map/ppermute | solution.py:45
  56.6 4.2 %collective-permute-done.8 = f32[1,320,128]{2,1,0:T(8,128)S(1)} collective-permute-done((f32[1,320,128]{2,1,0:T(8,128)S(1)}, f32[1,320,128]{2,1,0:T(8,128)S(1)}, u32[]{:S(2)}, u32[]{:S(2)}) %collective-permute-start.8) | collective-permute-done | bytes 163872 | tf_op jit(solution)/shard_map/ppermute | solution.py:45
  60.8 3.2 %collective-permute-start.9 = (f32[1,160,128]{2,1,0:T(8,128)S(1)}, f32[1,160,128]{2,1,0:T(8,128)S(1)}, u32[]{:S(2)}, u32[]{:S(2)}) collective-permute-start(f32[1,160,128]{2,1,0:T(8,128)S(1)} %constant_dynamic-slice_fusion), channel_id=1, source_target_pairs={{0,64},{8,72},{16,80},{24,88},{32,96},{40,104},{48,112},{56,120},{... | collective-permute-start | bytes 245768 | tf_op jit(solution)/shard_map/ppermute | solution.py:45
  64.0 2.0 %collective-permute-done.9 = f32[1,160,128]{2,1,0:T(8,128)S(1)} collective-permute-done((f32[1,160,128]{2,1,0:T(8,128)S(1)}, f32[1,160,128]{2,1,0:T(8,128)S(1)}, u32[]{:S(2)}, u32[]{:S(2)}) %collective-permute-start.9) | collective-permute-done | bytes 81952 | tf_op jit(solution)/shard_map/ppermute | solution.py:45
  66.0 4.6 %collective-permute-start.10 = (f32[1,160,128]{2,1,0:T(8,128)S(1)}, f32[1,160,128]{2,1,0:T(8,128)S(1)}, u32[]{:S(2)}, u32[]{:S(2)}) collective-permute-start(f32[1,160,128]{2,1,0:T(8,128)S(1)} %dynamic-slice_add_fusion.2), channel_id=1, source_target_pairs={{0,32},{8,40},{16,48},{24,56},{32,0},{40,8},{48,16},{56,24},{64,96... | collective-permute-start | bytes 245768 | tf_op jit(solution)/shard_map/ppermute | solution.py:34
  70.6 2.1 %collective-permute-done.10 = f32[1,160,128]{2,1,0:T(8,128)S(1)} collective-permute-done((f32[1,160,128]{2,1,0:T(8,128)S(1)}, f32[1,160,128]{2,1,0:T(8,128)S(1)}, u32[]{:S(2)}, u32[]{:S(2)}) %collective-permute-start.10) | collective-permute-done | bytes 81952 | tf_op jit(solution)/shard_map/ppermute | solution.py:34
  72.7 4.2 %collective-permute-start.11 = (f32[1,160,128]{2,1,0:T(8,128)S(1)}, f32[1,160,128]{2,1,0:T(8,128)S(1)}, u32[]{:S(2)}, u32[]{:S(2)}) collective-permute-start(f32[1,160,128]{2,1,0:T(8,128)S(1)} %add.103), channel_id=1, source_target_pairs={{0,128},{8,136},{16,144},{24,152},{32,160},{40,168},{48,176},{56,1... | collective-permute-start | bytes 245768 | tf_op jit(solution)/shard_map/ppermute | solution.py:34
  76.9 1.9 %collective-permute-done.11 = f32[1,160,128]{2,1,0:T(8,128)S(1)} collective-permute-done((f32[1,160,128]{2,1,0:T(8,128)S(1)}, f32[1,160,128]{2,1,0:T(8,128)S(1)}, u32[]{:S(2)}, u32[]{:S(2)}) %collective-permute-start.11) | collective-permute-done | bytes 81952 | tf_op jit(solution)/shard_map/ppermute | solution.py:34
  78.8 8.4 %collective-permute-start.12 = (f32[1,160,128]{2,1,0:T(8,128)S(1)}, f32[1,160,128]{2,1,0:T(8,128)S(1)}, u32[]{:S(2)}, u32[]{:S(2)}) collective-permute-start(f32[1,160,128]{2,1,0:T(8,128)S(1)} %add.104), channel_id=1, source_target_pairs={{0,256},{8,264},{16,272},{24,280},{32,288},{40,296},{48,304},{56,3... | collective-permute-start | bytes 245768 | tf_op jit(solution)/shard_map/ppermute | solution.py:34
  87.3 0.0 copy-start.3
  87.3 0.1 copy.22
  87.4 0.7 copy-done.3
  88.1 0.1 copy.26
  88.3 0.9 collective-permute-done.12
  89.2 2.9 %collective-permute-start.13 = (f32[1,160,128]{2,1,0:T(8,128)S(1)}, f32[1,160,128]{2,1,0:T(8,128)S(1)}, u32[]{:S(2)}, u32[]{:S(2)}) collective-permute-start(f32[1,160,128]{2,1,0:T(8,128)S(1)} %add.105), channel_id=1, source_target_pairs={{0,64},{8,72},{16,80},{24,88},{32,96},{40,104},{48,112},{56,120},{... | collective-permute-start | bytes 245768 | tf_op jit(solution)/shard_map/ppermute | solution.py:53
  92.1 0.2 divide_convert_fusion
  92.3 2.4 %collective-permute-start.3 = (bf16[2,192,32]{2,1,0:T(8,128)(2,1)S(1)}, bf16[2,192,32]{2,1,0:T(8,128)(2,1)S(1)}, u32[]{:S(2)}, u32[]{:S(2)}) collective-permute-start(bf16[2,192,32]{2,1,0:T(8,128)(2,1)S(1)} %get-tuple-element.14), channel_id=1, source_target_pairs={{0,1},{1,0},{2,3},{3,2},{4,5},{5,4},{6,7},{7,6},{8,9},{9,8},{10,11... | collective-permute-start | bytes 73736 | tf_op jit(solution)/shard_map/ppermute | solution.py:53
  94.8 0.8 collective-permute-done.13
  95.6 3.1 %collective-permute-start.14 = (f32[1,320,128]{2,1,0:T(8,128)S(1)}, f32[1,320,128]{2,1,0:T(8,128)S(1)}, u32[]{:S(2)}, u32[]{:S(2)}) collective-permute-start(f32[1,320,128]{2,1,0:T(8,128)S(1)} %pad_maximum_fusion.1), channel_id=1, source_target_pairs={{0,16},{8,24},{16,0},{24,8},{32,48},{40,56},{48,32},{56,40},{64,80... | collective-permute-start | bytes 491528 | tf_op jit(solution)/shard_map/ppermute | solution.py:53
  98.8 0.1 pad_maximum_fusion.3
  98.9 4.7 %collective-permute-start.4 = (bf16[2,192,64]{2,1,0:T(8,128)(2,1)S(1)}, bf16[2,192,64]{2,1,0:T(8,128)(2,1)S(1)}, u32[]{:S(2)}, u32[]{:S(2)}) collective-permute-start(bf16[2,192,64]{2,1,0:T(8,128)(2,1)S(1)} %pad_maximum_fusion.3), channel_id=1, source_target_pairs={{0,2},{1,3},{2,0},{3,1},{4,6},{5,7},{6,4},{7,5},{8,10},{9,11},{10,... | collective-permute-start | bytes 147464 | tf_op jit(solution)/shard_map/ppermute | solution.py:53
  103.6 0.0 collective-permute-done.14
  103.6 0.9 convolution_bitcast_fusion
  104.5 0.1 copy.40
  104.6 0.1 copy.41
  104.7 0.1 fusion.25
  104.8 0.1 copy.30
  105.0 3.3 %collective-permute-start.15 = (f32[1,257,128]{2,1,0:T(8,128)S(1)}, f32[1,257,128]{2,1,0:T(8,128)S(1)}, u32[]{:S(2)}, u32[]{:S(2)}) collective-permute-start(f32[1,257,128]{2,1,0:T(8,128)S(1)} %pad_maximum_fusion.2), channel_id=1, source_target_pairs={{0,1},{1,0},{2,3},{3,2},{4,5},{5,4},{6,7},{7,6},{8,9},{9,8},{10,11... | collective-permute-start | bytes 394760 | tf_op jit(solution)/shard_map/ppermute | solution.py:34
  108.3 0.1 broadcast_select_fusion.7
  108.4 2.6 %collective-permute-done.15 = f32[1,257,128]{2,1,0:T(8,128)S(1)} collective-permute-done((f32[1,257,128]{2,1,0:T(8,128)S(1)}, f32[1,257,128]{2,1,0:T(8,128)S(1)}, u32[]{:S(2)}, u32[]{:S(2)}) %collective-permute-start.15) | collective-permute-done | bytes 131616 | tf_op jit(solution)/shard_map/ppermute | solution.py:34
  111.0 2.5 %collective-permute-start.16 = (f32[1,257,128]{2,1,0:T(8,128)S(1)}, f32[1,257,128]{2,1,0:T(8,128)S(1)}, u32[]{:S(2)}, u32[]{:S(2)}) collective-permute-start(f32[1,257,128]{2,1,0:T(8,128)S(1)} %fusion.30), channel_id=1, source_target_pairs={{0,2},{1,3},{2,0},{3,1},{4,6},{5,7},{6,4},{7,5},{8,10},{9,11},{10,... | collective-permute-start | bytes 394760 | tf_op jit(solution)/shard_map/ppermute | solution.py:34
  113.5 0.1 pad_maximum_fusion.4
  113.6 5.7 %collective-permute-start.5 = (bf16[2,192,128]{2,1,0:T(8,128)(2,1)S(1)}, bf16[2,192,128]{2,1,0:T(8,128)(2,1)S(1)}, u32[]{:S(2)}, u32[]{:S(2)}) collective-permute-start(bf16[2,192,128]{2,1,0:T(8,128)(2,1)S(1)} %pad_maximum_fusion.4), channel_id=1, source_target_pairs={{0,4},{1,5},{2,6},{3,7},{4,0},{5,1},{6,2},{7,3},{8,12},{9,13},{10,... | collective-permute-start | bytes 294920 | tf_op jit(solution)/shard_map/ppermute | solution.py:53
  119.4 0.7 copy.36
  120.1 0.7 copy.37
  120.9 3.4 %collective-permute-start.17 = (f32[1,257,128]{2,1,0:T(8,128)S(1)}, f32[1,257,128]{2,1,0:T(8,128)S(1)}, u32[]{:S(2)}, u32[]{:S(2)}) collective-permute-start(f32[1,257,128]{2,1,0:T(8,128)S(1)} %add.107), channel_id=1, source_target_pairs={{0,4},{1,5},{2,6},{3,7},{4,0},{5,1},{6,2},{7,3},{8,12},{9,13},{10,... | collective-permute-start | bytes 394760 | tf_op jit(solution)/shard_map/ppermute | solution.py:34
  124.3 0.1 broadcast_select_fusion.9
  124.5 8.4 %collective-permute-done.17 = f32[1,257,128]{2,1,0:T(8,128)S(1)} collective-permute-done((f32[1,257,128]{2,1,0:T(8,128)S(1)}, f32[1,257,128]{2,1,0:T(8,128)S(1)}, u32[]{:S(2)}, u32[]{:S(2)}) %collective-permute-start.17) | collective-permute-done | bytes 131616 | tf_op jit(solution)/shard_map/ppermute | solution.py:34
  133.0 0.1 copy.42
  133.1 0.1 copy.33
  133.2 0.1 bitcast_select_fusion
  133.3 0.6 fusion.7
  134.7 0.0 copy-start.1
  134.7 0.5 fusion.4
  135.1 11.1 %collective-permute-start.18 = (bf16[1,320,256]{2,1,0:T(8,128)(2,1)S(1)}, bf16[1,320,256]{2,1,0:T(8,128)(2,1)S(1)}, u32[]{:S(2)}, u32[]{:S(2)}) collective-permute-start(bf16[1,320,256]{2,1,0:T(8,128)(2,1)S(1)} %fusion.4), channel_id=1, source_target_pairs={{0,8},{8,0},{16,24},{24,16},{32,40},{40,32},{48,56},{56,48},{64,72... | collective-permute-start | bytes 491528 | tf_op jit(solution)/shard_map/ppermute | solution.py:53
  146.3 1.1 fusion
  147.5 0.2 copy.34
  147.7 0.1 copy.35
  147.7 1.1 copy.38
  (37 shorter events, 0.6 us)
Async XLA Ops:
  0.6 1.4 copy-start
  2.4 7.9 %collective-permute-start = (f32[2,192,128]{2,1,0:T(8,128)S(1)}, f32[2,192,128]{2,1,0:T(8,128)S(1)}, u32[]{:S(2)}, u32[]{:S(2)}) collective-permute-start(f32[2,192,128]{2,1,0:T(8,128)S(1)} %constant_dynamic-slice_fusion.2), channel_id=1, source_target_pairs={{0,1},{1,0},{2,3},{3,2},{4,5},{5,4},{6,7},{7,6},{8,9},{9,8},{10,11... | collective-permute-start | bytes 589832 | tf_op jit(solution)/shard_map/ppermute | solution.py:45
  10.3 15.8 %collective-permute-start.1 = (f32[2,192,128]{2,1,0:T(8,128)S(1)}, f32[2,192,128]{2,1,0:T(8,128)S(1)}, u32[]{:S(2)}, u32[]{:S(2)}) collective-permute-start(f32[2,192,128]{2,1,0:T(8,128)S(1)} %dynamic-slice_add_fusion), channel_id=1, source_target_pairs={{0,2},{1,3},{2,0},{3,1},{4,6},{5,7},{6,4},{7,5},{8,10},{9,11},{10,... | collective-permute-start | bytes 589832 | tf_op jit(solution)/shard_map/ppermute | solution.py:34
  26.1 15.2 %collective-permute-start.2 = (f32[2,192,128]{2,1,0:T(8,128)S(1)}, f32[2,192,128]{2,1,0:T(8,128)S(1)}, u32[]{:S(2)}, u32[]{:S(2)}) collective-permute-start(f32[2,192,128]{2,1,0:T(8,128)S(1)} %add.86), channel_id=1, source_target_pairs={{0,4},{1,5},{2,6},{3,7},{4,0},{5,1},{6,2},{7,3},{8,12},{9,13},{10,... | collective-permute-start | bytes 589832 | tf_op jit(solution)/shard_map/ppermute | solution.py:34
  41.4 5.4 %collective-permute-start.6 = (bf16[2,192,128]{2,1,0:T(8,128)(2,1)S(1)}, bf16[2,192,128]{2,1,0:T(8,128)(2,1)S(1)}, u32[]{:S(2)}, u32[]{:S(2)}) collective-permute-start(bf16[2,192,128]{2,1,0:T(8,128)(2,1)S(1)} %get-tuple-element.12), channel_id=1, source_target_pairs={{0,1},{1,0},{2,3},{3,2},{4,5},{5,4},{6,7},{7,6},{8,9},{9,8},{10,11... | collective-permute-start | bytes 294920 | tf_op jit(solution)/shard_map/ppermute | solution.py:53
  47.1 6.3 %collective-permute-start.7 = (f32[1,320,256]{2,1,0:T(8,128)S(1)}, f32[1,320,256]{2,1,0:T(8,128)S(1)}, u32[]{:S(2)}, u32[]{:S(2)}) collective-permute-start(f32[1,320,256]{2,1,0:T(8,128)S(1)} %dynamic-slice_bitcast_fusion), channel_id=1, source_target_pairs={{0,8},{8,0},{16,24},{24,16},{32,40},{40,32},{48,56},{56,48},{64,72... | collective-permute-start | bytes 983048 | tf_op jit(solution)/shard_map/ppermute | solution.py:45
  53.5 7.3 %collective-permute-start.8 = (f32[1,320,128]{2,1,0:T(8,128)S(1)}, f32[1,320,128]{2,1,0:T(8,128)S(1)}, u32[]{:S(2)}, u32[]{:S(2)}) collective-permute-start(f32[1,320,128]{2,1,0:T(8,128)S(1)} %constant_dynamic-slice_fusion.1), channel_id=1, source_target_pairs={{0,16},{8,24},{16,0},{24,8},{32,48},{40,56},{48,32},{56,40},{64,80... | collective-permute-start | bytes 491528 | tf_op jit(solution)/shard_map/ppermute | solution.py:45
  60.8 5.2 %collective-permute-start.9 = (f32[1,160,128]{2,1,0:T(8,128)S(1)}, f32[1,160,128]{2,1,0:T(8,128)S(1)}, u32[]{:S(2)}, u32[]{:S(2)}) collective-permute-start(f32[1,160,128]{2,1,0:T(8,128)S(1)} %constant_dynamic-slice_fusion), channel_id=1, source_target_pairs={{0,64},{8,72},{16,80},{24,88},{32,96},{40,104},{48,112},{56,120},{... | collective-permute-start | bytes 245768 | tf_op jit(solution)/shard_map/ppermute | solution.py:45
  66.0 6.7 %collective-permute-start.10 = (f32[1,160,128]{2,1,0:T(8,128)S(1)}, f32[1,160,128]{2,1,0:T(8,128)S(1)}, u32[]{:S(2)}, u32[]{:S(2)}) collective-permute-start(f32[1,160,128]{2,1,0:T(8,128)S(1)} %dynamic-slice_add_fusion.2), channel_id=1, source_target_pairs={{0,32},{8,40},{16,48},{24,56},{32,0},{40,8},{48,16},{56,24},{64,96... | collective-permute-start | bytes 245768 | tf_op jit(solution)/shard_map/ppermute | solution.py:34
  72.7 6.1 %collective-permute-start.11 = (f32[1,160,128]{2,1,0:T(8,128)S(1)}, f32[1,160,128]{2,1,0:T(8,128)S(1)}, u32[]{:S(2)}, u32[]{:S(2)}) collective-permute-start(f32[1,160,128]{2,1,0:T(8,128)S(1)} %add.103), channel_id=1, source_target_pairs={{0,128},{8,136},{16,144},{24,152},{32,160},{40,168},{48,176},{56,1... | collective-permute-start | bytes 245768 | tf_op jit(solution)/shard_map/ppermute | solution.py:34
  78.8 8.5 %copy-start.2 = (f32[2,192,32]{1,2,0:T(8,128)S(1)}, f32[2,192,32]{1,2,0:T(8,128)}, u32[]{:S(2)}) copy-start(f32[2,192,32]{1,2,0:T(8,128)} %param.8) | copy-start | bytes 147460
  78.8 10.4 %collective-permute-start.12 = (f32[1,160,128]{2,1,0:T(8,128)S(1)}, f32[1,160,128]{2,1,0:T(8,128)S(1)}, u32[]{:S(2)}, u32[]{:S(2)}) collective-permute-start(f32[1,160,128]{2,1,0:T(8,128)S(1)} %add.104), channel_id=1, source_target_pairs={{0,256},{8,264},{16,272},{24,280},{32,288},{40,296},{48,304},{56,3... | collective-permute-start | bytes 245768 | tf_op jit(solution)/shard_map/ppermute | solution.py:34
  87.3 0.8 copy-start.3
  89.2 6.4 %collective-permute-start.13 = (f32[1,160,128]{2,1,0:T(8,128)S(1)}, f32[1,160,128]{2,1,0:T(8,128)S(1)}, u32[]{:S(2)}, u32[]{:S(2)}) collective-permute-start(f32[1,160,128]{2,1,0:T(8,128)S(1)} %add.105), channel_id=1, source_target_pairs={{0,64},{8,72},{16,80},{24,88},{32,96},{40,104},{48,112},{56,120},{... | collective-permute-start | bytes 245768 | tf_op jit(solution)/shard_map/ppermute | solution.py:53
  92.3 6.4 %collective-permute-start.3 = (bf16[2,192,32]{2,1,0:T(8,128)(2,1)S(1)}, bf16[2,192,32]{2,1,0:T(8,128)(2,1)S(1)}, u32[]{:S(2)}, u32[]{:S(2)}) collective-permute-start(bf16[2,192,32]{2,1,0:T(8,128)(2,1)S(1)} %get-tuple-element.14), channel_id=1, source_target_pairs={{0,1},{1,0},{2,3},{3,2},{4,5},{5,4},{6,7},{7,6},{8,9},{9,8},{10,11... | collective-permute-start | bytes 73736 | tf_op jit(solution)/shard_map/ppermute | solution.py:53
  95.6 8.0 %collective-permute-start.14 = (f32[1,320,128]{2,1,0:T(8,128)S(1)}, f32[1,320,128]{2,1,0:T(8,128)S(1)}, u32[]{:S(2)}, u32[]{:S(2)}) collective-permute-start(f32[1,320,128]{2,1,0:T(8,128)S(1)} %pad_maximum_fusion.1), channel_id=1, source_target_pairs={{0,16},{8,24},{16,0},{24,8},{32,48},{40,56},{48,32},{56,40},{64,80... | collective-permute-start | bytes 491528 | tf_op jit(solution)/shard_map/ppermute | solution.py:53
  98.9 9.4 %collective-permute-start.4 = (bf16[2,192,64]{2,1,0:T(8,128)(2,1)S(1)}, bf16[2,192,64]{2,1,0:T(8,128)(2,1)S(1)}, u32[]{:S(2)}, u32[]{:S(2)}) collective-permute-start(bf16[2,192,64]{2,1,0:T(8,128)(2,1)S(1)} %pad_maximum_fusion.3), channel_id=1, source_target_pairs={{0,2},{1,3},{2,0},{3,1},{4,6},{5,7},{6,4},{7,5},{8,10},{9,11},{10,... | collective-permute-start | bytes 147464 | tf_op jit(solution)/shard_map/ppermute | solution.py:53
  105.0 6.1 %collective-permute-start.15 = (f32[1,257,128]{2,1,0:T(8,128)S(1)}, f32[1,257,128]{2,1,0:T(8,128)S(1)}, u32[]{:S(2)}, u32[]{:S(2)}) collective-permute-start(f32[1,257,128]{2,1,0:T(8,128)S(1)} %pad_maximum_fusion.2), channel_id=1, source_target_pairs={{0,1},{1,0},{2,3},{3,2},{4,5},{5,4},{6,7},{7,6},{8,9},{9,8},{10,11... | collective-permute-start | bytes 394760 | tf_op jit(solution)/shard_map/ppermute | solution.py:34
  111.0 9.8 %collective-permute-start.16 = (f32[1,257,128]{2,1,0:T(8,128)S(1)}, f32[1,257,128]{2,1,0:T(8,128)S(1)}, u32[]{:S(2)}, u32[]{:S(2)}) collective-permute-start(f32[1,257,128]{2,1,0:T(8,128)S(1)} %fusion.30), channel_id=1, source_target_pairs={{0,2},{1,3},{2,0},{3,1},{4,6},{5,7},{6,4},{7,5},{8,10},{9,11},{10,... | collective-permute-start | bytes 394760 | tf_op jit(solution)/shard_map/ppermute | solution.py:34
  113.6 10.7 %collective-permute-start.5 = (bf16[2,192,128]{2,1,0:T(8,128)(2,1)S(1)}, bf16[2,192,128]{2,1,0:T(8,128)(2,1)S(1)}, u32[]{:S(2)}, u32[]{:S(2)}) collective-permute-start(bf16[2,192,128]{2,1,0:T(8,128)(2,1)S(1)} %pad_maximum_fusion.4), channel_id=1, source_target_pairs={{0,4},{1,5},{2,6},{3,7},{4,0},{5,1},{6,2},{7,3},{8,12},{9,13},{10,... | collective-permute-start | bytes 294920 | tf_op jit(solution)/shard_map/ppermute | solution.py:53
  120.9 12.0 %collective-permute-start.17 = (f32[1,257,128]{2,1,0:T(8,128)S(1)}, f32[1,257,128]{2,1,0:T(8,128)S(1)}, u32[]{:S(2)}, u32[]{:S(2)}) collective-permute-start(f32[1,257,128]{2,1,0:T(8,128)S(1)} %add.107), channel_id=1, source_target_pairs={{0,4},{1,5},{2,6},{3,7},{4,0},{5,1},{6,2},{7,3},{8,12},{9,13},{10,... | collective-permute-start | bytes 394760 | tf_op jit(solution)/shard_map/ppermute | solution.py:34
  134.7 11.6 %copy-start.1 = (f32[2,192,320]{2,1,0:T(8,128)S(1)}, f32[2,192,320]{2,1,0:T(8,128)}, u32[]{:S(2)}) copy-start(f32[2,192,320]{2,1,0:T(8,128)} %param.6) | copy-start | bytes 1474564
  135.1 12.2 %collective-permute-start.18 = (bf16[1,320,256]{2,1,0:T(8,128)(2,1)S(1)}, bf16[1,320,256]{2,1,0:T(8,128)(2,1)S(1)}, u32[]{:S(2)}, u32[]{:S(2)}) collective-permute-start(bf16[1,320,256]{2,1,0:T(8,128)(2,1)S(1)} %fusion.4), channel_id=1, source_target_pairs={{0,8},{8,0},{16,24},{24,16},{32,40},{40,32},{48,56},{56,48},{64,72... | collective-permute-start | bytes 491528 | tf_op jit(solution)/shard_map/ppermute | solution.py:53

commit v13 on v10

--- a/solution.py
+++ b/solution.py
@@ -130,8 +130,9 @@
     cross = gram * (factor * factor)[:, None, None]
     shaped = 1.5 * scaled - 0.5 * jnp.einsum("mdr,mrs->mds", scaled, cross, precision=highest)
     basis_own = (jnp.sqrt(D / rank_width) * shaped).astype(jnp.bfloat16)
-    basis_next = reverse_blocks(doubling_gather(basis_own, "fsdp", fsdp, stages[:1]), len(tp_bits), width)
-    return (weight_next, first_next, second_next, jnp.transpose(basis_next, (1, 0, 2)))
+    basis_own = jnp.transpose(reverse_blocks(basis_own, len(tp_bits), width), (1, 0, 2))
+    basis_next = doubling_gather(basis_own, "fsdp", fsdp, [(0, 1)])
+    return (weight_next, first_next, second_next, basis_next)
 
 
 def solution(mesh):

time: 151 us -> 151 us (level)
  no operation moved by 1% of the time
where the time goes in v13:
time: 151 us; the launch traced here: 149 us
  starting transfers between devices  92.5 us (61%)
  waiting for transfers between devices  44.2 us (29%)
  local copies, waits for them, and re-layouts  5.67 us (4%)
  matrix products  3 us (2%)
  other arithmetic  2.03 us (1%)
  between operations  1.94 us (1%)
    ppermute x8, starting transfers between devices, butterfly_sum(): value = value + lax.ppermute(value, axis, partner_perm(size, bit))  47.3 us
    ppermute x7, starting transfers between devices, doubling_gather(): other = lax.ppermute(value, axis, partner_perm(size, bit))  30.7 us
    ppermute x8, waiting for transfers between devices, butterfly_sum(): value = value + lax.ppermute(value, axis, partner_perm(size, bit))  27.4 us
    ppermute x4, starting transfers between devices, halving_scatter(): value = keep + lax.ppermute(send, axis, partner_perm(size, bit))  14.5 us
    ppermute x4, waiting for transfers between devices, halving_scatter(): value = keep + lax.ppermute(send, axis, partner_perm(size, bit))  10.3 us
    ppermute x7, waiting for transfers between devices, doubling_gather(): other = lax.ppermute(value, axis, partner_perm(size, bit))  6.55 us
    unnamed x17, local copies, waits for them, and re-layouts  5.12 us
  transfers between devices with their start and end apart: 19, of which 15 were waited for; matrix products, arithmetic and copies ran while one was open for 3% of the time, Pallas kernels for 0%

profile of v13, /device:TPU:1, one launch (start us, length us, event | category | flops | bytes accessed | tf_op | source)
XLA Modules:
  0.0 149.4 jit_solution(3533437882545132654)
XLA Ops:
  0.6 0.0 copy-start
  0.7 1.3 copy.23
  2.0 0.1 copy.24
  2.1 0.3 fusion.34
  2.4 4.8 %collective-permute-start = (f32[2,192,128]{2,1,0:T(8,128)S(1)}, f32[2,192,128]{2,1,0:T(8,128)S(1)}, u32[]{:S(2)}, u32[]{:S(2)}) collective-permute-start(f32[2,192,128]{2,1,0:T(8,128)S(1)} %constant_dynamic-slice_fusion.2), channel_id=1, source_target_pairs={{0,1},{1,0},{2,3},{3,2},{4,5},{5,4},{6,7},{7,6},{8,9},{9,8},{10,11... | collective-permute-start | bytes 589832 | tf_op jit(solution)/shard_map/ppermute | solution.py:45
  7.3 3.0 %collective-permute-done = f32[2,192,128]{2,1,0:T(8,128)S(1)} collective-permute-done((f32[2,192,128]{2,1,0:T(8,128)S(1)}, f32[2,192,128]{2,1,0:T(8,128)S(1)}, u32[]{:S(2)}, u32[]{:S(2)}) %collective-permute-start) | collective-permute-done | bytes 196640 | tf_op jit(solution)/shard_map/ppermute | solution.py:45
  10.3 11.3 %collective-permute-start.1 = (f32[2,192,128]{2,1,0:T(8,128)S(1)}, f32[2,192,128]{2,1,0:T(8,128)S(1)}, u32[]{:S(2)}, u32[]{:S(2)}) collective-permute-start(f32[2,192,128]{2,1,0:T(8,128)S(1)} %dynamic-slice_add_fusion), channel_id=1, source_target_pairs={{0,4},{1,5},{2,6},{3,7},{4,0},{5,1},{6,2},{7,3},{8,12},{9,13},{10,... | collective-permute-start | bytes 589832 | tf_op jit(solution)/shard_map/ppermute | solution.py:34
  21.6 3.1 %collective-permute-done.1 = f32[2,192,128]{2,1,0:T(8,128)S(1)} collective-permute-done((f32[2,192,128]{2,1,0:T(8,128)S(1)}, f32[2,192,128]{2,1,0:T(8,128)S(1)}, u32[]{:S(2)}, u32[]{:S(2)}) %collective-permute-start.1) | collective-permute-done | bytes 196640 | tf_op jit(solution)/shard_map/ppermute | solution.py:34
  24.8 10.4 %collective-permute-start.2 = (f32[2,192,128]{2,1,0:T(8,128)S(1)}, f32[2,192,128]{2,1,0:T(8,128)S(1)}, u32[]{:S(2)}, u32[]{:S(2)}) collective-permute-start(f32[2,192,128]{2,1,0:T(8,128)S(1)} %add.86), channel_id=1, source_target_pairs={{0,2},{1,3},{2,0},{3,1},{4,6},{5,7},{6,4},{7,5},{8,10},{9,11},{10,... | collective-permute-start | bytes 589832 | tf_op jit(solution)/shard_map/ppermute | solution.py:34
  35.2 8.2 %collective-permute-done.2 = f32[2,192,128]{2,1,0:T(8,128)S(1)} collective-permute-done((f32[2,192,128]{2,1,0:T(8,128)S(1)}, f32[2,192,128]{2,1,0:T(8,128)S(1)}, u32[]{:S(2)}, u32[]{:S(2)}) %collective-permute-start.2) | collective-permute-done | bytes 196640 | tf_op jit(solution)/shard_map/ppermute | solution.py:34
  43.5 1.9 %collective-permute-start.6 = (bf16[2,192,128]{2,1,0:T(8,128)(2,1)S(1)}, bf16[2,192,128]{2,1,0:T(8,128)(2,1)S(1)}, u32[]{:S(2)}, u32[]{:S(2)}) collective-permute-start(bf16[2,192,128]{2,1,0:T(8,128)(2,1)S(1)} %get-tuple-element.12), channel_id=1, source_target_pairs={{0,1},{1,0},{2,3},{3,2},{4,5},{5,4},{6,7},{7,6},{8,9},{9,8},{10,11... | collective-permute-start | bytes 294920 | tf_op jit(solution)/shard_map/ppermute | solution.py:53
  45.4 3.8 %collective-permute-done.6 = bf16[2,192,128]{2,1,0:T(8,128)(2,1)S(1)} collective-permute-done((bf16[2,192,128]{2,1,0:T(8,128)(2,1)S(1)}, bf16[2,192,128]{2,1,0:T(8,128)(2,1)S(1)}, u32[]{:S(2)}, u32[]{:S(2)}) %collective-permute-start.6) | collective-permute-done | bytes 98336 | tf_op jit(solution)/shard_map/ppermute | solution.py:53
  49.3 0.3 fusion.13
  49.6 3.2 %collective-permute-start.7 = (f32[1,320,256]{2,1,0:T(8,128)S(1)}, f32[1,320,256]{2,1,0:T(8,128)S(1)}, u32[]{:S(2)}, u32[]{:S(2)}) collective-permute-start(f32[1,320,256]{2,1,0:T(8,128)S(1)} %dynamic-slice_bitcast_fusion), channel_id=1, source_target_pairs={{0,8},{8,0},{16,24},{24,16},{32,40},{40,32},{48,56},{56,48},{64,72... | collective-permute-start | bytes 983048 | tf_op jit(solution)/shard_map/ppermute | solution.py:45
  52.9 1.2 collective-permute-done.7
  54.2 3.2 %collective-permute-start.8 = (f32[1,320,128]{2,1,0:T(8,128)S(1)}, f32[1,320,128]{2,1,0:T(8,128)S(1)}, u32[]{:S(2)}, u32[]{:S(2)}) collective-permute-start(f32[1,320,128]{2,1,0:T(8,128)S(1)} %constant_dynamic-slice_fusion.1), channel_id=1, source_target_pairs={{0,16},{8,24},{16,0},{24,8},{32,48},{40,56},{48,32},{56,40},{64,80... | collective-permute-start | bytes 491528 | tf_op jit(solution)/shard_map/ppermute | solution.py:45
  57.3 4.1 %collective-permute-done.8 = f32[1,320,128]{2,1,0:T(8,128)S(1)} collective-permute-done((f32[1,320,128]{2,1,0:T(8,128)S(1)}, f32[1,320,128]{2,1,0:T(8,128)S(1)}, u32[]{:S(2)}, u32[]{:S(2)}) %collective-permute-start.8) | collective-permute-done | bytes 163872 | tf_op jit(solution)/shard_map/ppermute | solution.py:45
  61.5 3.2 %collective-permute-start.9 = (f32[1,160,128]{2,1,0:T(8,128)S(1)}, f32[1,160,128]{2,1,0:T(8,128)S(1)}, u32[]{:S(2)}, u32[]{:S(2)}) collective-permute-start(f32[1,160,128]{2,1,0:T(8,128)S(1)} %constant_dynamic-slice_fusion), channel_id=1, source_target_pairs={{0,64},{8,72},{16,80},{24,88},{32,96},{40,104},{48,112},{56,120},{... | collective-permute-start | bytes 245768 | tf_op jit(solution)/shard_map/ppermute | solution.py:45
  64.7 1.9 %collective-permute-done.9 = f32[1,160,128]{2,1,0:T(8,128)S(1)} collective-permute-done((f32[1,160,128]{2,1,0:T(8,128)S(1)}, f32[1,160,128]{2,1,0:T(8,128)S(1)}, u32[]{:S(2)}, u32[]{:S(2)}) %collective-permute-start.9) | collective-permute-done | bytes 81952 | tf_op jit(solution)/shard_map/ppermute | solution.py:45
  66.7 4.7 %collective-permute-start.10 = (f32[1,160,128]{2,1,0:T(8,128)S(1)}, f32[1,160,128]{2,1,0:T(8,128)S(1)}, u32[]{:S(2)}, u32[]{:S(2)}) collective-permute-start(f32[1,160,128]{2,1,0:T(8,128)S(1)} %dynamic-slice_add_fusion.2), channel_id=1, source_target_pairs={{0,32},{8,40},{16,48},{24,56},{32,0},{40,8},{48,16},{56,24},{64,96... | collective-permute-start | bytes 245768 | tf_op jit(solution)/shard_map/ppermute | solution.py:34
  71.4 2.0 %collective-permute-done.10 = f32[1,160,128]{2,1,0:T(8,128)S(1)} collective-permute-done((f32[1,160,128]{2,1,0:T(8,128)S(1)}, f32[1,160,128]{2,1,0:T(8,128)S(1)}, u32[]{:S(2)}, u32[]{:S(2)}) %collective-permute-start.10) | collective-permute-done | bytes 81952 | tf_op jit(solution)/shard_map/ppermute | solution.py:34
  73.4 4.3 %collective-permute-start.11 = (f32[1,160,128]{2,1,0:T(8,128)S(1)}, f32[1,160,128]{2,1,0:T(8,128)S(1)}, u32[]{:S(2)}, u32[]{:S(2)}) collective-permute-start(f32[1,160,128]{2,1,0:T(8,128)S(1)} %add.103), channel_id=1, source_target_pairs={{0,128},{8,136},{16,144},{24,152},{32,160},{40,168},{48,176},{56,1... | collective-permute-start | bytes 245768 | tf_op jit(solution)/shard_map/ppermute | solution.py:34
  77.7 1.8 %collective-permute-done.11 = f32[1,160,128]{2,1,0:T(8,128)S(1)} collective-permute-done((f32[1,160,128]{2,1,0:T(8,128)S(1)}, f32[1,160,128]{2,1,0:T(8,128)S(1)}, u32[]{:S(2)}, u32[]{:S(2)}) %collective-permute-start.11) | collective-permute-done | bytes 81952 | tf_op jit(solution)/shard_map/ppermute | solution.py:34
  79.5 8.5 %collective-permute-start.12 = (f32[1,160,128]{2,1,0:T(8,128)S(1)}, f32[1,160,128]{2,1,0:T(8,128)S(1)}, u32[]{:S(2)}, u32[]{:S(2)}) collective-permute-start(f32[1,160,128]{2,1,0:T(8,128)S(1)} %add.104), channel_id=1, source_target_pairs={{0,256},{8,264},{16,272},{24,280},{32,288},{40,296},{48,304},{56,3... | collective-permute-start | bytes 245768 | tf_op jit(solution)/shard_map/ppermute | solution.py:34
  88.0 0.1 copy.22
  88.2 0.7 copy-done.3
  88.9 0.1 copy.26
  89.0 0.9 collective-permute-done.12
  89.9 2.8 %collective-permute-start.13 = (f32[1,160,128]{2,1,0:T(8,128)S(1)}, f32[1,160,128]{2,1,0:T(8,128)S(1)}, u32[]{:S(2)}, u32[]{:S(2)}) collective-permute-start(f32[1,160,128]{2,1,0:T(8,128)S(1)} %add.105), channel_id=1, source_target_pairs={{0,64},{8,72},{16,80},{24,88},{32,96},{40,104},{48,112},{56,120},{... | collective-permute-start | bytes 245768 | tf_op jit(solution)/shard_map/ppermute | solution.py:53
  92.7 0.2 divide_convert_fusion
  93.0 1.9 %collective-permute-start.3 = (bf16[2,192,32]{2,1,0:T(8,128)(2,1)S(1)}, bf16[2,192,32]{2,1,0:T(8,128)(2,1)S(1)}, u32[]{:S(2)}, u32[]{:S(2)}) collective-permute-start(bf16[2,192,32]{2,1,0:T(8,128)(2,1)S(1)} %get-tuple-element.14), channel_id=1, source_target_pairs={{0,1},{1,0},{2,3},{3,2},{4,5},{5,4},{6,7},{7,6},{8,9},{9,8},{10,11... | collective-permute-start | bytes 73736 | tf_op jit(solution)/shard_map/ppermute | solution.py:53
  94.9 1.4 collective-permute-done.13
  96.4 3.1 %collective-permute-start.14 = (f32[1,320,128]{2,1,0:T(8,128)S(1)}, f32[1,320,128]{2,1,0:T(8,128)S(1)}, u32[]{:S(2)}, u32[]{:S(2)}) collective-permute-start(f32[1,320,128]{2,1,0:T(8,128)S(1)} %pad_maximum_fusion.1), channel_id=1, source_target_pairs={{0,16},{8,24},{16,0},{24,8},{32,48},{40,56},{48,32},{56,40},{64,80... | collective-permute-start | bytes 491528 | tf_op jit(solution)/shard_map/ppermute | solution.py:53
  99.5 0.1 pad_maximum_fusion.3
  99.6 2.0 %collective-permute-start.4 = (bf16[2,192,64]{2,1,0:T(8,128)(2,1)S(1)}, bf16[2,192,64]{2,1,0:T(8,128)(2,1)S(1)}, u32[]{:S(2)}, u32[]{:S(2)}) collective-permute-start(bf16[2,192,64]{2,1,0:T(8,128)(2,1)S(1)} %pad_maximum_fusion.3), channel_id=1, source_target_pairs={{0,2},{1,3},{2,0},{3,1},{4,6},{5,7},{6,4},{7,5},{8,10},{9,11},{10,... | collective-permute-start | bytes 147464 | tf_op jit(solution)/shard_map/ppermute | solution.py:53
  101.6 0.8 collective-permute-done.14
  102.5 0.9 convolution_bitcast_fusion
  103.4 0.1 copy.40
  103.5 0.1 copy.41
  103.6 0.1 fusion.24
  103.7 0.1 copy.30
  103.8 2.4 %collective-permute-start.15 = (f32[1,257,128]{2,1,0:T(8,128)S(1)}, f32[1,257,128]{2,1,0:T(8,128)S(1)}, u32[]{:S(2)}, u32[]{:S(2)}) collective-permute-start(f32[1,257,128]{2,1,0:T(8,128)S(1)} %pad_maximum_fusion.2), channel_id=1, source_target_pairs={{0,1},{1,0},{2,3},{3,2},{4,5},{5,4},{6,7},{7,6},{8,9},{9,8},{10,11... | collective-permute-start | bytes 394760 | tf_op jit(solution)/shard_map/ppermute | solution.py:34
  106.2 0.5 collective-permute-done.4
  106.7 0.1 broadcast_select_fusion.7
  106.8 2.7 %collective-permute-done.15 = f32[1,257,128]{2,1,0:T(8,128)S(1)} collective-permute-done((f32[1,257,128]{2,1,0:T(8,128)S(1)}, f32[1,257,128]{2,1,0:T(8,128)S(1)}, u32[]{:S(2)}, u32[]{:S(2)}) %collective-permute-start.15) | collective-permute-done | bytes 131616 | tf_op jit(solution)/shard_map/ppermute | solution.py:34
  109.6 3.4 %collective-permute-start.16 = (f32[1,257,128]{2,1,0:T(8,128)S(1)}, f32[1,257,128]{2,1,0:T(8,128)S(1)}, u32[]{:S(2)}, u32[]{:S(2)}) collective-permute-start(f32[1,257,128]{2,1,0:T(8,128)S(1)} %fusion.29), channel_id=1, source_target_pairs={{0,2},{1,3},{2,0},{3,1},{4,6},{5,7},{6,4},{7,5},{8,10},{9,11},{10,... | collective-permute-start | bytes 394760 | tf_op jit(solution)/shard_map/ppermute | solution.py:34
  113.0 0.1 pad_maximum_fusion.4
  113.1 6.9 %collective-permute-start.5 = (bf16[2,192,128]{2,1,0:T(8,128)(2,1)S(1)}, bf16[2,192,128]{2,1,0:T(8,128)(2,1)S(1)}, u32[]{:S(2)}, u32[]{:S(2)}) collective-permute-start(bf16[2,192,128]{2,1,0:T(8,128)(2,1)S(1)} %pad_maximum_fusion.4), channel_id=1, source_target_pairs={{0,4},{1,5},{2,6},{3,7},{4,0},{5,1},{6,2},{7,3},{8,12},{9,13},{10,... | collective-permute-start | bytes 294920 | tf_op jit(solution)/shard_map/ppermute | solution.py:53
  120.0 0.7 copy.36
  120.7 0.7 copy.37
  121.5 2.3 %collective-permute-start.17 = (f32[1,257,128]{2,1,0:T(8,128)S(1)}, f32[1,257,128]{2,1,0:T(8,128)S(1)}, u32[]{:S(2)}, u32[]{:S(2)}) collective-permute-start(f32[1,257,128]{2,1,0:T(8,128)S(1)} %add.107), channel_id=1, source_target_pairs={{0,4},{1,5},{2,6},{3,7},{4,0},{5,1},{6,2},{7,3},{8,12},{9,13},{10,... | collective-permute-start | bytes 394760 | tf_op jit(solution)/shard_map/ppermute | solution.py:34
  123.8 0.1 broadcast_select_fusion.9
  124.0 8.6 %collective-permute-done.17 = f32[1,257,128]{2,1,0:T(8,128)S(1)} collective-permute-done((f32[1,257,128]{2,1,0:T(8,128)S(1)}, f32[1,257,128]{2,1,0:T(8,128)S(1)}, u32[]{:S(2)}, u32[]{:S(2)}) %collective-permute-start.17) | collective-permute-done | bytes 131616 | tf_op jit(solution)/shard_map/ppermute | solution.py:34
  132.6 0.1 copy.42
  132.7 0.1 copy.33
  132.8 0.1 bitcast_select_fusion
  132.9 0.6 fusion.6
  134.3 0.5 fusion.3
  134.8 0.2 copy.34
  135.0 12.1 %collective-permute-start.18 = (bf16[320,1,256]{0,2,1:T(8,128)(2,1)S(1)}, bf16[320,1,256]{0,2,1:T(8,128)(2,1)S(1)}, u32[]{:S(2)}, u32[]{:S(2)}) collective-permute-start(bf16[320,1,256]{0,2,1:T(8,128)(2,1)S(1)} %bitcast.39), channel_id=1, source_target_pairs={{0,8},{8,0},{16,24},{24,16},{32,40},{40,32},{48,56},{56,48},{64,72... | collective-permute-start | bytes 491528 | tf_op jit(solution)/shard_map/ppermute | solution.py:53
  147.1 1.1 fusion
  148.1 0.1 broadcast_select_fusion.1
  148.2 0.1 pad_maximum_fusion
  148.3 1.1 copy.38
  (37 shorter events, 0.5 us)
Async XLA Ops:
  0.6 1.4 copy-start
  2.4 7.9 %collective-permute-start = (f32[2,192,128]{2,1,0:T(8,128)S(1)}, f32[2,192,128]{2,1,0:T(8,128)S(1)}, u32[]{:S(2)}, u32[]{:S(2)}) collective-permute-start(f32[2,192,128]{2,1,0:T(8,128)S(1)} %constant_dynamic-slice_fusion.2), channel_id=1, source_target_pairs={{0,1},{1,0},{2,3},{3,2},{4,5},{5,4},{6,7},{7,6},{8,9},{9,8},{10,11... | collective-permute-start | bytes 589832 | tf_op jit(solution)/shard_map/ppermute | solution.py:45
  10.3 14.4 %collective-permute-start.1 = (f32[2,192,128]{2,1,0:T(8,128)S(1)}, f32[2,192,128]{2,1,0:T(8,128)S(1)}, u32[]{:S(2)}, u32[]{:S(2)}) collective-permute-start(f32[2,192,128]{2,1,0:T(8,128)S(1)} %dynamic-slice_add_fusion), channel_id=1, source_target_pairs={{0,4},{1,5},{2,6},{3,7},{4,0},{5,1},{6,2},{7,3},{8,12},{9,13},{10,... | collective-permute-start | bytes 589832 | tf_op jit(solution)/shard_map/ppermute | solution.py:34
  24.8 18.7 %collective-permute-start.2 = (f32[2,192,128]{2,1,0:T(8,128)S(1)}, f32[2,192,128]{2,1,0:T(8,128)S(1)}, u32[]{:S(2)}, u32[]{:S(2)}) collective-permute-start(f32[2,192,128]{2,1,0:T(8,128)S(1)} %add.86), channel_id=1, source_target_pairs={{0,2},{1,3},{2,0},{3,1},{4,6},{5,7},{6,4},{7,5},{8,10},{9,11},{10,... | collective-permute-start | bytes 589832 | tf_op jit(solution)/shard_map/ppermute | solution.py:34
  43.5 5.8 %collective-permute-start.6 = (bf16[2,192,128]{2,1,0:T(8,128)(2,1)S(1)}, bf16[2,192,128]{2,1,0:T(8,128)(2,1)S(1)}, u32[]{:S(2)}, u32[]{:S(2)}) collective-permute-start(bf16[2,192,128]{2,1,0:T(8,128)(2,1)S(1)} %get-tuple-element.12), channel_id=1, source_target_pairs={{0,1},{1,0},{2,3},{3,2},{4,5},{5,4},{6,7},{7,6},{8,9},{9,8},{10,11... | collective-permute-start | bytes 294920 | tf_op jit(solution)/shard_map/ppermute | solution.py:53
  49.6 4.5 %collective-permute-start.7 = (f32[1,320,256]{2,1,0:T(8,128)S(1)}, f32[1,320,256]{2,1,0:T(8,128)S(1)}, u32[]{:S(2)}, u32[]{:S(2)}) collective-permute-start(f32[1,320,256]{2,1,0:T(8,128)S(1)} %dynamic-slice_bitcast_fusion), channel_id=1, source_target_pairs={{0,8},{8,0},{16,24},{24,16},{32,40},{40,32},{48,56},{56,48},{64,72... | collective-permute-start | bytes 983048 | tf_op jit(solution)/shard_map/ppermute | solution.py:45
  54.2 7.3 %collective-permute-start.8 = (f32[1,320,128]{2,1,0:T(8,128)S(1)}, f32[1,320,128]{2,1,0:T(8,128)S(1)}, u32[]{:S(2)}, u32[]{:S(2)}) collective-permute-start(f32[1,320,128]{2,1,0:T(8,128)S(1)} %constant_dynamic-slice_fusion.1), channel_id=1, source_target_pairs={{0,16},{8,24},{16,0},{24,8},{32,48},{40,56},{48,32},{56,40},{64,80... | collective-permute-start | bytes 491528 | tf_op jit(solution)/shard_map/ppermute | solution.py:45
  61.5 5.2 %collective-permute-start.9 = (f32[1,160,128]{2,1,0:T(8,128)S(1)}, f32[1,160,128]{2,1,0:T(8,128)S(1)}, u32[]{:S(2)}, u32[]{:S(2)}) collective-permute-start(f32[1,160,128]{2,1,0:T(8,128)S(1)} %constant_dynamic-slice_fusion), channel_id=1, source_target_pairs={{0,64},{8,72},{16,80},{24,88},{32,96},{40,104},{48,112},{56,120},{... | collective-permute-start | bytes 245768 | tf_op jit(solution)/shard_map/ppermute | solution.py:45
  66.7 6.7 %collective-permute-start.10 = (f32[1,160,128]{2,1,0:T(8,128)S(1)}, f32[1,160,128]{2,1,0:T(8,128)S(1)}, u32[]{:S(2)}, u32[]{:S(2)}) collective-permute-start(f32[1,160,128]{2,1,0:T(8,128)S(1)} %dynamic-slice_add_fusion.2), channel_id=1, source_target_pairs={{0,32},{8,40},{16,48},{24,56},{32,0},{40,8},{48,16},{56,24},{64,96... | collective-permute-start | bytes 245768 | tf_op jit(solution)/shard_map/ppermute | solution.py:34
  73.4 6.1 %collective-permute-start.11 = (f32[1,160,128]{2,1,0:T(8,128)S(1)}, f32[1,160,128]{2,1,0:T(8,128)S(1)}, u32[]{:S(2)}, u32[]{:S(2)}) collective-permute-start(f32[1,160,128]{2,1,0:T(8,128)S(1)} %add.103), channel_id=1, source_target_pairs={{0,128},{8,136},{16,144},{24,152},{32,160},{40,168},{48,176},{56,1... | collective-permute-start | bytes 245768 | tf_op jit(solution)/shard_map/ppermute | solution.py:34
  79.5 8.5 %copy-start.2 = (f32[2,192,32]{1,2,0:T(8,128)S(1)}, f32[2,192,32]{1,2,0:T(8,128)}, u32[]{:S(2)}) copy-start(f32[2,192,32]{1,2,0:T(8,128)} %param.8) | copy-start | bytes 147460
  79.5 10.4 %collective-permute-start.12 = (f32[1,160,128]{2,1,0:T(8,128)S(1)}, f32[1,160,128]{2,1,0:T(8,128)S(1)}, u32[]{:S(2)}, u32[]{:S(2)}) collective-permute-start(f32[1,160,128]{2,1,0:T(8,128)S(1)} %add.104), channel_id=1, source_target_pairs={{0,256},{8,264},{16,272},{24,280},{32,288},{40,296},{48,304},{56,3... | collective-permute-start | bytes 245768 | tf_op jit(solution)/shard_map/ppermute | solution.py:34
  88.0 0.8 copy-start.3
  89.9 6.4 %collective-permute-start.13 = (f32[1,160,128]{2,1,0:T(8,128)S(1)}, f32[1,160,128]{2,1,0:T(8,128)S(1)}, u32[]{:S(2)}, u32[]{:S(2)}) collective-permute-start(f32[1,160,128]{2,1,0:T(8,128)S(1)} %add.105), channel_id=1, source_target_pairs={{0,64},{8,72},{16,80},{24,88},{32,96},{40,104},{48,112},{56,120},{... | collective-permute-start | bytes 245768 | tf_op jit(solution)/shard_map/ppermute | solution.py:53
  93.0 6.5 %collective-permute-start.3 = (bf16[2,192,32]{2,1,0:T(8,128)(2,1)S(1)}, bf16[2,192,32]{2,1,0:T(8,128)(2,1)S(1)}, u32[]{:S(2)}, u32[]{:S(2)}) collective-permute-start(bf16[2,192,32]{2,1,0:T(8,128)(2,1)S(1)} %get-tuple-element.14), channel_id=1, source_target_pairs={{0,1},{1,0},{2,3},{3,2},{4,5},{5,4},{6,7},{7,6},{8,9},{9,8},{10,11... | collective-permute-start | bytes 73736 | tf_op jit(solution)/shard_map/ppermute | solution.py:53
  96.4 6.1 %collective-permute-start.14 = (f32[1,320,128]{2,1,0:T(8,128)S(1)}, f32[1,320,128]{2,1,0:T(8,128)S(1)}, u32[]{:S(2)}, u32[]{:S(2)}) collective-permute-start(f32[1,320,128]{2,1,0:T(8,128)S(1)} %pad_maximum_fusion.1), channel_id=1, source_target_pairs={{0,16},{8,24},{16,0},{24,8},{32,48},{40,56},{48,32},{56,40},{64,80... | collective-permute-start | bytes 491528 | tf_op jit(solution)/shard_map/ppermute | solution.py:53
  99.6 7.1 %collective-permute-start.4 = (bf16[2,192,64]{2,1,0:T(8,128)(2,1)S(1)}, bf16[2,192,64]{2,1,0:T(8,128)(2,1)S(1)}, u32[]{:S(2)}, u32[]{:S(2)}) collective-permute-start(bf16[2,192,64]{2,1,0:T(8,128)(2,1)S(1)} %pad_maximum_fusion.3), channel_id=1, source_target_pairs={{0,2},{1,3},{2,0},{3,1},{4,6},{5,7},{6,4},{7,5},{8,10},{9,11},{10,... | collective-permute-start | bytes 147464 | tf_op jit(solution)/shard_map/ppermute | solution.py:53
  103.8 5.8 %collective-permute-start.15 = (f32[1,257,128]{2,1,0:T(8,128)S(1)}, f32[1,257,128]{2,1,0:T(8,128)S(1)}, u32[]{:S(2)}, u32[]{:S(2)}) collective-permute-start(f32[1,257,128]{2,1,0:T(8,128)S(1)} %pad_maximum_fusion.2), channel_id=1, source_target_pairs={{0,1},{1,0},{2,3},{3,2},{4,5},{5,4},{6,7},{7,6},{8,9},{9,8},{10,11... | collective-permute-start | bytes 394760 | tf_op jit(solution)/shard_map/ppermute | solution.py:34
  109.6 11.9 %collective-permute-start.16 = (f32[1,257,128]{2,1,0:T(8,128)S(1)}, f32[1,257,128]{2,1,0:T(8,128)S(1)}, u32[]{:S(2)}, u32[]{:S(2)}) collective-permute-start(f32[1,257,128]{2,1,0:T(8,128)S(1)} %fusion.29), channel_id=1, source_target_pairs={{0,2},{1,3},{2,0},{3,1},{4,6},{5,7},{6,4},{7,5},{8,10},{9,11},{10,... | collective-permute-start | bytes 394760 | tf_op jit(solution)/shard_map/ppermute | solution.py:34
  113.1 10.7 %collective-permute-start.5 = (bf16[2,192,128]{2,1,0:T(8,128)(2,1)S(1)}, bf16[2,192,128]{2,1,0:T(8,128)(2,1)S(1)}, u32[]{:S(2)}, u32[]{:S(2)}) collective-permute-start(bf16[2,192,128]{2,1,0:T(8,128)(2,1)S(1)} %pad_maximum_fusion.4), channel_id=1, source_target_pairs={{0,4},{1,5},{2,6},{3,7},{4,0},{5,1},{6,2},{7,3},{8,12},{9,13},{10,... | collective-permute-start | bytes 294920 | tf_op jit(solution)/shard_map/ppermute | solution.py:53
  121.5 11.1 %collective-permute-start.17 = (f32[1,257,128]{2,1,0:T(8,128)S(1)}, f32[1,257,128]{2,1,0:T(8,128)S(1)}, u32[]{:S(2)}, u32[]{:S(2)}) collective-permute-start(f32[1,257,128]{2,1,0:T(8,128)S(1)} %add.107), channel_id=1, source_target_pairs={{0,4},{1,5},{2,6},{3,7},{4,0},{5,1},{6,2},{7,3},{8,12},{9,13},{10,... | collective-permute-start | bytes 394760 | tf_op jit(solution)/shard_map/ppermute | solution.py:34
  134.8 12.3 %copy-start.1 = (f32[2,192,320]{2,1,0:T(8,128)S(1)}, f32[2,192,320]{2,1,0:T(8,128)}, u32[]{:S(2)}) copy-start(f32[2,192,320]{2,1,0:T(8,128)} %param.6) | copy-start | bytes 1474564
  135.0 13.2 %collective-permute-start.18 = (bf16[320,1,256]{0,2,1:T(8,128)(2,1)S(1)}, bf16[320,1,256]{0,2,1:T(8,128)(2,1)S(1)}, u32[]{:S(2)}, u32[]{:S(2)}) collective-permute-start(bf16[320,1,256]{0,2,1:T(8,128)(2,1)S(1)} %bitcast.39), channel_id=1, source_target_pairs={{0,8},{8,0},{16,24},{24,16},{32,40},{40,32},{48,56},{56,48},{64,72... | collective-permute-start | bytes 491528 | tf_op jit(solution)/shard_map/ppermute | solution.py:53
